TPU v7x, 128 devices: a whole 4x4x4 slice. The times are simulated.
128 devices in a mesh: seq: 32 (over x, z, core), tp: 4 (over y).
Axes of the slice: x: 4, y: 4, z: 4, core: 2. Of those that a mesh axis runs over, the one named last changes fastest.
Arguments:
- tokens: bfloat16 [8192, 2048], P('seq'), may hold values from -6 to 6
- norm_gain: float32 [2048], replicated, may hold values from 0.1 to 1.9
- qkv_weight: bfloat16 [2048, 4096], P(None, 'tp'), may hold values from -0.125 to 0.125
- conv_weight: float32 [4, 4096], P(None, 'tp'), may hold values from -3 to 3
- gate_down: bfloat16 [2048, 16], replicated, may hold values from -0.125 to 0.125
- gate_up: bfloat16 [16, 1024], P(None, 'tp'), may hold values from -6 to 6
- gate_bias: float32 [1024], P('tp'), may hold values from 0.3 to 8.5
- out_gate_weight: bfloat16 [2048, 2048], P(None, 'tp'), may hold values from -0.125 to 0.125
- head_gain: float32 [512], replicated, may hold values from 0.1 to 1.9
- out_weight: bfloat16 [2048, 2048], P('tp'), may hold values from -0.125 to 0.125
- final_gain: float32 [2048], replicated, may hold values from 0.1 to 1.9
- embedding: bfloat16 [32000, 2048], P(('seq', 'tp')), may hold values from -0.5 to 0.5
- lengths: int32 [8], replicated, may hold values from 1 to 4096, as said below
- packed_order: int32 [8], replicated, may hold values from 0 to 7, each once
Outputs:
- hidden: bfloat16 [8192, 2048], P('seq', 'tp')
- last_states: float32 [8, 4, 256, 512], P(None, 'tp')
- conv_edges: float32 [8, 3, 4096], P(None, None, 'tp')
- last_norms: float32 [8], replicated
- max_logits: float32 [8, 128], P(None, ('seq', 'tp'))
Inputs may be any that keep to these rules, and one draw needn't show every extreme that they name: Request r of the initial order has lengths[r] tokens; the lengths sum to 8192, the largest is 4096 and the smallest is 1 or 2. packed_order names every request once; the packed positions hold the tokens of request packed_order[0], then those of packed_order[1], and so on.
All inputs are finite; a program needn't handle non-finite values.
Results may differ from a plain program's by a relative error of at most 0.015.
Values may be sent and summed in bfloat16 or wider, within the bound.
No kernel may reach another device: no remote copies, remote signals or barrier semaphores. Data moves between devices by JAX's collectives and lax.ppermute only.
A program may use at most 128 MiB of HBM per device.

v0:
```python
from functools import partial

import jax
import jax.numpy as jnp
from jax import lax
from jax.sharding import PartitionSpec as P

DK = 256
DV = 512
KCONV = 4
BLOCK = 64


HIGHEST_PRECISION = lax.Precision.HIGHEST


def prefix(array, axis, combine, identity):
    peers, place = (lax.axis_size(axis), lax.axis_index(axis))
    everything = jax.tree.map(
        lambda part, kind: lax.all_gather(part.astype(kind), axis),
        array,
        (jnp.bfloat16, jnp.bfloat16),
    )
    start = jax.tree.map(
        lambda part, zero: jnp.broadcast_to(jnp.asarray(zero, part.dtype), part.shape),
        array,
        identity,
    )

    def hop(k, before):
        reached = k < place
        new = combine(
            before, jax.tree.map(lambda part, own: part[k].astype(own.dtype), everything, array)
        )
        return jax.tree.map(lambda a, b: jnp.where(reached, a, b), new, before)

    return lax.fori_loop(0, peers, hop, start)


def passed_along(array, axis, by):
    peers = lax.axis_size(axis)
    pairs = [(i, i + by) for i in range(peers) if 0 <= i + by < peers]
    return lax.ppermute(array, axis, pairs)


def segments(lengths, packed_order, positions):
    request_count = lengths.shape[0]
    select = (packed_order[:, None] == jnp.arange(request_count, dtype=jnp.int32)[None, :]).astype(
        jnp.int32
    )
    packed_len = jnp.sum(select * lengths[None, :], axis=1)
    end_points = jnp.cumsum(packed_len)
    starts = end_points - packed_len
    segment = jnp.sum((positions[:, None] >= starts[None, :]).astype(jnp.int32), axis=1) - 1
    last_index = jnp.sum(select * (end_points - 1)[:, None], axis=0)
    return (segment, last_index)


def causal_conv(padded, padded_segment, conv_weight, row_count):
    running = jnp.zeros((row_count, padded.shape[1]), jnp.float32)
    current = padded_segment[KCONV - 1 :]
    for offset in range(KCONV):
        window = padded[offset : offset + row_count]
        same_segment = (padded_segment[offset : offset + row_count] == current)[:, None]
        running = running + jnp.where(same_segment, window, 0.0) * conv_weight[offset]
    return running


def activate(convolved, head_count):
    shaped = convolved.reshape(convolved.shape[0], head_count, 2 * DK + DV)
    channel = jnp.arange(2 * DK + DV)
    return jnp.where(channel < 2 * DK, jax.nn.silu(shaped), shaped).astype(jnp.bfloat16)


def advance(carry_state, key_floats, values, cumulative, segment, segment_before):
    total_decay = cumulative[-1]
    same_tail = (segment == segment[-1])[:, None, None]
    scaled = jnp.where(same_tail, key_floats * jnp.exp(total_decay[None] - cumulative), 0.0).astype(
        jnp.bfloat16
    )
    added = jnp.einsum("jhc,jhv->hcv", scaled, values, preferred_element_type=jnp.float32)
    through = segment[-1] == segment_before
    return jnp.where(through, jnp.exp(total_decay)[:, :, None] * carry_state, 0.0) + added


def state_at_ends(
    end_states, carry_state, key_floats, values, cumulative, segment, segment_before, offset
):
    length = segment.shape[0]
    inside_block = (offset >= 0) & (offset < length)

    def add_ends(previous):
        end_row = jnp.clip(offset, 0, length - 1)
        end_decay = cumulative[end_row]
        end_segment = segment[end_row]
        indices = jnp.arange(length)
        allowed = (
            (indices[None, :] <= end_row[:, None]) & (segment[None, :] == end_segment[:, None])
        )[:, :, None, None]
        spread = jnp.where(allowed, end_decay[:, None] - cumulative[None], 0.0)
        weighted = jnp.where(allowed, key_floats[None] * jnp.exp(spread), 0.0).astype(jnp.bfloat16)
        within = jnp.einsum("rjhc,jhv->rhcv", weighted, values, preferred_element_type=jnp.float32)
        carried = (end_segment == segment_before)[:, None, None, None]
        reached = jnp.where(carried, jnp.exp(end_decay)[:, :, :, None] * carry_state[None], 0.0)
        return jnp.where(inside_block[:, None, None, None], within + reached, previous)

    def keep(previous):
        return previous

    return lax.cond(jnp.any(inside_block), add_ends, keep, end_states)


def block_step(last_index, carry, inputs):
    carry_state, end_states = carry
    queries, key_rows, values, decays, segment, segment_before, block_first = inputs
    cumulative = jnp.cumsum(decays, axis=0)
    length = segment.shape[0]
    indices = jnp.arange(length)
    causal = (indices[None, :] <= indices[:, None]) & (segment[None, :] == segment[:, None])
    allowed = causal[:, :, None, None]
    spread = jnp.where(allowed, cumulative[:, None] - cumulative[None, :], 0.0)
    weights = jnp.where(allowed, jnp.exp(spread), 0.0)
    query_rows = queries.astype(jnp.float32)
    key_floats = key_rows.astype(jnp.float32)
    scores = jnp.sum(query_rows[:, None] * key_floats[None, :] * weights, axis=-1).astype(
        jnp.bfloat16
    )
    inside = jnp.einsum("ijh,jhv->ihv", scores, values, preferred_element_type=jnp.float32)
    carried = (segment == segment_before)[:, None, None]
    outside = jnp.einsum(
        "ihc,hcv->ihv", query_rows * jnp.exp(cumulative), carry_state, precision=HIGHEST_PRECISION
    )
    output = inside + jnp.where(carried, outside, 0.0)
    new_state = advance(carry_state, key_floats, values, cumulative, segment, segment_before)
    end_states = state_at_ends(
        end_states,
        carry_state,
        key_floats,
        values,
        cumulative,
        segment,
        segment_before,
        last_index - block_first,
    )
    return ((new_state, end_states), output)


def state_only(carry_state, inputs):
    block_queries, block_keys, block_values, block_decays, block_segment, before, block_start = (
        inputs
    )
    cumulative = jnp.cumsum(block_decays, axis=0)
    return (
        advance(
            carry_state,
            block_keys.astype(jnp.float32),
            block_values,
            cumulative,
            block_segment,
            before,
        ),
        None,
    )


def head_output(attended, gate_out, head_gain):
    row_count, head_count, value_width = attended.shape
    mean_square = jnp.mean(attended * attended, axis=2, keepdims=True)
    gate_values = jax.nn.silu(
        gate_out.astype(jnp.float32).reshape(row_count, head_count, value_width)
    )
    gated = attended * lax.rsqrt(mean_square + 1e-05) * head_gain * gate_values
    return gated.reshape(row_count, head_count * value_width).astype(jnp.bfloat16)


def carry_in(decay_factor, local_state):

    def combine(earlier, later):
        return (earlier[0] * later[0], later[0][:, :, None] * earlier[1] + later[1])

    identity = (jnp.ones_like(decay_factor), jnp.zeros_like(local_state))
    result = prefix((decay_factor, local_state), "seq", combine, identity)
    return result[1]


def shards(
    tokens,
    norm_gain,
    qkv_weight,
    conv_weight,
    gate_down,
    gate_up,
    gate_bias,
    out_gate_weight,
    head_gain,
    out_weight,
    final_gain,
    embedding,
    lengths,
    packed_order,
):
    row_count = tokens.shape[0]
    head_count = out_weight.shape[0] // DV
    column_count = tokens.shape[1] // lax.axis_size("tp")
    start_row = lax.axis_index("seq") * row_count
    positions = start_row + jnp.arange(-(KCONV - 1), row_count, dtype=jnp.int32)
    segment_all, last_index = segments(lengths, packed_order, positions)
    segment = segment_all[KCONV - 1 :]
    segment_prior = segment_all[KCONV - 2]
    first_index = last_index - lengths + 1
    residual = tokens.astype(jnp.float32)
    normed = (
        residual
        * lax.rsqrt(jnp.mean(residual * residual, axis=1, keepdims=True) + 1e-06)
        * norm_gain
    ).astype(jnp.bfloat16)
    projected = jnp.dot(normed, qkv_weight, preferred_element_type=jnp.float32).astype(jnp.bfloat16)
    rim_rows = passed_along(projected[row_count - (KCONV - 1) :], "seq", 1)
    padded = jnp.concatenate([rim_rows, projected], axis=0)
    convolved = causal_conv(padded.astype(jnp.float32), segment_all, conv_weight, row_count)
    activated = activate(convolved, head_count)
    queries = activated[:, :, :DK]
    key_rows = activated[:, :, DK : 2 * DK]
    values = activated[:, :, 2 * DK :]
    lowrank = jnp.dot(normed, gate_down, preferred_element_type=jnp.float32)
    gate_logits = (
        jnp.dot(lowrank, gate_up.astype(jnp.float32), precision=HIGHEST_PRECISION) + gate_bias
    )
    decays = (jax.nn.log_sigmoid(gate_logits) / 16.0).reshape(row_count, head_count, DK)
    gate_out = jnp.dot(normed, out_gate_weight, preferred_element_type=jnp.float32).astype(
        jnp.bfloat16
    )
    block_count = row_count // BLOCK

    def split_blocks(array):
        return array.reshape((block_count, BLOCK) + array.shape[1:])

    segment_before = segment_all[KCONV - 2 : KCONV - 2 + row_count : BLOCK]
    block_first = start_row + jnp.arange(block_count, dtype=jnp.int32) * BLOCK
    block_inputs = (
        split_blocks(queries),
        split_blocks(key_rows),
        split_blocks(values),
        split_blocks(decays),
        split_blocks(segment),
        segment_before,
        block_first,
    )
    through_shard = segment[-1] == segment_prior
    empty_state = jnp.zeros((head_count, DK, DV), jnp.float32)
    empty_ends = jnp.zeros((lengths.shape[0], head_count, DK, DV), jnp.float32)
    stepper = partial(block_step, last_index)
    local_state, unused_steps = lax.scan(state_only, empty_state, block_inputs)
    decay_factor = jnp.where(through_shard, jnp.exp(jnp.sum(decays, axis=0)), 0.0)
    incoming = carry_in(decay_factor, local_state)
    (unused_state, end_states), attended = lax.scan(stepper, (incoming, empty_ends), block_inputs)
    attended = attended.reshape(row_count, head_count, DV)
    gated = head_output(attended, gate_out, head_gain)
    projected_out = jnp.dot(gated, out_weight, preferred_element_type=jnp.float32)
    summed = lax.psum_scatter(
        projected_out.astype(jnp.bfloat16), "tp", scatter_dimension=1, tiled=True
    ).astype(jnp.float32)
    column_start = lax.axis_index("tp") * column_count
    own_columns = lax.dynamic_slice_in_dim(residual, column_start, column_count, 1)
    hidden = (own_columns + summed).astype(jnp.bfloat16)
    owned_here = (last_index >= start_row) & (last_index < start_row + row_count)
    local_last = jnp.clip(last_index - start_row, 0, row_count - 1)
    last_rows = jnp.where(owned_here[:, None], hidden[local_last].astype(jnp.float32), 0.0)
    edge_list = []
    for offset in range(KCONV - 1):
        located = last_index - (KCONV - 2) + offset
        inside = owned_here & (located >= first_index)
        picked = padded[jnp.clip(located - start_row + KCONV - 1, 0, row_count + KCONV - 2)].astype(
            jnp.float32
        )
        edge_list.append(jnp.where(inside[:, None], picked, 0.0))
    conv_edges = jnp.stack(edge_list, axis=1)
    row_sums, conv_edges, last_states = (
        lax.psum(last_rows.astype(jnp.bfloat16), "seq").astype(jnp.float32),
        lax.psum(conv_edges.astype(jnp.bfloat16), "seq").astype(jnp.float32),
        lax.psum(end_states.astype(jnp.bfloat16), "seq").astype(jnp.float32),
    )
    full_rows = lax.all_gather(row_sums, "tp", axis=1, tiled=True)
    mean_square = jnp.mean(full_rows * full_rows, axis=1)
    last_norms = jnp.sqrt(mean_square)
    final_rows = (full_rows * lax.rsqrt(mean_square[:, None] + 1e-06) * final_gain).astype(
        jnp.bfloat16
    )
    logits = jnp.dot(final_rows, embedding.T, preferred_element_type=jnp.float32)
    max_logits = jnp.max(logits, axis=1, keepdims=True)
    return (hidden, last_states, conv_edges, last_norms, max_logits)


def solution(mesh):
    in_specs = (
        P("seq", None),
        P(),
        P(None, "tp"),
        P(None, "tp"),
        P(),
        P(None, "tp"),
        P("tp"),
        P(None, "tp"),
        P(),
        P("tp", None),
        P(),
        P(("seq", "tp"), None),
        P(),
        P(),
    )
    out_specs = (
        P("seq", "tp"),
        P(None, "tp", None, None),
        P(None, None, "tp"),
        P(),
        P(None, ("seq", "tp")),
    )
    return jax.shard_map(shards, mesh=mesh, in_specs=in_specs, out_specs=out_specs, check_vma=False)
```

profile of v0, /device:TPU:0, one launch (start us, length us, event | category | flops | bytes accessed | tf_op | source)
XLA Modules:
  0.0 476.7 jit_solution(16728195551736005816)
XLA Ops:
  7.2 1.6 multiply_reduce_fusion.1
  9.0 3.9 convolution_convert_fusion.1
  12.9 1.3 collective-permute-start
  14.8 1.7 fusion.70
  17.2 1.0 copy.52
  18.2 1.0 pad_maximum_fusion
  21.1 21.8 %while.43 = (s32[]{:T(128)}, f32[1,256,512]{2,1,0:T(8,128)S(1)}, s32[4,64]{1,0:T(4,128)S(1)}, s32[4]{0:T(128)S(1)}, f32[4,64,1,256]{3,2,1,0:T(1,128)}, /*index=5...) while((s32[]{:T(128)}, f32[1,256,512]{2,1,0:T(8,128)S(1)}, ...), condition=%wide.region_7.8_spmd.clone, body=%wide.region_5.7_spmd.clone.sunk | while | flops 18415684 | bytes 1417237 | solution.py:253
  25.3 1.2 fusion.123
  30.8 1.2 fusion.123
  36.2 1.2 fusion.123
  41.7 1.2 fusion.123
  45.5 26.3 %all-gather.2 = bf16[32,1,256]{2,1,0:T(2,128)(2,1)S(1)} all-gather(bf16[1,1,256]{2,1,0:T(2,128)(2,1)S(1)} %reshape.975), channel_id=2, replica_groups=mesh['seq'=32,'tp'=4] {'seq'}, dimensions={0}, use_global_device_ids=true | all-gather | bytes 16896 | tf_op jit(solution)/shard_map/all_gather | solution.py:20
  71.9 29.0 %all-gather.5.cloned.1.call-done = bf16[32,256,512]{2,1,0:T(8,128)(2,1)} async-done(((bf16[1,256,512]{2,1,0:T(8,128)(2,1)}), bf16[32,256,512]{2,1,0:T(8,128)(2,1)}) %all-gather.5.cloned.1.call-update) | async-done | bytes 8388624 | tf_op jit(solution)/shard_map/all_gather | solution.py:20
  101.0 36.2 %while.44 = (s32[]{:T(128)}, f32[1,256,512]{2,1,0:T(8,128)S(1)}, s32[]{:T(128)}, bf16[32,1,256]{2,1,0:T(2,128)(2,1)S(1)}, bf16[32,1,256,512]{3,2,1,0:T(8,128)(2,1)}, /*index=5*/s32[]{:T(128)}, s32[]{:T(128)}) while((s32[]{:T(128)}, f32[1,256,512]{2,1,0:T(8,128)S(1)}, s32[]{:T(128)}, bf16[32,1,256]{2,1,0:T(2,128)(2,1)S(1)}, ...), condition=%wide.region_9.10_spmd.clone, body=%wide.region_8.9_spmd.clone.sunk | while | flops 655620 | bytes 1313385 | solution.py:37
  101.0 1.1 fusion.124
  102.1 1.1 fusion.124
  103.2 1.1 fusion.124
  104.4 1.1 fusion.124
  105.5 1.1 fusion.124
  106.6 1.1 fusion.124
  107.7 1.1 fusion.124
  108.9 1.1 fusion.124
  110.0 1.1 fusion.124
  111.1 1.1 fusion.124
  112.3 1.1 fusion.124
  113.4 1.1 fusion.124
  114.5 1.1 fusion.124
  115.7 1.1 fusion.124
  116.8 1.1 fusion.124
  117.9 1.1 fusion.124
  119.1 1.1 fusion.124
  120.2 1.1 fusion.124
  121.3 1.1 fusion.124
  122.5 1.1 fusion.124
  123.6 1.1 fusion.124
  124.7 1.1 fusion.124
  125.9 1.1 fusion.124
  127.0 1.1 fusion.124
  128.1 1.1 fusion.124
  129.2 1.1 fusion.124
  130.4 1.1 fusion.124
  131.5 1.1 fusion.124
  132.6 1.1 fusion.124
  133.8 1.1 fusion.124
  134.9 1.1 fusion.124
  136.0 1.1 fusion.124
  137.1 1.5 broadcast_in_dim.240
  138.6 48.9 %while.42 = (s32[]{:T(128)}, f32[1,256,512]{2,1,0:T(8,128)S(1)}, bf16[8,1,256,512]{3,2,0,1:T(8,128)(2,1)}, f32[4,64,1,512]{3,1,2,0:T(8,128)}, s32[4,64]{1,0:T(4,...) while((s32[]{:T(128)}, f32[1,256,512]{2,1,0:T(8,128)S(1)}, ...), condition=%wide.region_17.18_spmd, body=%wide.region_11.17_spmd.sunk | while | flops 268659424 | bytes 8804605 | solution.py:256
  139.9 1.0 bitcast_multiply_fusion.3
  144.6 2.0 multiply_reduce_fusion.5
  152.1 1.0 bitcast_multiply_fusion.3
  156.8 2.0 multiply_reduce_fusion.5
  169.0 2.0 multiply_reduce_fusion.5
  181.3 2.0 multiply_reduce_fusion.5
  188.8 2.8 fusion.56
  191.6 1.7 convolution_convert_fusion
  193.3 2.8 convert_element_type.287
  198.2 102.0 %all-reduce.3.cloned.1.call-done = bf16[8,1,256,512]{3,2,1,0:T(8,128)(2,1)} async-done(((bf16[8,1,256,512]{3,2,1,0:T(8,128)(2,1)}), bf16[8,1,256,512]{3,2,1,0:T(8,128)(2,1)}) %all-reduce.3.cloned.1.call-update) | async-done | bytes 2097168 | tf_op jit(solution)/shard_map/psum | solution.py:281
  300.2 4.2 convert_element_type.304
  304.4 21.7 %reduce-scatter.2.cloned.1.call-done = bf16[256,512]{1,0:T(8,128)(2,1)} async-done(((bf16[256,2048]{1,0:T(8,128)(2,1)}), bf16[256,512]{1,0:T(8,128)(2,1)}) %reduce-scatter.2.cloned.1.call-update) | async-done | bytes 262160 | tf_op jit(solution)/shard_map/reduce_scatter | solution.py:260
  326.1 1.2 add_convert_fusion
  327.9 126.8 %all-reduce = (bf16[8,3,1024]{2,0,1:T(8,128)(2,1)S(1)}, bf16[8,512]{1,0:T(8,128)(2,1)S(1)}) all-reduce(bf16[8,3,1024]{2,0,1:T(8,128)(2,1)S(1)} %pad_maximum_fusion.1, bf16[8,512]{1,0:T(8,128)(2,1)S(1)} %select_convert_fusion.2), channel_id=1, replica_groups=mesh['seq'=32,'tp'=4] {'seq'}, use_global_device_ids=true, to_apply=%region_21.22 | all-reduce | flops 28672 | bytes 114688 | tf_op jit(solution)/shard_map/psum | solution.py:280
  454.8 11.9 %all_gather.16 = f32[8,2048]{1,0:T(8,128)S(1)} all-gather(f32[8,512]{1,0:T(8,128)S(1)} %convert_element_type.314), channel_id=1, replica_groups=mesh['seq'=32,'tp'=4] {'tp'}, dimensions={1}, use_global_device_ids=true | all-gather | bytes 81920 | tf_op jit(solution)/shard_map/all_gather | solution.py:283
  467.9 2.2 convolution_reduce_fusion
  (233 shorter events, 52.3 us)
Async XLA Ops:
  7.2 184.4 %copy-start = (bf16[512,2048]{1,0:T(8,128)(2,1)S(1)}, bf16[512,2048]{1,0:T(8,128)(2,1)}, u32[]{:S(2)}) copy-start(bf16[512,2048]{1,0:T(8,128)(2,1)} %param.31) | copy-start | bytes 6291460
  7.2 93.8 %all-gather.5.cloned.1.call-start = ((), (), s32[]{:S(2)}) async-start(), calls=%async_computation.3 | async-start | bytes 8650752 | tf_op jit(solution)/shard_map/all_gather | solution.py:20
  8.9 5.3 %copy-start.6 = (s32[8]{0:T(128)S(1)}, s32[8]{0:T(128)}, u32[]{:S(2)}) copy-start(s32[8]{0:T(128)} %param.34) | copy-start | bytes 100
  8.9 5.3 %copy-start.12 = (s32[8]{0:T(128)S(1)}, s32[8]{0:T(128)}, u32[]{:S(2)}) copy-start(s32[8]{0:T(128)} %param.35) | copy-start | bytes 100
  8.9 5.8 %copy-start.4 = (f32[4,1024]{1,0:T(4,128)S(1)}, f32[4,1024]{1,0:T(4,128)}, u32[]{:S(2)}) copy-start(f32[4,1024]{1,0:T(4,128)} %param.25) | copy-start | bytes 49156
  8.9 5.8 %copy-start.7 = (bf16[2048,16]{0,1:T(8,128)(2,1)S(1)}, bf16[2048,16]{0,1:T(8,128)(2,1)}, u32[]{:S(2)}) copy-start(bf16[2048,16]{0,1:T(8,128)(2,1)} %param.26) | copy-start | bytes 196612
  8.9 5.8 %copy-start.9 = (f32[2048]{0:T(1024)S(1)}, f32[2048]{0:T(1024)}, u32[]{:S(2)}) copy-start(f32[2048]{0:T(1024)} %param.23) | copy-start | bytes 24580
  8.9 7.5 %copy-start.8 = (bf16[16,256]{1,0:T(8,128)(2,1)S(1)}, bf16[16,256]{1,0:T(8,128)(2,1)}, u32[]{:S(2)}) copy-start(bf16[16,256]{1,0:T(8,128)(2,1)} %param.27) | copy-start | bytes 24580
  9.0 7.5 %copy-start.11 = (f32[256]{0:T(256)S(1)}, f32[256]{0:T(256)}, u32[]{:S(2)}) copy-start(f32[256]{0:T(256)} %param.28) | copy-start | bytes 3076
  12.9 5.3 %collective-permute-start = (bf16[3,1024]{1,0:T(4,128)(2,1)S(1)}, bf16[3,1024]{1,0:T(4,128)(2,1)S(1)}, u32[]{:S(2)}, u32[]{:S(2)}) collective-permute-start(bf16[3,1024]{1,0:T(4,128)(2,1)S(1)} %slice.111), channel_id=1, source_target_pairs={{0,4},{4,8},{8,12},{12,16},{16,20},{20,24},{24,28},{28,32},{32,36}... | collective-permute-start | bytes 18440 | tf_op jit(solution)/shard_map/ppermute | solution.py:43
  43.6 256.6 %all-reduce.3.cloned.1.call-start = ((), (), s32[]{:S(2)}) async-start(), calls=%async_computation.2 | async-start | bytes 4194304 | tf_op jit(solution)/shard_map/psum | solution.py:281
  187.5 1.0 copy-start.2
  187.5 1.2 copy-start.10
  187.6 138.5 %reduce-scatter.2.cloned.1.call-start = ((), (), s32[]{:S(2)}) async-start(), calls=%async_computation.1 | async-start | bytes 1310720 | tf_op jit(solution)/shard_map/reduce_scatter | solution.py:260
  193.3 2.9 copy-start.1
  198.2 269.8 %copy-start.5 = (f32[2048]{0:T(1024)S(1)}, f32[2048]{0:T(1024)}, u32[]{:S(2)}) copy-start(f32[2048]{0:T(1024)} %param.32) | copy-start | bytes 24580
  327.3 142.9 %copy-start.3 = (bf16[256,512]{1,0:T(8,128)(2,1)}, bf16[256,512]{1,0:T(8,128)(2,1)S(1)}, u32[]{:S(2)}) copy-start(bf16[256,512]{1,0:T(8,128)(2,1)S(1)} %add_convert_fusion) | copy-start | bytes 786436
Sparse Core Ops, SparseCore 0:
  43.7 57.1 all-gather.4
  187.7 112.4 all-reduce.2
  302.6 23.4 reduce-scatter.1
where the time goes:
time: 479 us; the launch traced here: 477 us
  blocking collectives  165 us (34%)
  waiting for transfers between devices  153 us (32%)
  other arithmetic  81 us (17%)
  matrix products  23.4 us (5%)
  local copies, waits for them, and re-layouts  23 us (5%)
  between operations  15.3 us (3%)
  loops' own time  14.8 us (3%)
    psum x1, blocking collectives, shards(): lax.psum(conv_edges.astype(jnp.bfloat16), 'seq').astype(jnp.float32)  127 us
    psum x1, waiting for transfers between devices, shards(): lax.psum(end_states.astype(jnp.bfloat16), 'seq').astype(jnp.float32)  102 us
    select_n x32, other arithmetic, hop(): return jax.tree.map(lambda a, b: jnp.where(reached, a, b), new, before)  34.9 us
    all_gather x1, waiting for transfers between devices, prefix(): lax.all_gather(part.astype(kind), axis)  29 us
    all_gather x1, blocking collectives, prefix(): lax.all_gather(part.astype(kind), axis)  26.3 us
    reduce_scatter x1, waiting for transfers between devices, shards(): lax.psum_scatter(projected_out.astype(jnp.bfloat16), 'tp', scatter_dimens...  21.7 us
    all_gather x1, blocking collectives, shards(): full_rows = lax.all_gather(row_sums, 'tp', axis=1, tiled=True)  11.9 us
    dynamic_slice x24, local copies, waits for them, and re-layouts, shards(): local_state, unused_steps = lax.scan(state_only, empty_state, block_inputs)  10.5 us
  transfers between devices with their start and end apart: 4, of which 3 were waited for; matrix products, arithmetic and copies ran while one was open for 4% of the time, Pallas kernels for 0%

commit v1 on v0

v1 whole, which is shorter than its diff:
```python
import jax
import jax.numpy as jnp
from jax import lax
from jax.sharding import PartitionSpec as P

DK = 256
DV = 512
KCONV = 4
BLOCK = 64


HIGHEST_PRECISION = lax.Precision.HIGHEST


def passed_along(array, axis, by):
    peers = lax.axis_size(axis)
    pairs = [(i, i + by) for i in range(peers) if 0 <= i + by < peers]
    return lax.ppermute(array, axis, pairs)


def butterfly_sum(array, axis):
    peers = lax.axis_size(axis)
    step = 1
    while step < peers:
        pairs = [(i, i ^ step) for i in range(peers)]
        array = array + lax.ppermute(array, axis, pairs)
        step *= 2
    return array


def state_prefix(decay_factor, local_state, axis):
    peers, place = lax.axis_size(axis), lax.axis_index(axis)
    decay = passed_along(decay_factor, axis, 1)
    state = passed_along(local_state.astype(jnp.bfloat16), axis, 1).astype(jnp.float32)
    step = 1
    while step < peers:
        earlier_decay = passed_along(decay, axis, step)
        earlier_state = passed_along(state.astype(jnp.bfloat16), axis, step).astype(jnp.float32)
        state = state + decay[..., None] * earlier_state
        decay = jnp.where(place >= step, decay * earlier_decay, decay)
        step *= 2
    return state


def segments(lengths, packed_order, positions):
    request_count = lengths.shape[0]
    select = (packed_order[:, None] == jnp.arange(request_count, dtype=jnp.int32)[None, :]).astype(
        jnp.int32
    )
    packed_len = jnp.sum(select * lengths[None, :], axis=1)
    end_points = jnp.cumsum(packed_len)
    starts = end_points - packed_len
    segment = jnp.sum((positions[:, None] >= starts[None, :]).astype(jnp.int32), axis=1) - 1
    last_index = jnp.sum(select * (end_points - 1)[:, None], axis=0)
    return (segment, last_index)


def causal_conv(padded, padded_segment, conv_weight, row_count):
    running = jnp.zeros((row_count, padded.shape[1]), jnp.float32)
    current = padded_segment[KCONV - 1 :]
    for offset in range(KCONV):
        window = padded[offset : offset + row_count]
        same_segment = (padded_segment[offset : offset + row_count] == current)[:, None]
        running = running + jnp.where(same_segment, window, 0.0) * conv_weight[offset]
    return running


def activate(convolved, head_count):
    shaped = convolved.reshape(convolved.shape[0], head_count, 2 * DK + DV)
    channel = jnp.arange(2 * DK + DV)
    return jnp.where(channel < 2 * DK, jax.nn.silu(shaped), shaped).astype(jnp.bfloat16)


def head_output(attended, gate_out, head_gain):
    row_count, head_count, value_width = attended.shape
    mean_square = jnp.mean(attended * attended, axis=2, keepdims=True)
    gate_values = jax.nn.silu(
        gate_out.astype(jnp.float32).reshape(row_count, head_count, value_width)
    )
    gated = attended * lax.rsqrt(mean_square + 1e-05) * head_gain * gate_values
    return gated.reshape(row_count, head_count * value_width).astype(jnp.bfloat16)


def shards(
    tokens,
    norm_gain,
    qkv_weight,
    conv_weight,
    gate_down,
    gate_up,
    gate_bias,
    out_gate_weight,
    head_gain,
    out_weight,
    final_gain,
    embedding,
    lengths,
    packed_order,
):
    row_count = tokens.shape[0]
    head_count = out_weight.shape[0] // DV
    tp_size = lax.axis_size("tp")
    tp_index = lax.axis_index("tp")
    column_count = tokens.shape[1] // tp_size
    request_count = lengths.shape[0]
    start_row = lax.axis_index("seq") * row_count
    positions = start_row + jnp.arange(-(KCONV - 1), row_count, dtype=jnp.int32)
    segment_all, last_index = segments(lengths, packed_order, positions)
    segment = segment_all[KCONV - 1 :]
    segment_prior = segment_all[KCONV - 2]
    first_index = last_index - lengths + 1
    residual = tokens.astype(jnp.float32)
    normed = (
        residual
        * lax.rsqrt(jnp.mean(residual * residual, axis=1, keepdims=True) + 1e-06)
        * norm_gain
    ).astype(jnp.bfloat16)
    projected = jnp.dot(normed, qkv_weight, preferred_element_type=jnp.float32).astype(jnp.bfloat16)
    rim_rows = passed_along(projected[row_count - (KCONV - 1) :], "seq", 1)
    padded = jnp.concatenate([rim_rows, projected], axis=0)
    convolved = causal_conv(padded.astype(jnp.float32), segment_all, conv_weight, row_count)
    activated = activate(convolved, head_count)
    lowrank = jnp.dot(normed, gate_down, preferred_element_type=jnp.float32)
    gate_logits = (
        jnp.dot(lowrank, gate_up.astype(jnp.float32), precision=HIGHEST_PRECISION) + gate_bias
    )
    decays = (jax.nn.log_sigmoid(gate_logits) / 16.0).reshape(row_count, head_count, DK)
    gate_out = jnp.dot(normed, out_gate_weight, preferred_element_type=jnp.float32).astype(
        jnp.bfloat16
    )

    offset = last_index - start_row
    owned_here = (offset >= 0) & (offset < row_count)
    edge_list = []
    for tap in range(KCONV - 1):
        located = last_index - (KCONV - 2) + tap
        inside = owned_here & (located >= first_index)
        picked = padded[jnp.clip(located - start_row + KCONV - 1, 0, row_count + KCONV - 2)].astype(
            jnp.float32
        )
        edge_list.append(jnp.where(inside[:, None], picked, 0.0))
    conv_edges = jnp.stack(edge_list, axis=1)

    block_count = row_count // BLOCK
    queries = activated[:, :, :DK].astype(jnp.float32).reshape(block_count, BLOCK, head_count, DK)
    key_rows = activated[:, :, DK : 2 * DK].astype(jnp.float32).reshape(
        block_count, BLOCK, head_count, DK
    )
    values = activated[:, :, 2 * DK :].reshape(block_count, BLOCK, head_count, DV)
    block_segment = segment.reshape(block_count, BLOCK)
    segment_before = segment_all[KCONV - 2 : KCONV - 2 + row_count : BLOCK]
    cumulative = jnp.cumsum(decays.reshape(block_count, BLOCK, head_count, DK), axis=1)
    indices = jnp.arange(BLOCK)
    causal = (indices[None, :] <= indices[:, None])[None] & (
        block_segment[:, None, :] == block_segment[:, :, None]
    )
    allowed = causal[:, :, :, None, None]
    spread = jnp.where(allowed, cumulative[:, :, None] - cumulative[:, None, :], 0.0)
    weights = jnp.where(allowed, jnp.exp(spread), 0.0)
    scores = jnp.sum(queries[:, :, None] * key_rows[:, None, :] * weights, axis=-1).astype(
        jnp.bfloat16
    )
    inside = jnp.einsum("bpqh,bqhv->bphv", scores, values, preferred_element_type=jnp.float32)

    same_tail = (block_segment == block_segment[:, -1:])[:, :, None, None]
    scaled = jnp.where(
        same_tail, key_rows * jnp.exp(cumulative[:, -1:] - cumulative), 0.0
    ).astype(jnp.bfloat16)
    added = jnp.einsum("bjhc,bjhv->bhcv", scaled, values, preferred_element_type=jnp.float32)
    through = block_segment[:, -1] == segment_before
    block_decay = jnp.exp(cumulative[:, -1])
    state = jnp.zeros((head_count, DK, DV), jnp.float32)
    prior = jnp.ones((head_count, DK), jnp.float32)
    states_before, priors = [], []
    for b in range(block_count):
        states_before.append(state)
        priors.append(prior)
        state = jnp.where(through[b], block_decay[b][:, :, None] * state, 0.0) + added[b]
        prior = prior * block_decay[b]
    states_before = jnp.stack(states_before)
    priors = jnp.stack(priors)
    local_state = state
    carried = (block_segment == segment_before[:, None])[:, :, None, None]
    outside = jnp.einsum(
        "bphc,bhcv->bphv", queries * jnp.exp(cumulative), states_before, precision=HIGHEST_PRECISION
    )
    attended = inside + jnp.where(carried, outside, 0.0)

    end_row = jnp.clip(offset, 0, row_count - 1)
    end_block, end_pos = end_row // BLOCK, end_row % BLOCK
    picks = jnp.arange(request_count)
    end_keys_rows = key_rows[end_block]
    end_values = values[end_block]
    end_cumulative = cumulative[end_block]
    end_segments = block_segment[end_block]
    end_decay = end_cumulative[picks, end_pos]
    end_segment = end_segments[picks, end_pos]
    end_allowed = (
        (indices[None, :] <= end_pos[:, None]) & (end_segments == end_segment[:, None])
    )[:, :, None, None]
    end_spread = jnp.where(end_allowed, end_decay[:, None] - end_cumulative, 0.0)
    end_weighted = jnp.where(end_allowed, end_keys_rows * jnp.exp(end_spread), 0.0).astype(
        jnp.bfloat16
    )
    within = jnp.einsum("rjhc,rjhv->rhcv", end_weighted, end_values, preferred_element_type=jnp.float32)
    end_carried = (end_segment == segment_before[end_block])[:, None, None, None]
    reached = jnp.where(end_carried, jnp.exp(end_decay)[:, :, :, None] * states_before[end_block], 0.0)
    local_ends = within + reached

    through_shard = segment[-1] == segment_prior
    decay_factor = jnp.where(through_shard, priors[-1] * block_decay[-1], 0.0)
    incoming = state_prefix(decay_factor, local_state, "seq")

    reach = jnp.exp(cumulative) * priors[:, None]
    from_before = (block_segment == segment_prior)[:, :, None, None]
    correction = jnp.einsum(
        "bphc,hcv->bphv",
        jnp.where(from_before, queries * reach, 0.0),
        incoming,
        precision=HIGHEST_PRECISION,
    )
    attended = (attended + correction).reshape(row_count, head_count, DV)
    end_reach = jnp.exp(end_decay) * priors[end_block]
    end_from_before = (end_segment == segment_prior)[:, None, None, None]
    end_states = local_ends + jnp.where(
        end_from_before, end_reach[:, :, :, None] * incoming[None], 0.0
    )
    end_states = jnp.where(owned_here[:, None, None, None], end_states, 0.0)
    state_width = head_count * DK * DV
    payload = jnp.concatenate(
        [end_states.reshape(request_count, state_width), conv_edges.reshape(request_count, -1)], axis=1
    )
    payload = lax.psum(payload.astype(jnp.bfloat16), "seq").astype(jnp.float32)
    last_states = payload[:, :state_width].reshape(end_states.shape)
    conv_edges = payload[:, state_width:].reshape(conv_edges.shape)

    gated = head_output(attended, gate_out, head_gain)
    partial = jnp.dot(gated, out_weight, preferred_element_type=jnp.float32).astype(jnp.bfloat16)
    pieces = partial.reshape(row_count, tp_size, column_count)
    arrived = [lax.dynamic_index_in_dim(pieces, tp_index, 1, keepdims=False)]
    for shift in range(1, tp_size):
        outgoing = lax.dynamic_index_in_dim(pieces, (tp_index + shift) % tp_size, 1, keepdims=False)
        arrived.append(
            lax.ppermute(outgoing, "tp", [(i, (i + shift) % tp_size) for i in range(tp_size)])
        )
    arrived = jnp.stack(arrived)
    summed = jnp.zeros((row_count, column_count), jnp.float32)
    for group in range(tp_size):
        summed = summed + lax.dynamic_index_in_dim(
            arrived, (tp_index - group) % tp_size, 0, keepdims=False
        ).astype(jnp.float32)
    column_start = tp_index * column_count
    own_columns = lax.dynamic_slice_in_dim(residual, column_start, column_count, 1)
    hidden = (own_columns + summed).astype(jnp.bfloat16)

    last_rows = jnp.where(owned_here[:, None], hidden[end_row], jnp.zeros((), jnp.bfloat16))
    placed = lax.dynamic_update_slice_in_dim(
        jnp.zeros((request_count, tokens.shape[1]), jnp.bfloat16), last_rows, column_start, 1
    )
    full_rows = butterfly_sum(butterfly_sum(placed, "seq"), "tp").astype(jnp.float32)
    mean_square = jnp.mean(full_rows * full_rows, axis=1)
    last_norms = jnp.sqrt(mean_square)
    final_rows = (full_rows * lax.rsqrt(mean_square[:, None] + 1e-06) * final_gain).astype(
        jnp.bfloat16
    )
    logits = jnp.dot(final_rows, embedding.T, preferred_element_type=jnp.float32)
    max_logits = jnp.max(logits, axis=1, keepdims=True)
    return (hidden, last_states, conv_edges, last_norms, max_logits)


def solution(mesh):
    in_specs = (
        P("seq", None),
        P(),
        P(None, "tp"),
        P(None, "tp"),
        P(),
        P(None, "tp"),
        P("tp"),
        P(None, "tp"),
        P(),
        P("tp", None),
        P(),
        P(("seq", "tp"), None),
        P(),
        P(),
    )
    out_specs = (
        P("seq", "tp"),
        P(None, "tp", None, None),
        P(None, None, "tp"),
        P(),
        P(None, ("seq", "tp")),
    )
    return jax.shard_map(shards, mesh=mesh, in_specs=in_specs, out_specs=out_specs, check_vma=False)
```

time: 479 us -> 296 us (0.62)
  blocking collectives: 165 us -> 0 us
  starting transfers between devices: 1.41 us -> 66.2 us
  waiting for transfers between devices: 153 us -> 103 us
  other arithmetic: 81 us -> 47.2 us
  local copies, waits for them, and re-layouts: 23 us -> 41 us
  loops' own time: 14.8 us -> 0 us
    psum x1 -> x0, blocking collectives: 127 us -> none  [shards(): lax.psum(conv_edges.astype(jnp.bfloat16), 'seq').astype(jnp.float32)]
    ppermute x1 -> x12, starting transfers between devices: 1.29 us -> 55.1 us  [passed_along(): return lax.ppermute(array, axis, pairs)]
    all_gather x2 -> x0, blocking collectives: 38.2 us -> none  [the longest x1 26.3 us: prefix(): lax.all_gather(part.astype(kind), axis)]
    psum x1, waiting for transfers between devices: 102 us -> 67.8 us  [shards(): payload = lax.psum(payload.astype(jnp.bfloat16), 'seq').astype(jnp.float32)]
    select_n x33 -> x8, other arithmetic: 34.9 us -> 2.82 us  [the longest x1 1.01 us: shards(): jnp.where(from_before, queries * reach, 0.0)]
    all_gather x1 -> x0, waiting for transfers between devices: 29 us -> none  [prefix(): lax.all_gather(part.astype(kind), axis)]
    ppermute x0 -> x10, waiting for transfers between devices: none -> 24.6 us  [the longest x7 24.6 us: butterfly_sum(): array = array + lax.ppermute(array, axis, pairs)]
    reduce_scatter x1 -> x0, waiting for transfers between devices: 21.7 us -> none  [shards(): lax.psum_scatter(projected_out.astype(jnp.bfloat16), 'tp', scatter_dimens...]
  transfers between devices with their start and end apart: 4 -> 23, of which waited for: 3 -> 13; matrix products, arithmetic and copies ran while one was open for 4% -> 24% of each run, Pallas kernels for 0% -> 0%
where the time goes in v1:
time: 296 us; the launch traced here: 294 us
  waiting for transfers between devices  103 us (35%)
  starting transfers between devices  66.2 us (22%)
  other arithmetic  47.2 us (16%)
  local copies, waits for them, and re-layouts  41 us (14%)
  matrix products  19.8 us (7%)
  between operations  16.5 us (6%)
    psum x1, waiting for transfers between devices, shards(): payload = lax.psum(payload.astype(jnp.bfloat16), 'seq').astype(jnp.float32)  67.8 us
    ppermute x12, starting transfers between devices, passed_along(): return lax.ppermute(array, axis, pairs)  55.1 us
    ppermute x7, waiting for transfers between devices, butterfly_sum(): array = array + lax.ppermute(array, axis, pairs)  24.6 us
    ppermute x12, waiting for transfers between devices, passed_along(): return lax.ppermute(array, axis, pairs)  10.5 us
    unnamed x115, local copies, waits for them, and re-layouts  9.94 us
    reduce_sum x1, other arithmetic, shards(): jnp.sum(queries[:, :, None] * key_rows[:, None, :] * weights, axis=-1)  7.85 us
  transfers between devices with their start and end apart: 23, of which 13 were waited for; matrix products, arithmetic and copies ran while one was open for 24% of the time, Pallas kernels for 0%

profile of v1, /device:TPU:0, one launch (start us, length us, event | category | flops | bytes accessed | tf_op | source)
XLA Modules:
  0.0 293.6 jit_solution(8515633158150943857)
XLA Ops:
  8.4 1.6 multiply_reduce_fusion.1
  10.8 1.7 fusion.70
  16.0 1.4 collective-permute-start.2
  17.4 3.5 %convolution_convert_fusion.1 = bf16[256,1024]{1,0:T(8,128)(2,1)S(1)} fusion(bf16[2048,1024]{1,0:T(8,128)(2,1)} %param.16, f32[2048]{0:T(1024)S(1)} %copy-done.49, f32[256]{0:T(256)S(1)} %add_rsqrt_fusion.1, bf16[256,2048]{1,0:T(8,128)(2,1)S(1)} %copy-done.4), kind=kOutput, calls=%fused_computation.23 | convolution fusion | flops 1076101120 | bytes 5776384 | tf_op jit(solution)/shard_map/dot_general | solution.py:118
  21.8 4.7 %collective-permute-start = (bf16[3,1024]{1,0:T(4,128)(2,1)S(1)}, bf16[3,1024]{1,0:T(4,128)(2,1)S(1)}, u32[]{:S(2)}, u32[]{:S(2)}) collective-permute-start(bf16[3,1024]{1,0:T(4,128)(2,1)S(1)} %slice.192), channel_id=1, source_target_pairs={{0,4},{4,8},{8,12},{12,16},{16,20},{20,24},{24,28},{28,32},{32,36}... | collective-permute-start | bytes 18440 | tf_op jit(solution)/shard_map/ppermute | solution.py:18
  28.1 1.2 broadcast_compare_fusion.2
  34.6 1.2 fusion.77
  38.4 2.3 gather_fusion.3
  40.8 1.3 gather_fusion.4
  42.0 1.3 pad_clamp_fusion.2
  43.9 1.9 collective-permute-start.4
  46.7 6.0 %collective-permute-start.6 = (f32[1,256]{1,0:T(1,128)S(1)}, f32[1,256]{1,0:T(1,128)S(1)}, u32[]{:S(2)}, u32[]{:S(2)}) collective-permute-start(f32[1,256]{1,0:T(1,128)S(1)} %broadcast_select_fusion.4), channel_id=1, source_target_pairs={{0,8},{4,12},{8,16},{12,20},{16,24},{20,28},{24,32},{28,36},{32,40... | collective-permute-start | bytes 3080 | tf_op jit(solution)/shard_map/ppermute | solution.py:18
  52.7 1.3 collective-permute-done.6
  53.9 5.8 %collective-permute-start.8 = (f32[1,256]{1,0:T(1,128)S(1)}, f32[1,256]{1,0:T(1,128)S(1)}, u32[]{:S(2)}, u32[]{:S(2)}) collective-permute-start(f32[1,256]{1,0:T(1,128)S(1)} %broadcast_select_fusion.3), channel_id=1, source_target_pairs={{0,16},{4,20},{8,24},{12,28},{16,32},{20,36},{24,40},{28,44},{32,4... | collective-permute-start | bytes 3080 | tf_op jit(solution)/shard_map/ppermute | solution.py:18
  59.8 1.6 convert_element_type.163
  61.4 8.3 %collective-permute-start.10 = (f32[1,256]{1,0:T(1,128)S(1)}, f32[1,256]{1,0:T(1,128)S(1)}, u32[]{:S(2)}, u32[]{:S(2)}) collective-permute-start(f32[1,256]{1,0:T(1,128)S(1)} %broadcast_select_fusion.2), channel_id=1, source_target_pairs={{0,32},{4,36},{8,40},{12,44},{16,48},{20,52},{24,56},{28,60},{32,6... | collective-permute-start | bytes 3080 | tf_op jit(solution)/shard_map/ppermute | solution.py:18
  70.3 1.7 copy.32
  72.6 2.0 pad_maximum_fusion.2
  76.3 2.9 fusion.14
  79.2 1.3 collective-permute-start.1
  80.5 7.9 %multiply_reduce_fusion = bf16[4,64,64]{2,1,0:T(8,128)(2,1)S(1)} fusion(f32[4,64,256]{2,1,0:T(8,128)S(1)} %bitcast.214, f32[4,64,256]{2,1,0:T(8,128)S(1)} %convert.22, f32[4,64,256]{2,1,0:T(8,128)S(1)} %bitcast.223, pred[4,64,64]{2,1,0:T(8,128)(4,1)S(1)} %compare_and_fusion), kind=kLoop, calls=%fused_computation.13 | loop fusion | flops 25149440 | bytes 835584 | tf_op jit(solution)/shard_map/reduce_sum | solution.py:160
  88.4 1.8 gather_fusion.10
  90.2 1.3 collective-permute-start.3
  92.3 1.8 gather_fusion.9
  94.1 1.8 gather_fusion.11
  96.8 3.4 %collective-permute-start.5 = (bf16[1,256,512]{2,1,0:T(8,128)(2,1)S(1)}, bf16[1,256,512]{2,1,0:T(8,128)(2,1)S(1)}, u32[]{:S(2)}, u32[]{:S(2)}) collective-permute-start(bf16[1,256,512]{2,1,0:T(8,128)(2,1)S(1)} %fusion.21), channel_id=1, source_target_pairs={{0,8},{4,12},{8,16},{12,20},{16,24},{20,28},{24,32},{28,36},{32,40... | collective-permute-start | bytes 786440 | tf_op jit(solution)/shard_map/ppermute | solution.py:18
  100.2 1.8 fusion.53
  102.0 3.9 %collective-permute-done.5 = bf16[1,256,512]{2,1,0:T(8,128)(2,1)S(1)} collective-permute-done((bf16[1,256,512]{2,1,0:T(8,128)(2,1)S(1)}, bf16[1,256,512]{2,1,0:T(8,128)(2,1)S(1)}, u32[]{:S(2)}, u32[]{:S(2)}) %collective-permute-start.5) | collective-permute-done | bytes 262176 | tf_op jit(solution)/shard_map/ppermute | solution.py:18
  106.1 7.5 %collective-permute-start.7 = (bf16[1,256,512]{2,1,0:T(8,128)(2,1)S(1)}, bf16[1,256,512]{2,1,0:T(8,128)(2,1)S(1)}, u32[]{:S(2)}, u32[]{:S(2)}) collective-permute-start(bf16[1,256,512]{2,1,0:T(8,128)(2,1)S(1)} %fusion.71), channel_id=1, source_target_pairs={{0,16},{4,20},{8,24},{12,28},{16,32},{20,36},{24,40},{28,44},{32,4... | collective-permute-start | bytes 786440 | tf_op jit(solution)/shard_map/ppermute | solution.py:18
  113.6 1.7 maximum_bitcast_fusion
  115.3 3.1 %collective-permute-done.7 = bf16[1,256,512]{2,1,0:T(8,128)(2,1)S(1)} collective-permute-done((bf16[1,256,512]{2,1,0:T(8,128)(2,1)S(1)}, bf16[1,256,512]{2,1,0:T(8,128)(2,1)S(1)}, u32[]{:S(2)}, u32[]{:S(2)}) %collective-permute-start.7) | collective-permute-done | bytes 262176 | tf_op jit(solution)/shard_map/ppermute | solution.py:18
  118.7 7.1 %collective-permute-start.9 = (bf16[1,256,512]{2,1,0:T(8,128)(2,1)S(1)}, bf16[1,256,512]{2,1,0:T(8,128)(2,1)S(1)}, u32[]{:S(2)}, u32[]{:S(2)}) collective-permute-start(bf16[1,256,512]{2,1,0:T(8,128)(2,1)S(1)} %fusion.23), channel_id=1, source_target_pairs={{0,32},{4,36},{8,40},{12,44},{16,48},{20,52},{24,56},{28,60},{32,6... | collective-permute-start | bytes 786440 | tf_op jit(solution)/shard_map/ppermute | solution.py:18
  125.9 2.3 fusion.5
  128.3 1.4 collective-permute-done.9
  130.7 6.4 %collective-permute-start.11 = (bf16[1,256,512]{2,1,0:T(8,128)(2,1)}, bf16[1,256,512]{2,1,0:T(8,128)(2,1)}, u32[]{:S(2)}, u32[]{:S(2)}) collective-permute-start(bf16[1,256,512]{2,1,0:T(8,128)(2,1)} %get-tuple-element.7), channel_id=1, source_target_pairs={{0,64},{4,68},{8,72},{12,76},{16,80},{20,84},{24,88},{28,92},{32,9... | collective-permute-start | bytes 786440 | tf_op jit(solution)/shard_map/ppermute | solution.py:18
  137.2 2.5 gather_fusion.2
  139.6 1.5 gather_fusion.5
  141.1 4.6 %gather_fusion.7 = f32[8,256,512]{2,1,0:T(8,128)} fusion(f32[4,256,512]{2,1,0:T(8,128)} %maximum_bitcast_fusion, s32[1024]{0:T(1024)} %copy-done.27), kind=kCustom, calls=%fused_computation.7 | custom fusion | bytes 8388640 | tf_op jit(solution)/shard_map/gather | solution.py:207
  146.7 1.2 fusion.3
  148.0 2.5 multiply_reduce_fusion.2
  150.6 2.8 fusion.18
  153.5 1.8 convolution_convert_fusion
  155.2 1.8 reshape.947
  157.1 3.0 %constant_dynamic-slice_fusion.3 = (bf16[256,1,512]{2,1,0:T(2,128)(2,1)}, bf16[256,1,512]{2,1,0:T(2,128)(2,1)S(1)}, bf16[256,1,512]{2,1,0:T(2,128)(2,1)S(1)}, bf16[256,1,512]{2,1,0:T(2,128)(2,1)S(1)}) fusion(bf16[256,4,512]{2,1,0:T(4,128)(2,1)S(1)} %reshape.947, s32[]{:T(128)S(6)} %select_n.406, s32[]{:T(128)S(6)} %select_n.410, s32[]{:T(128)S(6)} %select_n.408, ...), kind=kLoop, calls=%fused_computation.139 | loop fusion | bytes 2097168 | tf_op jit(solution)/shard_map/jit(dynamic_index_in_dim)/dynamic_slice | solution.py:240
  161.0 3.0 %collective-permute-start.14 = (bf16[256,512]{1,0:T(8,128)(2,1)}, bf16[256,512]{1,0:T(8,128)(2,1)}, u32[]{:S(2)}, u32[]{:S(2)}) collective-permute-start(bf16[256,512]{1,0:T(8,128)(2,1)} %bitcast.199), channel_id=1, source_target_pairs={{0,3},{1,0},{2,1},{3,2},{4,7},{5,4},{6,5},{7,6},{8,11},{9,8},{10,9... | collective-permute-start | bytes 786440 | tf_op jit(solution)/shard_map/ppermute | solution.py:244
  164.0 2.2 collective-permute-start.13
  167.4 1.9 fusion
  170.4 5.1 %pad_maximum_fusion = bf16[8,134144]{1,0:T(8,128)(2,1)} fusion(bf16[8,3072]{1,0:T(8,128)(2,1)S(1)} %bitcast.225, bf16[8,131072]{1,0:T(8,128)(2,1)S(1)} %bitcast.206), kind=kLoop, calls=%fused_computation.17 | loop fusion | flops 4292608 | bytes 4292608 | tf_op jit(solution)/shard_map/concatenate | solution.py:230
  175.6 1.3 pad_maximum_fusion.1
  176.9 1.2 fusion.15
  179.0 1.2 collective-permute-done.15
  180.5 3.9 %collective-permute-done.16 = bf16[8,2048]{1,0:T(8,128)(2,1)S(1)} collective-permute-done((bf16[8,2048]{1,0:T(8,128)(2,1)S(1)}, bf16[8,2048]{1,0:T(8,128)(2,1)S(1)}, u32[]{:S(2)}, u32[]{:S(2)}) %collective-permute-start.16) | collective-permute-done | bytes 32800 | tf_op jit(solution)/shard_map/ppermute | solution.py:26
  184.4 1.3 collective-permute-start.17
  185.7 4.2 %collective-permute-done.17 = bf16[8,2048]{1,0:T(8,128)(2,1)S(1)} collective-permute-done((bf16[8,2048]{1,0:T(8,128)(2,1)S(1)}, bf16[8,2048]{1,0:T(8,128)(2,1)S(1)}, u32[]{:S(2)}, u32[]{:S(2)}) %collective-permute-start.17) | collective-permute-done | bytes 32800 | tf_op jit(solution)/shard_map/ppermute | solution.py:26
  190.8 3.6 %collective-permute-done.18 = bf16[8,2048]{1,0:T(8,128)(2,1)S(1)} collective-permute-done((bf16[8,2048]{1,0:T(8,128)(2,1)S(1)}, bf16[8,2048]{1,0:T(8,128)(2,1)S(1)}, u32[]{:S(2)}, u32[]{:S(2)}) %collective-permute-start.18) | collective-permute-done | bytes 32800 | tf_op jit(solution)/shard_map/ppermute | solution.py:26
  194.5 5.5 %collective-permute-done.19 = bf16[8,2048]{1,0:T(8,128)(2,1)S(1)} collective-permute-done((bf16[8,2048]{1,0:T(8,128)(2,1)S(1)}, bf16[8,2048]{1,0:T(8,128)(2,1)S(1)}, u32[]{:S(2)}, u32[]{:S(2)}) %collective-permute-start.19) | collective-permute-done | bytes 32800 | tf_op jit(solution)/shard_map/ppermute | solution.py:26
  200.0 1.9 collective-permute-start.20
  201.8 2.1 collective-permute-done.20
  204.0 1.5 collective-permute-start.21
  205.4 4.0 %collective-permute-done.21 = bf16[8,2048]{1,0:T(8,128)(2,1)S(1)} collective-permute-done((bf16[8,2048]{1,0:T(8,128)(2,1)S(1)}, bf16[8,2048]{1,0:T(8,128)(2,1)S(1)}, u32[]{:S(2)}, u32[]{:S(2)}) %collective-permute-start.21) | collective-permute-done | bytes 32800 | tf_op jit(solution)/shard_map/ppermute | solution.py:26
  211.1 67.8 %all-reduce.2.cloned.1.call-done = bf16[8,134144]{1,0:T(8,128)(2,1)} async-done(((bf16[8,134144]{1,0:T(8,128)(2,1)}), bf16[8,134144]{1,0:T(8,128)(2,1)}) %all-reduce.2.cloned.1.call-update) | async-done | bytes 2146320 | tf_op jit(solution)/shard_map/psum | solution.py:233
  279.0 1.9 slice.209
  280.8 4.4 %copy.56 = f32[1,8,256,512]{3,2,1,0:T(8,128)} copy(f32[1,8,256,512]{3,1,2,0:T(8,128)S(1)} %bitcast.205) | data formatting | bytes 8388608
  285.3 1.4 slice.210
  (207 shorter events, 29.7 us)
Async XLA Ops:
  7.2 146.3 %copy-start = (bf16[512,2048]{1,0:T(8,128)(2,1)S(1)}, bf16[512,2048]{1,0:T(8,128)(2,1)}, u32[]{:S(2)}) copy-start(bf16[512,2048]{1,0:T(8,128)(2,1)} %param.23) | copy-start | bytes 6291460
  7.2 271.8 %all-reduce.2.cloned.1.call-start = ((), (), s32[]{:S(2)}) async-start(), calls=%async_computation | async-start | bytes 4292608 | tf_op jit(solution)/shard_map/psum | solution.py:233
  8.4 9.0 %copy-start.4 = (bf16[256,2048]{1,0:T(8,128)(2,1)S(1)}, bf16[256,2048]{1,0:T(8,128)(2,1)}, u32[]{:S(2)}) copy-start(bf16[256,2048]{1,0:T(8,128)(2,1)} %param.14) | copy-start | bytes 3145732
  8.4 9.0 %copy-start.49 = (f32[2048]{0:T(1024)S(1)}, f32[2048]{0:T(1024)}, u32[]{:S(2)}) copy-start(f32[2048]{0:T(1024)} %param.15) | copy-start | bytes 24580
  10.0 10.9 %copy-start.40 = (f32[256]{0:T(256)}, f32[256]{0:T(256)S(1)}, u32[]{:S(2)}) copy-start(f32[256]{0:T(256)S(1)} %add_rsqrt_fusion.1) | copy-start | bytes 3076
  14.1 61.6 %copy-start.7 = (f32[4,64,1,256]{3,2,1,0:T(1,128)}, f32[4,64,1,256]{3,2,1,0:T(1,128)S(1)}, u32[]{:S(2)}) copy-start(f32[4,64,1,256]{3,2,1,0:T(1,128)S(1)} %get-tuple-element.66) | copy-start | bytes 786436
  16.0 13.3 %copy-start.52 = (s32[8]{0:T(128)S(1)}, s32[8]{0:T(128)}, u32[]{:S(2)}) copy-start(s32[8]{0:T(128)} %param.27) | copy-start | bytes 100
  16.0 14.0 %copy-start.43 = (s32[8]{0:T(128)S(1)}, s32[8]{0:T(128)}, u32[]{:S(2)}) copy-start(s32[8]{0:T(128)} %param.26) | copy-start | bytes 100
  16.0 21.0 %copy-start.24 = (f32[4,1024]{1,0:T(4,128)S(1)}, f32[4,1024]{1,0:T(4,128)}, u32[]{:S(2)}) copy-start(f32[4,1024]{1,0:T(4,128)} %param.17) | copy-start | bytes 49156
  16.0 27.9 %collective-permute-start.2 = (f32[1,256]{1,0:T(1,128)}, f32[1,256]{1,0:T(1,128)S(1)}, u32[]{:S(2)}, u32[]{:S(2)}) collective-permute-start(f32[1,256]{1,0:T(1,128)} %get-tuple-element.9), channel_id=1, source_target_pairs={{0,4},{4,8},{8,12},{12,16},{16,20},{20,24},{24,28},{28,32},{32,36}... | collective-permute-start | bytes 3080 | tf_op jit(solution)/shard_map/ppermute | solution.py:18
  21.8 50.8 %collective-permute-start = (bf16[3,1024]{1,0:T(4,128)(2,1)S(1)}, bf16[3,1024]{1,0:T(4,128)(2,1)S(1)}, u32[]{:S(2)}, u32[]{:S(2)}) collective-permute-start(bf16[3,1024]{1,0:T(4,128)(2,1)S(1)} %slice.192), channel_id=1, source_target_pairs={{0,4},{4,8},{8,12},{12,16},{16,20},{20,24},{24,28},{28,32},{32,36}... | collective-permute-start | bytes 18440 | tf_op jit(solution)/shard_map/ppermute | solution.py:18
  30.7 30.7 %copy-start.27 = (s32[1024]{0:T(1024)}, s32[1024]{0:T(1024)S(1)}, u32[]{:S(2)}) copy-start(s32[1024]{0:T(1024)S(1)} %pad_clamp_fusion.4) | copy-start | bytes 12292
  31.9 44.4 %copy-start.28 = (f32[1,1,1,256]{3,2,1,0:T(1,128)}, f32[1,1,1,256]{3,2,1,0:T(1,128)S(1)}, u32[]{:S(2)}) copy-start(f32[1,1,1,256]{3,2,1,0:T(1,128)S(1)} %get-tuple-element.32) | copy-start | bytes 3076
  43.9 30.7 %copy-start.22 = (f32[1,256]{1,0:T(1,128)}, f32[1,256]{1,0:T(1,128)S(1)}, u32[]{:S(2)}) copy-start(f32[1,256]{1,0:T(1,128)S(1)} %collective-permute-done.2) | copy-start | bytes 3076
  43.9 2.7 collective-permute-start.4
  46.7 7.3 %collective-permute-start.6 = (f32[1,256]{1,0:T(1,128)S(1)}, f32[1,256]{1,0:T(1,128)S(1)}, u32[]{:S(2)}, u32[]{:S(2)}) collective-permute-start(f32[1,256]{1,0:T(1,128)S(1)} %broadcast_select_fusion.4), channel_id=1, source_target_pairs={{0,8},{4,12},{8,16},{12,20},{16,24},{20,28},{24,32},{28,36},{32,40... | collective-permute-start | bytes 3080 | tf_op jit(solution)/shard_map/ppermute | solution.py:18
  53.9 18.0 %copy-start.25 = (f32[1,256]{1,0:T(1,128)}, f32[1,256]{1,0:T(1,128)S(1)}, u32[]{:S(2)}) copy-start(f32[1,256]{1,0:T(1,128)S(1)} %broadcast_select_fusion.3) | copy-start | bytes 3076
  53.9 7.5 %collective-permute-start.8 = (f32[1,256]{1,0:T(1,128)S(1)}, f32[1,256]{1,0:T(1,128)S(1)}, u32[]{:S(2)}, u32[]{:S(2)}) collective-permute-start(f32[1,256]{1,0:T(1,128)S(1)} %broadcast_select_fusion.3), channel_id=1, source_target_pairs={{0,16},{4,20},{8,24},{12,28},{16,32},{20,36},{24,40},{28,44},{32,4... | collective-permute-start | bytes 3080 | tf_op jit(solution)/shard_map/ppermute | solution.py:18
  61.4 13.2 %copy-start.39 = (pred[1024]{0:T(1024)(128)(4,1)S(1)}, pred[1024]{0:T(1024)(128)(4,1)}, u32[]{:S(2)}) copy-start(pred[1024]{0:T(1024)(128)(4,1)} %iota_compare_fusion.3) | copy-start | bytes 3076
  61.4 14.1 %copy-start.30 = (f32[1,256]{1,0:T(1,128)}, f32[1,256]{1,0:T(1,128)S(1)}, u32[]{:S(2)}) copy-start(f32[1,256]{1,0:T(1,128)S(1)} %broadcast_select_fusion.2) | copy-start | bytes 3076
  61.4 10.6 %collective-permute-start.10 = (f32[1,256]{1,0:T(1,128)S(1)}, f32[1,256]{1,0:T(1,128)S(1)}, u32[]{:S(2)}, u32[]{:S(2)}) collective-permute-start(f32[1,256]{1,0:T(1,128)S(1)} %broadcast_select_fusion.2), channel_id=1, source_target_pairs={{0,32},{4,36},{8,40},{12,44},{16,48},{20,52},{24,56},{28,60},{32,6... | collective-permute-start | bytes 3080 | tf_op jit(solution)/shard_map/ppermute | solution.py:18
  76.3 12.1 %copy-start.1 = (f32[4,256,512]{2,1,0:T(8,128)}, f32[4,256,512]{2,1,0:T(8,128)S(1)}, u32[]{:S(2)}) copy-start(f32[4,256,512]{2,1,0:T(8,128)S(1)} %fusion.38) | copy-start | bytes 6291460
  79.2 11.1 %collective-permute-start.1 = (bf16[1,256,512]{2,1,0:T(8,128)(2,1)S(1)}, bf16[1,256,512]{2,1,0:T(8,128)(2,1)S(1)}, u32[]{:S(2)}, u32[]{:S(2)}) collective-permute-start(bf16[1,256,512]{2,1,0:T(8,128)(2,1)S(1)} %get-tuple-element.11), channel_id=1, source_target_pairs={{0,4},{4,8},{8,12},{12,16},{16,20},{20,24},{24,28},{28,32},{32,36}... | collective-permute-start | bytes 786440 | tf_op jit(solution)/shard_map/ppermute | solution.py:18
  80.5 16.1 %copy-start.23 = (f32[1,256]{1,0:T(1,128)S(1)}, f32[1,256]{1,0:T(1,128)}, u32[]{:S(2)}) copy-start(f32[1,256]{1,0:T(1,128)} %copy-done.22) | copy-start | bytes 3076
  80.5 19.6 %copy-start.29 = (f32[1,1,1,256]{3,2,1,0:T(1,128)S(1)}, f32[1,1,1,256]{3,2,1,0:T(1,128)}, u32[]{:S(2)}) copy-start(f32[1,1,1,256]{3,2,1,0:T(1,128)} %copy-done.28) | copy-start | bytes 3076
  88.4 25.2 %copy-start.47 = (f32[4]{0:T(128)S(1)}, f32[4]{0:T(128)}, u32[]{:S(2)}) copy-start(f32[4]{0:T(128)} %pad.13.clone) | copy-start | bytes 52
  90.2 6.4 %collective-permute-start.3 = (bf16[1,256,512]{2,1,0:T(8,128)(2,1)S(1)}, bf16[1,256,512]{2,1,0:T(8,128)(2,1)S(1)}, u32[]{:S(2)}, u32[]{:S(2)}) collective-permute-start(bf16[1,256,512]{2,1,0:T(8,128)(2,1)S(1)} %collective-permute-done.1), channel_id=1, source_target_pairs={{0,4},{4,8},{8,12},{12,16},{16,20},{20,24},{24,28},{28,32},{32,36}... | collective-permute-start | bytes 786440 | tf_op jit(solution)/shard_map/ppermute | solution.py:18
  95.9 17.7 %copy-start.11 = (f32[1,1,256,512]{3,2,1,0:T(8,128)S(1)}, f32[1,1,256,512]{3,2,1,0:T(8,128)}, u32[]{:S(2)}) copy-start(f32[1,1,256,512]{3,2,1,0:T(8,128)} %get-tuple-element.13) | copy-start | bytes 1572868
  96.8 9.1 %collective-permute-start.5 = (bf16[1,256,512]{2,1,0:T(8,128)(2,1)S(1)}, bf16[1,256,512]{2,1,0:T(8,128)(2,1)S(1)}, u32[]{:S(2)}, u32[]{:S(2)}) collective-permute-start(bf16[1,256,512]{2,1,0:T(8,128)(2,1)S(1)} %fusion.21), channel_id=1, source_target_pairs={{0,8},{4,12},{8,16},{12,20},{16,24},{20,28},{24,32},{28,36},{32,40... | collective-permute-start | bytes 786440 | tf_op jit(solution)/shard_map/ppermute | solution.py:18
  106.1 12.3 %copy-start.26 = (f32[1,256]{1,0:T(1,128)S(1)}, f32[1,256]{1,0:T(1,128)}, u32[]{:S(2)}) copy-start(f32[1,256]{1,0:T(1,128)} %copy-done.25) | copy-start | bytes 3076
  106.1 12.3 %collective-permute-start.7 = (bf16[1,256,512]{2,1,0:T(8,128)(2,1)S(1)}, bf16[1,256,512]{2,1,0:T(8,128)(2,1)S(1)}, u32[]{:S(2)}, u32[]{:S(2)}) collective-permute-start(bf16[1,256,512]{2,1,0:T(8,128)(2,1)S(1)} %fusion.71), channel_id=1, source_target_pairs={{0,16},{4,20},{8,24},{12,28},{16,32},{20,36},{24,40},{28,44},{32,4... | collective-permute-start | bytes 786440 | tf_op jit(solution)/shard_map/ppermute | solution.py:18
  113.6 12.2 %copy-start.37 = (pred[8]{0:T(512)(128)(4,1)S(1)}, pred[8]{0:T(512)(128)(4,1)}, u32[]{:S(2)}) copy-start(pred[8]{0:T(512)(128)(4,1)} %get-tuple-element.44) | copy-start | bytes 28
  113.6 12.3 %copy-start.8 = (f32[4,64,1,256]{3,2,1,0:T(1,128)S(1)}, f32[4,64,1,256]{3,2,1,0:T(1,128)}, u32[]{:S(2)}) copy-start(f32[4,64,1,256]{3,2,1,0:T(1,128)} %copy-done.7) | copy-start | bytes 786436
  113.6 12.3 %copy-start.21 = (f32[256,1,256]{2,0,1:T(8,128)S(1)}, f32[256,1,256]{2,0,1:T(8,128)}, u32[]{:S(2)}) copy-start(f32[256,1,256]{2,0,1:T(8,128)} %copy-done.20) | copy-start | bytes 786436
  113.6 12.3 %copy-start.46 = (pred[4,64]{1,0:T(4,128)(4,1)S(1)}, pred[4,64]{1,0:T(4,128)(4,1)}, u32[]{:S(2)}) copy-start(pred[4,64]{1,0:T(4,128)(4,1)} %get-tuple-element.43) | copy-start | bytes 772
  118.7 11.0 %copy-start.31 = (f32[1,256]{1,0:T(1,128)S(1)}, f32[1,256]{1,0:T(1,128)}, u32[]{:S(2)}) copy-start(f32[1,256]{1,0:T(1,128)} %copy-done.30) | copy-start | bytes 3076
  118.7 11.0 %collective-permute-start.9 = (bf16[1,256,512]{2,1,0:T(8,128)(2,1)S(1)}, bf16[1,256,512]{2,1,0:T(8,128)(2,1)S(1)}, u32[]{:S(2)}, u32[]{:S(2)}) collective-permute-start(bf16[1,256,512]{2,1,0:T(8,128)(2,1)S(1)} %fusion.23), channel_id=1, source_target_pairs={{0,32},{4,36},{8,40},{12,44},{16,48},{20,52},{24,56},{28,60},{32,6... | collective-permute-start | bytes 786440 | tf_op jit(solution)/shard_map/ppermute | solution.py:18
  130.7 17.3 %copy-start.2 = (f32[1,256,512]{2,1,0:T(8,128)}, f32[1,256,512]{2,1,0:T(8,128)S(1)}, u32[]{:S(2)}) copy-start(f32[1,256,512]{2,1,0:T(8,128)S(1)} %get-tuple-element.8) | copy-start | bytes 1572868
  130.7 17.2 %collective-permute-start.11 = (bf16[1,256,512]{2,1,0:T(8,128)(2,1)}, bf16[1,256,512]{2,1,0:T(8,128)(2,1)}, u32[]{:S(2)}, u32[]{:S(2)}) collective-permute-start(bf16[1,256,512]{2,1,0:T(8,128)(2,1)} %get-tuple-element.7), channel_id=1, source_target_pairs={{0,64},{4,68},{8,72},{12,76},{16,80},{20,84},{24,88},{28,92},{32,9... | collective-permute-start | bytes 786440 | tf_op jit(solution)/shard_map/ppermute | solution.py:18
  141.1 6.9 %copy-start.32 = (f32[1,256]{1,0:T(1,128)S(1)}, f32[1,256]{1,0:T(1,128)}, u32[]{:S(2)}) copy-start(f32[1,256]{1,0:T(1,128)} %broadcast_select_fusion.1) | copy-start | bytes 3076
  157.1 10.2 %copy-start.5 = (f32[8,256,512]{2,1,0:T(8,128)S(1)}, f32[8,256,512]{2,1,0:T(8,128)}, u32[]{:S(2)}) copy-start(f32[8,256,512]{2,1,0:T(8,128)} %gather_fusion.7) | copy-start | bytes 12582916
  160.1 6.1 %copy-start.3 = (f32[1,256,512]{2,1,0:T(8,128)S(1)}, f32[1,256,512]{2,1,0:T(8,128)}, u32[]{:S(2)}) copy-start(f32[1,256,512]{2,1,0:T(8,128)} %copy-done.2) | copy-start | bytes 1572868
  160.1 7.2 %copy-start.15 = (f32[8,64,256]{2,1,0:T(8,128)S(1)}, f32[8,64,256]{2,1,0:T(8,128)}, u32[]{:S(2)}) copy-start(f32[8,64,256]{2,1,0:T(8,128)} %gather_fusion.3) | copy-start | bytes 1572868
  160.1 7.2 %copy-start.17 = (f32[8,64,256]{2,1,0:T(8,128)S(1)}, f32[8,64,256]{2,1,0:T(8,128)}, u32[]{:S(2)}) copy-start(f32[8,64,256]{2,1,0:T(8,128)} %gather_fusion.2) | copy-start | bytes 1572868
  160.1 7.2 %copy-start.18 = (bf16[8,64,512]{2,1,0:T(8,128)(2,1)S(1)}, bf16[8,64,512]{2,1,0:T(8,128)(2,1)}, u32[]{:S(2)}) copy-start(bf16[8,64,512]{2,1,0:T(8,128)(2,1)} %gather_fusion.5) | copy-start | bytes 1572868
  160.1 7.2 %copy-start.34 = (f32[8,256]{1,0:T(8,128)S(1)}, f32[8,256]{1,0:T(8,128)}, u32[]{:S(2)}) copy-start(f32[8,256]{1,0:T(8,128)} %get-tuple-element.28) | copy-start | bytes 24580
  160.1 7.2 %copy-start.35 = (f32[8,256]{1,0:T(8,128)S(1)}, f32[8,256]{1,0:T(8,128)}, u32[]{:S(2)}) copy-start(f32[8,256]{1,0:T(8,128)} %get-tuple-element.29) | copy-start | bytes 24580
  160.1 7.2 %copy-start.36 = (pred[8]{0:T(512)(128)(4,1)S(1)}, pred[8]{0:T(512)(128)(4,1)}, u32[]{:S(2)}) copy-start(pred[8]{0:T(512)(128)(4,1)} %get-tuple-element.49) | copy-start | bytes 28
  160.1 7.2 %copy-start.42 = (pred[8,64]{1,0:T(8,128)(4,1)S(1)}, pred[8,64]{1,0:T(8,128)(4,1)}, u32[]{:S(2)}) copy-start(pred[8,64]{1,0:T(8,128)(4,1)} %fusion.55) | copy-start | bytes 1540
  160.1 7.2 %copy-start.44 = (pred[8]{0:T(512)(128)(4,1)S(1)}, pred[8]{0:T(512)(128)(4,1)}, u32[]{:S(2)}) copy-start(pred[8]{0:T(512)(128)(4,1)} %get-tuple-element.50) | copy-start | bytes 28
  160.1 7.2 %copy-start.45 = (pred[8]{0:T(512)(128)(4,1)S(1)}, pred[8]{0:T(512)(128)(4,1)}, u32[]{:S(2)}) copy-start(pred[8]{0:T(512)(128)(4,1)} %get-tuple-element.51) | copy-start | bytes 28
  161.0 14.6 %collective-permute-start.14 = (bf16[256,512]{1,0:T(8,128)(2,1)}, bf16[256,512]{1,0:T(8,128)(2,1)}, u32[]{:S(2)}, u32[]{:S(2)}) collective-permute-start(bf16[256,512]{1,0:T(8,128)(2,1)} %bitcast.199), channel_id=1, source_target_pairs={{0,3},{1,0},{2,1},{3,2},{4,7},{5,4},{6,5},{7,6},{8,11},{9,8},{10,9... | collective-permute-start | bytes 786440 | tf_op jit(solution)/shard_map/ppermute | solution.py:244
  164.0 11.6 %collective-permute-start.12 = (bf16[256,512]{1,0:T(8,128)(2,1)S(1)}, bf16[256,512]{1,0:T(8,128)(2,1)}, u32[]{:S(2)}, u32[]{:S(2)}) collective-permute-start(bf16[256,512]{1,0:T(8,128)(2,1)S(1)} %bitcast.221), channel_id=1, source_target_pairs={{0,1},{1,2},{2,3},{3,0},{4,5},{5,6},{6,7},{7,4},{8,9},{9,10},{10,1... | collective-permute-start | bytes 786440 | tf_op jit(solution)/shard_map/ppermute | solution.py:244
  164.0 11.6 %collective-permute-start.13 = (bf16[256,512]{1,0:T(8,128)(2,1)S(1)}, bf16[256,512]{1,0:T(8,128)(2,1)}, u32[]{:S(2)}, u32[]{:S(2)}) collective-permute-start(bf16[256,512]{1,0:T(8,128)(2,1)S(1)} %bitcast.220), channel_id=1, source_target_pairs={{0,2},{1,3},{2,0},{3,1},{4,6},{5,7},{6,4},{7,5},{8,10},{9,11},{10,... | collective-permute-start | bytes 786440 | tf_op jit(solution)/shard_map/ppermute | solution.py:244
  175.6 34.5 %copy-start.13 = (bf16[250,2048]{1,0:T(8,128)(2,1)S(1)}, bf16[250,2048]{1,0:T(8,128)(2,1)}, u32[]{:S(2)}) copy-start(bf16[250,2048]{1,0:T(8,128)(2,1)} %param.25) | copy-start | bytes 3072004
  175.6 34.5 %copy-start.33 = (f32[2048]{0:T(1024)S(1)}, f32[2048]{0:T(1024)}, u32[]{:S(2)}) copy-start(f32[2048]{0:T(1024)} %param.24) | copy-start | bytes 24580
  178.2 102.7 %copy-start.19 = (bf16[256,512]{1,0:T(8,128)(2,1)}, bf16[256,512]{1,0:T(8,128)(2,1)S(1)}, u32[]{:S(2)}) copy-start(bf16[256,512]{1,0:T(8,128)(2,1)S(1)} %fusion.15) | copy-start | bytes 786436
  179.0 1.2 collective-permute-start.15
  180.3 4.1 %collective-permute-start.16 = (bf16[8,2048]{1,0:T(8,128)(2,1)S(1)}, bf16[8,2048]{1,0:T(8,128)(2,1)S(1)}, u32[]{:S(2)}, u32[]{:S(2)}) collective-permute-start(bf16[8,2048]{1,0:T(8,128)(2,1)S(1)} %add_dynamic-update-slice_fusion), channel_id=1, source_target_pairs={{0,8},{4,12},{8,0},{12,4},{16,24},{20,28},{24,16},{28,20},{32,40},... | collective-permute-start | bytes 98312 | tf_op jit(solution)/shard_map/ppermute | solution.py:26
  184.4 5.6 %collective-permute-start.17 = (bf16[8,2048]{1,0:T(8,128)(2,1)S(1)}, bf16[8,2048]{1,0:T(8,128)(2,1)S(1)}, u32[]{:S(2)}, u32[]{:S(2)}) collective-permute-start(bf16[8,2048]{1,0:T(8,128)(2,1)S(1)} %add.488), channel_id=1, source_target_pairs={{0,16},{4,20},{8,24},{12,28},{16,0},{20,4},{24,8},{28,12},{32,48},... | collective-permute-start | bytes 98312 | tf_op jit(solution)/shard_map/ppermute | solution.py:26
  190.0 4.3 %collective-permute-start.18 = (bf16[8,2048]{1,0:T(8,128)(2,1)S(1)}, bf16[8,2048]{1,0:T(8,128)(2,1)S(1)}, u32[]{:S(2)}, u32[]{:S(2)}) collective-permute-start(bf16[8,2048]{1,0:T(8,128)(2,1)S(1)} %add.489), channel_id=1, source_target_pairs={{0,32},{4,36},{8,40},{12,44},{16,48},{20,52},{24,56},{28,60},{32,0... | collective-permute-start | bytes 98312 | tf_op jit(solution)/shard_map/ppermute | solution.py:26
  194.4 5.6 %collective-permute-start.19 = (bf16[8,2048]{1,0:T(8,128)(2,1)S(1)}, bf16[8,2048]{1,0:T(8,128)(2,1)S(1)}, u32[]{:S(2)}, u32[]{:S(2)}) collective-permute-start(bf16[8,2048]{1,0:T(8,128)(2,1)S(1)} %add.490), channel_id=1, source_target_pairs={{0,64},{4,68},{8,72},{12,76},{16,80},{20,84},{24,88},{28,92},{32,9... | collective-permute-start | bytes 98312 | tf_op jit(solution)/shard_map/ppermute | solution.py:26
  200.0 4.0 %collective-permute-start.20 = (bf16[8,2048]{1,0:T(8,128)(2,1)S(1)}, bf16[8,2048]{1,0:T(8,128)(2,1)S(1)}, u32[]{:S(2)}, u32[]{:S(2)}) collective-permute-start(bf16[8,2048]{1,0:T(8,128)(2,1)S(1)} %add.491), channel_id=1, source_target_pairs={{0,1},{1,0},{2,3},{3,2},{4,5},{5,4},{6,7},{7,6},{8,9},{9,8},{10,11... | collective-permute-start | bytes 98312 | tf_op jit(solution)/shard_map/ppermute | solution.py:26
  204.0 5.5 %collective-permute-start.21 = (bf16[8,2048]{1,0:T(8,128)(2,1)S(1)}, bf16[8,2048]{1,0:T(8,128)(2,1)S(1)}, u32[]{:S(2)}, u32[]{:S(2)}) collective-permute-start(bf16[8,2048]{1,0:T(8,128)(2,1)S(1)} %add.492), channel_id=1, source_target_pairs={{0,2},{1,3},{2,0},{3,1},{4,6},{5,7},{6,4},{7,5},{8,10},{9,11},{10,... | collective-permute-start | bytes 98312 | tf_op jit(solution)/shard_map/ppermute | solution.py:26
  (12 other events, 50.2 us)
Sparse Core Ops, SparseCore 0:
  175.7 103.2 all-reduce.1

commit v2 on v1

--- a/solution.py
+++ b/solution.py
@@ -7,6 +7,7 @@
 DV = 512
 KCONV = 4
 BLOCK = 64
+MAXLEN = 4096
 
 
 HIGHEST_PRECISION = lax.Precision.HIGHEST
@@ -28,12 +29,12 @@
     return array
 
 
-def state_prefix(decay_factor, local_state, axis):
+def state_prefix(decay_factor, local_state, axis, reach):
     peers, place = lax.axis_size(axis), lax.axis_index(axis)
     decay = passed_along(decay_factor, axis, 1)
     state = passed_along(local_state.astype(jnp.bfloat16), axis, 1).astype(jnp.float32)
     step = 1
-    while step < peers:
+    while step < min(peers, reach):
         earlier_decay = passed_along(decay, axis, step)
         earlier_state = passed_along(state.astype(jnp.bfloat16), axis, step).astype(jnp.float32)
         state = state + decay[..., None] * earlier_state
@@ -207,10 +208,40 @@
     reached = jnp.where(end_carried, jnp.exp(end_decay)[:, :, :, None] * states_before[end_block], 0.0)
     local_ends = within + reached
 
+    seq_size, seq_index = lax.axis_size("seq"), lax.axis_index("seq")
     through_shard = segment[-1] == segment_prior
     decay_factor = jnp.where(through_shard, priors[-1] * block_decay[-1], 0.0)
-    incoming = state_prefix(decay_factor, local_state, "seq")
-
+    end_reach = jnp.exp(end_decay) * priors[end_block]
+    end_from_before = end_segment == segment_prior
+    reach_here = jnp.where((owned_here & end_from_before)[:, None, None], end_reach, 0.0)
+    table = jnp.concatenate(
+        [
+            jnp.where((jnp.arange(seq_size) == seq_index)[:, None, None], decay_factor[None], 0.0),
+            reach_here,
+        ]
+    )
+    table = butterfly_sum(table, "seq")
+    shard_decays, end_reaches = table[:seq_size], table[seq_size:]
+    end_shard = last_index // row_count
+    shard_ids = jnp.arange(seq_size)
+    between = (shard_ids[None, :] > seq_index) & (shard_ids[None, :] < end_shard[:, None])
+    spanned = jnp.prod(
+        jnp.where(between[:, :, None, None], shard_decays[None], 1.0), axis=1
+    )
+    from_here = (seq_index < end_shard)[:, None, None, None]
+    end_terms = jnp.where(owned_here[:, None, None, None], local_ends, 0.0) + jnp.where(
+        from_here, (end_reaches * spanned)[:, :, :, None] * local_state[None], 0.0
+    )
+    state_width = head_count * DK * DV
+    payload = jnp.concatenate(
+        [end_terms.reshape(request_count, state_width), conv_edges.reshape(request_count, -1)], axis=1
+    )
+    payload = lax.psum(payload.astype(jnp.bfloat16), "seq").astype(jnp.float32)
+
+    incoming = state_prefix(decay_factor, local_state, "seq", -(-MAXLEN // row_count))
+    payload, incoming = lax.optimization_barrier((payload, incoming))
+    last_states = payload[:, :state_width].reshape(local_ends.shape)
+    conv_edges = payload[:, state_width:].reshape(conv_edges.shape)
     reach = jnp.exp(cumulative) * priors[:, None]
     from_before = (block_segment == segment_prior)[:, :, None, None]
     correction = jnp.einsum(
@@ -220,19 +251,6 @@
         precision=HIGHEST_PRECISION,
     )
     attended = (attended + correction).reshape(row_count, head_count, DV)
-    end_reach = jnp.exp(end_decay) * priors[end_block]
-    end_from_before = (end_segment == segment_prior)[:, None, None, None]
-    end_states = local_ends + jnp.where(
-        end_from_before, end_reach[:, :, :, None] * incoming[None], 0.0
-    )
-    end_states = jnp.where(owned_here[:, None, None, None], end_states, 0.0)
-    state_width = head_count * DK * DV
-    payload = jnp.concatenate(
-        [end_states.reshape(request_count, state_width), conv_edges.reshape(request_count, -1)], axis=1
-    )
-    payload = lax.psum(payload.astype(jnp.bfloat16), "seq").astype(jnp.float32)
-    last_states = payload[:, :state_width].reshape(end_states.shape)
-    conv_edges = payload[:, state_width:].reshape(conv_edges.shape)
 
     gated = head_output(attended, gate_out, head_gain)
     partial = jnp.dot(gated, out_weight, preferred_element_type=jnp.float32).astype(jnp.bfloat16)

time: 296 us -> 315 us (1.064)
  waiting for transfers between devices: 103 us -> 118 us
  other arithmetic: 47.2 us -> 53.3 us
    ppermute x12 -> x10, starting transfers between devices: 55.1 us -> 34.1 us  [passed_along(): return lax.ppermute(array, axis, pairs)]
    ppermute x7 -> x12, starting transfers between devices: 5.77 us -> 25.3 us  [butterfly_sum(): array = array + lax.ppermute(array, axis, pairs)]
    psum x1, waiting for transfers between devices: 67.8 us -> 82.5 us  [shards(): payload = lax.psum(payload.astype(jnp.bfloat16), 'seq').astype(jnp.float32)]
    ppermute x3, waiting for transfers between devices: 0.01 us -> 10.1 us  [shards(): lax.ppermute(outgoing, 'tp', [(i, (i + shift) % tp_size) for i in range(t...]
    ppermute x12 -> x10, waiting for transfers between devices: 10.5 us -> 2.92 us  [passed_along(): return lax.ppermute(array, axis, pairs)]
    convert_element_type x0 -> x1, other arithmetic: none -> 3.48 us  [shards(): payload = lax.psum(payload.astype(jnp.bfloat16), 'seq').astype(jnp.float32)]
    ppermute x7 -> x12, waiting for transfers between devices: 24.6 us -> 22 us  [butterfly_sum(): array = array + lax.ppermute(array, axis, pairs)]
    unnamed x115 -> x141, local copies, waits for them, and re-layouts: 9.94 us -> 10.9 us
  transfers between devices with their start and end apart: 23 -> 26, of which waited for: 13 -> 15; matrix products, arithmetic and copies ran while one was open for 24% -> 28% of each run, Pallas kernels for 0% -> 0%
where the time goes in v2:
time: 315 us; the launch traced here: 313 us
  waiting for transfers between devices  118 us (37%)
  starting transfers between devices  64.5 us (20%)
  other arithmetic  53.3 us (17%)
  local copies, waits for them, and re-layouts  41.7 us (13%)
  matrix products  19.9 us (6%)
  between operations  16.5 us (5%)
    psum x1, waiting for transfers between devices, shards(): payload = lax.psum(payload.astype(jnp.bfloat16), 'seq').astype(jnp.float32)  82.5 us
    ppermute x10, starting transfers between devices, passed_along(): return lax.ppermute(array, axis, pairs)  34.1 us
    ppermute x12, starting transfers between devices, butterfly_sum(): array = array + lax.ppermute(array, axis, pairs)  25.3 us
    ppermute x12, waiting for transfers between devices, butterfly_sum(): array = array + lax.ppermute(array, axis, pairs)  22 us
    unnamed x141, local copies, waits for them, and re-layouts  10.9 us
    ppermute x3, waiting for transfers between devices, shards(): lax.ppermute(outgoing, 'tp', [(i, (i + shift) % tp_size) for i in range(t...  10.1 us
    reduce_sum x1, other arithmetic, shards(): jnp.sum(queries[:, :, None] * key_rows[:, None, :] * weights, axis=-1)  7.86 us
  transfers between devices with their start and end apart: 26, of which 15 were waited for; matrix products, arithmetic and copies ran while one was open for 28% of the time, Pallas kernels for 0%

profile of v2, /device:TPU:0, one launch (start us, length us, event | category | flops | bytes accessed | tf_op | source)
XLA Modules:
  0.0 313.3 jit_solution(4579414701252384022)
XLA Ops:
  8.4 1.5 multiply_reduce_fusion.1
  10.7 1.7 fusion.70
  15.4 1.3 collective-permute-start.7
  22.8 2.3 gather_fusion.3
  25.8 1.3 gather_fusion.4
  27.1 1.3 fusion.76
  29.1 2.8 collective-permute-start.1
  31.9 3.5 %convolution_convert_fusion.1 = bf16[256,1024]{1,0:T(8,128)(2,1)S(1)} fusion(bf16[2048,1024]{1,0:T(8,128)(2,1)} %param.16, f32[2048]{0:T(1024)S(1)} %copy-done.61, f32[256]{0:T(256)S(1)} %add_rsqrt_fusion.1, bf16[256,2048]{1,0:T(8,128)(2,1)S(1)} %copy-done.1), kind=kOutput, calls=%fused_computation.23 | convolution fusion | flops 1076101120 | bytes 5776384 | tf_op jit(solution)/shard_map/dot_general | solution.py:119
  35.4 1.9 collective-permute-start
  41.4 3.9 %collective-permute-start.9 = (f32[1,256]{1,0:T(1,128)S(1)}, f32[1,256]{1,0:T(1,128)S(1)}, u32[]{:S(2)}, u32[]{:S(2)}) collective-permute-start(f32[1,256]{1,0:T(1,128)S(1)} %collective-permute-done.7), channel_id=1, source_target_pairs={{0,4},{4,8},{8,12},{12,16},{16,20},{20,24},{24,28},{28,32},{32,36}... | collective-permute-start | bytes 3080 | tf_op jit(solution)/shard_map/ppermute | solution.py:19
  46.1 4.0 %collective-permute-start.11 = (f32[1,256]{1,0:T(1,128)S(1)}, f32[1,256]{1,0:T(1,128)S(1)}, u32[]{:S(2)}, u32[]{:S(2)}) collective-permute-start(f32[1,256]{1,0:T(1,128)S(1)} %broadcast_select_fusion.4), channel_id=1, source_target_pairs={{0,8},{4,12},{8,16},{12,20},{16,24},{20,28},{24,32},{28,36},{32,40... | collective-permute-start | bytes 3080 | tf_op jit(solution)/shard_map/ppermute | solution.py:19
  50.1 1.3 collective-permute-done.11
  51.4 5.8 %collective-permute-start.13 = (f32[1,256]{1,0:T(1,128)S(1)}, f32[1,256]{1,0:T(1,128)S(1)}, u32[]{:S(2)}, u32[]{:S(2)}) collective-permute-start(f32[1,256]{1,0:T(1,128)S(1)} %broadcast_select_fusion.3), channel_id=1, source_target_pairs={{0,16},{4,20},{8,24},{12,28},{16,32},{20,36},{24,40},{28,44},{32,4... | collective-permute-start | bytes 3080 | tf_op jit(solution)/shard_map/ppermute | solution.py:19
  57.9 1.7 copy.32
  60.1 2.0 pad_maximum_fusion.2
  64.6 3.1 fusion.72
  68.5 1.4 collective-permute-start.6
  69.9 1.6 maximum_bitcast_fusion
  71.6 1.7 gather_fusion.9
  73.3 1.7 gather_fusion.10
  75.8 1.9 collective-permute-start.2
  77.8 1.7 gather_fusion.11
  79.8 5.7 %collective-permute-start.3 = (f32[40,1,256]{2,0,1:T(8,128)S(1)}, f32[40,1,256]{2,0,1:T(8,128)S(1)}, u32[]{:S(2)}, u32[]{:S(2)}) collective-permute-start(f32[40,1,256]{2,0,1:T(8,128)S(1)} %add.473), channel_id=1, source_target_pairs={{0,16},{4,20},{8,24},{12,28},{16,0},{20,4},{24,8},{28,12},{32,48},... | collective-permute-start | bytes 122888 | tf_op jit(solution)/shard_map/ppermute | solution.py:27
  85.6 2.2 collective-permute-done.3
  87.8 3.8 %collective-permute-start.4 = (f32[40,1,256]{2,0,1:T(8,128)S(1)}, f32[40,1,256]{2,0,1:T(8,128)S(1)}, u32[]{:S(2)}, u32[]{:S(2)}) collective-permute-start(f32[40,1,256]{2,0,1:T(8,128)S(1)} %add.474), channel_id=1, source_target_pairs={{0,32},{4,36},{8,40},{12,44},{16,48},{20,52},{24,56},{28,60},{32,0... | collective-permute-start | bytes 122888 | tf_op jit(solution)/shard_map/ppermute | solution.py:27
  91.8 1.9 collective-permute-done.4
  94.3 3.6 %collective-permute-start.5 = (f32[40,1,256]{2,0,1:T(8,128)}, f32[40,1,256]{2,0,1:T(8,128)}, u32[]{:S(2)}, u32[]{:S(2)}) collective-permute-start(f32[40,1,256]{2,0,1:T(8,128)} %add.475), channel_id=1, source_target_pairs={{0,64},{4,68},{8,72},{12,76},{16,80},{20,84},{24,88},{28,92},{32,9... | collective-permute-start | bytes 122888 | tf_op jit(solution)/shard_map/ppermute | solution.py:27
  98.5 1.5 gather_fusion.5
  100.0 1.5 gather_fusion.2
  101.6 4.5 %gather_fusion.7 = f32[8,256,512]{2,1,0:T(8,128)} fusion(f32[4,256,512]{2,1,0:T(8,128)} %maximum_bitcast_fusion, s32[1024]{0:T(1024)} %copy-done.36), kind=kCustom, calls=%fused_computation.7 | custom fusion | bytes 8388640 | tf_op jit(solution)/shard_map/gather | solution.py:208
  107.1 1.3 collective-permute-start.8
  108.5 4.5 %fusion = bf16[1,8,256,512]{3,2,1,0:T(8,128)(2,1)S(1)} fusion(f32[8,256,512]{2,1,0:T(8,128)} %gather_fusion.7, f32[256,512]{1,0:T(8,128)} %bitcast.233, f32[8,256]{1,0:T(8,128)S(1)} %fusion.52, f32[8,256]{1,0:T(8,128)S(1)} %copy-done.39, pred[8]{0:T(512)(128)(4,1)S(1)} %copy-done.57, pred[8]{0:T(512)(128)(4,1)S(1)} %copy-done.56, ...), kind=kOutput, calls=%fused_computation.18 | convolution fusion | flops 143261696 | bytes 8413720 | tf_op jit(solution)/shard_map/rjhc,rjhv->rhcv/dot_general | solution.py:206
  115.0 3.3 %collective-permute-start.10 = (bf16[1,256,512]{2,1,0:T(8,128)(2,1)}, bf16[1,256,512]{2,1,0:T(8,128)(2,1)}, u32[]{:S(2)}, u32[]{:S(2)}) collective-permute-start(bf16[1,256,512]{2,1,0:T(8,128)(2,1)} %fusion.20), channel_id=1, source_target_pairs={{0,8},{4,12},{8,16},{12,20},{16,24},{20,28},{24,32},{28,36},{32,40... | collective-permute-start | bytes 786440 | tf_op jit(solution)/shard_map/ppermute | solution.py:19
  118.4 5.0 %pad_maximum_fusion = bf16[8,134144]{1,0:T(8,128)(2,1)} fusion(bf16[8,3072]{1,0:T(8,128)(2,1)S(1)} %bitcast.238, bf16[8,131072]{1,0:T(8,128)(2,1)S(1)} %bitcast.219), kind=kLoop, calls=%fused_computation.17 | loop fusion | flops 4292608 | bytes 4292608 | tf_op jit(solution)/shard_map/concatenate | solution.py:236
  125.5 4.7 %collective-permute-start.12 = (bf16[1,256,512]{2,1,0:T(8,128)(2,1)S(1)}, bf16[1,256,512]{2,1,0:T(8,128)(2,1)S(1)}, u32[]{:S(2)}, u32[]{:S(2)}) collective-permute-start(bf16[1,256,512]{2,1,0:T(8,128)(2,1)S(1)} %fusion.71), channel_id=1, source_target_pairs={{0,16},{4,20},{8,24},{12,28},{16,32},{20,36},{24,40},{28,44},{32,4... | collective-permute-start | bytes 786440 | tf_op jit(solution)/shard_map/ppermute | solution.py:19
  130.3 7.9 %multiply_reduce_fusion = bf16[4,64,64]{2,1,0:T(8,128)(2,1)S(1)} fusion(f32[4,64,256]{2,1,0:T(8,128)} %bitcast.227, f32[4,64,256]{2,1,0:T(8,128)} %copy-done.9, f32[4,64,256]{2,1,0:T(8,128)} %bitcast.236, pred[4,64,64]{2,1,0:T(8,128)(4,1)S(1)} %copy-done.30), kind=kLoop, calls=%fused_computation.13 | loop fusion | flops 25149440 | bytes 835584 | tf_op jit(solution)/shard_map/reduce_sum | solution.py:161
  138.2 2.0 fusion.22
  140.2 6.3 %collective-permute-start.14 = (bf16[1,256,512]{2,1,0:T(8,128)(2,1)}, bf16[1,256,512]{2,1,0:T(8,128)(2,1)}, u32[]{:S(2)}, u32[]{:S(2)}) collective-permute-start(bf16[1,256,512]{2,1,0:T(8,128)(2,1)} %fusion.22), channel_id=1, source_target_pairs={{0,32},{4,36},{8,40},{12,44},{16,48},{20,52},{24,56},{28,60},{32,6... | collective-permute-start | bytes 786440 | tf_op jit(solution)/shard_map/ppermute | solution.py:19
  146.5 1.5 fusion.5
  148.0 1.7 fusion.27
  150.8 82.5 %all-reduce.2.cloned.1.call-done = bf16[8,134144]{1,0:T(8,128)(2,1)} async-done(((bf16[8,134144]{1,0:T(8,128)(2,1)}), bf16[8,134144]{1,0:T(8,128)(2,1)}) %all-reduce.2.cloned.1.call-update) | async-done | bytes 2146320 | tf_op jit(solution)/shard_map/psum | solution.py:239
  233.3 3.5 %convert_element_type.175 = f32[8,134144]{1,0:T(8,128)} convert(bf16[8,134144]{1,0:T(8,128)(2,1)} %all-reduce.2.cloned.1.call-done) | non-fusion elementwise | flops 1073152 | bytes 6438912 | tf_op jit(solution)/shard_map/convert_element_type | solution.py:239
  236.8 1.4 multiply_add_fusion
  238.3 1.4 multiply_reduce_fusion.2
  239.9 2.5 fusion.17
  242.4 1.7 convolution_convert_fusion
  244.1 1.8 reshape.1153
  246.0 3.0 constant_dynamic-slice_fusion.3
  250.5 2.7 collective-permute-start.17
  253.2 2.3 collective-permute-start.16
  255.6 1.6 convert_element_type.157
  258.2 6.7 %collective-permute-done.17 = bf16[256,512]{1,0:T(8,128)(2,1)} collective-permute-done((bf16[256,512]{1,0:T(8,128)(2,1)}, bf16[256,512]{1,0:T(8,128)(2,1)}, u32[]{:S(2)}, u32[]{:S(2)}) %collective-permute-start.17) | collective-permute-done | bytes 262176 | tf_op jit(solution)/shard_map/ppermute | solution.py:262
  264.9 3.4 %collective-permute-done.15 = bf16[256,512]{1,0:T(8,128)(2,1)} collective-permute-done((bf16[256,512]{1,0:T(8,128)(2,1)}, bf16[256,512]{1,0:T(8,128)(2,1)}, u32[]{:S(2)}, u32[]{:S(2)}) %collective-permute-start.15) | collective-permute-done | bytes 262176 | tf_op jit(solution)/shard_map/ppermute | solution.py:262
  268.3 1.2 pad_maximum_fusion.1
  273.6 3.0 collective-permute-done.19
  276.7 2.5 collective-permute-start.20
  279.2 3.0 collective-permute-done.20
  283.4 3.0 collective-permute-done.21
  286.5 2.2 collective-permute-start.22
  288.7 3.3 %collective-permute-done.22 = bf16[8,2048]{1,0:T(8,128)(2,1)S(1)} collective-permute-done((bf16[8,2048]{1,0:T(8,128)(2,1)S(1)}, bf16[8,2048]{1,0:T(8,128)(2,1)S(1)}, u32[]{:S(2)}, u32[]{:S(2)}) %collective-permute-start.22) | collective-permute-done | bytes 32800 | tf_op jit(solution)/shard_map/ppermute | solution.py:27
  292.1 3.9 %collective-permute-done.23 = bf16[8,2048]{1,0:T(8,128)(2,1)S(1)} collective-permute-done((bf16[8,2048]{1,0:T(8,128)(2,1)S(1)}, bf16[8,2048]{1,0:T(8,128)(2,1)S(1)}, u32[]{:S(2)}, u32[]{:S(2)}) %collective-permute-start.23) | collective-permute-done | bytes 32800 | tf_op jit(solution)/shard_map/ppermute | solution.py:27
  296.6 1.5 slice.176
  298.2 2.2 slice-done
  300.4 4.4 %copy.56 = f32[1,8,256,512]{3,2,1,0:T(8,128)} copy(f32[1,8,256,512]{3,1,2,0:T(8,128)S(1)} %bitcast.218) | data formatting | bytes 8388608
  (252 shorter events, 39.4 us)
Async XLA Ops:
  7.2 235.2 %copy-start = (bf16[512,2048]{1,0:T(8,128)(2,1)S(1)}, bf16[512,2048]{1,0:T(8,128)(2,1)}, u32[]{:S(2)}) copy-start(bf16[512,2048]{1,0:T(8,128)(2,1)} %param.23) | copy-start | bytes 6291460
  7.2 226.1 %all-reduce.2.cloned.1.call-start = ((), (), s32[]{:S(2)}) async-start(), calls=%async_computation | async-start | bytes 4292608 | tf_op jit(solution)/shard_map/psum | solution.py:239
  9.9 8.2 %copy-start.65 = (s32[8]{0:T(128)S(1)}, s32[8]{0:T(128)}, u32[]{:S(2)}) copy-start(s32[8]{0:T(128)} %param.27) | copy-start | bytes 100
  10.0 21.9 %copy-start.51 = (f32[256]{0:T(256)}, f32[256]{0:T(256)S(1)}, u32[]{:S(2)}) copy-start(f32[256]{0:T(256)S(1)} %add_rsqrt_fusion.1) | copy-start | bytes 3076
  12.4 14.7 %copy-start.55 = (s32[8]{0:T(128)S(1)}, s32[8]{0:T(128)}, u32[]{:S(2)}) copy-start(s32[8]{0:T(128)} %param.26) | copy-start | bytes 100
  12.8 19.1 %copy-start.1 = (bf16[256,2048]{1,0:T(8,128)(2,1)S(1)}, bf16[256,2048]{1,0:T(8,128)(2,1)}, u32[]{:S(2)}) copy-start(bf16[256,2048]{1,0:T(8,128)(2,1)} %param.14) | copy-start | bytes 3145732
  12.8 19.0 %copy-start.61 = (f32[2048]{0:T(1024)S(1)}, f32[2048]{0:T(1024)}, u32[]{:S(2)}) copy-start(f32[2048]{0:T(1024)} %param.15) | copy-start | bytes 24580
  14.0 49.9 %copy-start.7 = (f32[4,64,1,256]{3,2,1,0:T(1,128)}, f32[4,64,1,256]{3,2,1,0:T(1,128)S(1)}, u32[]{:S(2)}) copy-start(f32[4,64,1,256]{3,2,1,0:T(1,128)S(1)} %get-tuple-element.78) | copy-start | bytes 786436
  15.4 26.0 %collective-permute-start.7 = (f32[1,256]{1,0:T(1,128)S(1)}, f32[1,256]{1,0:T(1,128)S(1)}, u32[]{:S(2)}, u32[]{:S(2)}) collective-permute-start(f32[1,256]{1,0:T(1,128)S(1)} %get-tuple-element.11), channel_id=1, source_target_pairs={{0,4},{4,8},{8,12},{12,16},{16,20},{20,24},{24,28},{28,32},{32,36}... | collective-permute-start | bytes 3080 | tf_op jit(solution)/shard_map/ppermute | solution.py:19
  27.1 30.2 %copy-start.26 = (f32[8,256]{1,0:T(8,128)}, f32[8,256]{1,0:T(8,128)S(1)}, u32[]{:S(2)}) copy-start(f32[8,256]{1,0:T(8,128)S(1)} %gather_fusion.4) | copy-start | bytes 24580
  29.1 10.9 %copy-start.35 = (f32[4,1024]{1,0:T(4,128)S(1)}, f32[4,1024]{1,0:T(4,128)}, u32[]{:S(2)}) copy-start(f32[4,1024]{1,0:T(4,128)} %param.17) | copy-start | bytes 49156
  29.1 45.9 %collective-permute-start.1 = (f32[40,1,256]{2,0,1:T(8,128)}, f32[40,1,256]{2,0,1:T(8,128)}, u32[]{:S(2)}, u32[]{:S(2)}) collective-permute-start(f32[40,1,256]{2,0,1:T(8,128)} %pad_maximum_fusion.4), channel_id=1, source_target_pairs={{0,4},{4,0},{8,12},{12,8},{16,20},{20,16},{24,28},{28,24},{32,36},... | collective-permute-start | bytes 122888 | tf_op jit(solution)/shard_map/ppermute | solution.py:27
  35.4 24.7 %collective-permute-start = (bf16[3,1024]{1,0:T(4,128)(2,1)S(1)}, bf16[3,1024]{1,0:T(4,128)(2,1)S(1)}, u32[]{:S(2)}, u32[]{:S(2)}) collective-permute-start(bf16[3,1024]{1,0:T(4,128)(2,1)S(1)} %slice.203), channel_id=1, source_target_pairs={{0,4},{4,8},{8,12},{12,16},{16,20},{20,24},{24,28},{28,32},{32,36}... | collective-permute-start | bytes 18440 | tf_op jit(solution)/shard_map/ppermute | solution.py:19
  41.4 4.7 %collective-permute-start.9 = (f32[1,256]{1,0:T(1,128)S(1)}, f32[1,256]{1,0:T(1,128)S(1)}, u32[]{:S(2)}, u32[]{:S(2)}) collective-permute-start(f32[1,256]{1,0:T(1,128)S(1)} %collective-permute-done.7), channel_id=1, source_target_pairs={{0,4},{4,8},{8,12},{12,16},{16,20},{20,24},{24,28},{28,32},{32,36}... | collective-permute-start | bytes 3080 | tf_op jit(solution)/shard_map/ppermute | solution.py:19
  46.1 16.9 %copy-start.31 = (f32[1,256]{1,0:T(1,128)}, f32[1,256]{1,0:T(1,128)S(1)}, u32[]{:S(2)}) copy-start(f32[1,256]{1,0:T(1,128)S(1)} %broadcast_select_fusion.4) | copy-start | bytes 3076
  46.1 5.3 %collective-permute-start.11 = (f32[1,256]{1,0:T(1,128)S(1)}, f32[1,256]{1,0:T(1,128)S(1)}, u32[]{:S(2)}, u32[]{:S(2)}) collective-permute-start(f32[1,256]{1,0:T(1,128)S(1)} %broadcast_select_fusion.4), channel_id=1, source_target_pairs={{0,8},{4,12},{8,16},{12,20},{16,24},{20,28},{24,32},{28,36},{32,40... | collective-permute-start | bytes 3080 | tf_op jit(solution)/shard_map/ppermute | solution.py:19
  51.4 11.7 %copy-start.33 = (f32[1,256]{1,0:T(1,128)}, f32[1,256]{1,0:T(1,128)S(1)}, u32[]{:S(2)}) copy-start(f32[1,256]{1,0:T(1,128)S(1)} %broadcast_select_fusion.3) | copy-start | bytes 3076
  51.4 8.2 %collective-permute-start.13 = (f32[1,256]{1,0:T(1,128)S(1)}, f32[1,256]{1,0:T(1,128)S(1)}, u32[]{:S(2)}, u32[]{:S(2)}) collective-permute-start(f32[1,256]{1,0:T(1,128)S(1)} %broadcast_select_fusion.3), channel_id=1, source_target_pairs={{0,16},{4,20},{8,24},{12,28},{16,32},{20,36},{24,40},{28,44},{32,4... | collective-permute-start | bytes 3080 | tf_op jit(solution)/shard_map/ppermute | solution.py:19
  57.9 12.0 %copy-start.58 = (f32[4]{0:T(128)}, f32[4]{0:T(128)S(1)}, u32[]{:S(2)}) copy-start(f32[4]{0:T(128)S(1)} %pad.15.clone) | copy-start | bytes 52
  68.4 6.6 %copy-start.23 = (f32[32,1,256]{2,0,1:T(8,128)S(1)}, f32[32,1,256]{2,0,1:T(8,128)}, u32[]{:S(2)}) copy-start(f32[32,1,256]{2,0,1:T(8,128)} %copy-done.22) | copy-start | bytes 98308
  68.4 9.3 %copy-start.48 = (pred[8]{0:T(512)(128)(4,1)S(1)}, pred[8]{0:T(512)(128)(4,1)}, u32[]{:S(2)}) copy-start(pred[8]{0:T(512)(128)(4,1)} %get-tuple-element.62) | copy-start | bytes 28
  68.5 38.6 %collective-permute-start.6 = (bf16[1,256,512]{2,1,0:T(8,128)(2,1)}, bf16[1,256,512]{2,1,0:T(8,128)(2,1)S(1)}, u32[]{:S(2)}, u32[]{:S(2)}) collective-permute-start(bf16[1,256,512]{2,1,0:T(8,128)(2,1)} %get-tuple-element.13), channel_id=1, source_target_pairs={{0,4},{4,8},{8,12},{12,16},{16,20},{20,24},{24,28},{28,32},{32,36}... | collective-permute-start | bytes 786440 | tf_op jit(solution)/shard_map/ppermute | solution.py:19
  69.9 15.6 %copy-start.47 = (pred[8]{0:T(512)(128)(4,1)S(1)}, pred[8]{0:T(512)(128)(4,1)}, u32[]{:S(2)}) copy-start(pred[8]{0:T(512)(128)(4,1)} %get-tuple-element.61) | copy-start | bytes 28
  69.9 21.8 %copy-start.46 = (pred[8]{0:T(512)(128)(4,1)S(1)}, pred[8]{0:T(512)(128)(4,1)}, u32[]{:S(2)}) copy-start(pred[8]{0:T(512)(128)(4,1)} %get-tuple-element.63) | copy-start | bytes 28
  75.8 4.0 %collective-permute-start.2 = (f32[40,1,256]{2,0,1:T(8,128)S(1)}, f32[40,1,256]{2,0,1:T(8,128)S(1)}, u32[]{:S(2)}, u32[]{:S(2)}) collective-permute-start(f32[40,1,256]{2,0,1:T(8,128)S(1)} %fusion.68), channel_id=1, source_target_pairs={{0,8},{4,12},{8,0},{12,4},{16,24},{20,28},{24,16},{28,20},{32,40},... | collective-permute-start | bytes 122888 | tf_op jit(solution)/shard_map/ppermute | solution.py:27
  79.8 8.0 %collective-permute-start.3 = (f32[40,1,256]{2,0,1:T(8,128)S(1)}, f32[40,1,256]{2,0,1:T(8,128)S(1)}, u32[]{:S(2)}, u32[]{:S(2)}) collective-permute-start(f32[40,1,256]{2,0,1:T(8,128)S(1)} %add.473), channel_id=1, source_target_pairs={{0,16},{4,20},{8,24},{12,28},{16,0},{20,4},{24,8},{28,12},{32,48},... | collective-permute-start | bytes 122888 | tf_op jit(solution)/shard_map/ppermute | solution.py:27
  87.8 5.8 %collective-permute-start.4 = (f32[40,1,256]{2,0,1:T(8,128)S(1)}, f32[40,1,256]{2,0,1:T(8,128)S(1)}, u32[]{:S(2)}, u32[]{:S(2)}) collective-permute-start(f32[40,1,256]{2,0,1:T(8,128)S(1)} %add.474), channel_id=1, source_target_pairs={{0,32},{4,36},{8,40},{12,44},{16,48},{20,52},{24,56},{28,60},{32,0... | collective-permute-start | bytes 122888 | tf_op jit(solution)/shard_map/ppermute | solution.py:27
  94.3 11.8 %collective-permute-start.5 = (f32[40,1,256]{2,0,1:T(8,128)}, f32[40,1,256]{2,0,1:T(8,128)}, u32[]{:S(2)}, u32[]{:S(2)}) collective-permute-start(f32[40,1,256]{2,0,1:T(8,128)} %add.475), channel_id=1, source_target_pairs={{0,64},{4,68},{8,72},{12,76},{16,80},{20,84},{24,88},{28,92},{32,9... | collective-permute-start | bytes 122888 | tf_op jit(solution)/shard_map/ppermute | solution.py:27
  98.5 7.6 %copy-start.9 = (f32[4,64,256]{2,1,0:T(8,128)}, f32[4,64,256]{2,1,0:T(8,128)S(1)}, u32[]{:S(2)}) copy-start(f32[4,64,256]{2,1,0:T(8,128)S(1)} %convert.22) | copy-start | bytes 786436
  101.5 6.9 %copy-start.27 = (f32[8,256]{1,0:T(8,128)S(1)}, f32[8,256]{1,0:T(8,128)}, u32[]{:S(2)}) copy-start(f32[8,256]{1,0:T(8,128)} %copy-done.26) | copy-start | bytes 24580
  101.5 6.9 %copy-start.39 = (f32[8,256]{1,0:T(8,128)S(1)}, f32[8,256]{1,0:T(8,128)}, u32[]{:S(2)}) copy-start(f32[8,256]{1,0:T(8,128)} %exp.97) | copy-start | bytes 24580
  101.5 6.9 %copy-start.40 = (pred[8]{0:T(512)(128)(4,1)S(1)}, pred[8]{0:T(512)(128)(4,1)}, u32[]{:S(2)}) copy-start(pred[8]{0:T(512)(128)(4,1)} %get-tuple-element.60) | copy-start | bytes 28
  101.5 6.9 %copy-start.53 = (pred[8,64]{1,0:T(8,128)(4,1)S(1)}, pred[8,64]{1,0:T(8,128)(4,1)}, u32[]{:S(2)}) copy-start(pred[8,64]{1,0:T(8,128)(4,1)} %fusion.53) | copy-start | bytes 1540
  101.5 6.9 %copy-start.56 = (pred[8]{0:T(512)(128)(4,1)S(1)}, pred[8]{0:T(512)(128)(4,1)}, u32[]{:S(2)}) copy-start(pred[8]{0:T(512)(128)(4,1)} %get-tuple-element.56) | copy-start | bytes 28
  101.6 6.9 %copy-start.57 = (pred[8]{0:T(512)(128)(4,1)S(1)}, pred[8]{0:T(512)(128)(4,1)}, u32[]{:S(2)}) copy-start(pred[8]{0:T(512)(128)(4,1)} %get-tuple-element.58) | copy-start | bytes 28
  107.1 7.0 %collective-permute-start.8 = (bf16[1,256,512]{2,1,0:T(8,128)(2,1)S(1)}, bf16[1,256,512]{2,1,0:T(8,128)(2,1)S(1)}, u32[]{:S(2)}, u32[]{:S(2)}) collective-permute-start(bf16[1,256,512]{2,1,0:T(8,128)(2,1)S(1)} %collective-permute-done.6), channel_id=1, source_target_pairs={{0,4},{4,8},{8,12},{12,16},{16,20},{20,24},{24,28},{28,32},{32,36}... | collective-permute-start | bytes 786440 | tf_op jit(solution)/shard_map/ppermute | solution.py:19
  114.1 24.1 %copy-start.4 = (bf16[1,256,512]{2,1,0:T(8,128)(2,1)}, bf16[1,256,512]{2,1,0:T(8,128)(2,1)S(1)}, u32[]{:S(2)}) copy-start(bf16[1,256,512]{2,1,0:T(8,128)(2,1)S(1)} %collective-permute-done.8) | copy-start | bytes 786436
  115.0 9.3 %collective-permute-start.10 = (bf16[1,256,512]{2,1,0:T(8,128)(2,1)}, bf16[1,256,512]{2,1,0:T(8,128)(2,1)}, u32[]{:S(2)}, u32[]{:S(2)}) collective-permute-start(bf16[1,256,512]{2,1,0:T(8,128)(2,1)} %fusion.20), channel_id=1, source_target_pairs={{0,8},{4,12},{8,16},{12,20},{16,24},{20,28},{24,32},{28,36},{32,40... | collective-permute-start | bytes 786440 | tf_op jit(solution)/shard_map/ppermute | solution.py:19
  123.4 6.8 %copy-start.30 = (pred[4,64,64]{2,1,0:T(8,128)(4,1)S(1)}, pred[4,64,64]{2,1,0:T(8,128)(4,1)}, u32[]{:S(2)}) copy-start(pred[4,64,64]{2,1,0:T(8,128)(4,1)} %compare_and_fusion) | copy-start | bytes 49156
  125.5 12.7 %collective-permute-start.12 = (bf16[1,256,512]{2,1,0:T(8,128)(2,1)S(1)}, bf16[1,256,512]{2,1,0:T(8,128)(2,1)S(1)}, u32[]{:S(2)}, u32[]{:S(2)}) collective-permute-start(bf16[1,256,512]{2,1,0:T(8,128)(2,1)S(1)} %fusion.71), channel_id=1, source_target_pairs={{0,16},{4,20},{8,24},{12,28},{16,32},{20,36},{24,40},{28,44},{32,4... | collective-permute-start | bytes 786440 | tf_op jit(solution)/shard_map/ppermute | solution.py:19
  130.2 8.0 %copy-start.34 = (f32[1,256]{1,0:T(1,128)S(1)}, f32[1,256]{1,0:T(1,128)}, u32[]{:S(2)}) copy-start(f32[1,256]{1,0:T(1,128)} %copy-done.33) | copy-start | bytes 3076
  130.2 16.3 %copy-start.8 = (f32[4,64,1,256]{3,2,1,0:T(1,128)S(1)}, f32[4,64,1,256]{3,2,1,0:T(1,128)}, u32[]{:S(2)}) copy-start(f32[4,64,1,256]{3,2,1,0:T(1,128)} %copy-done.7) | copy-start | bytes 786436
  130.2 16.3 %copy-start.11 = (f32[1,1,256,512]{3,2,1,0:T(8,128)S(1)}, f32[1,1,256,512]{3,2,1,0:T(8,128)}, u32[]{:S(2)}) copy-start(f32[1,1,256,512]{3,2,1,0:T(8,128)} %copy-done.10) | copy-start | bytes 1572868
  130.3 16.3 %copy-start.13 = (f32[1,1,256,512]{3,2,1,0:T(8,128)S(1)}, f32[1,1,256,512]{3,2,1,0:T(8,128)}, u32[]{:S(2)}) copy-start(f32[1,1,256,512]{3,2,1,0:T(8,128)} %copy-done.12) | copy-start | bytes 1572868
  130.3 16.2 %copy-start.24 = (f32[256,1,256]{2,0,1:T(8,128)S(1)}, f32[256,1,256]{2,0,1:T(8,128)}, u32[]{:S(2)}) copy-start(f32[256,1,256]{2,0,1:T(8,128)} %get-tuple-element.28) | copy-start | bytes 786436
  130.3 16.2 %copy-start.54 = (pred[4,64]{1,0:T(4,128)(4,1)S(1)}, pred[4,64]{1,0:T(4,128)(4,1)}, u32[]{:S(2)}) copy-start(pred[4,64]{1,0:T(4,128)(4,1)} %get-tuple-element.47) | copy-start | bytes 772
  130.3 16.2 %copy-start.59 = (f32[4]{0:T(128)S(1)}, f32[4]{0:T(128)}, u32[]{:S(2)}) copy-start(f32[4]{0:T(128)} %copy-done.58) | copy-start | bytes 52
  140.2 7.8 %copy-start.16 = (f32[4,64,1,256]{3,1,2,0:T(8,128)S(1)}, f32[4,64,1,256]{3,1,2,0:T(8,128)}, u32[]{:S(2)}) copy-start(f32[4,64,1,256]{3,1,2,0:T(8,128)} %copy.32) | copy-start | bytes 786436
  140.2 7.9 %copy-start.50 = (pred[256]{0:T(512)(128)(4,1)S(1)}, pred[256]{0:T(512)(128)(4,1)}, u32[]{:S(2)}) copy-start(pred[256]{0:T(512)(128)(4,1)} %get-tuple-element.40) | copy-start | bytes 772
  140.2 96.6 %collective-permute-start.14 = (bf16[1,256,512]{2,1,0:T(8,128)(2,1)}, bf16[1,256,512]{2,1,0:T(8,128)(2,1)}, u32[]{:S(2)}, u32[]{:S(2)}) collective-permute-start(bf16[1,256,512]{2,1,0:T(8,128)(2,1)} %fusion.22), channel_id=1, source_target_pairs={{0,32},{4,36},{8,40},{12,44},{16,48},{20,52},{24,56},{28,60},{32,6... | collective-permute-start | bytes 786440 | tf_op jit(solution)/shard_map/ppermute | solution.py:19
  150.8 86.1 %copy-start.41 = (f32[1,256]{1,0:T(1,128)S(1)}, f32[1,256]{1,0:T(1,128)}, u32[]{:S(2)}) copy-start(f32[1,256]{1,0:T(1,128)} %broadcast_select_fusion.2) | copy-start | bytes 3076
  249.0 6.6 %copy-start.3 = (bf16[256,2048]{1,0:T(8,128)(2,1)S(1)}, bf16[256,2048]{1,0:T(8,128)(2,1)}, u32[]{:S(2)}) copy-start(bf16[256,2048]{1,0:T(8,128)(2,1)} %param.14) | copy-start | bytes 3145732
  249.8 7.3 %copy-start.49 = (s32[8]{0:T(128)S(1)}, s32[8]{0:T(128)}, u32[]{:S(2)}) copy-start(s32[8]{0:T(128)} %get-tuple-element.69) | copy-start | bytes 100
  250.5 14.4 %collective-permute-start.17 = (bf16[256,512]{1,0:T(8,128)(2,1)}, bf16[256,512]{1,0:T(8,128)(2,1)}, u32[]{:S(2)}, u32[]{:S(2)}) collective-permute-start(bf16[256,512]{1,0:T(8,128)(2,1)} %bitcast.212), channel_id=1, source_target_pairs={{0,3},{1,0},{2,1},{3,2},{4,7},{5,4},{6,5},{7,6},{8,11},{9,8},{10,9... | collective-permute-start | bytes 786440 | tf_op jit(solution)/shard_map/ppermute | solution.py:262
  253.2 15.0 %collective-permute-start.15 = (bf16[256,512]{1,0:T(8,128)(2,1)}, bf16[256,512]{1,0:T(8,128)(2,1)}, u32[]{:S(2)}, u32[]{:S(2)}) collective-permute-start(bf16[256,512]{1,0:T(8,128)(2,1)} %bitcast.214), channel_id=1, source_target_pairs={{0,1},{1,2},{2,3},{3,0},{4,5},{5,6},{6,7},{7,4},{8,9},{9,10},{10,1... | collective-permute-start | bytes 786440 | tf_op jit(solution)/shard_map/ppermute | solution.py:262
  253.2 15.0 %collective-permute-start.16 = (bf16[256,512]{1,0:T(8,128)(2,1)S(1)}, bf16[256,512]{1,0:T(8,128)(2,1)}, u32[]{:S(2)}, u32[]{:S(2)}) collective-permute-start(bf16[256,512]{1,0:T(8,128)(2,1)S(1)} %bitcast.234), channel_id=1, source_target_pairs={{0,2},{1,3},{2,0},{3,1},{4,6},{5,7},{6,4},{7,5},{8,10},{9,11},{10,... | collective-permute-start | bytes 786440 | tf_op jit(solution)/shard_map/ppermute | solution.py:262
  270.8 27.4 %copy-start.21 = (bf16[256,512]{1,0:T(8,128)(2,1)}, bf16[256,512]{1,0:T(8,128)(2,1)S(1)}, u32[]{:S(2)}) copy-start(bf16[256,512]{1,0:T(8,128)(2,1)S(1)} %fusion.14) | copy-start | bytes 786436
  271.4 1.2 collective-permute-start.18
  272.7 3.9 %collective-permute-start.19 = (bf16[8,2048]{1,0:T(8,128)(2,1)S(1)}, bf16[8,2048]{1,0:T(8,128)(2,1)S(1)}, u32[]{:S(2)}, u32[]{:S(2)}) collective-permute-start(bf16[8,2048]{1,0:T(8,128)(2,1)S(1)} %add_dynamic-update-slice_fusion), channel_id=1, source_target_pairs={{0,8},{4,12},{8,0},{12,4},{16,24},{20,28},{24,16},{28,20},{32,40},... | collective-permute-start | bytes 98312 | tf_op jit(solution)/shard_map/ppermute | solution.py:27
  276.7 5.5 %collective-permute-start.20 = (bf16[8,2048]{1,0:T(8,128)(2,1)S(1)}, bf16[8,2048]{1,0:T(8,128)(2,1)S(1)}, u32[]{:S(2)}, u32[]{:S(2)}) collective-permute-start(bf16[8,2048]{1,0:T(8,128)(2,1)S(1)} %add.517), channel_id=1, source_target_pairs={{0,16},{4,20},{8,24},{12,28},{16,0},{20,4},{24,8},{28,12},{32,48},... | collective-permute-start | bytes 98312 | tf_op jit(solution)/shard_map/ppermute | solution.py:27
  282.2 4.3 %collective-permute-start.21 = (bf16[8,2048]{1,0:T(8,128)(2,1)S(1)}, bf16[8,2048]{1,0:T(8,128)(2,1)S(1)}, u32[]{:S(2)}, u32[]{:S(2)}) collective-permute-start(bf16[8,2048]{1,0:T(8,128)(2,1)S(1)} %add.518), channel_id=1, source_target_pairs={{0,32},{4,36},{8,40},{12,44},{16,48},{20,52},{24,56},{28,60},{32,0... | collective-permute-start | bytes 98312 | tf_op jit(solution)/shard_map/ppermute | solution.py:27
  286.5 5.5 %collective-permute-start.22 = (bf16[8,2048]{1,0:T(8,128)(2,1)S(1)}, bf16[8,2048]{1,0:T(8,128)(2,1)S(1)}, u32[]{:S(2)}, u32[]{:S(2)}) collective-permute-start(bf16[8,2048]{1,0:T(8,128)(2,1)S(1)} %add.519), channel_id=1, source_target_pairs={{0,64},{4,68},{8,72},{12,76},{16,80},{20,84},{24,88},{28,92},{32,9... | collective-permute-start | bytes 98312 | tf_op jit(solution)/shard_map/ppermute | solution.py:27
  292.0 4.0 %collective-permute-start.23 = (bf16[8,2048]{1,0:T(8,128)(2,1)S(1)}, bf16[8,2048]{1,0:T(8,128)(2,1)S(1)}, u32[]{:S(2)}, u32[]{:S(2)}) collective-permute-start(bf16[8,2048]{1,0:T(8,128)(2,1)S(1)} %add.520), channel_id=1, source_target_pairs={{0,1},{1,0},{2,3},{3,2},{4,5},{5,4},{6,7},{7,6},{8,9},{9,8},{10,11... | collective-permute-start | bytes 98312 | tf_op jit(solution)/shard_map/ppermute | solution.py:27
  296.0 8.8 %collective-permute-start.24 = (bf16[8,2048]{1,0:T(8,128)(2,1)S(1)}, bf16[8,2048]{1,0:T(8,128)(2,1)S(1)}, u32[]{:S(2)}, u32[]{:S(2)}) collective-permute-start(bf16[8,2048]{1,0:T(8,128)(2,1)S(1)} %add.521), channel_id=1, source_target_pairs={{0,2},{1,3},{2,0},{3,1},{4,6},{5,7},{6,4},{7,5},{8,10},{9,11},{10,... | collective-permute-start | bytes 98312 | tf_op jit(solution)/shard_map/ppermute | solution.py:27
  (29 other events, 99.3 us)
Sparse Core Ops, SparseCore 0:
  123.6 109.6 all-reduce.1

commit v3 on v1

--- a/solution.py
+++ b/solution.py
@@ -7,6 +7,7 @@
 DV = 512
 KCONV = 4
 BLOCK = 64
+MAXLEN = 4096
 
 
 HIGHEST_PRECISION = lax.Precision.HIGHEST
@@ -28,14 +29,22 @@
     return array
 
 
-def state_prefix(decay_factor, local_state, axis):
+def send_pair(decay, state, axis, by):
+    high = decay.astype(jnp.bfloat16)
+    low = (decay - high.astype(jnp.float32)).astype(jnp.bfloat16)
+    row = jnp.concatenate([high, low], axis=-1)[:, None, :]
+    packed = jnp.concatenate([state.astype(jnp.bfloat16), row], axis=1)
+    got = passed_along(packed, axis, by)
+    tail = got[:, DK].astype(jnp.float32)
+    return tail[:, :DK] + tail[:, DK:], got[:, :DK].astype(jnp.float32)
+
+
+def state_prefix(decay_factor, local_state, axis, reach):
     peers, place = lax.axis_size(axis), lax.axis_index(axis)
-    decay = passed_along(decay_factor, axis, 1)
-    state = passed_along(local_state.astype(jnp.bfloat16), axis, 1).astype(jnp.float32)
+    decay, state = send_pair(decay_factor, local_state, axis, 1)
     step = 1
-    while step < peers:
-        earlier_decay = passed_along(decay, axis, step)
-        earlier_state = passed_along(state.astype(jnp.bfloat16), axis, step).astype(jnp.float32)
+    while step < min(peers, reach):
+        earlier_decay, earlier_state = send_pair(decay, state, axis, step)
         state = state + decay[..., None] * earlier_state
         decay = jnp.where(place >= step, decay * earlier_decay, decay)
         step *= 2
@@ -209,7 +218,7 @@
 
     through_shard = segment[-1] == segment_prior
     decay_factor = jnp.where(through_shard, priors[-1] * block_decay[-1], 0.0)
-    incoming = state_prefix(decay_factor, local_state, "seq")
+    incoming = state_prefix(decay_factor, local_state, "seq", -(-MAXLEN // row_count))
 
     reach = jnp.exp(cumulative) * priors[:, None]
     from_before = (block_segment == segment_prior)[:, :, None, None]

time: 296 us -> 265 us (0.90)
  starting transfers between devices: 66.2 us -> 42.9 us
  waiting for transfers between devices: 103 us -> 97.4 us
    ppermute x12 -> x6, starting transfers between devices: 55.1 us -> 30.5 us  [passed_along(): return lax.ppermute(array, axis, pairs)]
    ppermute x12 -> x6, waiting for transfers between devices: 10.5 us -> 4.97 us  [passed_along(): return lax.ppermute(array, axis, pairs)]
    unnamed x115 -> x133, local copies, waits for them, and re-layouts: 9.94 us -> 11.3 us
  transfers between devices with their start and end apart: 23 -> 17, of which waited for: 13 -> 10; matrix products, arithmetic and copies ran while one was open for 24% -> 26% of each run, Pallas kernels for 0% -> 0%
where the time goes in v3:
time: 265 us; the launch traced here: 263 us
  waiting for transfers between devices  97.4 us (37%)
  other arithmetic  46.9 us (18%)
  starting transfers between devices  42.9 us (16%)
  local copies, waits for them, and re-layouts  41.3 us (16%)
  matrix products  18.2 us (7%)
  between operations  16.5 us (6%)
    psum x1, waiting for transfers between devices, shards(): payload = lax.psum(payload.astype(jnp.bfloat16), 'seq').astype(jnp.float32)  69.1 us
    ppermute x6, starting transfers between devices, passed_along(): return lax.ppermute(array, axis, pairs)  30.5 us
    ppermute x7, waiting for transfers between devices, butterfly_sum(): array = array + lax.ppermute(array, axis, pairs)  23.3 us
    unnamed x133, local copies, waits for them, and re-layouts  11.3 us
    reduce_sum x1, other arithmetic, shards(): jnp.sum(queries[:, :, None] * key_rows[:, None, :] * weights, axis=-1)  8.55 us
    ppermute x7, starting transfers between devices, butterfly_sum(): array = array + lax.ppermute(array, axis, pairs)  7.15 us
  transfers between devices with their start and end apart: 17, of which 10 were waited for; matrix products, arithmetic and copies ran while one was open for 26% of the time, Pallas kernels for 0%

profile of v3, /device:TPU:0, one launch (start us, length us, event | category | flops | bytes accessed | tf_op | source)
XLA Modules:
  0.0 263.1 jit_solution(11880094256266116889)
XLA Ops:
  7.2 1.6 multiply_reduce_fusion.1
  9.0 3.9 %convolution_convert_fusion.1 = bf16[256,1024]{1,0:T(8,128)(2,1)S(1)} fusion(bf16[2048,1024]{1,0:T(8,128)(2,1)} %param.16, f32[2048]{0:T(1024)} %param.15, f32[256]{0:T(256)S(1)} %add_rsqrt_fusion.1, bf16[256,2048]{1,0:T(8,128)(2,1)} %param.14), kind=kOutput, calls=%fused_computation.23 | convolution fusion | flops 1076101120 | bytes 5776384 | tf_op jit(solution)/shard_map/dot_general | solution.py:127
  12.9 0.8 copy-done.21
  13.7 1.4 collective-permute-start
  21.4 1.2 fusion.85
  23.3 1.3 broadcast_compare_fusion.2
  27.8 1.2 fusion.83
  31.1 2.4 gather_fusion.3
  33.5 1.3 gather_fusion.4
  34.7 1.3 pad_clamp_fusion.2
  36.6 1.6 convert_element_type.286
  38.7 1.7 copy.32
  40.4 2.1 pad_maximum_fusion.2
  42.4 0.9 fusion.20
  43.3 0.8 fusion.79
  45.5 1.3 copy-done.1
  46.8 2.8 %fusion.14 = (bf16[1,256,512]{2,1,0:T(8,128)(2,1)S(1)}, f32[1,256,512]{2,1,0:T(8,128)S(1)}, f32[1,1,256,512]{3,2,1,0:T(8,128)}) fusion(f32[4,256,512]{2,1,0:T(8,128)S(1)} %fusion.35, f32[256]{0:T(256)S(1)} %bitcast.281, pred[]{:T(512)} %bitcast.26, f32[256]{0:T(256)S(1)} %bitcast.278, pred[]{:T(512)} %bitcast.20, f32[256]{0:T(256)S(1)} %bitcast.280, ...), kind=kLoop, calls=%fused_computation.51 | loop fusion | flops 1441792 | bytes 3411971 | tf_op jit(solution)/shard_map/convert_element_type | solution.py:36
  50.3 4.7 %collective-permute-start.1 = (bf16[1,257,512]{2,1,0:T(8,128)(2,1)}, bf16[1,257,512]{2,1,0:T(8,128)(2,1)S(1)}, u32[]{:S(2)}, u32[]{:S(2)}) collective-permute-start(bf16[1,257,512]{2,1,0:T(8,128)(2,1)} %pad_maximum_fusion.3), channel_id=1, source_target_pairs={{0,4},{4,8},{8,12},{12,16},{16,20},{20,24},{24,28},{28,32},{32,36}... | collective-permute-start | bytes 789512 | tf_op jit(solution)/shard_map/ppermute | solution.py:19
  55.0 1.7 gather_fusion.10
  56.7 8.6 %multiply_reduce_fusion = bf16[4,64,64]{2,1,0:T(8,128)(2,1)S(1)} fusion(f32[4,64,256]{2,1,0:T(8,128)S(1)} %bitcast.246, f32[4,64,256]{2,1,0:T(8,128)} %convert.26, f32[4,64,256]{2,1,0:T(8,128)} %bitcast.254, pred[4,64,64]{2,1,0:T(8,128)(4,1)S(1)} %compare_and_fusion), kind=kLoop, calls=%fused_computation.13 | loop fusion | flops 25149440 | bytes 835584 | tf_op jit(solution)/shard_map/reduce_sum | solution.py:169
  65.4 1.8 gather_fusion.9
  67.2 1.7 gather_fusion.11
  69.8 1.9 collective-permute-start.2
  71.7 1.7 fusion.50
  73.7 7.9 %collective-permute-start.3 = (bf16[1,257,512]{2,1,0:T(8,128)(2,1)S(1)}, bf16[1,257,512]{2,1,0:T(8,128)(2,1)S(1)}, u32[]{:S(2)}, u32[]{:S(2)}) collective-permute-start(bf16[1,257,512]{2,1,0:T(8,128)(2,1)S(1)} %pad_maximum_fusion.5), channel_id=1, source_target_pairs={{0,8},{4,12},{8,16},{12,20},{16,24},{20,28},{24,32},{28,36},{32,40... | collective-permute-start | bytes 789512 | tf_op jit(solution)/shard_map/ppermute | solution.py:19
  81.7 1.7 maximum_bitcast_fusion
  83.4 3.4 %collective-permute-done.3 = bf16[1,257,512]{2,1,0:T(8,128)(2,1)S(1)} collective-permute-done((bf16[1,257,512]{2,1,0:T(8,128)(2,1)S(1)}, bf16[1,257,512]{2,1,0:T(8,128)(2,1)S(1)}, u32[]{:S(2)}, u32[]{:S(2)}) %collective-permute-start.3) | collective-permute-done | bytes 263200 | tf_op jit(solution)/shard_map/ppermute | solution.py:19
  87.1 4.9 %collective-permute-start.4 = (bf16[1,257,512]{2,1,0:T(8,128)(2,1)S(1)}, bf16[1,257,512]{2,1,0:T(8,128)(2,1)S(1)}, u32[]{:S(2)}, u32[]{:S(2)}) collective-permute-start(bf16[1,257,512]{2,1,0:T(8,128)(2,1)S(1)} %pad_maximum_fusion.6), channel_id=1, source_target_pairs={{0,16},{4,20},{8,24},{12,28},{16,32},{20,36},{24,40},{28,44},{32,4... | collective-permute-start | bytes 789512 | tf_op jit(solution)/shard_map/ppermute | solution.py:19
  92.1 2.3 fusion.5
  94.4 1.5 collective-permute-done.4
  97.0 9.7 %collective-permute-start.5 = (bf16[1,257,512]{2,1,0:T(8,128)(2,1)}, bf16[1,257,512]{2,1,0:T(8,128)(2,1)}, u32[]{:S(2)}, u32[]{:S(2)}) collective-permute-start(bf16[1,257,512]{2,1,0:T(8,128)(2,1)} %pad_maximum_fusion.7), channel_id=1, source_target_pairs={{0,32},{4,36},{8,40},{12,44},{16,48},{20,52},{24,56},{28,60},{32,6... | collective-permute-start | bytes 789512 | tf_op jit(solution)/shard_map/ppermute | solution.py:19
  106.7 1.5 gather_fusion.2
  108.2 1.5 gather_fusion.5
  109.7 4.6 %gather_fusion.7 = f32[8,256,512]{2,1,0:T(8,128)} fusion(f32[4,256,512]{2,1,0:T(8,128)} %maximum_bitcast_fusion, s32[1024]{0:T(1024)} %copy-done.34), kind=kCustom, calls=%fused_computation.7 | custom fusion | bytes 8388640 | tf_op jit(solution)/shard_map/gather | solution.py:216
  114.4 1.0 fusion.27
  115.7 3.0 %multiply_reduce_fusion.2 = (f32[4,64]{1,0:T(4,128)S(1)}, f32[4,64,1,512]{3,1,0,2:T(8,128)}) fusion(f32[4,64,1,512]{3,1,0,2:T(8,128)S(1)} %fusion.3, f32[4,64,256]{2,1,0:T(8,128)S(1)} %bitcast.256, bf16[1,257,512]{2,1,0:T(8,128)(2,1)} %collective-permute-done.5, f32[256]{0:T(256)S(1)} %bitcast.276, bf16[1,257,512]{2,1,0:T(8,128)(2,1)} %copy-done.18, ...), kind=kOutput, calls=%fused_computation.63 | convolution fusion | flops 404750080 | bytes 2626560 | tf_op jit(solution)/shard_map/bphc,hcv->bphv/dot_general | solution.py:225
  118.8 2.5 fusion.18
  121.3 1.8 convolution_convert_fusion
  123.1 1.8 reshape.1032
  125.0 3.0 %constant_dynamic-slice_fusion.3 = (bf16[256,1,512]{2,1,0:T(2,128)(2,1)}, bf16[256,1,512]{2,1,0:T(2,128)(2,1)S(1)}, bf16[256,1,512]{2,1,0:T(2,128)(2,1)S(1)}, bf16[256,1,512]{2,1,0:T(2,128)(2,1)S(1)}) fusion(bf16[256,4,512]{2,1,0:T(4,128)(2,1)S(1)} %reshape.1032, s32[]{:T(128)S(6)} %select_n.402, s32[]{:T(128)S(6)} %select_n.406, s32[]{:T(128)S(6)} %select_n.404, ...), kind=kLoop, calls=%fused_computation.140 | loop fusion | bytes 2097168 | tf_op jit(solution)/shard_map/jit(dynamic_index_in_dim)/dynamic_slice | solution.py:249
  128.9 3.0 %collective-permute-start.8 = (bf16[256,512]{1,0:T(8,128)(2,1)}, bf16[256,512]{1,0:T(8,128)(2,1)}, u32[]{:S(2)}, u32[]{:S(2)}) collective-permute-start(bf16[256,512]{1,0:T(8,128)(2,1)} %bitcast.231), channel_id=1, source_target_pairs={{0,3},{1,0},{2,1},{3,2},{4,7},{5,4},{6,5},{7,6},{8,11},{9,8},{10,9... | collective-permute-start | bytes 786440 | tf_op jit(solution)/shard_map/ppermute | solution.py:253
  131.9 2.2 collective-permute-start.7
  134.1 1.2 fusion.70
  135.5 2.0 fusion
  137.4 1.2 copy.37
  138.6 5.1 %pad_maximum_fusion = bf16[8,134144]{1,0:T(8,128)(2,1)} fusion(bf16[8,3072]{1,0:T(8,128)(2,1)S(1)} %bitcast.257, bf16[8,131072]{1,0:T(8,128)(2,1)S(1)} %bitcast.238), kind=kLoop, calls=%fused_computation.17 | loop fusion | flops 4292608 | bytes 4292608 | tf_op jit(solution)/shard_map/concatenate | solution.py:239
  143.8 1.3 pad_maximum_fusion.1
  145.1 1.2 fusion.15
  147.4 1.2 collective-permute-done.9
  148.7 4.0 %collective-permute-done.10 = bf16[8,2048]{1,0:T(8,128)(2,1)S(1)} collective-permute-done((bf16[8,2048]{1,0:T(8,128)(2,1)S(1)}, bf16[8,2048]{1,0:T(8,128)(2,1)S(1)}, u32[]{:S(2)}, u32[]{:S(2)}) %collective-permute-start.10) | collective-permute-done | bytes 32800 | tf_op jit(solution)/shard_map/ppermute | solution.py:27
  152.8 5.4 %collective-permute-done.11 = bf16[8,2048]{1,0:T(8,128)(2,1)S(1)} collective-permute-done((bf16[8,2048]{1,0:T(8,128)(2,1)S(1)}, bf16[8,2048]{1,0:T(8,128)(2,1)S(1)}, u32[]{:S(2)}, u32[]{:S(2)}) %collective-permute-start.11) | collective-permute-done | bytes 32800 | tf_op jit(solution)/shard_map/ppermute | solution.py:27
  158.3 1.2 collective-permute-start.12
  159.4 3.3 %collective-permute-done.12 = bf16[8,2048]{1,0:T(8,128)(2,1)S(1)} collective-permute-done((bf16[8,2048]{1,0:T(8,128)(2,1)S(1)}, bf16[8,2048]{1,0:T(8,128)(2,1)S(1)}, u32[]{:S(2)}, u32[]{:S(2)}) %collective-permute-start.12) | collective-permute-done | bytes 32800 | tf_op jit(solution)/shard_map/ppermute | solution.py:27
  162.7 2.2 collective-permute-start.13
  164.9 3.3 %collective-permute-done.13 = bf16[8,2048]{1,0:T(8,128)(2,1)S(1)} collective-permute-done((bf16[8,2048]{1,0:T(8,128)(2,1)S(1)}, bf16[8,2048]{1,0:T(8,128)(2,1)S(1)}, u32[]{:S(2)}, u32[]{:S(2)}) %collective-permute-start.13) | collective-permute-done | bytes 32800 | tf_op jit(solution)/shard_map/ppermute | solution.py:27
  168.3 1.8 collective-permute-start.14
  170.1 2.2 collective-permute-done.14
  172.3 1.6 collective-permute-start.15
  173.9 3.9 %collective-permute-done.15 = bf16[8,2048]{1,0:T(8,128)(2,1)S(1)} collective-permute-done((bf16[8,2048]{1,0:T(8,128)(2,1)S(1)}, bf16[8,2048]{1,0:T(8,128)(2,1)S(1)}, u32[]{:S(2)}, u32[]{:S(2)}) %collective-permute-start.15) | collective-permute-done | bytes 32800 | tf_op jit(solution)/shard_map/ppermute | solution.py:27
  178.4 1.0 convolution_reduce_fusion
  179.5 69.1 %all-reduce.2.cloned.1.call-done = bf16[8,134144]{1,0:T(8,128)(2,1)} async-done(((bf16[8,134144]{1,0:T(8,128)(2,1)}), bf16[8,134144]{1,0:T(8,128)(2,1)}) %all-reduce.2.cloned.1.call-update) | async-done | bytes 2146320 | tf_op jit(solution)/shard_map/psum | solution.py:242
  248.5 1.9 slice.294
  250.4 4.4 %copy.56 = f32[1,8,256,512]{3,2,1,0:T(8,128)} copy(f32[1,8,256,512]{3,1,2,0:T(8,128)S(1)} %bitcast.237) | data formatting | bytes 8388608
  254.8 1.4 slice.295
  (232 shorter events, 20.0 us)
Async XLA Ops:
  7.2 114.1 %copy-start = (bf16[512,2048]{1,0:T(8,128)(2,1)S(1)}, bf16[512,2048]{1,0:T(8,128)(2,1)}, u32[]{:S(2)}) copy-start(bf16[512,2048]{1,0:T(8,128)(2,1)} %param.23) | copy-start | bytes 6291460
  7.2 241.3 %all-reduce.2.cloned.1.call-start = ((), (), s32[]{:S(2)}) async-start(), calls=%async_computation | async-start | bytes 4292608 | tf_op jit(solution)/shard_map/psum | solution.py:242
  8.9 11.5 %copy-start.47 = (f32[256]{0:T(256)}, f32[256]{0:T(256)S(1)}, u32[]{:S(2)}) copy-start(f32[256]{0:T(256)S(1)} %add_rsqrt_fusion.1) | copy-start | bytes 3076
  8.9 6.8 %copy-start.50 = (s32[8]{0:T(128)S(1)}, s32[8]{0:T(128)}, u32[]{:S(2)}) copy-start(s32[8]{0:T(128)} %param.26) | copy-start | bytes 100
  8.9 6.8 %copy-start.61 = (s32[8]{0:T(128)S(1)}, s32[8]{0:T(128)}, u32[]{:S(2)}) copy-start(s32[8]{0:T(128)} %param.27) | copy-start | bytes 100
  8.9 11.5 %copy-start.2 = (bf16[256,2048]{1,0:T(8,128)(2,1)S(1)}, bf16[256,2048]{1,0:T(8,128)(2,1)}, u32[]{:S(2)}) copy-start(bf16[256,2048]{1,0:T(8,128)(2,1)} %param.14) | copy-start | bytes 3145732
  8.9 11.5 %copy-start.55 = (bf16[2048,16]{0,1:T(8,128)(2,1)S(1)}, bf16[2048,16]{0,1:T(8,128)(2,1)}, u32[]{:S(2)}) copy-start(bf16[2048,16]{0,1:T(8,128)(2,1)} %param.18) | copy-start | bytes 196612
  8.9 11.5 %copy-start.57 = (f32[2048]{0:T(1024)S(1)}, f32[2048]{0:T(1024)}, u32[]{:S(2)}) copy-start(f32[2048]{0:T(1024)} %param.15) | copy-start | bytes 24580
  13.7 7.3 %copy-start.56 = (bf16[16,256]{1,0:T(8,128)(2,1)S(1)}, bf16[16,256]{1,0:T(8,128)(2,1)}, u32[]{:S(2)}) copy-start(bf16[16,256]{1,0:T(8,128)(2,1)} %param.19) | copy-start | bytes 24580
  13.7 7.3 %copy-start.60 = (f32[256]{0:T(256)S(1)}, f32[256]{0:T(256)}, u32[]{:S(2)}) copy-start(f32[256]{0:T(256)} %param.20) | copy-start | bytes 3076
  13.7 26.7 %collective-permute-start = (bf16[3,1024]{1,0:T(4,128)(2,1)S(1)}, bf16[3,1024]{1,0:T(4,128)(2,1)S(1)}, u32[]{:S(2)}, u32[]{:S(2)}) collective-permute-start(bf16[3,1024]{1,0:T(4,128)(2,1)S(1)} %slice.260), channel_id=1, source_target_pairs={{0,4},{4,8},{8,12},{12,16},{16,20},{20,24},{24,28},{28,32},{32,36}... | collective-permute-start | bytes 18440 | tf_op jit(solution)/shard_map/ppermute | solution.py:19
  19.2 11.9 %copy-start.34 = (s32[1024]{0:T(1024)}, s32[1024]{0:T(1024)S(1)}, u32[]{:S(2)}) copy-start(s32[1024]{0:T(1024)S(1)} %pad_clamp_fusion.4) | copy-start | bytes 12292
  20.5 9.1 %copy-start.33 = (f32[4,1024]{1,0:T(4,128)S(1)}, f32[4,1024]{1,0:T(4,128)}, u32[]{:S(2)}) copy-start(f32[4,1024]{1,0:T(4,128)} %param.17) | copy-start | bytes 49156
  22.5 22.3 %copy-start.8 = (f32[4,64,1,256]{3,2,1,0:T(1,128)}, f32[4,64,1,256]{3,2,1,0:T(1,128)S(1)}, u32[]{:S(2)}) copy-start(f32[4,64,1,256]{3,2,1,0:T(1,128)S(1)} %get-tuple-element.73) | copy-start | bytes 786436
  29.7 15.8 %copy-start.38 = (f32[1,1,1,256]{3,2,1,0:T(1,128)}, f32[1,1,1,256]{3,2,1,0:T(1,128)S(1)}, u32[]{:S(2)}) copy-start(f32[1,1,1,256]{3,2,1,0:T(1,128)S(1)} %get-tuple-element.39) | copy-start | bytes 3076
  34.7 7.7 %copy-start.29 = (f32[8,256]{1,0:T(8,128)}, f32[8,256]{1,0:T(8,128)S(1)}, u32[]{:S(2)}) copy-start(f32[8,256]{1,0:T(8,128)S(1)} %gather_fusion.4) | copy-start | bytes 24580
  45.5 11.2 %copy-start.10 = (f32[4,64,1,256]{3,1,2,0:T(8,128)S(1)}, f32[4,64,1,256]{3,1,2,0:T(8,128)}, u32[]{:S(2)}) copy-start(f32[4,64,1,256]{3,1,2,0:T(8,128)} %copy.61) | copy-start | bytes 786436
  50.3 19.4 %collective-permute-start.1 = (bf16[1,257,512]{2,1,0:T(8,128)(2,1)}, bf16[1,257,512]{2,1,0:T(8,128)(2,1)S(1)}, u32[]{:S(2)}, u32[]{:S(2)}) collective-permute-start(bf16[1,257,512]{2,1,0:T(8,128)(2,1)} %pad_maximum_fusion.3), channel_id=1, source_target_pairs={{0,4},{4,8},{8,12},{12,16},{16,20},{20,24},{24,28},{28,32},{32,36}... | collective-permute-start | bytes 789512 | tf_op jit(solution)/shard_map/ppermute | solution.py:19
  56.7 8.6 %copy-start.44 = (pred[8]{0:T(512)(128)(4,1)S(1)}, pred[8]{0:T(512)(128)(4,1)}, u32[]{:S(2)}) copy-start(pred[8]{0:T(512)(128)(4,1)} %get-tuple-element.53) | copy-start | bytes 28
  67.2 14.4 %copy-start.54 = (f32[4]{0:T(128)S(1)}, f32[4]{0:T(128)}, u32[]{:S(2)}) copy-start(f32[4]{0:T(128)} %pad.33.clone) | copy-start | bytes 52
  68.9 12.7 %copy-start.14 = (f32[1,1,256,512]{3,2,1,0:T(8,128)S(1)}, f32[1,1,256,512]{3,2,1,0:T(8,128)}, u32[]{:S(2)}) copy-start(f32[1,1,256,512]{3,2,1,0:T(8,128)} %get-tuple-element.20) | copy-start | bytes 1572868
  69.8 3.6 %collective-permute-start.2 = (bf16[1,257,512]{2,1,0:T(8,128)(2,1)S(1)}, bf16[1,257,512]{2,1,0:T(8,128)(2,1)S(1)}, u32[]{:S(2)}, u32[]{:S(2)}) collective-permute-start(bf16[1,257,512]{2,1,0:T(8,128)(2,1)S(1)} %pad_maximum_fusion.4), channel_id=1, source_target_pairs={{0,4},{4,8},{8,12},{12,16},{16,20},{20,24},{24,28},{28,32},{32,36}... | collective-permute-start | bytes 789512 | tf_op jit(solution)/shard_map/ppermute | solution.py:19
  73.4 22.5 %copy-start.5 = (bf16[1,257,512]{2,1,0:T(8,128)(2,1)}, bf16[1,257,512]{2,1,0:T(8,128)(2,1)S(1)}, u32[]{:S(2)}) copy-start(bf16[1,257,512]{2,1,0:T(8,128)(2,1)S(1)} %collective-permute-done.2) | copy-start | bytes 789508
  73.5 22.5 %copy-start.27 = (f32[1,256]{1,0:T(1,128)}, f32[1,256]{1,0:T(1,128)S(1)}, u32[]{:S(2)}) copy-start(f32[1,256]{1,0:T(1,128)S(1)} %get-tuple-element.12) | copy-start | bytes 3076
  73.7 13.1 %collective-permute-start.3 = (bf16[1,257,512]{2,1,0:T(8,128)(2,1)S(1)}, bf16[1,257,512]{2,1,0:T(8,128)(2,1)S(1)}, u32[]{:S(2)}, u32[]{:S(2)}) collective-permute-start(bf16[1,257,512]{2,1,0:T(8,128)(2,1)S(1)} %pad_maximum_fusion.5), channel_id=1, source_target_pairs={{0,8},{4,12},{8,16},{12,20},{16,24},{20,28},{24,32},{28,36},{32,40... | collective-permute-start | bytes 789512 | tf_op jit(solution)/shard_map/ppermute | solution.py:19
  81.6 10.3 %copy-start.43 = (pred[8]{0:T(512)(128)(4,1)S(1)}, pred[8]{0:T(512)(128)(4,1)}, u32[]{:S(2)}) copy-start(pred[8]{0:T(512)(128)(4,1)} %get-tuple-element.51) | copy-start | bytes 28
  81.7 10.4 %copy-start.9 = (f32[4,64,1,256]{3,2,1,0:T(1,128)S(1)}, f32[4,64,1,256]{3,2,1,0:T(1,128)}, u32[]{:S(2)}) copy-start(f32[4,64,1,256]{3,2,1,0:T(1,128)} %copy-done.8) | copy-start | bytes 786436
  81.7 10.4 %copy-start.26 = (f32[256,1,256]{2,0,1:T(8,128)S(1)}, f32[256,1,256]{2,0,1:T(8,128)}, u32[]{:S(2)}) copy-start(f32[256,1,256]{2,0,1:T(8,128)} %get-tuple-element.28) | copy-start | bytes 786436
  81.7 10.4 %copy-start.53 = (pred[4,64]{1,0:T(4,128)(4,1)S(1)}, pred[4,64]{1,0:T(4,128)(4,1)}, u32[]{:S(2)}) copy-start(pred[4,64]{1,0:T(4,128)(4,1)} %get-tuple-element.50) | copy-start | bytes 772
  86.8 9.2 %copy-start.12 = (bf16[1,257,512]{2,1,0:T(8,128)(2,1)}, bf16[1,257,512]{2,1,0:T(8,128)(2,1)S(1)}, u32[]{:S(2)}) copy-start(bf16[1,257,512]{2,1,0:T(8,128)(2,1)S(1)} %collective-permute-done.3) | copy-start | bytes 789508
  86.8 9.2 %copy-start.31 = (f32[1,256]{1,0:T(1,128)}, f32[1,256]{1,0:T(1,128)S(1)}, u32[]{:S(2)}) copy-start(f32[1,256]{1,0:T(1,128)S(1)} %get-tuple-element.10) | copy-start | bytes 3076
  87.1 8.8 %collective-permute-start.4 = (bf16[1,257,512]{2,1,0:T(8,128)(2,1)S(1)}, bf16[1,257,512]{2,1,0:T(8,128)(2,1)S(1)}, u32[]{:S(2)}, u32[]{:S(2)}) collective-permute-start(bf16[1,257,512]{2,1,0:T(8,128)(2,1)S(1)} %pad_maximum_fusion.6), channel_id=1, source_target_pairs={{0,16},{4,20},{8,24},{12,28},{16,32},{20,36},{24,40},{28,44},{32,4... | collective-permute-start | bytes 789512 | tf_op jit(solution)/shard_map/ppermute | solution.py:19
  94.4 12.3 %copy-start.11 = (f32[4,64,256]{2,1,0:T(8,128)S(1)}, f32[4,64,256]{2,1,0:T(8,128)}, u32[]{:S(2)}) copy-start(f32[4,64,256]{2,1,0:T(8,128)} %convert.26) | copy-start | bytes 786436
  97.0 18.6 %collective-permute-start.5 = (bf16[1,257,512]{2,1,0:T(8,128)(2,1)}, bf16[1,257,512]{2,1,0:T(8,128)(2,1)}, u32[]{:S(2)}, u32[]{:S(2)}) collective-permute-start(bf16[1,257,512]{2,1,0:T(8,128)(2,1)} %pad_maximum_fusion.7), channel_id=1, source_target_pairs={{0,32},{4,36},{8,40},{12,44},{16,48},{20,52},{24,56},{28,60},{32,6... | collective-permute-start | bytes 789512 | tf_op jit(solution)/shard_map/ppermute | solution.py:19
  109.7 5.9 %copy-start.32 = (f32[1,256]{1,0:T(1,128)S(1)}, f32[1,256]{1,0:T(1,128)}, u32[]{:S(2)}) copy-start(f32[1,256]{1,0:T(1,128)} %copy-done.31) | copy-start | bytes 3076
  109.7 5.9 %copy-start.36 = (f32[1,256]{1,0:T(1,128)S(1)}, f32[1,256]{1,0:T(1,128)}, u32[]{:S(2)}) copy-start(f32[1,256]{1,0:T(1,128)} %copy-done.35) | copy-start | bytes 3076
  125.0 9.1 %copy-start.6 = (bf16[1,257,512]{2,1,0:T(8,128)(2,1)S(1)}, bf16[1,257,512]{2,1,0:T(8,128)(2,1)}, u32[]{:S(2)}) copy-start(bf16[1,257,512]{2,1,0:T(8,128)(2,1)} %copy-done.5) | copy-start | bytes 789508
  125.0 9.1 %copy-start.13 = (bf16[1,257,512]{2,1,0:T(8,128)(2,1)S(1)}, bf16[1,257,512]{2,1,0:T(8,128)(2,1)}, u32[]{:S(2)}) copy-start(bf16[1,257,512]{2,1,0:T(8,128)(2,1)} %copy-done.12) | copy-start | bytes 789508
  125.0 9.1 %copy-start.19 = (bf16[1,257,512]{2,1,0:T(8,128)(2,1)S(1)}, bf16[1,257,512]{2,1,0:T(8,128)(2,1)}, u32[]{:S(2)}) copy-start(bf16[1,257,512]{2,1,0:T(8,128)(2,1)} %copy-done.18) | copy-start | bytes 789508
  125.0 10.4 %copy-start.20 = (f32[8,64,256]{2,1,0:T(8,128)S(1)}, f32[8,64,256]{2,1,0:T(8,128)}, u32[]{:S(2)}) copy-start(f32[8,64,256]{2,1,0:T(8,128)} %gather_fusion.3) | copy-start | bytes 1572868
  125.0 10.4 %copy-start.23 = (f32[8,64,256]{2,1,0:T(8,128)S(1)}, f32[8,64,256]{2,1,0:T(8,128)}, u32[]{:S(2)}) copy-start(f32[8,64,256]{2,1,0:T(8,128)} %gather_fusion.2) | copy-start | bytes 1572868
  125.0 10.4 %copy-start.24 = (bf16[8,64,512]{2,1,0:T(8,128)(2,1)S(1)}, bf16[8,64,512]{2,1,0:T(8,128)(2,1)}, u32[]{:S(2)}) copy-start(bf16[8,64,512]{2,1,0:T(8,128)(2,1)} %gather_fusion.5) | copy-start | bytes 1572868
  125.0 10.4 %copy-start.41 = (f32[8,256]{1,0:T(8,128)S(1)}, f32[8,256]{1,0:T(8,128)}, u32[]{:S(2)}) copy-start(f32[8,256]{1,0:T(8,128)} %get-tuple-element.36) | copy-start | bytes 24580
  128.0 6.1 %copy-start.37 = (f32[1,256]{1,0:T(1,128)S(1)}, f32[1,256]{1,0:T(1,128)}, u32[]{:S(2)}) copy-start(f32[1,256]{1,0:T(1,128)} %copy-done.35) | copy-start | bytes 3076
  128.0 7.4 %copy-start.4 = (f32[8,256,512]{2,1,0:T(8,128)S(1)}, f32[8,256,512]{2,1,0:T(8,128)}, u32[]{:S(2)}) copy-start(f32[8,256,512]{2,1,0:T(8,128)} %gather_fusion.7) | copy-start | bytes 12582916
  128.0 7.4 %copy-start.30 = (f32[8,256]{1,0:T(8,128)S(1)}, f32[8,256]{1,0:T(8,128)}, u32[]{:S(2)}) copy-start(f32[8,256]{1,0:T(8,128)} %copy-done.29) | copy-start | bytes 24580
  128.0 7.4 %copy-start.40 = (f32[8,256]{1,0:T(8,128)S(1)}, f32[8,256]{1,0:T(8,128)}, u32[]{:S(2)}) copy-start(f32[8,256]{1,0:T(8,128)} %get-tuple-element.35) | copy-start | bytes 24580
  128.0 7.4 %copy-start.42 = (pred[8]{0:T(512)(128)(4,1)S(1)}, pred[8]{0:T(512)(128)(4,1)}, u32[]{:S(2)}) copy-start(pred[8]{0:T(512)(128)(4,1)} %get-tuple-element.56) | copy-start | bytes 28
  128.0 7.4 %copy-start.49 = (pred[8,64]{1,0:T(8,128)(4,1)S(1)}, pred[8,64]{1,0:T(8,128)(4,1)}, u32[]{:S(2)}) copy-start(pred[8,64]{1,0:T(8,128)(4,1)} %fusion.52) | copy-start | bytes 1540
  128.0 7.4 %copy-start.51 = (pred[8]{0:T(512)(128)(4,1)S(1)}, pred[8]{0:T(512)(128)(4,1)}, u32[]{:S(2)}) copy-start(pred[8]{0:T(512)(128)(4,1)} %get-tuple-element.57) | copy-start | bytes 28
  128.0 7.4 %copy-start.52 = (pred[8]{0:T(512)(128)(4,1)S(1)}, pred[8]{0:T(512)(128)(4,1)}, u32[]{:S(2)}) copy-start(pred[8]{0:T(512)(128)(4,1)} %get-tuple-element.58) | copy-start | bytes 28
  128.9 14.9 %collective-permute-start.8 = (bf16[256,512]{1,0:T(8,128)(2,1)}, bf16[256,512]{1,0:T(8,128)(2,1)}, u32[]{:S(2)}, u32[]{:S(2)}) collective-permute-start(bf16[256,512]{1,0:T(8,128)(2,1)} %bitcast.231), channel_id=1, source_target_pairs={{0,3},{1,0},{2,1},{3,2},{4,7},{5,4},{6,5},{7,6},{8,11},{9,8},{10,9... | collective-permute-start | bytes 786440 | tf_op jit(solution)/shard_map/ppermute | solution.py:253
  131.9 11.9 %collective-permute-start.6 = (bf16[256,512]{1,0:T(8,128)(2,1)S(1)}, bf16[256,512]{1,0:T(8,128)(2,1)}, u32[]{:S(2)}, u32[]{:S(2)}) collective-permute-start(bf16[256,512]{1,0:T(8,128)(2,1)S(1)} %bitcast.252), channel_id=1, source_target_pairs={{0,1},{1,2},{2,3},{3,0},{4,5},{5,6},{6,7},{7,4},{8,9},{9,10},{10,1... | collective-permute-start | bytes 786440 | tf_op jit(solution)/shard_map/ppermute | solution.py:253
  131.9 11.9 %collective-permute-start.7 = (bf16[256,512]{1,0:T(8,128)(2,1)S(1)}, bf16[256,512]{1,0:T(8,128)(2,1)}, u32[]{:S(2)}, u32[]{:S(2)}) collective-permute-start(bf16[256,512]{1,0:T(8,128)(2,1)S(1)} %bitcast.251), channel_id=1, source_target_pairs={{0,2},{1,3},{2,0},{3,1},{4,6},{5,7},{6,4},{7,5},{8,10},{9,11},{10,... | collective-permute-start | bytes 786440 | tf_op jit(solution)/shard_map/ppermute | solution.py:253
  143.8 34.7 %copy-start.16 = (bf16[250,2048]{1,0:T(8,128)(2,1)S(1)}, bf16[250,2048]{1,0:T(8,128)(2,1)}, u32[]{:S(2)}) copy-start(bf16[250,2048]{1,0:T(8,128)(2,1)} %param.25) | copy-start | bytes 3072004
  143.8 34.7 %copy-start.39 = (f32[2048]{0:T(1024)S(1)}, f32[2048]{0:T(1024)}, u32[]{:S(2)}) copy-start(f32[2048]{0:T(1024)} %param.24) | copy-start | bytes 24580
  146.3 104.0 %copy-start.25 = (bf16[256,512]{1,0:T(8,128)(2,1)}, bf16[256,512]{1,0:T(8,128)(2,1)S(1)}, u32[]{:S(2)}) copy-start(bf16[256,512]{1,0:T(8,128)(2,1)S(1)} %fusion.15) | copy-start | bytes 786436
  147.1 1.4 collective-permute-start.9
  148.7 4.1 %collective-permute-start.10 = (bf16[8,2048]{1,0:T(8,128)(2,1)S(1)}, bf16[8,2048]{1,0:T(8,128)(2,1)S(1)}, u32[]{:S(2)}, u32[]{:S(2)}) collective-permute-start(bf16[8,2048]{1,0:T(8,128)(2,1)S(1)} %add_dynamic-update-slice_fusion), channel_id=1, source_target_pairs={{0,8},{4,12},{8,0},{12,4},{16,24},{20,28},{24,16},{28,20},{32,40},... | collective-permute-start | bytes 98312 | tf_op jit(solution)/shard_map/ppermute | solution.py:27
  152.7 5.5 %collective-permute-start.11 = (bf16[8,2048]{1,0:T(8,128)(2,1)S(1)}, bf16[8,2048]{1,0:T(8,128)(2,1)S(1)}, u32[]{:S(2)}, u32[]{:S(2)}) collective-permute-start(bf16[8,2048]{1,0:T(8,128)(2,1)S(1)} %add.500), channel_id=1, source_target_pairs={{0,16},{4,20},{8,24},{12,28},{16,0},{20,4},{24,8},{28,12},{32,48},... | collective-permute-start | bytes 98312 | tf_op jit(solution)/shard_map/ppermute | solution.py:27
  158.3 4.5 %collective-permute-start.12 = (bf16[8,2048]{1,0:T(8,128)(2,1)S(1)}, bf16[8,2048]{1,0:T(8,128)(2,1)S(1)}, u32[]{:S(2)}, u32[]{:S(2)}) collective-permute-start(bf16[8,2048]{1,0:T(8,128)(2,1)S(1)} %add.501), channel_id=1, source_target_pairs={{0,32},{4,36},{8,40},{12,44},{16,48},{20,52},{24,56},{28,60},{32,0... | collective-permute-start | bytes 98312 | tf_op jit(solution)/shard_map/ppermute | solution.py:27
  162.7 5.5 %collective-permute-start.13 = (bf16[8,2048]{1,0:T(8,128)(2,1)S(1)}, bf16[8,2048]{1,0:T(8,128)(2,1)S(1)}, u32[]{:S(2)}, u32[]{:S(2)}) collective-permute-start(bf16[8,2048]{1,0:T(8,128)(2,1)S(1)} %add.502), channel_id=1, source_target_pairs={{0,64},{4,68},{8,72},{12,76},{16,80},{20,84},{24,88},{28,92},{32,9... | collective-permute-start | bytes 98312 | tf_op jit(solution)/shard_map/ppermute | solution.py:27
  168.3 4.0 %collective-permute-start.14 = (bf16[8,2048]{1,0:T(8,128)(2,1)S(1)}, bf16[8,2048]{1,0:T(8,128)(2,1)S(1)}, u32[]{:S(2)}, u32[]{:S(2)}) collective-permute-start(bf16[8,2048]{1,0:T(8,128)(2,1)S(1)} %add.503), channel_id=1, source_target_pairs={{0,1},{1,0},{2,3},{3,2},{4,5},{5,4},{6,7},{7,6},{8,9},{9,8},{10,11... | collective-permute-start | bytes 98312 | tf_op jit(solution)/shard_map/ppermute | solution.py:27
  172.3 5.5 %collective-permute-start.15 = (bf16[8,2048]{1,0:T(8,128)(2,1)S(1)}, bf16[8,2048]{1,0:T(8,128)(2,1)S(1)}, u32[]{:S(2)}, u32[]{:S(2)}) collective-permute-start(bf16[8,2048]{1,0:T(8,128)(2,1)S(1)} %add.504), channel_id=1, source_target_pairs={{0,2},{1,3},{2,0},{3,1},{4,6},{5,7},{6,4},{7,5},{8,10},{9,11},{10,... | collective-permute-start | bytes 98312 | tf_op jit(solution)/shard_map/ppermute | solution.py:27
  (15 other events, 49.3 us)
Sparse Core Ops, SparseCore 0:
  143.8 104.6 all-reduce.1

commit v4 on v3

--- a/solution.py
+++ b/solution.py
@@ -23,9 +23,13 @@
     peers = lax.axis_size(axis)
     step = 1
     while step < peers:
-        pairs = [(i, i ^ step) for i in range(peers)]
-        array = array + lax.ppermute(array, axis, pairs)
-        step *= 2
+        radix = 4 if peers % (step * 4) == 0 else 2
+        total = array
+        for digit in range(1, radix):
+            pairs = [(i, i ^ (digit * step)) for i in range(peers)]
+            total = total + lax.ppermute(array, axis, pairs)
+        array = total
+        step *= radix
     return array
 
 
@@ -198,10 +202,17 @@
     end_row = jnp.clip(offset, 0, row_count - 1)
     end_block, end_pos = end_row // BLOCK, end_row % BLOCK
     picks = jnp.arange(request_count)
-    end_keys_rows = key_rows[end_block]
-    end_values = values[end_block]
-    end_cumulative = cumulative[end_block]
-    end_segments = block_segment[end_block]
+    def at_end_block(array):
+        chosen = array[0]
+        for b in range(1, block_count):
+            hit = (end_block == b).reshape((request_count,) + (1,) * (array.ndim - 1))
+            chosen = jnp.where(hit, array[b][None], chosen)
+        return chosen
+
+    end_keys_rows = at_end_block(key_rows)
+    end_values = at_end_block(values)
+    end_cumulative = at_end_block(cumulative)
+    end_segments = at_end_block(block_segment)
     end_decay = end_cumulative[picks, end_pos]
     end_segment = end_segments[picks, end_pos]
     end_allowed = (
@@ -212,8 +223,8 @@
         jnp.bfloat16
     )
     within = jnp.einsum("rjhc,rjhv->rhcv", end_weighted, end_values, preferred_element_type=jnp.float32)
-    end_carried = (end_segment == segment_before[end_block])[:, None, None, None]
-    reached = jnp.where(end_carried, jnp.exp(end_decay)[:, :, :, None] * states_before[end_block], 0.0)
+    end_carried = (end_segment == at_end_block(segment_before))[:, None, None, None]
+    reached = jnp.where(end_carried, jnp.exp(end_decay)[:, :, :, None] * at_end_block(states_before), 0.0)
     local_ends = within + reached
 
     through_shard = segment[-1] == segment_prior
@@ -229,7 +240,7 @@
         precision=HIGHEST_PRECISION,
     )
     attended = (attended + correction).reshape(row_count, head_count, DV)
-    end_reach = jnp.exp(end_decay) * priors[end_block]
+    end_reach = jnp.exp(end_decay) * at_end_block(priors)
     end_from_before = (end_segment == segment_prior)[:, None, None, None]
     end_states = local_ends + jnp.where(
         end_from_before, end_reach[:, :, :, None] * incoming[None], 0.0

time: 265 us -> 295 us (1.11)
  other arithmetic: 46.9 us -> 59.5 us
  waiting for transfers between devices: 97.4 us -> 110 us
  starting transfers between devices: 42.9 us -> 49.8 us
  local copies, waits for them, and re-layouts: 41.3 us -> 37 us
    psum x1, waiting for transfers between devices: 69.1 us -> 91.9 us  [shards(): payload = lax.psum(payload.astype(jnp.bfloat16), 'seq').astype(jnp.float32)]
    ppermute x7 -> x10, waiting for transfers between devices: 23.3 us -> 6.33 us  [butterfly_sum(): total = total + lax.ppermute(array, axis, pairs)]
    gather x7 -> x0, local copies, waits for them, and re-layouts: 11.7 us -> none  [the longest x1 4.61 us: shards(): states_before[end_block]]
    ppermute x7 -> x10, starting transfers between devices: 7.15 us -> 15.6 us  [butterfly_sum(): total = total + lax.ppermute(array, axis, pairs)]
    ppermute x3, waiting for transfers between devices: 0.01 us -> 6.1 us  [shards(): lax.ppermute(outgoing, 'tp', [(i, (i + shift) % tp_size) for i in range(t...]
    eq x2 -> x4, other arithmetic: 1.86 us -> 5.65 us  [the longest x1 4.45 us: shards(): end_segment == at_end_block(segment_before)]
    select_n x0 -> x3, other arithmetic: none -> 3.58 us  [the longest x1 1.8 us: shards(): jnp.where(through[b], block_decay[b][:, :, None] * state, 0.0) + added[b]]
    another operation x7 -> x5, other arithmetic: 5.69 us -> 2.46 us
  transfers between devices with their start and end apart: 17 -> 20, of which waited for: 10 -> 11; matrix products, arithmetic and copies ran while one was open for 26% -> 25% of each run, Pallas kernels for 0% -> 0%
where the time goes in v4:
time: 295 us; the launch traced here: 293 us
  waiting for transfers between devices  110 us (37%)
  other arithmetic  59.5 us (20%)
  starting transfers between devices  49.8 us (17%)
  local copies, waits for them, and re-layouts  37 us (13%)
  matrix products  20.5 us (7%)
  between operations  16.5 us (6%)
    psum x1, waiting for transfers between devices, shards(): payload = lax.psum(payload.astype(jnp.bfloat16), 'seq').astype(jnp.float32)  91.9 us
    ppermute x6, starting transfers between devices, passed_along(): return lax.ppermute(array, axis, pairs)  28.9 us
    ppermute x10, starting transfers between devices, butterfly_sum(): total = total + lax.ppermute(array, axis, pairs)  15.6 us
    unnamed x161, local copies, waits for them, and re-layouts  11.7 us
    reduce_sum x1, other arithmetic, shards(): jnp.sum(queries[:, :, None] * key_rows[:, None, :] * weights, axis=-1)  8.48 us
    ppermute x10, waiting for transfers between devices, butterfly_sum(): total = total + lax.ppermute(array, axis, pairs)  6.33 us
    convert_element_type x4, other arithmetic, send_pair(): packed = jnp.concatenate([state.astype(jnp.bfloat16), row], axis=1)  6.11 us
    ppermute x3, waiting for transfers between devices, shards(): lax.ppermute(outgoing, 'tp', [(i, (i + shift) % tp_size) for i in range(t...  6.1 us
  transfers between devices with their start and end apart: 20, of which 11 were waited for; matrix products, arithmetic and copies ran while one was open for 25% of the time, Pallas kernels for 0%

profile of v4, /device:TPU:0, one launch (start us, length us, event | category | flops | bytes accessed | tf_op | source)
XLA Modules:
  0.0 293.0 jit_solution(9667305537926375431)
XLA Ops:
  7.2 1.6 multiply_reduce_fusion.1
  9.0 3.9 %convolution_convert_fusion.1 = bf16[256,1024]{1,0:T(8,128)(2,1)S(1)} fusion(bf16[2048,1024]{1,0:T(8,128)(2,1)} %param.16, f32[2048]{0:T(1024)} %param.15, f32[256]{0:T(256)S(1)} %add_rsqrt_fusion.1, bf16[256,2048]{1,0:T(8,128)(2,1)} %param.14), kind=kOutput, calls=%fused_computation.22 | convolution fusion | flops 1076101120 | bytes 5776384 | tf_op jit(solution)/shard_map/dot_general | solution.py:131
  14.3 1.9 collective-permute-start
  21.8 1.2 fusion.113
  24.4 1.3 broadcast_compare_fusion.2
  33.1 1.1 gather_fusion
  36.7 1.7 select_bitcast_fusion
  38.4 1.3 gather_fusion.1
  39.8 1.4 fusion.79
  41.1 1.3 pad_clamp_fusion.2
  42.4 1.2 maximum_bitcast_fusion.7
  43.7 1.8 multiply_select_fusion.1
  45.5 1.3 maximum_bitcast_fusion.6
  46.8 1.4 fusion.108
  48.1 4.5 %select_compare_fusion = (pred[8]{0:T(512)(128)(4,1)}, pred[8]{0:T(512)(128)(4,1)}) fusion(s32[8]{0:T(128)} %gather_fusion, s32[]{:T(128)} %bitcast.81, s32[]{:T(128)} %bitcast.80, s32[]{:T(128)} %bitcast.79, s32[]{:T(128)} %bitcast.78, s32[8]{0:T(128)} %copy-done.64, s32[]{:T(128)} %bitcast.27), kind=kLoop, calls=%fused_computation.248 | loop fusion | flops 64 | bytes 100 | tf_op jit(solution)/shard_map/eq | solution.py:226
  53.3 1.6 convert_element_type.286
  54.9 1.7 copy.41
  56.7 2.0 pad_maximum_fusion.2
  60.5 3.5 %fusion.22 = (bf16[1,256,512]{2,1,0:T(8,128)(2,1)S(1)}, f32[1,256,512]{2,1,0:T(8,128)}, f32[1,256,512]{2,1,0:T(8,128)}, f32[256,512]{1,0:T(8,128)}, f32[1,1,256,512]{3,2,1,0:T(8,128)}) fusion(f32[4,256,512]{2,1,0:T(8,128)S(1)} %fusion.65, f32[256]{0:T(256)S(1)} %bitcast.305, pred[]{:T(512)} %bitcast.24, f32[256]{0:T(256)S(1)} %bitcast.306, pred[]{:T(512)} %bitcast.18, ...), kind=kLoop, calls=%fused_computation.51 | loop fusion | flops 1441792 | bytes 4460547 | tf_op jit(solution)/shard_map/convert_element_type | solution.py:40
  64.0 4.1 %collective-permute-start.1 = (bf16[1,257,512]{2,1,0:T(8,128)(2,1)S(1)}, bf16[1,257,512]{2,1,0:T(8,128)(2,1)S(1)}, u32[]{:S(2)}, u32[]{:S(2)}) collective-permute-start(bf16[1,257,512]{2,1,0:T(8,128)(2,1)S(1)} %pad_maximum_fusion.3), channel_id=1, source_target_pairs={{0,4},{4,8},{8,12},{12,16},{16,20},{20,24},{24,28},{28,32},{32,36}... | collective-permute-start | bytes 789512 | tf_op jit(solution)/shard_map/ppermute | solution.py:19
  68.2 8.5 %multiply_reduce_fusion = bf16[4,64,64]{2,1,0:T(8,128)(2,1)} fusion(f32[4,64,256]{2,1,0:T(8,128)S(1)} %bitcast.275, f32[4,64,256]{2,1,0:T(8,128)S(1)} %bitcast.260, f32[4,64,256]{2,1,0:T(8,128)S(1)} %bitcast.269, pred[4,64,64]{2,1,0:T(8,128)(4,1)S(1)} %copy-done.30), kind=kLoop, calls=%fused_computation.6 | loop fusion | flops 25149440 | bytes 835584 | tf_op jit(solution)/shard_map/reduce_sum | solution.py:173
  76.7 1.8 gather_fusion.3
  79.3 1.9 collective-permute-start.2
  81.3 1.8 gather_fusion.4
  83.2 1.7 slice_bitcast_fusion.3
  85.8 7.0 %collective-permute-start.3 = (bf16[1,257,512]{2,1,0:T(8,128)(2,1)}, bf16[1,257,512]{2,1,0:T(8,128)(2,1)}, u32[]{:S(2)}, u32[]{:S(2)}) collective-permute-start(bf16[1,257,512]{2,1,0:T(8,128)(2,1)} %pad_maximum_fusion.5), channel_id=1, source_target_pairs={{0,8},{4,12},{8,16},{12,20},{16,24},{20,28},{24,32},{28,36},{32,40... | collective-permute-start | bytes 789512 | tf_op jit(solution)/shard_map/ppermute | solution.py:19
  92.8 1.8 gather_fusion.2
  95.4 2.2 collective-permute-done.3
  98.3 1.2 fusion.100
  99.6 4.8 %collective-permute-start.4 = (bf16[1,257,512]{2,1,0:T(8,128)(2,1)S(1)}, bf16[1,257,512]{2,1,0:T(8,128)(2,1)S(1)}, u32[]{:S(2)}, u32[]{:S(2)}) collective-permute-start(bf16[1,257,512]{2,1,0:T(8,128)(2,1)S(1)} %pad_maximum_fusion.6), channel_id=1, source_target_pairs={{0,16},{4,20},{8,24},{12,28},{16,32},{20,36},{24,40},{28,44},{32,4... | collective-permute-start | bytes 789512 | tf_op jit(solution)/shard_map/ppermute | solution.py:19
  104.5 2.5 fusion.12
  107.0 1.3 collective-permute-done.4
  108.3 1.3 fusion.38
  109.7 9.2 %collective-permute-start.5 = (bf16[1,257,512]{2,1,0:T(8,128)(2,1)S(1)}, bf16[1,257,512]{2,1,0:T(8,128)(2,1)S(1)}, u32[]{:S(2)}, u32[]{:S(2)}) collective-permute-start(bf16[1,257,512]{2,1,0:T(8,128)(2,1)S(1)} %pad_maximum_fusion.7), channel_id=1, source_target_pairs={{0,32},{4,36},{8,40},{12,44},{16,48},{20,52},{24,56},{28,60},{32,6... | collective-permute-start | bytes 789512 | tf_op jit(solution)/shard_map/ppermute | solution.py:19
  120.8 1.9 collective-permute-done.5
  122.7 2.8 multiply_reduce_fusion.2
  126.1 1.3 rsqrt.29
  127.4 2.6 fusion.26
  130.1 1.7 convolution_convert_fusion
  131.8 1.8 reshape.1345
  133.7 2.2 constant_dynamic-slice_fusion.3
  136.1 3.1 %collective-permute-start.8 = (bf16[256,512]{1,0:T(8,128)(2,1)S(1)}, bf16[256,512]{1,0:T(8,128)(2,1)S(1)}, u32[]{:S(2)}, u32[]{:S(2)}) collective-permute-start(bf16[256,512]{1,0:T(8,128)(2,1)S(1)} %bitcast.273), channel_id=1, source_target_pairs={{0,3},{1,0},{2,1},{3,2},{4,7},{5,4},{6,5},{7,6},{8,11},{9,8},{10,9... | collective-permute-start | bytes 786440 | tf_op jit(solution)/shard_map/ppermute | solution.py:264
  139.1 2.2 collective-permute-start.7
  141.4 2.1 fusion.97
  143.4 6.1 %collective-permute-done.6 = bf16[256,512]{1,0:T(8,128)(2,1)S(1)} collective-permute-done((bf16[256,512]{1,0:T(8,128)(2,1)S(1)}, bf16[256,512]{1,0:T(8,128)(2,1)S(1)}, u32[]{:S(2)}, u32[]{:S(2)}) %collective-permute-start.6) | collective-permute-done | bytes 262176 | tf_op jit(solution)/shard_map/ppermute | solution.py:264
  149.7 1.2 fusion.23
  152.3 4.2 %fusion.6 = bf16[1,8,256,512]{3,2,1,0:T(8,128)(2,1)S(1)} fusion(f32[256,512]{1,0:T(8,128)} %fusion.97, f32[8,256]{1,0:T(8,128)} %get-tuple-element.56, pred[8]{0:T(512)(128)(4,1)} %get-tuple-element.81, f32[256,512]{1,0:T(8,128)} %get-tuple-element.27, pred[8]{0:T(512)(128)(4,1)} %copy-done.47, f32[256,512]{1,0:T(8,128)S(1)} %bitcast.268, ...), kind=kOutput, calls=%fused_computation.20 | convolution fusion | flops 147980288 | bytes 5005872 | tf_op jit(solution)/shard_map/rjhc,rjhv->rhcv/dot_general | solution.py:225
  156.6 1.2 copy.50
  158.1 1.8 collective-permute-start.10
  160.0 1.1 collective-permute-done.11
  161.2 1.1 collective-permute-done.10
  162.2 3.7 %collective-permute-start.14 = (bf16[8,2048]{1,0:T(8,128)(2,1)S(1)}, bf16[8,2048]{1,0:T(8,128)(2,1)S(1)}, u32[]{:S(2)}, u32[]{:S(2)}) collective-permute-start(bf16[8,2048]{1,0:T(8,128)(2,1)S(1)} %add_add_fusion.2), channel_id=1, source_target_pairs={{0,48},{4,52},{8,56},{12,60},{16,32},{20,36},{24,40},{28,44},{32,1... | collective-permute-start | bytes 98312 | tf_op jit(solution)/shard_map/ppermute | solution.py:30
  165.9 1.8 collective-permute-start.12
  167.8 5.0 %pad_maximum_fusion = bf16[8,134144]{1,0:T(8,128)(2,1)} fusion(bf16[8,3072]{1,0:T(8,128)(2,1)S(1)} %bitcast.280, bf16[8,131072]{1,0:T(8,128)(2,1)S(1)} %bitcast.257), kind=kLoop, calls=%fused_computation.10 | loop fusion | flops 4292608 | bytes 4292608 | tf_op jit(solution)/shard_map/concatenate | solution.py:250
  172.9 3.7 %collective-permute-start.15 = (bf16[8,2048]{1,0:T(8,128)(2,1)S(1)}, bf16[8,2048]{1,0:T(8,128)(2,1)S(1)}, u32[]{:S(2)}, u32[]{:S(2)}) collective-permute-start(bf16[8,2048]{1,0:T(8,128)(2,1)S(1)} %add_add_fusion.1), channel_id=1, source_target_pairs={{0,64},{4,68},{8,72},{12,76},{16,80},{20,84},{24,88},{28,92},{32,9... | collective-permute-start | bytes 98312 | tf_op jit(solution)/shard_map/ppermute | solution.py:30
  176.5 1.9 collective-permute-done.15
  179.2 3.4 %collective-permute-start.16 = (bf16[8,2048]{1,0:T(8,128)(2,1)S(1)}, bf16[8,2048]{1,0:T(8,128)(2,1)S(1)}, u32[]{:S(2)}, u32[]{:S(2)}) collective-permute-start(bf16[8,2048]{1,0:T(8,128)(2,1)S(1)} %add.523), channel_id=1, source_target_pairs={{0,1},{1,0},{2,3},{3,2},{4,5},{5,4},{6,7},{7,6},{8,9},{9,8},{10,11... | collective-permute-start | bytes 98312 | tf_op jit(solution)/shard_map/ppermute | solution.py:30
  182.6 1.0 collective-permute-done.18
  183.6 1.0 collective-permute-done.17
  185.5 1.0 convolution_reduce_fusion
  186.5 91.9 %all-reduce.2.cloned.1.call-done = bf16[8,134144]{1,0:T(8,128)(2,1)} async-done(((bf16[8,134144]{1,0:T(8,128)(2,1)}), bf16[8,134144]{1,0:T(8,128)(2,1)}) %all-reduce.2.cloned.1.call-update) | async-done | bytes 2146320 | tf_op jit(solution)/shard_map/psum | solution.py:253
  278.4 1.9 slice.392
  280.3 4.4 %copy.73 = f32[1,8,256,512]{3,2,1,0:T(8,128)} copy(f32[1,8,256,512]{3,1,2,0:T(8,128)S(1)} %bitcast.256) | data formatting | bytes 8388608
  284.7 1.4 slice.393
  (262 shorter events, 29.2 us)
Async XLA Ops:
  7.2 122.9 %copy-start = (bf16[512,2048]{1,0:T(8,128)(2,1)S(1)}, bf16[512,2048]{1,0:T(8,128)(2,1)}, u32[]{:S(2)}) copy-start(bf16[512,2048]{1,0:T(8,128)(2,1)} %param.23) | copy-start | bytes 6291460
  7.2 271.2 %all-reduce.2.cloned.1.call-start = ((), (), s32[]{:S(2)}) async-start(), calls=%async_computation | async-start | bytes 4292608 | tf_op jit(solution)/shard_map/psum | solution.py:253
  8.9 11.9 %copy-start.67 = (f32[256]{0:T(256)}, f32[256]{0:T(256)S(1)}, u32[]{:S(2)}) copy-start(f32[256]{0:T(256)S(1)} %add_rsqrt_fusion.1) | copy-start | bytes 3076
  8.9 7.8 %copy-start.68 = (s32[8]{0:T(128)S(1)}, s32[8]{0:T(128)}, u32[]{:S(2)}) copy-start(s32[8]{0:T(128)} %param.26) | copy-start | bytes 100
  8.9 7.8 %copy-start.74 = (s32[8]{0:T(128)S(1)}, s32[8]{0:T(128)}, u32[]{:S(2)}) copy-start(s32[8]{0:T(128)} %param.27) | copy-start | bytes 100
  8.9 11.9 %copy-start.1 = (bf16[256,2048]{1,0:T(8,128)(2,1)S(1)}, bf16[256,2048]{1,0:T(8,128)(2,1)}, u32[]{:S(2)}) copy-start(bf16[256,2048]{1,0:T(8,128)(2,1)} %param.14) | copy-start | bytes 3145732
  8.9 11.9 %copy-start.70 = (bf16[2048,16]{0,1:T(8,128)(2,1)S(1)}, bf16[2048,16]{0,1:T(8,128)(2,1)}, u32[]{:S(2)}) copy-start(bf16[2048,16]{0,1:T(8,128)(2,1)} %param.18) | copy-start | bytes 196612
  8.9 11.9 %copy-start.72 = (f32[2048]{0:T(1024)S(1)}, f32[2048]{0:T(1024)}, u32[]{:S(2)}) copy-start(f32[2048]{0:T(1024)} %param.15) | copy-start | bytes 24580
  9.0 12.4 %copy-start.71 = (bf16[16,256]{1,0:T(8,128)(2,1)S(1)}, bf16[16,256]{1,0:T(8,128)(2,1)}, u32[]{:S(2)}) copy-start(bf16[16,256]{1,0:T(8,128)(2,1)} %param.19) | copy-start | bytes 24580
  9.0 12.4 %copy-start.73 = (f32[256]{0:T(256)S(1)}, f32[256]{0:T(256)}, u32[]{:S(2)}) copy-start(f32[256]{0:T(256)} %param.20) | copy-start | bytes 3076
  14.3 42.4 %collective-permute-start = (bf16[3,1024]{1,0:T(4,128)(2,1)}, bf16[3,1024]{1,0:T(4,128)(2,1)}, u32[]{:S(2)}, u32[]{:S(2)}) collective-permute-start(bf16[3,1024]{1,0:T(4,128)(2,1)} %slice.346), channel_id=1, source_target_pairs={{0,4},{4,8},{8,12},{12,16},{16,20},{20,24},{24,28},{28,32},{32,36}... | collective-permute-start | bytes 18440 | tf_op jit(solution)/shard_map/ppermute | solution.py:19
  19.5 9.9 %copy-start.40 = (f32[4,1024]{1,0:T(4,128)S(1)}, f32[4,1024]{1,0:T(4,128)}, u32[]{:S(2)}) copy-start(f32[4,1024]{1,0:T(4,128)} %param.17) | copy-start | bytes 49156
  20.8 12.2 %copy-start.49 = (s32[64]{0:T(128)}, s32[64]{0:T(128)S(1)}, u32[]{:S(2)}) copy-start(s32[64]{0:T(128)S(1)} %get-tuple-element.62) | copy-start | bytes 772
  20.8 12.2 %copy-start.50 = (s32[64]{0:T(128)}, s32[64]{0:T(128)S(1)}, u32[]{:S(2)}) copy-start(s32[64]{0:T(128)S(1)} %get-tuple-element.63) | copy-start | bytes 772
  20.8 12.2 %copy-start.51 = (s32[64]{0:T(128)}, s32[64]{0:T(128)S(1)}, u32[]{:S(2)}) copy-start(s32[64]{0:T(128)S(1)} %get-tuple-element.64) | copy-start | bytes 772
  20.8 12.2 %copy-start.52 = (s32[64]{0:T(128)}, s32[64]{0:T(128)S(1)}, u32[]{:S(2)}) copy-start(s32[64]{0:T(128)S(1)} %get-tuple-element.65) | copy-start | bytes 772
  28.2 7.8 %copy-start.41 = (pred[8]{0:T(512)(128)(4,1)}, pred[8]{0:T(512)(128)(4,1)S(1)}, u32[]{:S(2)}) copy-start(pred[8]{0:T(512)(128)(4,1)S(1)} %get-tuple-element.11) | copy-start | bytes 28
  28.3 7.8 %copy-start.46 = (pred[8]{0:T(512)(128)(4,1)}, pred[8]{0:T(512)(128)(4,1)S(1)}, u32[]{:S(2)}) copy-start(pred[8]{0:T(512)(128)(4,1)S(1)} %get-tuple-element.88) | copy-start | bytes 28
  39.7 16.9 %copy-start.28 = (f32[8,256]{1,0:T(8,128)}, f32[8,256]{1,0:T(8,128)S(1)}, u32[]{:S(2)}) copy-start(f32[8,256]{1,0:T(8,128)S(1)} %gather_fusion.1) | copy-start | bytes 24580
  59.6 17.0 %copy-start.6 = (bf16[256,1,1024]{2,0,1:T(8,128)(2,1)}, bf16[256,1,1024]{2,0,1:T(8,128)(2,1)S(1)}, u32[]{:S(2)}) copy-start(bf16[256,1,1024]{2,0,1:T(8,128)(2,1)S(1)} %fusion.34) | copy-start | bytes 1572868
  59.8 8.4 %copy-start.20 = (f32[256,1,256]{2,0,1:T(8,128)}, f32[256,1,256]{2,0,1:T(8,128)S(1)}, u32[]{:S(2)}) copy-start(f32[256,1,256]{2,0,1:T(8,128)S(1)} %get-tuple-element.39) | copy-start | bytes 786436
  60.5 7.7 %copy-start.21 = (f32[4,64,1,256]{3,1,2,0:T(8,128)S(1)}, f32[4,64,1,256]{3,1,2,0:T(8,128)}, u32[]{:S(2)}) copy-start(f32[4,64,1,256]{3,1,2,0:T(8,128)} %copy.78) | copy-start | bytes 786436
  60.5 7.7 %copy-start.30 = (pred[4,64,64]{2,1,0:T(8,128)(4,1)S(1)}, pred[4,64,64]{2,1,0:T(8,128)(4,1)}, u32[]{:S(2)}) copy-start(pred[4,64,64]{2,1,0:T(8,128)(4,1)} %compare_and_fusion) | copy-start | bytes 49156
  64.0 14.5 %collective-permute-start.1 = (bf16[1,257,512]{2,1,0:T(8,128)(2,1)S(1)}, bf16[1,257,512]{2,1,0:T(8,128)(2,1)S(1)}, u32[]{:S(2)}, u32[]{:S(2)}) collective-permute-start(bf16[1,257,512]{2,1,0:T(8,128)(2,1)S(1)} %pad_maximum_fusion.3), channel_id=1, source_target_pairs={{0,4},{4,8},{8,12},{12,16},{16,20},{20,24},{24,28},{28,32},{32,36}... | collective-permute-start | bytes 789512 | tf_op jit(solution)/shard_map/ppermute | solution.py:19
  68.2 13.1 %copy-start.59 = (pred[8]{0:T(512)(128)(4,1)S(1)}, pred[8]{0:T(512)(128)(4,1)}, u32[]{:S(2)}) copy-start(pred[8]{0:T(512)(128)(4,1)} %get-tuple-element.90) | copy-start | bytes 28
  76.7 16.1 %copy-start.58 = (pred[8]{0:T(512)(128)(4,1)S(1)}, pred[8]{0:T(512)(128)(4,1)}, u32[]{:S(2)}) copy-start(pred[8]{0:T(512)(128)(4,1)} %get-tuple-element.91) | copy-start | bytes 28
  79.3 5.5 %collective-permute-start.2 = (bf16[1,257,512]{2,1,0:T(8,128)(2,1)}, bf16[1,257,512]{2,1,0:T(8,128)(2,1)S(1)}, u32[]{:S(2)}, u32[]{:S(2)}) collective-permute-start(bf16[1,257,512]{2,1,0:T(8,128)(2,1)} %pad_maximum_fusion.4), channel_id=1, source_target_pairs={{0,4},{4,8},{8,12},{12,16},{16,20},{20,24},{24,28},{28,32},{32,36}... | collective-permute-start | bytes 789512 | tf_op jit(solution)/shard_map/ppermute | solution.py:19
  83.1 21.2 %copy-start.57 = (pred[8]{0:T(512)(128)(4,1)S(1)}, pred[8]{0:T(512)(128)(4,1)}, u32[]{:S(2)}) copy-start(pred[8]{0:T(512)(128)(4,1)} %get-tuple-element.92) | copy-start | bytes 28
  83.2 21.3 %copy-start.69 = (pred[4,64]{1,0:T(4,128)(4,1)S(1)}, pred[4,64]{1,0:T(4,128)(4,1)}, u32[]{:S(2)}) copy-start(pred[4,64]{1,0:T(4,128)(4,1)} %get-tuple-element.72) | copy-start | bytes 772
  84.8 23.5 %copy-start.3 = (bf16[1,257,512]{2,1,0:T(8,128)(2,1)}, bf16[1,257,512]{2,1,0:T(8,128)(2,1)S(1)}, u32[]{:S(2)}) copy-start(bf16[1,257,512]{2,1,0:T(8,128)(2,1)S(1)} %collective-permute-done.2) | copy-start | bytes 789508
  85.8 11.8 %collective-permute-start.3 = (bf16[1,257,512]{2,1,0:T(8,128)(2,1)}, bf16[1,257,512]{2,1,0:T(8,128)(2,1)}, u32[]{:S(2)}, u32[]{:S(2)}) collective-permute-start(bf16[1,257,512]{2,1,0:T(8,128)(2,1)} %pad_maximum_fusion.5), channel_id=1, source_target_pairs={{0,8},{4,12},{8,16},{12,20},{16,24},{20,28},{24,32},{28,36},{32,40... | collective-permute-start | bytes 789512 | tf_op jit(solution)/shard_map/ppermute | solution.py:19
  94.6 9.8 %copy-start.14 = (f32[1,256,512]{2,1,0:T(8,128)S(1)}, f32[1,256,512]{2,1,0:T(8,128)}, u32[]{:S(2)}) copy-start(f32[1,256,512]{2,1,0:T(8,128)} %get-tuple-element.22) | copy-start | bytes 1572868
  94.7 9.8 %copy-start.16 = (f32[1,256,512]{2,1,0:T(8,128)S(1)}, f32[1,256,512]{2,1,0:T(8,128)}, u32[]{:S(2)}) copy-start(f32[1,256,512]{2,1,0:T(8,128)} %get-tuple-element.23) | copy-start | bytes 1572868
  94.7 9.8 %copy-start.18 = (f32[1,1,256,512]{3,2,1,0:T(8,128)S(1)}, f32[1,1,256,512]{3,2,1,0:T(8,128)}, u32[]{:S(2)}) copy-start(f32[1,1,256,512]{3,2,1,0:T(8,128)} %get-tuple-element.28) | copy-start | bytes 1572868
  98.3 24.4 %copy-start.31 = (f32[1,256]{1,0:T(1,128)}, f32[1,256]{1,0:T(1,128)S(1)}, u32[]{:S(2)}) copy-start(f32[1,256]{1,0:T(1,128)S(1)} %get-tuple-element.16) | copy-start | bytes 3076
  99.6 8.7 %collective-permute-start.4 = (bf16[1,257,512]{2,1,0:T(8,128)(2,1)S(1)}, bf16[1,257,512]{2,1,0:T(8,128)(2,1)S(1)}, u32[]{:S(2)}, u32[]{:S(2)}) collective-permute-start(bf16[1,257,512]{2,1,0:T(8,128)(2,1)S(1)} %pad_maximum_fusion.6), channel_id=1, source_target_pairs={{0,16},{4,20},{8,24},{12,28},{16,32},{20,36},{24,40},{28,44},{32,4... | collective-permute-start | bytes 789512 | tf_op jit(solution)/shard_map/ppermute | solution.py:19
  104.4 15.1 %copy-start.10 = (f32[4,64,1,256]{3,1,2,0:T(8,128)S(1)}, f32[4,64,1,256]{3,1,2,0:T(8,128)}, u32[]{:S(2)}) copy-start(f32[4,64,1,256]{3,1,2,0:T(8,128)} %copy.41) | copy-start | bytes 786436
  104.5 15.1 %copy-start.33 = (f32[4,256]{1,0:T(4,128)S(1)}, f32[4,256]{1,0:T(4,128)}, u32[]{:S(2)}) copy-start(f32[4,256]{1,0:T(4,128)} %maximum_bitcast_fusion.6) | copy-start | bytes 12292
  104.5 15.1 %copy-start.65 = (pred[256]{0:T(512)(128)(4,1)S(1)}, pred[256]{0:T(512)(128)(4,1)}, u32[]{:S(2)}) copy-start(pred[256]{0:T(512)(128)(4,1)} %get-tuple-element.66) | copy-start | bytes 772
  107.0 13.6 %copy-start.8 = (bf16[256,1,512]{2,0,1:T(8,128)(2,1)S(1)}, bf16[256,1,512]{2,0,1:T(8,128)(2,1)}, u32[]{:S(2)}) copy-start(bf16[256,1,512]{2,0,1:T(8,128)(2,1)} %copy-done.7) | copy-start | bytes 786436
  107.0 13.6 %copy-start.27 = (bf16[4,64,64]{2,1,0:T(8,128)(2,1)S(1)}, bf16[4,64,64]{2,1,0:T(8,128)(2,1)}, u32[]{:S(2)}) copy-start(bf16[4,64,64]{2,1,0:T(8,128)(2,1)} %multiply_reduce_fusion) | copy-start | bytes 98308
  108.3 17.2 %copy-start.11 = (bf16[1,257,512]{2,1,0:T(8,128)(2,1)}, bf16[1,257,512]{2,1,0:T(8,128)(2,1)S(1)}, u32[]{:S(2)}) copy-start(bf16[1,257,512]{2,1,0:T(8,128)(2,1)S(1)} %collective-permute-done.4) | copy-start | bytes 789508
  108.3 17.2 %copy-start.42 = (f32[1,256]{1,0:T(1,128)}, f32[1,256]{1,0:T(1,128)S(1)}, u32[]{:S(2)}) copy-start(f32[1,256]{1,0:T(1,128)S(1)} %get-tuple-element.14) | copy-start | bytes 3076
  109.6 13.1 %copy-start.4 = (bf16[1,257,512]{2,1,0:T(8,128)(2,1)S(1)}, bf16[1,257,512]{2,1,0:T(8,128)(2,1)}, u32[]{:S(2)}) copy-start(bf16[1,257,512]{2,1,0:T(8,128)(2,1)} %copy-done.3) | copy-start | bytes 789508
  109.7 13.0 %collective-permute-start.5 = (bf16[1,257,512]{2,1,0:T(8,128)(2,1)S(1)}, bf16[1,257,512]{2,1,0:T(8,128)(2,1)S(1)}, u32[]{:S(2)}, u32[]{:S(2)}) collective-permute-start(bf16[1,257,512]{2,1,0:T(8,128)(2,1)S(1)} %pad_maximum_fusion.7), channel_id=1, source_target_pairs={{0,32},{4,36},{8,40},{12,44},{16,48},{20,52},{24,56},{28,60},{32,6... | collective-permute-start | bytes 789512 | tf_op jit(solution)/shard_map/ppermute | solution.py:19
  136.1 7.4 %collective-permute-start.8 = (bf16[256,512]{1,0:T(8,128)(2,1)S(1)}, bf16[256,512]{1,0:T(8,128)(2,1)S(1)}, u32[]{:S(2)}, u32[]{:S(2)}) collective-permute-start(bf16[256,512]{1,0:T(8,128)(2,1)S(1)} %bitcast.273), channel_id=1, source_target_pairs={{0,3},{1,0},{2,1},{3,2},{4,7},{5,4},{6,5},{7,6},{8,11},{9,8},{10,9... | collective-permute-start | bytes 786440 | tf_op jit(solution)/shard_map/ppermute | solution.py:264
  139.1 10.4 %collective-permute-start.6 = (bf16[256,512]{1,0:T(8,128)(2,1)S(1)}, bf16[256,512]{1,0:T(8,128)(2,1)S(1)}, u32[]{:S(2)}, u32[]{:S(2)}) collective-permute-start(bf16[256,512]{1,0:T(8,128)(2,1)S(1)} %bitcast.272), channel_id=1, source_target_pairs={{0,1},{1,2},{2,3},{3,0},{4,5},{5,6},{6,7},{7,4},{8,9},{9,10},{10,1... | collective-permute-start | bytes 786440 | tf_op jit(solution)/shard_map/ppermute | solution.py:264
  139.1 10.4 %collective-permute-start.7 = (bf16[256,512]{1,0:T(8,128)(2,1)S(1)}, bf16[256,512]{1,0:T(8,128)(2,1)S(1)}, u32[]{:S(2)}, u32[]{:S(2)}) collective-permute-start(bf16[256,512]{1,0:T(8,128)(2,1)S(1)} %bitcast.271), channel_id=1, source_target_pairs={{0,2},{1,3},{2,0},{3,1},{4,6},{5,7},{6,4},{7,5},{8,10},{9,11},{10,... | collective-permute-start | bytes 786440 | tf_op jit(solution)/shard_map/ppermute | solution.py:264
  143.4 8.9 %copy-start.15 = (f32[1,256,512]{2,1,0:T(8,128)S(1)}, f32[1,256,512]{2,1,0:T(8,128)}, u32[]{:S(2)}) copy-start(f32[1,256,512]{2,1,0:T(8,128)} %get-tuple-element.22) | copy-start | bytes 1572868
  143.4 8.9 %copy-start.17 = (f32[1,256,512]{2,1,0:T(8,128)S(1)}, f32[1,256,512]{2,1,0:T(8,128)}, u32[]{:S(2)}) copy-start(f32[1,256,512]{2,1,0:T(8,128)} %get-tuple-element.23) | copy-start | bytes 1572868
  143.4 8.9 %copy-start.29 = (f32[8,256]{1,0:T(8,128)S(1)}, f32[8,256]{1,0:T(8,128)}, u32[]{:S(2)}) copy-start(f32[8,256]{1,0:T(8,128)} %copy-done.28) | copy-start | bytes 24580
  152.3 7.6 %collective-permute-start.9 = (bf16[8,2048]{1,0:T(8,128)(2,1)S(1)}, bf16[8,2048]{1,0:T(8,128)(2,1)S(1)}, u32[]{:S(2)}, u32[]{:S(2)}) collective-permute-start(bf16[8,2048]{1,0:T(8,128)(2,1)S(1)} %fusion.80), channel_id=1, source_target_pairs={{0,4},{4,0},{8,12},{12,8},{16,20},{20,16},{24,28},{28,24},{32,36},... | collective-permute-start | bytes 98312 | tf_op jit(solution)/shard_map/ppermute | solution.py:30
  156.6 11.2 %copy-start.26 = (bf16[8,3,1024]{2,0,1:T(8,128)(2,1)S(1)}, bf16[8,3,1024]{2,0,1:T(8,128)(2,1)}, u32[]{:S(2)}) copy-start(bf16[8,3,1024]{2,0,1:T(8,128)(2,1)} %pad_maximum_fusion.8) | copy-start | bytes 147460
  157.7 3.4 %collective-permute-start.11 = (bf16[8,2048]{1,0:T(8,128)(2,1)S(1)}, bf16[8,2048]{1,0:T(8,128)(2,1)S(1)}, u32[]{:S(2)}, u32[]{:S(2)}) collective-permute-start(bf16[8,2048]{1,0:T(8,128)(2,1)S(1)} %fusion.80), channel_id=1, source_target_pairs={{0,12},{4,8},{8,4},{12,0},{16,28},{20,24},{24,20},{28,16},{32,44},... | collective-permute-start | bytes 98312 | tf_op jit(solution)/shard_map/ppermute | solution.py:30
  158.1 4.1 %collective-permute-start.10 = (bf16[8,2048]{1,0:T(8,128)(2,1)S(1)}, bf16[8,2048]{1,0:T(8,128)(2,1)S(1)}, u32[]{:S(2)}, u32[]{:S(2)}) collective-permute-start(bf16[8,2048]{1,0:T(8,128)(2,1)S(1)} %fusion.80), channel_id=1, source_target_pairs={{0,8},{4,12},{8,0},{12,4},{16,24},{20,28},{24,16},{28,20},{32,40},... | collective-permute-start | bytes 98312 | tf_op jit(solution)/shard_map/ppermute | solution.py:30
  162.2 10.6 %collective-permute-start.14 = (bf16[8,2048]{1,0:T(8,128)(2,1)S(1)}, bf16[8,2048]{1,0:T(8,128)(2,1)S(1)}, u32[]{:S(2)}, u32[]{:S(2)}) collective-permute-start(bf16[8,2048]{1,0:T(8,128)(2,1)S(1)} %add_add_fusion.2), channel_id=1, source_target_pairs={{0,48},{4,52},{8,56},{12,60},{16,32},{20,36},{24,40},{28,44},{32,1... | collective-permute-start | bytes 98312 | tf_op jit(solution)/shard_map/ppermute | solution.py:30
  165.9 6.9 %collective-permute-start.13 = (bf16[8,2048]{1,0:T(8,128)(2,1)S(1)}, bf16[8,2048]{1,0:T(8,128)(2,1)S(1)}, u32[]{:S(2)}, u32[]{:S(2)}) collective-permute-start(bf16[8,2048]{1,0:T(8,128)(2,1)S(1)} %add_add_fusion.2), channel_id=1, source_target_pairs={{0,32},{4,36},{8,40},{12,44},{16,48},{20,52},{24,56},{28,60},{32,0... | collective-permute-start | bytes 98312 | tf_op jit(solution)/shard_map/ppermute | solution.py:30
  165.9 6.9 %collective-permute-start.12 = (bf16[8,2048]{1,0:T(8,128)(2,1)S(1)}, bf16[8,2048]{1,0:T(8,128)(2,1)S(1)}, u32[]{:S(2)}, u32[]{:S(2)}) collective-permute-start(bf16[8,2048]{1,0:T(8,128)(2,1)S(1)} %add_add_fusion.2), channel_id=1, source_target_pairs={{0,16},{4,20},{8,24},{12,28},{16,0},{20,4},{24,8},{28,12},{32,48},... | collective-permute-start | bytes 98312 | tf_op jit(solution)/shard_map/ppermute | solution.py:30
  172.8 12.7 %copy-start.9 = (bf16[250,2048]{1,0:T(8,128)(2,1)S(1)}, bf16[250,2048]{1,0:T(8,128)(2,1)}, u32[]{:S(2)}) copy-start(bf16[250,2048]{1,0:T(8,128)(2,1)} %param.25) | copy-start | bytes 3072004
  172.8 12.7 %copy-start.44 = (f32[2048]{0:T(1024)S(1)}, f32[2048]{0:T(1024)}, u32[]{:S(2)}) copy-start(f32[2048]{0:T(1024)} %param.24) | copy-start | bytes 24580
  172.9 5.6 %collective-permute-start.15 = (bf16[8,2048]{1,0:T(8,128)(2,1)S(1)}, bf16[8,2048]{1,0:T(8,128)(2,1)S(1)}, u32[]{:S(2)}, u32[]{:S(2)}) collective-permute-start(bf16[8,2048]{1,0:T(8,128)(2,1)S(1)} %add_add_fusion.1), channel_id=1, source_target_pairs={{0,64},{4,68},{8,72},{12,76},{16,80},{20,84},{24,88},{28,92},{32,9... | collective-permute-start | bytes 98312 | tf_op jit(solution)/shard_map/ppermute | solution.py:30
  178.4 5.2 %collective-permute-start.18 = (bf16[8,2048]{1,0:T(8,128)(2,1)S(1)}, bf16[8,2048]{1,0:T(8,128)(2,1)S(1)}, u32[]{:S(2)}, u32[]{:S(2)}) collective-permute-start(bf16[8,2048]{1,0:T(8,128)(2,1)S(1)} %add.523), channel_id=1, source_target_pairs={{0,3},{1,2},{2,1},{3,0},{4,7},{5,6},{6,5},{7,4},{8,11},{9,10},{10,... | collective-permute-start | bytes 98312 | tf_op jit(solution)/shard_map/ppermute | solution.py:30
  179.2 5.4 %collective-permute-start.17 = (bf16[8,2048]{1,0:T(8,128)(2,1)S(1)}, bf16[8,2048]{1,0:T(8,128)(2,1)S(1)}, u32[]{:S(2)}, u32[]{:S(2)}) collective-permute-start(bf16[8,2048]{1,0:T(8,128)(2,1)S(1)} %add.523), channel_id=1, source_target_pairs={{0,2},{1,3},{2,0},{3,1},{4,6},{5,7},{6,4},{7,5},{8,10},{9,11},{10,... | collective-permute-start | bytes 98312 | tf_op jit(solution)/shard_map/ppermute | solution.py:30
  179.2 5.6 %collective-permute-start.16 = (bf16[8,2048]{1,0:T(8,128)(2,1)S(1)}, bf16[8,2048]{1,0:T(8,128)(2,1)S(1)}, u32[]{:S(2)}, u32[]{:S(2)}) collective-permute-start(bf16[8,2048]{1,0:T(8,128)(2,1)S(1)} %add.523), channel_id=1, source_target_pairs={{0,1},{1,0},{2,3},{3,2},{4,5},{5,4},{6,7},{7,6},{8,9},{9,8},{10,11... | collective-permute-start | bytes 98312 | tf_op jit(solution)/shard_map/ppermute | solution.py:30
  (31 other events, 109.3 us)
Sparse Core Ops, SparseCore 0:
  172.9 105.4 all-reduce.1

commit v5 on v3

--- a/solution.py
+++ b/solution.py
@@ -239,7 +239,7 @@
     payload = jnp.concatenate(
         [end_states.reshape(request_count, state_width), conv_edges.reshape(request_count, -1)], axis=1
     )
-    payload = lax.psum(payload.astype(jnp.bfloat16), "seq").astype(jnp.float32)
+    payload = lax.psum(payload, "seq")
     last_states = payload[:, :state_width].reshape(end_states.shape)
     conv_edges = payload[:, state_width:].reshape(conv_edges.shape)
 

time: 265 us -> 249 us (0.940)
  waiting for transfers between devices: 97.4 us -> 85.1 us
  other arithmetic: 46.9 us -> 41.3 us
  matrix products: 18.2 us -> 21.5 us
    psum x1, waiting for transfers between devices: 69.1 us -> 49.3 us  [shards(): payload = lax.psum(payload, 'seq')]
    ppermute x3, waiting for transfers between devices: 0.01 us -> 5.84 us  [shards(): lax.ppermute(outgoing, 'tp', [(i, (i + shift) % tp_size) for i in range(t...]
    unnamed x133 -> x105, local copies, waits for them, and re-layouts: 11.3 us -> 13.7 us
  transfers between devices with their start and end apart: 17 -> 17, of which waited for: 10 -> 11; matrix products, arithmetic and copies ran while one was open for 26% -> 26% of each run, Pallas kernels for 0% -> 0%
where the time goes in v5:
time: 249 us; the launch traced here: 247 us
  waiting for transfers between devices  85.1 us (34%)
  local copies, waits for them, and re-layouts  42.1 us (17%)
  other arithmetic  41.3 us (17%)
  starting transfers between devices  40.9 us (16%)
  matrix products  21.5 us (9%)
  between operations  16.3 us (7%)
    psum x1, waiting for transfers between devices, shards(): payload = lax.psum(payload, 'seq')  49.3 us
    ppermute x6, starting transfers between devices, passed_along(): return lax.ppermute(array, axis, pairs)  30.4 us
    ppermute x7, waiting for transfers between devices, butterfly_sum(): array = array + lax.ppermute(array, axis, pairs)  25 us
    unnamed x105, local copies, waits for them, and re-layouts  13.7 us
    reduce_sum x1, other arithmetic, shards(): jnp.sum(queries[:, :, None] * key_rows[:, None, :] * weights, axis=-1)  8.6 us
    ppermute x3, waiting for transfers between devices, shards(): lax.ppermute(outgoing, 'tp', [(i, (i + shift) % tp_size) for i in range(t...  5.84 us
    ppermute x3, starting transfers between devices, shards(): lax.ppermute(outgoing, 'tp', [(i, (i + shift) % tp_size) for i in range(t...  5.24 us
    ppermute x7, starting transfers between devices, butterfly_sum(): array = array + lax.ppermute(array, axis, pairs)  5.24 us
  transfers between devices with their start and end apart: 17, of which 11 were waited for; matrix products, arithmetic and copies ran while one was open for 26% of the time, Pallas kernels for 0%

profile of v5, /device:TPU:0, one launch (start us, length us, event | category | flops | bytes accessed | tf_op | source)
XLA Modules:
  0.0 247.3 jit_solution(13836252278814026302)
XLA Ops:
  7.2 1.6 multiply_reduce_fusion.1
  9.0 3.9 %convolution_convert_fusion.1 = bf16[256,1024]{1,0:T(8,128)(2,1)S(1)} fusion(bf16[2048,1024]{1,0:T(8,128)(2,1)} %param.16, f32[2048]{0:T(1024)} %param.15, f32[256]{0:T(256)S(1)} %add_rsqrt_fusion.1, bf16[256,2048]{1,0:T(8,128)(2,1)} %param.14), kind=kOutput, calls=%fused_computation.22 | convolution fusion | flops 1076101120 | bytes 5776384 | tf_op jit(solution)/shard_map/dot_general | solution.py:127
  12.9 0.8 copy-done.14
  13.7 1.4 collective-permute-start
  21.2 1.3 broadcast_compare_fusion.2
  25.8 1.2 fusion.79
  28.6 1.4 gather_fusion.3
  29.9 1.3 gather_fusion.4
  33.1 2.0 pad_maximum_fusion.2
  35.2 0.9 fusion.19
  36.1 0.8 fusion.75
  38.2 1.3 copy-done.1
  39.5 2.9 %fusion.13 = (bf16[1,256,512]{2,1,0:T(8,128)(2,1)S(1)}, f32[1,256,512]{2,1,0:T(8,128)S(1)}, f32[1,1,256,512]{3,2,1,0:T(8,128)}) fusion(f32[4,256,512]{2,1,0:T(8,128)S(1)} %fusion.34, f32[256]{0:T(256)S(1)} %bitcast.282, pred[]{:T(512)} %bitcast.26, f32[256]{0:T(256)S(1)} %bitcast.279, pred[]{:T(512)} %bitcast.20, f32[256]{0:T(256)S(1)} %bitcast.281, ...), kind=kLoop, calls=%fused_computation.50 | loop fusion | flops 1441792 | bytes 3411971 | tf_op jit(solution)/shard_map/convert_element_type | solution.py:36
  42.4 0.8 pad_maximum_fusion.3
  43.2 4.7 %collective-permute-start.1 = (bf16[1,257,512]{2,1,0:T(8,128)(2,1)}, bf16[1,257,512]{2,1,0:T(8,128)(2,1)S(1)}, u32[]{:S(2)}, u32[]{:S(2)}) collective-permute-start(bf16[1,257,512]{2,1,0:T(8,128)(2,1)} %pad_maximum_fusion.3), channel_id=1, source_target_pairs={{0,4},{4,8},{8,12},{12,16},{16,20},{20,24},{24,28},{28,32},{32,36}... | collective-permute-start | bytes 789512 | tf_op jit(solution)/shard_map/ppermute | solution.py:19
  47.9 1.7 gather_fusion.11
  49.6 8.6 %multiply_reduce_fusion = bf16[4,64,64]{2,1,0:T(8,128)(2,1)S(1)} fusion(f32[4,64,256]{2,1,0:T(8,128)S(1)} %bitcast.248, f32[4,64,256]{2,1,0:T(8,128)} %convert.7, f32[4,64,256]{2,1,0:T(8,128)} %bitcast.256, pred[4,64,64]{2,1,0:T(8,128)(4,1)S(1)} %compare_and_fusion), kind=kLoop, calls=%fused_computation.13 | loop fusion | flops 25149440 | bytes 835584 | tf_op jit(solution)/shard_map/reduce_sum | solution.py:169
  58.3 1.7 gather_fusion.10
  60.0 1.7 gather_fusion.9
  61.9 1.9 collective-permute-start.2
  63.8 1.7 fusion.46
  65.8 7.9 %collective-permute-start.3 = (bf16[1,257,512]{2,1,0:T(8,128)(2,1)S(1)}, bf16[1,257,512]{2,1,0:T(8,128)(2,1)S(1)}, u32[]{:S(2)}, u32[]{:S(2)}) collective-permute-start(bf16[1,257,512]{2,1,0:T(8,128)(2,1)S(1)} %pad_maximum_fusion.5), channel_id=1, source_target_pairs={{0,8},{4,12},{8,16},{12,20},{16,24},{20,28},{24,32},{28,36},{32,40... | collective-permute-start | bytes 789512 | tf_op jit(solution)/shard_map/ppermute | solution.py:19
  73.8 1.7 maximum_bitcast_fusion
  75.5 3.4 %collective-permute-done.3 = bf16[1,257,512]{2,1,0:T(8,128)(2,1)S(1)} collective-permute-done((bf16[1,257,512]{2,1,0:T(8,128)(2,1)S(1)}, bf16[1,257,512]{2,1,0:T(8,128)(2,1)S(1)}, u32[]{:S(2)}, u32[]{:S(2)}) %collective-permute-start.3) | collective-permute-done | bytes 263200 | tf_op jit(solution)/shard_map/ppermute | solution.py:19
  79.2 4.9 %collective-permute-start.4 = (bf16[1,257,512]{2,1,0:T(8,128)(2,1)S(1)}, bf16[1,257,512]{2,1,0:T(8,128)(2,1)S(1)}, u32[]{:S(2)}, u32[]{:S(2)}) collective-permute-start(bf16[1,257,512]{2,1,0:T(8,128)(2,1)S(1)} %pad_maximum_fusion.6), channel_id=1, source_target_pairs={{0,16},{4,20},{8,24},{12,28},{16,32},{20,36},{24,40},{28,44},{32,4... | collective-permute-start | bytes 789512 | tf_op jit(solution)/shard_map/ppermute | solution.py:19
  84.2 2.3 fusion.4
  86.5 1.5 collective-permute-done.4
  89.1 9.6 %collective-permute-start.5 = (bf16[1,257,512]{2,1,0:T(8,128)(2,1)}, bf16[1,257,512]{2,1,0:T(8,128)(2,1)}, u32[]{:S(2)}, u32[]{:S(2)}) collective-permute-start(bf16[1,257,512]{2,1,0:T(8,128)(2,1)} %pad_maximum_fusion.7), channel_id=1, source_target_pairs={{0,32},{4,36},{8,40},{12,44},{16,48},{20,52},{24,56},{28,60},{32,6... | collective-permute-start | bytes 789512 | tf_op jit(solution)/shard_map/ppermute | solution.py:19
  98.7 1.5 gather_fusion.2
  100.2 1.5 gather_fusion.5
  101.7 4.6 %gather_fusion.7 = f32[8,256,512]{2,1,0:T(8,128)} fusion(f32[4,256,512]{2,1,0:T(8,128)} %maximum_bitcast_fusion, s32[1024]{0:T(1024)} %copy-done.20), kind=kCustom, calls=%fused_computation.7 | custom fusion | bytes 8388640 | tf_op jit(solution)/shard_map/gather | solution.py:216
  106.3 1.1 fusion.26
  107.4 1.2 fusion.2
  108.8 2.8 %multiply_reduce_fusion.2 = (f32[4,64]{1,0:T(4,128)S(1)}, f32[4,64,1,512]{3,1,0,2:T(8,128)}) fusion(f32[4,64,1,512]{3,1,0,2:T(8,128)S(1)} %fusion.2, f32[4,64,256]{2,1,0:T(8,128)S(1)} %bitcast.258, bf16[1,257,512]{2,1,0:T(8,128)(2,1)} %collective-permute-done.5, f32[256]{0:T(256)S(1)} %bitcast.277, bf16[1,257,512]{2,1,0:T(8,128)(2,1)} %copy-done.13, ...), kind=kOutput, calls=%fused_computation.62 | convolution fusion | flops 404750080 | bytes 2626560 | tf_op jit(solution)/shard_map/bphc,hcv->bphv/dot_general | solution.py:225
  111.6 1.3 fusion.66
  113.0 4.5 %select_bitcast_fusion = f32[1,8,256,512]{3,2,1,0:T(8,128)S(1)} fusion(f32[8,256,512]{2,1,0:T(8,128)} %gather_fusion.7, bf16[8,64,512]{2,1,0:T(8,128)(2,1)} %gather_fusion.5, f32[256,512]{1,0:T(8,128)S(1)} %fusion.66, f32[8,256]{1,0:T(8,128)S(1)} %copy-done.23, f32[8,256]{1,0:T(8,128)S(1)} %copy-done.22, pred[8]{0:T(512)(128)(4,1)S(1)} %copy-done.35, ...), kind=kOutput, calls=%fused_computation.16 | convolution fusion | flops 142213120 | bytes 10510872 | tf_op jit(solution)/shard_map/rjhc,rjhv->rhcv/dot_general | solution.py:214
  117.5 2.4 copy.37
  119.9 2.9 %pad_maximum_fusion = f32[8,134144]{1,0:T(8,128)} fusion(f32[8,3072]{1,0:T(8,128)S(1)} %bitcast.253, f32[8,131072]{1,0:T(8,128)S(1)} %bitcast.237), kind=kLoop, calls=%fused_computation.14 | loop fusion | flops 1073152 | bytes 8585216 | tf_op jit(solution)/shard_map/concatenate | solution.py:239
  122.9 1.2 copy-done.3
  124.1 2.5 %fusion.17 = bf16[256,512]{1,0:T(8,128)(2,1)S(1)} fusion(f32[4,64,1,512]{3,1,0,2:T(8,128)} %get-tuple-element.75, bf16[2048,512]{1,0:T(8,128)(2,1)} %param.21, f32[512]{0:T(512)S(1)} %copy-done.43, f32[256]{0:T(256)S(1)} %rsqrt.29, f32[2048]{0:T(1024)S(1)} %copy-done.42, f32[256]{0:T(256)S(1)} %copy-done.31, bf16[256,2048]{1,0:T(8,128)(2,1)S(1)} %copy-done.3), kind=kOutput, calls=%fused_computation.59 | convolution fusion | flops 540278784 | bytes 3944448 | tf_op jit(solution)/shard_map/dot_general | solution.py:137
  126.6 1.7 convolution_convert_fusion
  128.3 1.8 reshape.1030
  130.2 3.0 %constant_dynamic-slice_fusion.3 = (bf16[256,1,512]{2,1,0:T(2,128)(2,1)}, bf16[256,1,512]{2,1,0:T(2,128)(2,1)S(1)}, bf16[256,1,512]{2,1,0:T(2,128)(2,1)S(1)}, bf16[256,1,512]{2,1,0:T(2,128)(2,1)S(1)}) fusion(bf16[256,4,512]{2,1,0:T(4,128)(2,1)S(1)} %reshape.1030, s32[]{:T(128)S(6)} %select_n.402, s32[]{:T(128)S(6)} %select_n.406, s32[]{:T(128)S(6)} %select_n.404, ...), kind=kLoop, calls=%fused_computation.136 | loop fusion | bytes 2097168 | tf_op jit(solution)/shard_map/jit(dynamic_index_in_dim)/dynamic_slice | solution.py:249
  134.7 3.1 %collective-permute-start.8 = (bf16[256,512]{1,0:T(8,128)(2,1)}, bf16[256,512]{1,0:T(8,128)(2,1)}, u32[]{:S(2)}, u32[]{:S(2)}) collective-permute-start(bf16[256,512]{1,0:T(8,128)(2,1)} %bitcast.231), channel_id=1, source_target_pairs={{0,3},{1,0},{2,1},{3,2},{4,7},{5,4},{6,5},{7,6},{8,11},{9,8},{10,9... | collective-permute-start | bytes 786440 | tf_op jit(solution)/shard_map/ppermute | solution.py:253
  137.7 2.2 collective-permute-start.7
  139.9 1.6 convert_element_type.282
  141.5 1.1 copy.60
  142.6 5.8 %collective-permute-done.6 = bf16[256,512]{1,0:T(8,128)(2,1)} collective-permute-done((bf16[256,512]{1,0:T(8,128)(2,1)}, bf16[256,512]{1,0:T(8,128)(2,1)}, u32[]{:S(2)}, u32[]{:S(2)}) %collective-permute-start.6) | collective-permute-done | bytes 262176 | tf_op jit(solution)/shard_map/ppermute | solution.py:253
  148.4 1.4 pad_maximum_fusion.1
  149.8 1.2 fusion.14
  151.7 1.2 collective-permute-done.9
  153.4 3.5 %collective-permute-done.10 = bf16[8,2048]{1,0:T(8,128)(2,1)S(1)} collective-permute-done((bf16[8,2048]{1,0:T(8,128)(2,1)S(1)}, bf16[8,2048]{1,0:T(8,128)(2,1)S(1)}, u32[]{:S(2)}, u32[]{:S(2)}) %collective-permute-start.10) | collective-permute-done | bytes 32800 | tf_op jit(solution)/shard_map/ppermute | solution.py:27
  156.9 0.9 collective-permute-start.11
  157.9 4.6 %collective-permute-done.11 = bf16[8,2048]{1,0:T(8,128)(2,1)S(1)} collective-permute-done((bf16[8,2048]{1,0:T(8,128)(2,1)S(1)}, bf16[8,2048]{1,0:T(8,128)(2,1)S(1)}, u32[]{:S(2)}, u32[]{:S(2)}) %collective-permute-start.11) | collective-permute-done | bytes 32800 | tf_op jit(solution)/shard_map/ppermute | solution.py:27
  162.5 1.1 collective-permute-start.12
  163.6 3.4 %collective-permute-done.12 = bf16[8,2048]{1,0:T(8,128)(2,1)S(1)} collective-permute-done((bf16[8,2048]{1,0:T(8,128)(2,1)S(1)}, bf16[8,2048]{1,0:T(8,128)(2,1)S(1)}, u32[]{:S(2)}, u32[]{:S(2)}) %collective-permute-start.12) | collective-permute-done | bytes 32800 | tf_op jit(solution)/shard_map/ppermute | solution.py:27
  167.0 2.6 %collective-permute-start.13 = (bf16[8,2048]{1,0:T(8,128)(2,1)S(1)}, bf16[8,2048]{1,0:T(8,128)(2,1)S(1)}, u32[]{:S(2)}, u32[]{:S(2)}) collective-permute-start(bf16[8,2048]{1,0:T(8,128)(2,1)S(1)} %add.502), channel_id=1, source_target_pairs={{0,64},{4,68},{8,72},{12,76},{16,80},{20,84},{24,88},{28,92},{32,9... | collective-permute-start | bytes 98312 | tf_op jit(solution)/shard_map/ppermute | solution.py:27
  169.6 3.0 %collective-permute-done.13 = bf16[8,2048]{1,0:T(8,128)(2,1)S(1)} collective-permute-done((bf16[8,2048]{1,0:T(8,128)(2,1)S(1)}, bf16[8,2048]{1,0:T(8,128)(2,1)S(1)}, u32[]{:S(2)}, u32[]{:S(2)}) %collective-permute-start.13) | collective-permute-done | bytes 32800 | tf_op jit(solution)/shard_map/ppermute | solution.py:27
  172.7 3.9 %collective-permute-done.14 = bf16[8,2048]{1,0:T(8,128)(2,1)S(1)} collective-permute-done((bf16[8,2048]{1,0:T(8,128)(2,1)S(1)}, bf16[8,2048]{1,0:T(8,128)(2,1)S(1)}, u32[]{:S(2)}, u32[]{:S(2)}) %collective-permute-start.14) | collective-permute-done | bytes 32800 | tf_op jit(solution)/shard_map/ppermute | solution.py:27
  176.8 5.4 %collective-permute-done.15 = bf16[8,2048]{1,0:T(8,128)(2,1)S(1)} collective-permute-done((bf16[8,2048]{1,0:T(8,128)(2,1)S(1)}, bf16[8,2048]{1,0:T(8,128)(2,1)S(1)}, u32[]{:S(2)}, u32[]{:S(2)}) %collective-permute-start.15) | collective-permute-done | bytes 32800 | tf_op jit(solution)/shard_map/ppermute | solution.py:27
  182.8 1.0 convolution_reduce_fusion
  183.8 49.3 %all-reduce.2.cloned.1.call-done = f32[8,134144]{1,0:T(8,128)} async-done(((f32[8,134144]{1,0:T(8,128)}), f32[8,134144]{1,0:T(8,128)}) %all-reduce.2.cloned.1.call-update) | async-done | bytes 4292624 | tf_op jit(solution)/shard_map/psum | solution.py:242
  233.1 2.2 slice-done.2
  235.3 4.4 %copy.56 = f32[1,8,256,512]{3,2,1,0:T(8,128)} copy(f32[1,8,256,512]{3,1,2,0:T(8,128)S(1)} %bitcast.240) | data formatting | bytes 8388608
  (206 shorter events, 19.0 us)
Async XLA Ops:
  7.2 119.4 %copy-start = (bf16[512,2048]{1,0:T(8,128)(2,1)S(1)}, bf16[512,2048]{1,0:T(8,128)(2,1)}, u32[]{:S(2)}) copy-start(bf16[512,2048]{1,0:T(8,128)(2,1)} %param.23) | copy-start | bytes 6291460
  7.2 225.9 %all-reduce.2.cloned.1.call-start = ((), (), s32[]{:S(2)}) async-start(), calls=%async_computation | async-start | bytes 8585216 | tf_op jit(solution)/shard_map/psum | solution.py:242
  8.9 10.9 %copy-start.30 = (f32[256]{0:T(256)}, f32[256]{0:T(256)S(1)}, u32[]{:S(2)}) copy-start(f32[256]{0:T(256)S(1)} %add_rsqrt_fusion.1) | copy-start | bytes 3076
  8.9 6.2 %copy-start.33 = (s32[8]{0:T(128)S(1)}, s32[8]{0:T(128)}, u32[]{:S(2)}) copy-start(s32[8]{0:T(128)} %param.26) | copy-start | bytes 100
  8.9 6.2 %copy-start.45 = (s32[8]{0:T(128)S(1)}, s32[8]{0:T(128)}, u32[]{:S(2)}) copy-start(s32[8]{0:T(128)} %param.27) | copy-start | bytes 100
  8.9 10.8 %copy-start.2 = (bf16[256,2048]{1,0:T(8,128)(2,1)S(1)}, bf16[256,2048]{1,0:T(8,128)(2,1)}, u32[]{:S(2)}) copy-start(bf16[256,2048]{1,0:T(8,128)(2,1)} %param.14) | copy-start | bytes 3145732
  8.9 10.8 %copy-start.39 = (bf16[2048,16]{0,1:T(8,128)(2,1)S(1)}, bf16[2048,16]{0,1:T(8,128)(2,1)}, u32[]{:S(2)}) copy-start(bf16[2048,16]{0,1:T(8,128)(2,1)} %param.18) | copy-start | bytes 196612
  8.9 10.8 %copy-start.41 = (f32[2048]{0:T(1024)S(1)}, f32[2048]{0:T(1024)}, u32[]{:S(2)}) copy-start(f32[2048]{0:T(1024)} %param.15) | copy-start | bytes 24580
  13.7 6.6 %copy-start.40 = (bf16[16,256]{1,0:T(8,128)(2,1)S(1)}, bf16[16,256]{1,0:T(8,128)(2,1)}, u32[]{:S(2)}) copy-start(bf16[16,256]{1,0:T(8,128)(2,1)} %param.19) | copy-start | bytes 24580
  13.7 6.6 %copy-start.44 = (f32[256]{0:T(256)S(1)}, f32[256]{0:T(256)}, u32[]{:S(2)}) copy-start(f32[256]{0:T(256)} %param.20) | copy-start | bytes 3076
  13.7 19.4 %collective-permute-start = (bf16[3,1024]{1,0:T(4,128)(2,1)S(1)}, bf16[3,1024]{1,0:T(4,128)(2,1)S(1)}, u32[]{:S(2)}, u32[]{:S(2)}) collective-permute-start(bf16[3,1024]{1,0:T(4,128)(2,1)S(1)} %slice.260), channel_id=1, source_target_pairs={{0,4},{4,8},{8,12},{12,16},{16,20},{20,24},{24,28},{28,32},{32,36}... | collective-permute-start | bytes 18440 | tf_op jit(solution)/shard_map/ppermute | solution.py:19
  18.5 10.1 %copy-start.20 = (s32[1024]{0:T(1024)}, s32[1024]{0:T(1024)S(1)}, u32[]{:S(2)}) copy-start(s32[1024]{0:T(1024)S(1)} %pad_clamp_fusion.4) | copy-start | bytes 12292
  19.8 7.3 %copy-start.19 = (f32[4,1024]{1,0:T(4,128)S(1)}, f32[4,1024]{1,0:T(4,128)}, u32[]{:S(2)}) copy-start(f32[4,1024]{1,0:T(4,128)} %param.17) | copy-start | bytes 49156
  21.2 16.4 %copy-start.6 = (f32[4,64,1,256]{3,2,1,0:T(1,128)}, f32[4,64,1,256]{3,2,1,0:T(1,128)S(1)}, u32[]{:S(2)}) copy-start(f32[4,64,1,256]{3,2,1,0:T(1,128)S(1)} %get-tuple-element.73) | copy-start | bytes 786436
  31.2 4.0 %copy-start.17 = (f32[8,256]{1,0:T(8,128)}, f32[8,256]{1,0:T(8,128)S(1)}, u32[]{:S(2)}) copy-start(f32[8,256]{1,0:T(8,128)S(1)} %gather_fusion.4) | copy-start | bytes 24580
  36.0 2.2 copy-start.5
  38.2 1.3 copy-start.1
  43.2 18.6 %collective-permute-start.1 = (bf16[1,257,512]{2,1,0:T(8,128)(2,1)}, bf16[1,257,512]{2,1,0:T(8,128)(2,1)S(1)}, u32[]{:S(2)}, u32[]{:S(2)}) collective-permute-start(bf16[1,257,512]{2,1,0:T(8,128)(2,1)} %pad_maximum_fusion.3), channel_id=1, source_target_pairs={{0,4},{4,8},{8,12},{12,16},{16,20},{20,24},{24,28},{28,32},{32,36}... | collective-permute-start | bytes 789512 | tf_op jit(solution)/shard_map/ppermute | solution.py:19
  49.6 8.6 %copy-start.27 = (pred[8]{0:T(512)(128)(4,1)S(1)}, pred[8]{0:T(512)(128)(4,1)}, u32[]{:S(2)}) copy-start(pred[8]{0:T(512)(128)(4,1)} %get-tuple-element.52) | copy-start | bytes 28
  49.6 12.1 %copy-start.26 = (pred[8]{0:T(512)(128)(4,1)S(1)}, pred[8]{0:T(512)(128)(4,1)}, u32[]{:S(2)}) copy-start(pred[8]{0:T(512)(128)(4,1)} %get-tuple-element.51) | copy-start | bytes 28
  60.0 13.7 %copy-start.37 = (f32[4]{0:T(128)S(1)}, f32[4]{0:T(128)}, u32[]{:S(2)}) copy-start(f32[4]{0:T(128)} %pad.33.clone) | copy-start | bytes 52
  61.7 12.0 %copy-start.11 = (f32[1,1,256,512]{3,2,1,0:T(8,128)S(1)}, f32[1,1,256,512]{3,2,1,0:T(8,128)}, u32[]{:S(2)}) copy-start(f32[1,1,256,512]{3,2,1,0:T(8,128)} %get-tuple-element.20) | copy-start | bytes 1572868
  61.9 3.7 %collective-permute-start.2 = (bf16[1,257,512]{2,1,0:T(8,128)(2,1)S(1)}, bf16[1,257,512]{2,1,0:T(8,128)(2,1)S(1)}, u32[]{:S(2)}, u32[]{:S(2)}) collective-permute-start(bf16[1,257,512]{2,1,0:T(8,128)(2,1)S(1)} %pad_maximum_fusion.4), channel_id=1, source_target_pairs={{0,4},{4,8},{8,12},{12,16},{16,20},{20,24},{24,28},{28,32},{32,36}... | collective-permute-start | bytes 789512 | tf_op jit(solution)/shard_map/ppermute | solution.py:19
  65.8 13.0 %collective-permute-start.3 = (bf16[1,257,512]{2,1,0:T(8,128)(2,1)S(1)}, bf16[1,257,512]{2,1,0:T(8,128)(2,1)S(1)}, u32[]{:S(2)}, u32[]{:S(2)}) collective-permute-start(bf16[1,257,512]{2,1,0:T(8,128)(2,1)S(1)} %pad_maximum_fusion.5), channel_id=1, source_target_pairs={{0,8},{4,12},{8,16},{12,20},{16,24},{20,28},{24,32},{28,36},{32,40... | collective-permute-start | bytes 789512 | tf_op jit(solution)/shard_map/ppermute | solution.py:19
  73.8 10.3 %copy-start.25 = (pred[8]{0:T(512)(128)(4,1)S(1)}, pred[8]{0:T(512)(128)(4,1)}, u32[]{:S(2)}) copy-start(pred[8]{0:T(512)(128)(4,1)} %get-tuple-element.53) | copy-start | bytes 28
  73.8 10.4 %copy-start.7 = (f32[4,64,1,256]{3,2,1,0:T(1,128)S(1)}, f32[4,64,1,256]{3,2,1,0:T(1,128)}, u32[]{:S(2)}) copy-start(f32[4,64,1,256]{3,2,1,0:T(1,128)} %copy-done.6) | copy-start | bytes 786436
  73.8 10.4 %copy-start.16 = (f32[256,1,256]{2,0,1:T(8,128)S(1)}, f32[256,1,256]{2,0,1:T(8,128)}, u32[]{:S(2)}) copy-start(f32[256,1,256]{2,0,1:T(8,128)} %get-tuple-element.28) | copy-start | bytes 786436
  73.8 10.4 %copy-start.36 = (pred[4,64]{1,0:T(4,128)(4,1)S(1)}, pred[4,64]{1,0:T(4,128)(4,1)}, u32[]{:S(2)}) copy-start(pred[4,64]{1,0:T(4,128)(4,1)} %get-tuple-element.50) | copy-start | bytes 772
  73.8 10.4 %copy-start.38 = (f32[4]{0:T(128)S(1)}, f32[4]{0:T(128)}, u32[]{:S(2)}) copy-start(f32[4]{0:T(128)} %pad.33.clone) | copy-start | bytes 52
  78.9 9.2 %copy-start.9 = (bf16[1,257,512]{2,1,0:T(8,128)(2,1)}, bf16[1,257,512]{2,1,0:T(8,128)(2,1)S(1)}, u32[]{:S(2)}) copy-start(bf16[1,257,512]{2,1,0:T(8,128)(2,1)S(1)} %collective-permute-done.3) | copy-start | bytes 789508
  79.2 8.8 %collective-permute-start.4 = (bf16[1,257,512]{2,1,0:T(8,128)(2,1)S(1)}, bf16[1,257,512]{2,1,0:T(8,128)(2,1)S(1)}, u32[]{:S(2)}, u32[]{:S(2)}) collective-permute-start(bf16[1,257,512]{2,1,0:T(8,128)(2,1)S(1)} %pad_maximum_fusion.6), channel_id=1, source_target_pairs={{0,16},{4,20},{8,24},{12,28},{16,32},{20,36},{24,40},{28,44},{32,4... | collective-permute-start | bytes 789512 | tf_op jit(solution)/shard_map/ppermute | solution.py:19
  86.5 12.2 %copy-start.8 = (f32[4,64,256]{2,1,0:T(8,128)S(1)}, f32[4,64,256]{2,1,0:T(8,128)}, u32[]{:S(2)}) copy-start(f32[4,64,256]{2,1,0:T(8,128)} %convert.7) | copy-start | bytes 786436
  89.1 19.6 %collective-permute-start.5 = (bf16[1,257,512]{2,1,0:T(8,128)(2,1)}, bf16[1,257,512]{2,1,0:T(8,128)(2,1)}, u32[]{:S(2)}, u32[]{:S(2)}) collective-permute-start(bf16[1,257,512]{2,1,0:T(8,128)(2,1)} %pad_maximum_fusion.7), channel_id=1, source_target_pairs={{0,32},{4,36},{8,40},{12,44},{16,48},{20,52},{24,56},{28,60},{32,6... | collective-permute-start | bytes 789512 | tf_op jit(solution)/shard_map/ppermute | solution.py:19
  101.7 4.6 %copy-start.29 = (pred[256]{0:T(512)(128)(4,1)S(1)}, pred[256]{0:T(512)(128)(4,1)}, u32[]{:S(2)}) copy-start(pred[256]{0:T(512)(128)(4,1)} %get-tuple-element.43) | copy-start | bytes 772
  101.7 6.9 %copy-start.10 = (bf16[1,257,512]{2,1,0:T(8,128)(2,1)S(1)}, bf16[1,257,512]{2,1,0:T(8,128)(2,1)}, u32[]{:S(2)}) copy-start(bf16[1,257,512]{2,1,0:T(8,128)(2,1)} %copy-done.9) | copy-start | bytes 789508
  108.7 4.3 %copy-start.18 = (f32[8,256]{1,0:T(8,128)S(1)}, f32[8,256]{1,0:T(8,128)}, u32[]{:S(2)}) copy-start(f32[8,256]{1,0:T(8,128)} %copy-done.17) | copy-start | bytes 24580
  108.7 4.3 %copy-start.22 = (f32[8,256]{1,0:T(8,128)S(1)}, f32[8,256]{1,0:T(8,128)}, u32[]{:S(2)}) copy-start(f32[8,256]{1,0:T(8,128)} %get-tuple-element.35) | copy-start | bytes 24580
  108.7 4.3 %copy-start.23 = (f32[8,256]{1,0:T(8,128)S(1)}, f32[8,256]{1,0:T(8,128)}, u32[]{:S(2)}) copy-start(f32[8,256]{1,0:T(8,128)} %get-tuple-element.36) | copy-start | bytes 24580
  108.7 4.3 %copy-start.24 = (pred[8]{0:T(512)(128)(4,1)S(1)}, pred[8]{0:T(512)(128)(4,1)}, u32[]{:S(2)}) copy-start(pred[8]{0:T(512)(128)(4,1)} %get-tuple-element.56) | copy-start | bytes 28
  108.7 4.3 %copy-start.32 = (pred[8,64]{1,0:T(8,128)(4,1)S(1)}, pred[8,64]{1,0:T(8,128)(4,1)}, u32[]{:S(2)}) copy-start(pred[8,64]{1,0:T(8,128)(4,1)} %fusion.48) | copy-start | bytes 1540
  108.7 4.3 %copy-start.34 = (pred[8]{0:T(512)(128)(4,1)S(1)}, pred[8]{0:T(512)(128)(4,1)}, u32[]{:S(2)}) copy-start(pred[8]{0:T(512)(128)(4,1)} %get-tuple-element.57) | copy-start | bytes 28
  108.8 4.3 %copy-start.35 = (pred[8]{0:T(512)(128)(4,1)S(1)}, pred[8]{0:T(512)(128)(4,1)}, u32[]{:S(2)}) copy-start(pred[8]{0:T(512)(128)(4,1)} %get-tuple-element.58) | copy-start | bytes 28
  122.8 1.2 copy-start.3
  122.8 1.2 copy-start.31
  122.8 1.2 copy-start.42
  122.8 1.2 copy-start.43
  133.1 6.8 %copy-start.4 = (bf16[256,2048]{1,0:T(8,128)(2,1)S(1)}, bf16[256,2048]{1,0:T(8,128)(2,1)}, u32[]{:S(2)}) copy-start(bf16[256,2048]{1,0:T(8,128)(2,1)} %param.14) | copy-start | bytes 3145732
  133.9 7.5 %copy-start.28 = (s32[8]{0:T(128)S(1)}, s32[8]{0:T(128)}, u32[]{:S(2)}) copy-start(s32[8]{0:T(128)} %get-tuple-element.64) | copy-start | bytes 100
  134.7 7.9 %collective-permute-start.8 = (bf16[256,512]{1,0:T(8,128)(2,1)}, bf16[256,512]{1,0:T(8,128)(2,1)}, u32[]{:S(2)}, u32[]{:S(2)}) collective-permute-start(bf16[256,512]{1,0:T(8,128)(2,1)} %bitcast.231), channel_id=1, source_target_pairs={{0,3},{1,0},{2,1},{3,2},{4,7},{5,4},{6,5},{7,6},{8,11},{9,8},{10,9... | collective-permute-start | bytes 786440 | tf_op jit(solution)/shard_map/ppermute | solution.py:253
  137.7 10.7 %collective-permute-start.6 = (bf16[256,512]{1,0:T(8,128)(2,1)}, bf16[256,512]{1,0:T(8,128)(2,1)}, u32[]{:S(2)}, u32[]{:S(2)}) collective-permute-start(bf16[256,512]{1,0:T(8,128)(2,1)} %bitcast.233), channel_id=1, source_target_pairs={{0,1},{1,2},{2,3},{3,0},{4,5},{5,6},{6,7},{7,4},{8,9},{9,10},{10,1... | collective-permute-start | bytes 786440 | tf_op jit(solution)/shard_map/ppermute | solution.py:253
  137.7 10.7 %collective-permute-start.7 = (bf16[256,512]{1,0:T(8,128)(2,1)S(1)}, bf16[256,512]{1,0:T(8,128)(2,1)}, u32[]{:S(2)}, u32[]{:S(2)}) collective-permute-start(bf16[256,512]{1,0:T(8,128)(2,1)S(1)} %bitcast.254), channel_id=1, source_target_pairs={{0,2},{1,3},{2,0},{3,1},{4,6},{5,7},{6,4},{7,5},{8,10},{9,11},{10,... | collective-permute-start | bytes 786440 | tf_op jit(solution)/shard_map/ppermute | solution.py:253
  148.4 34.4 %copy-start.12 = (bf16[250,2048]{1,0:T(8,128)(2,1)S(1)}, bf16[250,2048]{1,0:T(8,128)(2,1)}, u32[]{:S(2)}) copy-start(bf16[250,2048]{1,0:T(8,128)(2,1)} %param.25) | copy-start | bytes 3072004
  148.4 34.4 %copy-start.21 = (f32[2048]{0:T(1024)S(1)}, f32[2048]{0:T(1024)}, u32[]{:S(2)}) copy-start(f32[2048]{0:T(1024)} %param.24) | copy-start | bytes 24580
  151.0 82.1 %copy-start.15 = (bf16[256,512]{1,0:T(8,128)(2,1)}, bf16[256,512]{1,0:T(8,128)(2,1)S(1)}, u32[]{:S(2)}) copy-start(bf16[256,512]{1,0:T(8,128)(2,1)S(1)} %fusion.14) | copy-start | bytes 786436
  151.7 1.2 collective-permute-start.9
  153.0 3.9 %collective-permute-start.10 = (bf16[8,2048]{1,0:T(8,128)(2,1)S(1)}, bf16[8,2048]{1,0:T(8,128)(2,1)S(1)}, u32[]{:S(2)}, u32[]{:S(2)}) collective-permute-start(bf16[8,2048]{1,0:T(8,128)(2,1)S(1)} %add_dynamic-update-slice_fusion), channel_id=1, source_target_pairs={{0,8},{4,12},{8,0},{12,4},{16,24},{20,28},{24,16},{28,20},{32,40},... | collective-permute-start | bytes 98312 | tf_op jit(solution)/shard_map/ppermute | solution.py:27
  156.9 5.5 %collective-permute-start.11 = (bf16[8,2048]{1,0:T(8,128)(2,1)S(1)}, bf16[8,2048]{1,0:T(8,128)(2,1)S(1)}, u32[]{:S(2)}, u32[]{:S(2)}) collective-permute-start(bf16[8,2048]{1,0:T(8,128)(2,1)S(1)} %add.500), channel_id=1, source_target_pairs={{0,16},{4,20},{8,24},{12,28},{16,0},{20,4},{24,8},{28,12},{32,48},... | collective-permute-start | bytes 98312 | tf_op jit(solution)/shard_map/ppermute | solution.py:27
  162.5 4.5 %collective-permute-start.12 = (bf16[8,2048]{1,0:T(8,128)(2,1)S(1)}, bf16[8,2048]{1,0:T(8,128)(2,1)S(1)}, u32[]{:S(2)}, u32[]{:S(2)}) collective-permute-start(bf16[8,2048]{1,0:T(8,128)(2,1)S(1)} %add.501), channel_id=1, source_target_pairs={{0,32},{4,36},{8,40},{12,44},{16,48},{20,52},{24,56},{28,60},{32,0... | collective-permute-start | bytes 98312 | tf_op jit(solution)/shard_map/ppermute | solution.py:27
  167.0 5.6 %collective-permute-start.13 = (bf16[8,2048]{1,0:T(8,128)(2,1)S(1)}, bf16[8,2048]{1,0:T(8,128)(2,1)S(1)}, u32[]{:S(2)}, u32[]{:S(2)}) collective-permute-start(bf16[8,2048]{1,0:T(8,128)(2,1)S(1)} %add.502), channel_id=1, source_target_pairs={{0,64},{4,68},{8,72},{12,76},{16,80},{20,84},{24,88},{28,92},{32,9... | collective-permute-start | bytes 98312 | tf_op jit(solution)/shard_map/ppermute | solution.py:27
  172.7 4.0 %collective-permute-start.14 = (bf16[8,2048]{1,0:T(8,128)(2,1)S(1)}, bf16[8,2048]{1,0:T(8,128)(2,1)S(1)}, u32[]{:S(2)}, u32[]{:S(2)}) collective-permute-start(bf16[8,2048]{1,0:T(8,128)(2,1)S(1)} %add.503), channel_id=1, source_target_pairs={{0,1},{1,0},{2,3},{3,2},{4,5},{5,4},{6,7},{7,6},{8,9},{9,8},{10,11... | collective-permute-start | bytes 98312 | tf_op jit(solution)/shard_map/ppermute | solution.py:27
  176.7 5.5 %collective-permute-start.15 = (bf16[8,2048]{1,0:T(8,128)(2,1)S(1)}, bf16[8,2048]{1,0:T(8,128)(2,1)S(1)}, u32[]{:S(2)}, u32[]{:S(2)}) collective-permute-start(bf16[8,2048]{1,0:T(8,128)(2,1)S(1)} %add.504), channel_id=1, source_target_pairs={{0,2},{1,3},{2,0},{3,1},{4,6},{5,7},{6,4},{7,5},{8,10},{9,11},{10,... | collective-permute-start | bytes 98312 | tf_op jit(solution)/shard_map/ppermute | solution.py:27
  233.1 2.2 slice-start.2
  233.1 6.6 %slice-start = ((s8[4292608]{0:T(1024)(128)(4,1)}), s8[4194304]{0:T(1024)(128)(4,1)S(1)}, s32[]{:S(2)}) async-start(s8[4292608]{0:T(1024)(128)(4,1)} %bitcast.238), calls=%async_computation.1 | async-start | bytes 8388608
  233.1 6.6 %slice-start.1 = ((s8[4292608]{0:T(1024)(128)(4,1)}), s8[98304]{0:T(1024)(128)(4,1)S(1)}, s32[]{:S(2)}) async-start(s8[4292608]{0:T(1024)(128)(4,1)} %bitcast.238), calls=%async_computation.2 | async-start | bytes 196608
  (2 other events, 1.8 us)
Sparse Core Ops, SparseCore 0:
  123.0 110.0 all-reduce.1

commit v6 on v2

--- a/solution.py
+++ b/solution.py
@@ -29,14 +29,22 @@
     return array
 
 
+def send_pair(decay, state, axis, by):
+    high = decay.astype(jnp.bfloat16)
+    low = (decay - high.astype(jnp.float32)).astype(jnp.bfloat16)
+    row = jnp.concatenate([high, low], axis=-1)[:, None, :]
+    packed = jnp.concatenate([state.astype(jnp.bfloat16), row], axis=1)
+    got = passed_along(packed, axis, by)
+    tail = got[:, DK].astype(jnp.float32)
+    return tail[:, :DK] + tail[:, DK:], got[:, :DK].astype(jnp.float32)
+
+
 def state_prefix(decay_factor, local_state, axis, reach):
     peers, place = lax.axis_size(axis), lax.axis_index(axis)
-    decay = passed_along(decay_factor, axis, 1)
-    state = passed_along(local_state.astype(jnp.bfloat16), axis, 1).astype(jnp.float32)
+    decay, state = send_pair(decay_factor, local_state, axis, 1)
     step = 1
     while step < min(peers, reach):
-        earlier_decay = passed_along(decay, axis, step)
-        earlier_state = passed_along(state.astype(jnp.bfloat16), axis, step).astype(jnp.float32)
+        earlier_decay, earlier_state = send_pair(decay, state, axis, step)
         state = state + decay[..., None] * earlier_state
         decay = jnp.where(place >= step, decay * earlier_decay, decay)
         step *= 2
@@ -225,9 +233,7 @@
     end_shard = last_index // row_count
     shard_ids = jnp.arange(seq_size)
     between = (shard_ids[None, :] > seq_index) & (shard_ids[None, :] < end_shard[:, None])
-    spanned = jnp.prod(
-        jnp.where(between[:, :, None, None], shard_decays[None], 1.0), axis=1
-    )
+    spanned = jnp.prod(jnp.where(between[:, :, None, None], shard_decays[None], 1.0), axis=1)
     from_here = (seq_index < end_shard)[:, None, None, None]
     end_terms = jnp.where(owned_here[:, None, None, None], local_ends, 0.0) + jnp.where(
         from_here, (end_reaches * spanned)[:, :, :, None] * local_state[None], 0.0
@@ -236,12 +242,11 @@
     payload = jnp.concatenate(
         [end_terms.reshape(request_count, state_width), conv_edges.reshape(request_count, -1)], axis=1
     )
-    payload = lax.psum(payload.astype(jnp.bfloat16), "seq").astype(jnp.float32)
-
-    incoming = state_prefix(decay_factor, local_state, "seq", -(-MAXLEN // row_count))
-    payload, incoming = lax.optimization_barrier((payload, incoming))
+    payload = lax.psum(payload, "seq")
     last_states = payload[:, :state_width].reshape(local_ends.shape)
     conv_edges = payload[:, state_width:].reshape(conv_edges.shape)
+
+    incoming = state_prefix(decay_factor, local_state, "seq", -(-MAXLEN // row_count))
     reach = jnp.exp(cumulative) * priors[:, None]
     from_before = (block_segment == segment_prior)[:, :, None, None]
     correction = jnp.einsum(

time: 315 us -> 265 us (0.84)
  waiting for transfers between devices: 118 us -> 84 us
  starting transfers between devices: 64.5 us -> 45.4 us
  local copies, waits for them, and re-layouts: 41.7 us -> 45.5 us
  other arithmetic: 53.3 us -> 50.1 us
    psum x1, waiting for transfers between devices: 82.5 us -> 40.5 us  [shards(): payload = lax.psum(payload, 'seq')]
    ppermute x12, starting transfers between devices: 25.3 us -> 14.7 us  [butterfly_sum(): array = array + lax.ppermute(array, axis, pairs)]
    ppermute x10 -> x6, starting transfers between devices: 34.1 us -> 25.4 us  [passed_along(): return lax.ppermute(array, axis, pairs)]
    ppermute x12, waiting for transfers between devices: 22 us -> 27.6 us  [butterfly_sum(): array = array + lax.ppermute(array, axis, pairs)]
    ppermute x10 -> x6, waiting for transfers between devices: 2.92 us -> 7.62 us  [passed_along(): return lax.ppermute(array, axis, pairs)]
    convert_element_type x5 -> x18, other arithmetic: 10.6 us -> 8.3 us  [the longest x4 6.82 us: send_pair(): packed = jnp.concatenate([state.astype(jnp.bfloat16), row], axis=1)]
    unnamed x141 -> x111, local copies, waits for them, and re-layouts: 10.9 us -> 12.8 us
  transfers between devices with their start and end apart: 26 -> 22, of which waited for: 15 -> 13; matrix products, arithmetic and copies ran while one was open for 28% -> 32% of each run, Pallas kernels for 0% -> 0%
where the time goes in v6:
time: 265 us; the launch traced here: 262 us
  waiting for transfers between devices  84 us (32%)
  other arithmetic  50.1 us (19%)
  local copies, waits for them, and re-layouts  45.5 us (17%)
  starting transfers between devices  45.4 us (17%)
  matrix products  20.8 us (8%)
  between operations  16.4 us (6%)
    psum x1, waiting for transfers between devices, shards(): payload = lax.psum(payload, 'seq')  40.5 us
    ppermute x12, waiting for transfers between devices, butterfly_sum(): array = array + lax.ppermute(array, axis, pairs)  27.6 us
    ppermute x6, starting transfers between devices, passed_along(): return lax.ppermute(array, axis, pairs)  25.4 us
    ppermute x12, starting transfers between devices, butterfly_sum(): array = array + lax.ppermute(array, axis, pairs)  14.7 us
    unnamed x111, local copies, waits for them, and re-layouts  12.8 us
    ppermute x3, waiting for transfers between devices, shards(): lax.ppermute(outgoing, 'tp', [(i, (i + shift) % tp_size) for i in range(t...  8.28 us
    reduce_sum x1, other arithmetic, shards(): jnp.sum(queries[:, :, None] * key_rows[:, None, :] * weights, axis=-1)  7.84 us
    ppermute x6, waiting for transfers between devices, passed_along(): return lax.ppermute(array, axis, pairs)  7.62 us
  transfers between devices with their start and end apart: 22, of which 13 were waited for; matrix products, arithmetic and copies ran while one was open for 32% of the time, Pallas kernels for 0%

profile of v6, /device:TPU:0, one launch (start us, length us, event | category | flops | bytes accessed | tf_op | source)
XLA Modules:
  0.0 262.3 jit_solution(15217576205005517650)
XLA Ops:
  9.3 1.5 multiply_reduce_fusion.1
  10.8 1.7 fusion.77
  22.1 2.3 gather_fusion.3
  25.1 1.3 gather_fusion.4
  26.4 1.2 fusion.88
  27.9 3.5 %convolution_convert_fusion.1 = bf16[256,1024]{1,0:T(8,128)(2,1)S(1)} fusion(bf16[2048,1024]{1,0:T(8,128)(2,1)} %param.16, f32[2048]{0:T(1024)S(1)} %copy-done.44, f32[256]{0:T(256)S(1)} %add_rsqrt_fusion.1, bf16[256,2048]{1,0:T(8,128)(2,1)S(1)} %copy-done.1), kind=kOutput, calls=%fused_computation.22 | convolution fusion | flops 1076101120 | bytes 5776384 | tf_op jit(solution)/shard_map/dot_general | solution.py:127
  31.4 2.4 collective-permute-start
  34.5 1.2 broadcast_compare_fusion.2
  40.1 1.7 copy.32
  41.8 2.0 pad_maximum_fusion.2
  45.6 3.0 %fusion.83 = (bf16[1,256,512]{2,1,0:T(8,128)(2,1)S(1)}, f32[1,256,512]{2,1,0:T(8,128)}, f32[1,256,512]{2,1,0:T(8,128)S(1)}, f32[1,1,256,512]{3,2,1,0:T(8,128)S(1)}) fusion(f32[4,256,512]{2,1,0:T(8,128)S(1)} %fusion.41, f32[256]{0:T(256)S(1)} %bitcast.289, pred[]{:T(512)} %bitcast.20, f32[256]{0:T(256)S(1)} %bitcast.294, pred[]{:T(512)} %bitcast.26, ...), kind=kLoop, calls=%fused_computation.252 | loop fusion | flops 1441792 | bytes 3936259 | tf_op jit(solution)/shard_map/convert_element_type | solution.py:36
  50.0 4.3 %collective-permute-start.1 = (bf16[1,257,512]{2,1,0:T(8,128)(2,1)}, bf16[1,257,512]{2,1,0:T(8,128)(2,1)}, u32[]{:S(2)}, u32[]{:S(2)}) collective-permute-start(bf16[1,257,512]{2,1,0:T(8,128)(2,1)} %pad_maximum_fusion.3), channel_id=1, source_target_pairs={{0,4},{4,8},{8,12},{12,16},{16,20},{20,24},{24,28},{28,32},{32,36}... | collective-permute-start | bytes 789512 | tf_op jit(solution)/shard_map/ppermute | solution.py:19
  54.3 1.7 maximum_bitcast_fusion
  55.9 1.5 fusion.4
  57.5 7.8 %multiply_reduce_fusion = bf16[4,64,64]{2,1,0:T(8,128)(2,1)S(1)} fusion(f32[4,64,256]{2,1,0:T(8,128)S(1)} %bitcast.262, f32[4,64,256]{2,1,0:T(8,128)S(1)} %convert.7, f32[4,64,256]{2,1,0:T(8,128)S(1)} %bitcast.273, pred[4,64,64]{2,1,0:T(8,128)(4,1)S(1)} %copy-done.21), kind=kLoop, calls=%fused_computation.13 | loop fusion | flops 25149440 | bytes 835584 | tf_op jit(solution)/shard_map/reduce_sum | solution.py:169
  66.3 1.8 gather_fusion.11
  68.2 1.3 collective-permute-start.10
  69.5 1.3 convert_select_fusion
  70.8 1.8 gather_fusion.9
  72.6 2.5 collective-permute-start.11
  75.1 1.3 convert_select_fusion.2
  76.4 1.8 gather_fusion.10
  78.3 1.6 collective-permute-start.12
  79.9 2.4 collective-permute-done.12
  82.4 3.0 %collective-permute-start.13 = (f32[40,1,256]{2,0,1:T(8,128)S(1)}, f32[40,1,256]{2,0,1:T(8,128)}, u32[]{:S(2)}, u32[]{:S(2)}) collective-permute-start(f32[40,1,256]{2,0,1:T(8,128)S(1)} %add.523), channel_id=1, source_target_pairs={{0,64},{4,68},{8,72},{12,76},{16,80},{20,84},{24,88},{28,92},{32,9... | collective-permute-start | bytes 122888 | tf_op jit(solution)/shard_map/ppermute | solution.py:27
  87.8 2.0 collective-permute-start.2
  90.6 2.5 gather_fusion.2
  93.1 1.5 gather_fusion.5
  94.6 4.6 %gather_fusion.7 = f32[8,256,512]{2,1,0:T(8,128)} fusion(f32[4,256,512]{2,1,0:T(8,128)} %maximum_bitcast_fusion, s32[1024]{0:T(1024)} %copy-done.23), kind=kCustom, calls=%fused_computation.7 | custom fusion | bytes 8388640 | tf_op jit(solution)/shard_map/gather | solution.py:216
  99.3 1.8 fusion.30
  103.9 2.5 collective-permute-start.3
  106.5 6.0 %collective-permute-done.3 = bf16[1,257,512]{2,1,0:T(8,128)(2,1)S(1)} collective-permute-done((bf16[1,257,512]{2,1,0:T(8,128)(2,1)S(1)}, bf16[1,257,512]{2,1,0:T(8,128)(2,1)S(1)}, u32[]{:S(2)}, u32[]{:S(2)}) %collective-permute-start.3) | collective-permute-done | bytes 263200 | tf_op jit(solution)/shard_map/ppermute | solution.py:19
  112.6 1.3 fusion.78
  113.9 6.5 %collective-permute-start.4 = (bf16[1,257,512]{2,1,0:T(8,128)(2,1)S(1)}, bf16[1,257,512]{2,1,0:T(8,128)(2,1)S(1)}, u32[]{:S(2)}, u32[]{:S(2)}) collective-permute-start(bf16[1,257,512]{2,1,0:T(8,128)(2,1)S(1)} %pad_maximum_fusion.6), channel_id=1, source_target_pairs={{0,16},{4,20},{8,24},{12,28},{16,32},{20,36},{24,40},{28,44},{32,4... | collective-permute-start | bytes 789512 | tf_op jit(solution)/shard_map/ppermute | solution.py:19
  120.6 3.4 %add_bitcast_fusion = f32[1,8,256,512]{3,2,1,0:T(8,128)S(1)} fusion(f32[8,256,512]{2,1,0:T(8,128)} %gather_fusion.7, f32[256,512]{1,0:T(8,128)S(1)} %bitcast.267, f32[8,256]{1,0:T(8,128)S(1)} %fusion.55, f32[8,256]{1,0:T(8,128)S(1)} %copy-done.25, pred[8]{0:T(512)(128)(4,1)S(1)} %copy-done.41, pred[8]{0:T(512)(128)(4,1)S(1)} %copy-done.40, ...), kind=kOutput, calls=%fused_computation.16 | convolution fusion | flops 142213120 | bytes 10510872 | tf_op jit(solution)/shard_map/rjhc,rjhv->rhcv/dot_general | solution.py:214
  124.0 2.4 copy.37
  126.5 1.3 fusion.24
  128.6 7.7 %collective-permute-start.5 = (bf16[1,257,512]{2,1,0:T(8,128)(2,1)}, bf16[1,257,512]{2,1,0:T(8,128)(2,1)}, u32[]{:S(2)}, u32[]{:S(2)}) collective-permute-start(bf16[1,257,512]{2,1,0:T(8,128)(2,1)} %pad_maximum_fusion.7), channel_id=1, source_target_pairs={{0,32},{4,36},{8,40},{12,44},{16,48},{20,52},{24,56},{28,60},{32,6... | collective-permute-start | bytes 789512 | tf_op jit(solution)/shard_map/ppermute | solution.py:19
  136.3 2.9 %pad_maximum_fusion = f32[8,134144]{1,0:T(8,128)} fusion(f32[8,3072]{1,0:T(8,128)S(1)} %bitcast.268, f32[8,131072]{1,0:T(8,128)S(1)} %bitcast.251), kind=kLoop, calls=%fused_computation.14 | loop fusion | flops 1073152 | bytes 8585216 | tf_op jit(solution)/shard_map/concatenate | solution.py:242
  139.2 1.6 collective-permute-done.5
  140.9 3.2 %multiply_reduce_fusion.2 = (f32[4,64]{1,0:T(4,128)S(1)}, f32[4,64,1,512]{3,1,0,2:T(8,128)}) fusion(f32[4,64,1,512]{3,1,0,2:T(8,128)} %fusion.2, f32[4,64,256]{2,1,0:T(8,128)S(1)} %bitcast.271, bf16[1,257,512]{2,1,0:T(8,128)(2,1)} %collective-permute-done.5, f32[256]{0:T(256)S(1)} %bitcast.292, f32[256]{0:T(256)S(1)} %bitcast.288, ...), kind=kOutput, calls=%fused_computation.61 | convolution fusion | flops 404750080 | bytes 2626560 | tf_op jit(solution)/shard_map/bphc,hcv->bphv/dot_general | solution.py:252
  144.1 2.7 %fusion.16 = bf16[256,512]{1,0:T(8,128)(2,1)S(1)} fusion(f32[4,64,1,512]{3,1,0,2:T(8,128)} %get-tuple-element.85, bf16[2048,512]{1,0:T(8,128)(2,1)} %param.21, f32[512]{0:T(512)S(1)} %copy-done.46, f32[256]{0:T(256)S(1)} %rsqrt.29, f32[2048]{0:T(1024)S(1)} %copy-done.45, f32[256]{0:T(256)S(1)} %copy-done.36, bf16[256,2048]{1,0:T(8,128)(2,1)S(1)} %copy-done.1), kind=kOutput, calls=%fused_computation.58 | convolution fusion | flops 540278784 | bytes 3944448 | tf_op jit(solution)/shard_map/dot_general | solution.py:137
  146.9 1.7 convolution_convert_fusion
  148.6 1.8 reshape.1238
  150.4 3.0 %constant_dynamic-slice_fusion.3 = (bf16[256,1,512]{2,1,0:T(2,128)(2,1)}, bf16[256,1,512]{2,1,0:T(2,128)(2,1)S(1)}, bf16[256,1,512]{2,1,0:T(2,128)(2,1)S(1)}, bf16[256,1,512]{2,1,0:T(2,128)(2,1)S(1)}) fusion(bf16[256,4,512]{2,1,0:T(4,128)(2,1)S(1)} %reshape.1238, s32[]{:T(128)S(6)} %select_n.460, s32[]{:T(128)S(6)} %select_n.464, s32[]{:T(128)S(6)} %select_n.462, ...), kind=kLoop, calls=%fused_computation.151 | loop fusion | bytes 2097168 | tf_op jit(solution)/shard_map/jit(dynamic_index_in_dim)/dynamic_slice | solution.py:263
  154.9 3.0 %collective-permute-start.8 = (bf16[256,512]{1,0:T(8,128)(2,1)}, bf16[256,512]{1,0:T(8,128)(2,1)}, u32[]{:S(2)}, u32[]{:S(2)}) collective-permute-start(bf16[256,512]{1,0:T(8,128)(2,1)} %bitcast.245), channel_id=1, source_target_pairs={{0,3},{1,0},{2,1},{3,2},{4,7},{5,4},{6,5},{7,6},{8,11},{9,8},{10,9... | collective-permute-start | bytes 786440 | tf_op jit(solution)/shard_map/ppermute | solution.py:267
  157.9 2.2 collective-permute-start.7
  160.2 1.6 convert_element_type.282
  162.8 4.9 %collective-permute-done.8 = bf16[256,512]{1,0:T(8,128)(2,1)} collective-permute-done((bf16[256,512]{1,0:T(8,128)(2,1)}, bf16[256,512]{1,0:T(8,128)(2,1)}, u32[]{:S(2)}, u32[]{:S(2)}) %collective-permute-start.8) | collective-permute-done | bytes 262176 | tf_op jit(solution)/shard_map/ppermute | solution.py:267
  167.7 3.4 %collective-permute-done.6 = bf16[256,512]{1,0:T(8,128)(2,1)} collective-permute-done((bf16[256,512]{1,0:T(8,128)(2,1)}, bf16[256,512]{1,0:T(8,128)(2,1)}, u32[]{:S(2)}, u32[]{:S(2)}) %collective-permute-start.6) | collective-permute-done | bytes 262176 | tf_op jit(solution)/shard_map/ppermute | solution.py:267
  171.1 1.4 pad_maximum_fusion.1
  172.5 1.2 fusion.13
  174.4 1.2 collective-permute-done.14
  175.9 3.9 %collective-permute-done.15 = bf16[8,2048]{1,0:T(8,128)(2,1)S(1)} collective-permute-done((bf16[8,2048]{1,0:T(8,128)(2,1)S(1)}, bf16[8,2048]{1,0:T(8,128)(2,1)S(1)}, u32[]{:S(2)}, u32[]{:S(2)}) %collective-permute-start.15) | collective-permute-done | bytes 32800 | tf_op jit(solution)/shard_map/ppermute | solution.py:27
  180.1 5.2 %collective-permute-done.16 = bf16[8,2048]{1,0:T(8,128)(2,1)S(1)} collective-permute-done((bf16[8,2048]{1,0:T(8,128)(2,1)S(1)}, bf16[8,2048]{1,0:T(8,128)(2,1)S(1)}, u32[]{:S(2)}, u32[]{:S(2)}) %collective-permute-start.16) | collective-permute-done | bytes 32800 | tf_op jit(solution)/shard_map/ppermute | solution.py:27
  185.4 3.7 %collective-permute-start.17 = (bf16[8,2048]{1,0:T(8,128)(2,1)S(1)}, bf16[8,2048]{1,0:T(8,128)(2,1)S(1)}, u32[]{:S(2)}, u32[]{:S(2)}) collective-permute-start(bf16[8,2048]{1,0:T(8,128)(2,1)S(1)} %add.534), channel_id=1, source_target_pairs={{0,32},{4,36},{8,40},{12,44},{16,48},{20,52},{24,56},{28,60},{32,0... | collective-permute-start | bytes 98312 | tf_op jit(solution)/shard_map/ppermute | solution.py:27
  189.1 1.9 collective-permute-done.17
  191.0 1.8 collective-permute-start.18
  192.9 3.7 %collective-permute-done.18 = bf16[8,2048]{1,0:T(8,128)(2,1)S(1)} collective-permute-done((bf16[8,2048]{1,0:T(8,128)(2,1)S(1)}, bf16[8,2048]{1,0:T(8,128)(2,1)S(1)}, u32[]{:S(2)}, u32[]{:S(2)}) %collective-permute-start.18) | collective-permute-done | bytes 32800 | tf_op jit(solution)/shard_map/ppermute | solution.py:27
  196.6 3.9 %collective-permute-done.19 = bf16[8,2048]{1,0:T(8,128)(2,1)S(1)} collective-permute-done((bf16[8,2048]{1,0:T(8,128)(2,1)S(1)}, bf16[8,2048]{1,0:T(8,128)(2,1)S(1)}, u32[]{:S(2)}, u32[]{:S(2)}) %collective-permute-start.19) | collective-permute-done | bytes 32800 | tf_op jit(solution)/shard_map/ppermute | solution.py:27
  200.6 5.4 %collective-permute-done.20 = bf16[8,2048]{1,0:T(8,128)(2,1)S(1)} collective-permute-done((bf16[8,2048]{1,0:T(8,128)(2,1)S(1)}, bf16[8,2048]{1,0:T(8,128)(2,1)S(1)}, u32[]{:S(2)}, u32[]{:S(2)}) %collective-permute-start.20) | collective-permute-done | bytes 32800 | tf_op jit(solution)/shard_map/ppermute | solution.py:27
  207.7 40.5 %all-reduce.2.cloned.1.call-done = f32[8,134144]{1,0:T(8,128)} async-done(((f32[8,134144]{1,0:T(8,128)}), f32[8,134144]{1,0:T(8,128)}) %all-reduce.2.cloned.1.call-update) | async-done | bytes 4292624 | tf_op jit(solution)/shard_map/psum | solution.py:245
  248.2 2.2 slice-done.2
  250.4 4.4 %copy.56 = f32[1,8,256,512]{3,2,1,0:T(8,128)} copy(f32[1,8,256,512]{3,1,2,0:T(8,128)S(1)} %bitcast.254) | data formatting | bytes 8388608
  (234 shorter events, 33.8 us)
Async XLA Ops:
  7.2 139.7 %copy-start = (bf16[512,2048]{1,0:T(8,128)(2,1)S(1)}, bf16[512,2048]{1,0:T(8,128)(2,1)}, u32[]{:S(2)}) copy-start(bf16[512,2048]{1,0:T(8,128)(2,1)} %param.23) | copy-start | bytes 6291460
  7.2 5.3 %copy-start.47 = (f32[256]{0:T(256)S(1)}, f32[256]{0:T(256)}, u32[]{:S(2)}) copy-start(f32[256]{0:T(256)} %param.20) | copy-start | bytes 3076
  7.2 5.3 %copy-start.43 = (bf16[16,256]{1,0:T(8,128)(2,1)S(1)}, bf16[16,256]{1,0:T(8,128)(2,1)}, u32[]{:S(2)}) copy-start(bf16[16,256]{1,0:T(8,128)(2,1)} %param.19) | copy-start | bytes 24580
  7.2 241.0 %all-reduce.2.cloned.1.call-start = ((), (), s32[]{:S(2)}) async-start(), calls=%async_computation | async-start | bytes 8585216 | tf_op jit(solution)/shard_map/psum | solution.py:245
  10.8 4.8 %copy-start.48 = (s32[8]{0:T(128)S(1)}, s32[8]{0:T(128)}, u32[]{:S(2)}) copy-start(s32[8]{0:T(128)} %param.27) | copy-start | bytes 100
  10.8 17.0 %copy-start.35 = (f32[256]{0:T(256)}, f32[256]{0:T(256)S(1)}, u32[]{:S(2)}) copy-start(f32[256]{0:T(256)S(1)} %add_rsqrt_fusion.1) | copy-start | bytes 3076
  12.5 13.9 %copy-start.39 = (s32[8]{0:T(128)S(1)}, s32[8]{0:T(128)}, u32[]{:S(2)}) copy-start(s32[8]{0:T(128)} %param.26) | copy-start | bytes 100
  13.0 14.9 %copy-start.1 = (bf16[256,2048]{1,0:T(8,128)(2,1)S(1)}, bf16[256,2048]{1,0:T(8,128)(2,1)}, u32[]{:S(2)}) copy-start(bf16[256,2048]{1,0:T(8,128)(2,1)} %param.14) | copy-start | bytes 3145732
  13.0 14.9 %copy-start.44 = (f32[2048]{0:T(1024)S(1)}, f32[2048]{0:T(1024)}, u32[]{:S(2)}) copy-start(f32[2048]{0:T(1024)} %param.15) | copy-start | bytes 24580
  16.5 7.9 %copy-start.23 = (s32[1024]{0:T(1024)}, s32[1024]{0:T(1024)S(1)}, u32[]{:S(2)}) copy-start(s32[1024]{0:T(1024)S(1)} %pad_clamp_fusion.4) | copy-start | bytes 12292
  26.4 12.6 %copy-start.19 = (f32[8,256]{1,0:T(8,128)}, f32[8,256]{1,0:T(8,128)S(1)}, u32[]{:S(2)}) copy-start(f32[8,256]{1,0:T(8,128)S(1)} %gather_fusion.4) | copy-start | bytes 24580
  27.8 9.2 %copy-start.22 = (f32[4,1024]{1,0:T(4,128)S(1)}, f32[4,1024]{1,0:T(4,128)}, u32[]{:S(2)}) copy-start(f32[4,1024]{1,0:T(4,128)} %param.17) | copy-start | bytes 49156
  27.8 40.4 %collective-permute-start.9 = (f32[40,1,256]{2,0,1:T(8,128)S(1)}, f32[40,1,256]{2,0,1:T(8,128)S(1)}, u32[]{:S(2)}, u32[]{:S(2)}) collective-permute-start(f32[40,1,256]{2,0,1:T(8,128)S(1)} %pad_maximum_fusion.9), channel_id=1, source_target_pairs={{0,4},{4,0},{8,12},{12,8},{16,20},{20,16},{24,28},{28,24},{32,36},... | collective-permute-start | bytes 122888 | tf_op jit(solution)/shard_map/ppermute | solution.py:27
  31.4 6.3 %copy-start.12 = (bf16[256,1024]{1,0:T(8,128)(2,1)}, bf16[256,1024]{1,0:T(8,128)(2,1)S(1)}, u32[]{:S(2)}) copy-start(bf16[256,1024]{1,0:T(8,128)(2,1)S(1)} %convolution_convert_fusion.1) | copy-start | bytes 1572868
  31.4 10.4 %collective-permute-start = (bf16[3,1024]{1,0:T(4,128)(2,1)S(1)}, bf16[3,1024]{1,0:T(4,128)(2,1)S(1)}, u32[]{:S(2)}, u32[]{:S(2)}) collective-permute-start(bf16[3,1024]{1,0:T(4,128)(2,1)S(1)} %slice.271), channel_id=1, source_target_pairs={{0,4},{4,8},{8,12},{12,16},{16,20},{20,24},{24,28},{28,32},{32,36}... | collective-permute-start | bytes 18440 | tf_op jit(solution)/shard_map/ppermute | solution.py:19
  44.8 12.6 %copy-start.7 = (f32[4,64,256]{2,1,0:T(8,128)}, f32[4,64,256]{2,1,0:T(8,128)S(1)}, u32[]{:S(2)}) copy-start(f32[4,64,256]{2,1,0:T(8,128)S(1)} %convert.7) | copy-start | bytes 786436
  45.5 8.7 %copy-start.42 = (f32[4]{0:T(128)S(1)}, f32[4]{0:T(128)}, u32[]{:S(2)}) copy-start(f32[4]{0:T(128)} %pad.35.clone) | copy-start | bytes 52
  49.2 6.7 %copy-start.38 = (pred[4,64]{1,0:T(4,128)(4,1)S(1)}, pred[4,64]{1,0:T(4,128)(4,1)}, u32[]{:S(2)}) copy-start(pred[4,64]{1,0:T(4,128)(4,1)} %get-tuple-element.52) | copy-start | bytes 772
  50.0 35.4 %collective-permute-start.1 = (bf16[1,257,512]{2,1,0:T(8,128)(2,1)}, bf16[1,257,512]{2,1,0:T(8,128)(2,1)}, u32[]{:S(2)}, u32[]{:S(2)}) collective-permute-start(bf16[1,257,512]{2,1,0:T(8,128)(2,1)} %pad_maximum_fusion.3), channel_id=1, source_target_pairs={{0,4},{4,8},{8,12},{12,16},{16,20},{20,24},{24,28},{28,32},{32,36}... | collective-permute-start | bytes 789512 | tf_op jit(solution)/shard_map/ppermute | solution.py:19
  65.3 14.5 %copy-start.33 = (pred[8]{0:T(512)(128)(4,1)S(1)}, pred[8]{0:T(512)(128)(4,1)}, u32[]{:S(2)}) copy-start(pred[8]{0:T(512)(128)(4,1)} %get-tuple-element.67) | copy-start | bytes 28
  68.2 4.4 %collective-permute-start.10 = (f32[40,1,256]{2,0,1:T(8,128)S(1)}, f32[40,1,256]{2,0,1:T(8,128)S(1)}, u32[]{:S(2)}, u32[]{:S(2)}) collective-permute-start(f32[40,1,256]{2,0,1:T(8,128)S(1)} %fusion.75), channel_id=1, source_target_pairs={{0,8},{4,12},{8,0},{12,4},{16,24},{20,28},{24,16},{28,20},{32,40},... | collective-permute-start | bytes 122888 | tf_op jit(solution)/shard_map/ppermute | solution.py:27
  72.6 5.6 %collective-permute-start.11 = (f32[40,1,256]{2,0,1:T(8,128)S(1)}, f32[40,1,256]{2,0,1:T(8,128)S(1)}, u32[]{:S(2)}, u32[]{:S(2)}) collective-permute-start(f32[40,1,256]{2,0,1:T(8,128)S(1)} %add.521), channel_id=1, source_target_pairs={{0,16},{4,20},{8,24},{12,28},{16,0},{20,4},{24,8},{28,12},{32,48},... | collective-permute-start | bytes 122888 | tf_op jit(solution)/shard_map/ppermute | solution.py:27
  78.3 4.1 %collective-permute-start.12 = (f32[40,1,256]{2,0,1:T(8,128)S(1)}, f32[40,1,256]{2,0,1:T(8,128)S(1)}, u32[]{:S(2)}, u32[]{:S(2)}) collective-permute-start(f32[40,1,256]{2,0,1:T(8,128)S(1)} %add.522), channel_id=1, source_target_pairs={{0,32},{4,36},{8,40},{12,44},{16,48},{20,52},{24,56},{28,60},{32,0... | collective-permute-start | bytes 122888 | tf_op jit(solution)/shard_map/ppermute | solution.py:27
  82.4 18.8 %collective-permute-start.13 = (f32[40,1,256]{2,0,1:T(8,128)S(1)}, f32[40,1,256]{2,0,1:T(8,128)}, u32[]{:S(2)}, u32[]{:S(2)}) collective-permute-start(f32[40,1,256]{2,0,1:T(8,128)S(1)} %add.523), channel_id=1, source_target_pairs={{0,64},{4,68},{8,72},{12,76},{16,80},{20,84},{24,88},{28,92},{32,9... | collective-permute-start | bytes 122888 | tf_op jit(solution)/shard_map/ppermute | solution.py:27
  87.8 14.1 %collective-permute-start.2 = (bf16[1,257,512]{2,1,0:T(8,128)(2,1)}, bf16[1,257,512]{2,1,0:T(8,128)(2,1)}, u32[]{:S(2)}, u32[]{:S(2)}) collective-permute-start(bf16[1,257,512]{2,1,0:T(8,128)(2,1)} %pad_maximum_fusion.4), channel_id=1, source_target_pairs={{0,4},{4,8},{8,12},{12,16},{16,20},{20,24},{24,28},{28,32},{32,36}... | collective-permute-start | bytes 789512 | tf_op jit(solution)/shard_map/ppermute | solution.py:19
  94.6 4.7 %copy-start.9 = (f32[4,64,1,256]{3,1,2,0:T(8,128)S(1)}, f32[4,64,1,256]{3,1,2,0:T(8,128)}, u32[]{:S(2)}) copy-start(f32[4,64,1,256]{3,1,2,0:T(8,128)} %copy.32) | copy-start | bytes 786436
  99.2 7.2 %copy-start.28 = (pred[8,32]{1,0:T(8,128)(4,1)S(1)}, pred[8,32]{1,0:T(8,128)(4,1)}, u32[]{:S(2)}) copy-start(pred[8,32]{1,0:T(8,128)(4,1)} %fusion.57) | copy-start | bytes 772
  99.2 21.3 %copy-start.11 = (f32[8,64,256]{2,1,0:T(8,128)S(1)}, f32[8,64,256]{2,1,0:T(8,128)}, u32[]{:S(2)}) copy-start(f32[8,64,256]{2,1,0:T(8,128)} %gather_fusion.3) | copy-start | bytes 1572868
  99.2 21.3 %copy-start.13 = (f32[1,256,512]{2,1,0:T(8,128)S(1)}, f32[1,256,512]{2,1,0:T(8,128)}, u32[]{:S(2)}) copy-start(f32[1,256,512]{2,1,0:T(8,128)} %get-tuple-element.21) | copy-start | bytes 1572868
  99.2 21.3 %copy-start.14 = (f32[8,64,256]{2,1,0:T(8,128)S(1)}, f32[8,64,256]{2,1,0:T(8,128)}, u32[]{:S(2)}) copy-start(f32[8,64,256]{2,1,0:T(8,128)} %gather_fusion.2) | copy-start | bytes 1572868
  99.2 21.3 %copy-start.15 = (bf16[8,64,512]{2,1,0:T(8,128)(2,1)S(1)}, bf16[8,64,512]{2,1,0:T(8,128)(2,1)}, u32[]{:S(2)}) copy-start(bf16[8,64,512]{2,1,0:T(8,128)(2,1)} %gather_fusion.5) | copy-start | bytes 1572868
  99.2 21.3 %copy-start.20 = (f32[8,256]{1,0:T(8,128)S(1)}, f32[8,256]{1,0:T(8,128)}, u32[]{:S(2)}) copy-start(f32[8,256]{1,0:T(8,128)} %copy-done.19) | copy-start | bytes 24580
  99.2 21.3 %copy-start.25 = (f32[8,256]{1,0:T(8,128)S(1)}, f32[8,256]{1,0:T(8,128)}, u32[]{:S(2)}) copy-start(f32[8,256]{1,0:T(8,128)} %exp.100) | copy-start | bytes 24580
  99.2 21.3 %copy-start.26 = (pred[8]{0:T(512)(128)(4,1)S(1)}, pred[8]{0:T(512)(128)(4,1)}, u32[]{:S(2)}) copy-start(pred[8]{0:T(512)(128)(4,1)} %get-tuple-element.65) | copy-start | bytes 28
  99.2 21.3 %copy-start.37 = (pred[8,64]{1,0:T(8,128)(4,1)S(1)}, pred[8,64]{1,0:T(8,128)(4,1)}, u32[]{:S(2)}) copy-start(pred[8,64]{1,0:T(8,128)(4,1)} %fusion.56) | copy-start | bytes 1540
  99.2 21.3 %copy-start.40 = (pred[8]{0:T(512)(128)(4,1)S(1)}, pred[8]{0:T(512)(128)(4,1)}, u32[]{:S(2)}) copy-start(pred[8]{0:T(512)(128)(4,1)} %get-tuple-element.61) | copy-start | bytes 28
  99.2 21.3 %copy-start.41 = (pred[8]{0:T(512)(128)(4,1)S(1)}, pred[8]{0:T(512)(128)(4,1)}, u32[]{:S(2)}) copy-start(pred[8]{0:T(512)(128)(4,1)} %get-tuple-element.63) | copy-start | bytes 28
  103.9 8.7 %collective-permute-start.3 = (bf16[1,257,512]{2,1,0:T(8,128)(2,1)S(1)}, bf16[1,257,512]{2,1,0:T(8,128)(2,1)S(1)}, u32[]{:S(2)}, u32[]{:S(2)}) collective-permute-start(bf16[1,257,512]{2,1,0:T(8,128)(2,1)S(1)} %pad_maximum_fusion.5), channel_id=1, source_target_pairs={{0,8},{4,12},{8,16},{12,20},{16,24},{20,28},{24,32},{28,36},{32,40... | collective-permute-start | bytes 789512 | tf_op jit(solution)/shard_map/ppermute | solution.py:19
  112.5 14.0 %copy-start.10 = (bf16[1,257,512]{2,1,0:T(8,128)(2,1)}, bf16[1,257,512]{2,1,0:T(8,128)(2,1)S(1)}, u32[]{:S(2)}) copy-start(bf16[1,257,512]{2,1,0:T(8,128)(2,1)S(1)} %collective-permute-done.3) | copy-start | bytes 789508
  113.9 12.5 %collective-permute-start.4 = (bf16[1,257,512]{2,1,0:T(8,128)(2,1)S(1)}, bf16[1,257,512]{2,1,0:T(8,128)(2,1)S(1)}, u32[]{:S(2)}, u32[]{:S(2)}) collective-permute-start(bf16[1,257,512]{2,1,0:T(8,128)(2,1)S(1)} %pad_maximum_fusion.6), channel_id=1, source_target_pairs={{0,16},{4,20},{8,24},{12,28},{16,32},{20,36},{24,40},{28,44},{32,4... | collective-permute-start | bytes 789512 | tf_op jit(solution)/shard_map/ppermute | solution.py:19
  126.4 2.1 copy-start.18
  128.6 12.3 %collective-permute-start.5 = (bf16[1,257,512]{2,1,0:T(8,128)(2,1)}, bf16[1,257,512]{2,1,0:T(8,128)(2,1)}, u32[]{:S(2)}, u32[]{:S(2)}) collective-permute-start(bf16[1,257,512]{2,1,0:T(8,128)(2,1)} %pad_maximum_fusion.7), channel_id=1, source_target_pairs={{0,32},{4,36},{8,40},{12,44},{16,48},{20,52},{24,56},{28,60},{32,6... | collective-permute-start | bytes 789512 | tf_op jit(solution)/shard_map/ppermute | solution.py:19
  139.2 4.9 %copy-start.36 = (f32[256]{0:T(256)S(1)}, f32[256]{0:T(256)}, u32[]{:S(2)}) copy-start(f32[256]{0:T(256)} %copy-done.35) | copy-start | bytes 3076
  139.2 4.9 %copy-start.45 = (f32[2048]{0:T(1024)S(1)}, f32[2048]{0:T(1024)}, u32[]{:S(2)}) copy-start(f32[2048]{0:T(1024)} %param.15) | copy-start | bytes 24580
  139.2 4.9 %copy-start.46 = (f32[512]{0:T(512)S(1)}, f32[512]{0:T(512)}, u32[]{:S(2)}) copy-start(f32[512]{0:T(512)} %param.22) | copy-start | bytes 6148
  153.4 6.7 %copy-start.2 = (bf16[256,2048]{1,0:T(8,128)(2,1)S(1)}, bf16[256,2048]{1,0:T(8,128)(2,1)}, u32[]{:S(2)}) copy-start(bf16[256,2048]{1,0:T(8,128)(2,1)} %param.14) | copy-start | bytes 3145732
  154.2 7.5 %copy-start.34 = (s32[8]{0:T(128)S(1)}, s32[8]{0:T(128)}, u32[]{:S(2)}) copy-start(s32[8]{0:T(128)} %get-tuple-element.74) | copy-start | bytes 100
  154.9 12.7 %collective-permute-start.8 = (bf16[256,512]{1,0:T(8,128)(2,1)}, bf16[256,512]{1,0:T(8,128)(2,1)}, u32[]{:S(2)}, u32[]{:S(2)}) collective-permute-start(bf16[256,512]{1,0:T(8,128)(2,1)} %bitcast.245), channel_id=1, source_target_pairs={{0,3},{1,0},{2,1},{3,2},{4,7},{5,4},{6,5},{7,6},{8,11},{9,8},{10,9... | collective-permute-start | bytes 786440 | tf_op jit(solution)/shard_map/ppermute | solution.py:267
  157.9 13.2 %collective-permute-start.6 = (bf16[256,512]{1,0:T(8,128)(2,1)}, bf16[256,512]{1,0:T(8,128)(2,1)}, u32[]{:S(2)}, u32[]{:S(2)}) collective-permute-start(bf16[256,512]{1,0:T(8,128)(2,1)} %bitcast.247), channel_id=1, source_target_pairs={{0,1},{1,2},{2,3},{3,0},{4,5},{5,6},{6,7},{7,4},{8,9},{9,10},{10,1... | collective-permute-start | bytes 786440 | tf_op jit(solution)/shard_map/ppermute | solution.py:267
  157.9 13.2 %collective-permute-start.7 = (bf16[256,512]{1,0:T(8,128)(2,1)S(1)}, bf16[256,512]{1,0:T(8,128)(2,1)}, u32[]{:S(2)}, u32[]{:S(2)}) collective-permute-start(bf16[256,512]{1,0:T(8,128)(2,1)S(1)} %bitcast.269), channel_id=1, source_target_pairs={{0,2},{1,3},{2,0},{3,1},{4,6},{5,7},{6,4},{7,5},{8,10},{9,11},{10,... | collective-permute-start | bytes 786440 | tf_op jit(solution)/shard_map/ppermute | solution.py:267
  162.8 11.5 %copy-start.27 = (pred[8]{0:T(512)(128)(4,1)S(1)}, pred[8]{0:T(512)(128)(4,1)}, u32[]{:S(2)}) copy-start(pred[8]{0:T(512)(128)(4,1)} %get-tuple-element.65) | copy-start | bytes 28
  171.1 35.6 %copy-start.8 = (bf16[250,2048]{1,0:T(8,128)(2,1)S(1)}, bf16[250,2048]{1,0:T(8,128)(2,1)}, u32[]{:S(2)}) copy-start(bf16[250,2048]{1,0:T(8,128)(2,1)} %param.25) | copy-start | bytes 3072004
  171.1 35.6 %copy-start.24 = (f32[2048]{0:T(1024)S(1)}, f32[2048]{0:T(1024)}, u32[]{:S(2)}) copy-start(f32[2048]{0:T(1024)} %param.24) | copy-start | bytes 24580
  173.7 74.5 %copy-start.16 = (bf16[256,512]{1,0:T(8,128)(2,1)}, bf16[256,512]{1,0:T(8,128)(2,1)S(1)}, u32[]{:S(2)}) copy-start(bf16[256,512]{1,0:T(8,128)(2,1)S(1)} %fusion.13) | copy-start | bytes 786436
  174.4 1.2 collective-permute-start.14
  175.7 4.1 %collective-permute-start.15 = (bf16[8,2048]{1,0:T(8,128)(2,1)S(1)}, bf16[8,2048]{1,0:T(8,128)(2,1)S(1)}, u32[]{:S(2)}, u32[]{:S(2)}) collective-permute-start(bf16[8,2048]{1,0:T(8,128)(2,1)S(1)} %add_dynamic-update-slice_fusion), channel_id=1, source_target_pairs={{0,8},{4,12},{8,0},{12,4},{16,24},{20,28},{24,16},{28,20},{32,40},... | collective-permute-start | bytes 98312 | tf_op jit(solution)/shard_map/ppermute | solution.py:27
  179.8 5.5 %collective-permute-start.16 = (bf16[8,2048]{1,0:T(8,128)(2,1)S(1)}, bf16[8,2048]{1,0:T(8,128)(2,1)S(1)}, u32[]{:S(2)}, u32[]{:S(2)}) collective-permute-start(bf16[8,2048]{1,0:T(8,128)(2,1)S(1)} %add.533), channel_id=1, source_target_pairs={{0,16},{4,20},{8,24},{12,28},{16,0},{20,4},{24,8},{28,12},{32,48},... | collective-permute-start | bytes 98312 | tf_op jit(solution)/shard_map/ppermute | solution.py:27
  185.4 5.6 %collective-permute-start.17 = (bf16[8,2048]{1,0:T(8,128)(2,1)S(1)}, bf16[8,2048]{1,0:T(8,128)(2,1)S(1)}, u32[]{:S(2)}, u32[]{:S(2)}) collective-permute-start(bf16[8,2048]{1,0:T(8,128)(2,1)S(1)} %add.534), channel_id=1, source_target_pairs={{0,32},{4,36},{8,40},{12,44},{16,48},{20,52},{24,56},{28,60},{32,0... | collective-permute-start | bytes 98312 | tf_op jit(solution)/shard_map/ppermute | solution.py:27
  191.0 5.5 %collective-permute-start.18 = (bf16[8,2048]{1,0:T(8,128)(2,1)S(1)}, bf16[8,2048]{1,0:T(8,128)(2,1)S(1)}, u32[]{:S(2)}, u32[]{:S(2)}) collective-permute-start(bf16[8,2048]{1,0:T(8,128)(2,1)S(1)} %add.535), channel_id=1, source_target_pairs={{0,64},{4,68},{8,72},{12,76},{16,80},{20,84},{24,88},{28,92},{32,9... | collective-permute-start | bytes 98312 | tf_op jit(solution)/shard_map/ppermute | solution.py:27
  196.5 4.0 %collective-permute-start.19 = (bf16[8,2048]{1,0:T(8,128)(2,1)S(1)}, bf16[8,2048]{1,0:T(8,128)(2,1)S(1)}, u32[]{:S(2)}, u32[]{:S(2)}) collective-permute-start(bf16[8,2048]{1,0:T(8,128)(2,1)S(1)} %add.536), channel_id=1, source_target_pairs={{0,1},{1,0},{2,3},{3,2},{4,5},{5,4},{6,7},{7,6},{8,9},{9,8},{10,11... | collective-permute-start | bytes 98312 | tf_op jit(solution)/shard_map/ppermute | solution.py:27
  200.5 5.5 %collective-permute-start.20 = (bf16[8,2048]{1,0:T(8,128)(2,1)S(1)}, bf16[8,2048]{1,0:T(8,128)(2,1)S(1)}, u32[]{:S(2)}, u32[]{:S(2)}) collective-permute-start(bf16[8,2048]{1,0:T(8,128)(2,1)S(1)} %add.537), channel_id=1, source_target_pairs={{0,2},{1,3},{2,0},{3,1},{4,6},{5,7},{6,4},{7,5},{8,10},{9,11},{10,... | collective-permute-start | bytes 98312 | tf_op jit(solution)/shard_map/ppermute | solution.py:27
  248.2 2.2 slice-start.2
  248.2 6.6 %slice-start = ((s8[4292608]{0:T(1024)(128)(4,1)}), s8[4194304]{0:T(1024)(128)(4,1)S(1)}, s32[]{:S(2)}) async-start(s8[4292608]{0:T(1024)(128)(4,1)} %bitcast.252), calls=%async_computation.1 | async-start | bytes 8388608
  248.2 6.6 %slice-start.1 = ((s8[4292608]{0:T(1024)(128)(4,1)}), s8[98304]{0:T(1024)(128)(4,1)S(1)}, s32[]{:S(2)}) async-start(s8[4292608]{0:T(1024)(128)(4,1)} %bitcast.252), calls=%async_computation.2 | async-start | bytes 196608
  (10 other events, 10.7 us)
Sparse Core Ops, SparseCore 0:
  139.3 108.7 all-reduce.1

commit v7 on v4

--- a/solution.py
+++ b/solution.py
@@ -23,13 +23,9 @@
     peers = lax.axis_size(axis)
     step = 1
     while step < peers:
-        radix = 4 if peers % (step * 4) == 0 else 2
-        total = array
-        for digit in range(1, radix):
-            pairs = [(i, i ^ (digit * step)) for i in range(peers)]
-            total = total + lax.ppermute(array, axis, pairs)
-        array = total
-        step *= radix
+        pairs = [(i, i ^ step) for i in range(peers)]
+        array = array + lax.ppermute(array, axis, pairs)
+        step *= 2
     return array
 
 
@@ -246,13 +242,10 @@
         end_from_before, end_reach[:, :, :, None] * incoming[None], 0.0
     )
     end_states = jnp.where(owned_here[:, None, None, None], end_states, 0.0)
-    state_width = head_count * DK * DV
-    payload = jnp.concatenate(
-        [end_states.reshape(request_count, state_width), conv_edges.reshape(request_count, -1)], axis=1
-    )
-    payload = lax.psum(payload.astype(jnp.bfloat16), "seq").astype(jnp.float32)
-    last_states = payload[:, :state_width].reshape(end_states.shape)
-    conv_edges = payload[:, state_width:].reshape(conv_edges.shape)
+    edge_rows = conv_edges.reshape(request_count, head_count, -1, DV)
+    payload = lax.psum(jnp.concatenate([end_states, edge_rows], axis=2), "seq")
+    last_states = payload[:, :, :DK]
+    conv_edges = payload[:, :, DK:].reshape(conv_edges.shape)
 
     gated = head_output(attended, gate_out, head_gain)
     partial = jnp.dot(gated, out_weight, preferred_element_type=jnp.float32).astype(jnp.bfloat16)

time: 295 us -> 239 us (0.81)
  waiting for transfers between devices: 110 us -> 77.1 us
  other arithmetic: 59.5 us -> 41.6 us
  local copies, waits for them, and re-layouts: 37 us -> 33.7 us
    psum x1, waiting for transfers between devices: 91.9 us -> 52 us  [shards(): payload = lax.psum(jnp.concatenate([end_states, edge_rows], axis=2), 'seq')]
    ppermute x10 -> x7, waiting for transfers between devices: 6.33 us -> 18.6 us  [butterfly_sum(): array = array + lax.ppermute(array, axis, pairs)]
    ppermute x10 -> x7, starting transfers between devices: 15.6 us -> 11.6 us  [butterfly_sum(): array = array + lax.ppermute(array, axis, pairs)]
    ppermute x3, waiting for transfers between devices: 6.1 us -> 2.65 us  [shards(): lax.ppermute(outgoing, 'tp', [(i, (i + shift) % tp_size) for i in range(t...]
    unnamed x161 -> x137, local copies, waits for them, and re-layouts: 11.7 us -> 13.7 us
  transfers between devices with their start and end apart: 20 -> 17, of which waited for: 11 -> 12; matrix products, arithmetic and copies ran while one was open for 25% -> 24% of each run, Pallas kernels for 0% -> 0%
where the time goes in v7:
time: 239 us; the launch traced here: 237 us
  waiting for transfers between devices  77.1 us (32%)
  starting transfers between devices  46.9 us (20%)
  other arithmetic  41.6 us (17%)
  local copies, waits for them, and re-layouts  33.7 us (14%)
  matrix products  21.3 us (9%)
  between operations  16.6 us (7%)
    psum x1, waiting for transfers between devices, shards(): payload = lax.psum(jnp.concatenate([end_states, edge_rows], axis=2), 'seq')  52 us
    ppermute x6, starting transfers between devices, passed_along(): return lax.ppermute(array, axis, pairs)  29.5 us
    ppermute x7, waiting for transfers between devices, butterfly_sum(): array = array + lax.ppermute(array, axis, pairs)  18.6 us
    unnamed x137, local copies, waits for them, and re-layouts  13.7 us
    ppermute x7, starting transfers between devices, butterfly_sum(): array = array + lax.ppermute(array, axis, pairs)  11.6 us
    reduce_sum x1, other arithmetic, shards(): jnp.sum(queries[:, :, None] * key_rows[:, None, :] * weights, axis=-1)  8.48 us
    convert_element_type x4, other arithmetic, send_pair(): packed = jnp.concatenate([state.astype(jnp.bfloat16), row], axis=1)  6.06 us
    ppermute x3, starting transfers between devices, shards(): lax.ppermute(outgoing, 'tp', [(i, (i + shift) % tp_size) for i in range(t...  5.83 us
  transfers between devices with their start and end apart: 17, of which 12 were waited for; matrix products, arithmetic and copies ran while one was open for 24% of the time, Pallas kernels for 0%

profile of v7, /device:TPU:0, one launch (start us, length us, event | category | flops | bytes accessed | tf_op | source)
XLA Modules:
  0.0 237.2 jit_solution(10789050269790574456)
XLA Ops:
  7.2 1.6 multiply_reduce_fusion.1
  9.0 3.9 %convolution_convert_fusion.1 = bf16[256,1024]{1,0:T(8,128)(2,1)S(1)} fusion(bf16[2048,1024]{1,0:T(8,128)(2,1)} %param.16, f32[2048]{0:T(1024)} %param.15, f32[256]{0:T(256)S(1)} %add_rsqrt_fusion.1, bf16[256,2048]{1,0:T(8,128)(2,1)} %param.14), kind=kOutput, calls=%fused_computation.21 | convolution fusion | flops 1076101120 | bytes 5776384 | tf_op jit(solution)/shard_map/dot_general | solution.py:127
  12.9 0.8 copy-done.10
  13.7 1.3 collective-permute-start
  19.7 1.2 broadcast_compare_fusion.2
  28.5 3.7 %select_compare_fusion = (pred[8]{0:T(512)(128)(4,1)}, pred[8]{0:T(512)(128)(4,1)}) fusion(s32[8]{0:T(128)S(1)} %gather_fusion, s32[]{:T(128)} %bitcast.81, s32[]{:T(128)} %bitcast.80, s32[]{:T(128)} %bitcast.79, s32[]{:T(128)} %bitcast.78, s32[8]{0:T(128)S(1)} %get-tuple-element.30, s32[]{:T(128)} %bitcast.27), kind=kLoop, calls=%fused_computation.242 | loop fusion | flops 64 | bytes 100 | tf_op jit(solution)/shard_map/eq | solution.py:222
  33.6 1.0 pad_maximum_fusion.2
  34.6 0.9 fusion.33
  35.6 0.8 copy-done.5
  37.0 3.5 %fusion.21 = (bf16[1,256,512]{2,1,0:T(8,128)(2,1)S(1)}, f32[1,256,512]{2,1,0:T(8,128)}, f32[1,256,512]{2,1,0:T(8,128)}, f32[256,512]{1,0:T(8,128)}, f32[1,1,256,512]{3,2,1,0:T(8,128)}) fusion(f32[4,256,512]{2,1,0:T(8,128)S(1)} %fusion.64, f32[256]{0:T(256)S(1)} %bitcast.290, pred[]{:T(512)} %bitcast.24, f32[256]{0:T(256)S(1)} %bitcast.291, pred[]{:T(512)} %bitcast.18, ...), kind=kLoop, calls=%fused_computation.50 | loop fusion | flops 1441792 | bytes 4460547 | tf_op jit(solution)/shard_map/convert_element_type | solution.py:36
  40.5 4.7 %collective-permute-start.1 = (bf16[1,257,512]{2,1,0:T(8,128)(2,1)S(1)}, bf16[1,257,512]{2,1,0:T(8,128)(2,1)S(1)}, u32[]{:S(2)}, u32[]{:S(2)}) collective-permute-start(bf16[1,257,512]{2,1,0:T(8,128)(2,1)S(1)} %pad_maximum_fusion.3), channel_id=1, source_target_pairs={{0,4},{4,8},{8,12},{12,16},{16,20},{20,24},{24,28},{28,32},{32,36}... | collective-permute-start | bytes 789512 | tf_op jit(solution)/shard_map/ppermute | solution.py:19
  45.2 8.5 %multiply_reduce_fusion = bf16[4,64,64]{2,1,0:T(8,128)(2,1)} fusion(f32[4,64,256]{2,1,0:T(8,128)S(1)} %bitcast.265, f32[4,64,256]{2,1,0:T(8,128)S(1)} %bitcast.253, f32[4,64,256]{2,1,0:T(8,128)S(1)} %bitcast.262, pred[4,64,64]{2,1,0:T(8,128)(4,1)S(1)} %compare_and_fusion), kind=kLoop, calls=%fused_computation.6 | loop fusion | flops 25149440 | bytes 835584 | tf_op jit(solution)/shard_map/reduce_sum | solution.py:169
  53.7 1.7 gather_fusion.3
  55.5 0.7 pad_maximum_fusion.4
  56.2 1.9 collective-permute-start.2
  58.2 1.7 gather_fusion.2
  59.9 1.6 slice_bitcast_fusion.8
  62.5 7.2 %collective-permute-start.3 = (bf16[1,257,512]{2,1,0:T(8,128)(2,1)}, bf16[1,257,512]{2,1,0:T(8,128)(2,1)}, u32[]{:S(2)}, u32[]{:S(2)}) collective-permute-start(bf16[1,257,512]{2,1,0:T(8,128)(2,1)} %pad_maximum_fusion.5), channel_id=1, source_target_pairs={{0,8},{4,12},{8,16},{12,20},{16,24},{20,28},{24,32},{28,36},{32,40... | collective-permute-start | bytes 789512 | tf_op jit(solution)/shard_map/ppermute | solution.py:19
  69.7 1.7 gather_fusion.4
  72.2 2.3 collective-permute-done.3
  75.3 1.2 fusion.97
  76.5 4.8 %collective-permute-start.4 = (bf16[1,257,512]{2,1,0:T(8,128)(2,1)S(1)}, bf16[1,257,512]{2,1,0:T(8,128)(2,1)S(1)}, u32[]{:S(2)}, u32[]{:S(2)}) collective-permute-start(bf16[1,257,512]{2,1,0:T(8,128)(2,1)S(1)} %pad_maximum_fusion.6), channel_id=1, source_target_pairs={{0,16},{4,20},{8,24},{12,28},{16,32},{20,36},{24,40},{28,44},{32,4... | collective-permute-start | bytes 789512 | tf_op jit(solution)/shard_map/ppermute | solution.py:19
  81.4 2.3 fusion.11
  83.7 1.5 collective-permute-done.4
  85.3 1.2 fusion.37
  87.3 9.6 %collective-permute-start.5 = (bf16[1,257,512]{2,1,0:T(8,128)(2,1)}, bf16[1,257,512]{2,1,0:T(8,128)(2,1)}, u32[]{:S(2)}, u32[]{:S(2)}) collective-permute-start(bf16[1,257,512]{2,1,0:T(8,128)(2,1)} %pad_maximum_fusion.7), channel_id=1, source_target_pairs={{0,32},{4,36},{8,40},{12,44},{16,48},{20,52},{24,56},{28,60},{32,6... | collective-permute-start | bytes 789512 | tf_op jit(solution)/shard_map/ppermute | solution.py:19
  97.6 1.0 reshape.1337
  98.6 1.1 fusion.41
  99.7 1.3 fusion.9
  101.2 3.0 %multiply_reduce_fusion.2 = (f32[4,64]{1,0:T(4,128)S(1)}, f32[4,64,1,512]{3,1,0,2:T(8,128)}) fusion(f32[4,64,1,512]{3,1,0,2:T(8,128)S(1)} %fusion.9, f32[4,64,256]{2,1,0:T(8,128)S(1)} %bitcast.266, bf16[1,257,512]{2,1,0:T(8,128)(2,1)} %collective-permute-done.5, f32[256]{0:T(256)} %bitcast.285, bf16[1,257,512]{2,1,0:T(8,128)(2,1)} %copy-done.8, ...), kind=kOutput, calls=%fused_computation.66 | convolution fusion | flops 404750080 | bytes 2626560 | tf_op jit(solution)/shard_map/bphc,hcv->bphv/dot_general | solution.py:232
  104.9 1.3 fusion.94
  106.3 4.0 %select_bitcast_fusion = f32[8,1,256,512]{3,2,0,1:T(8,128)S(1)} fusion(f32[256,512]{1,0:T(8,128)S(1)} %fusion.94, f32[8,256]{1,0:T(8,128)S(1)} %copy-done.45, f32[256,512]{1,0:T(8,128)} %get-tuple-element.45, f32[256,512]{1,0:T(8,128)} %bitcast.260, f32[256,512]{1,0:T(8,128)} %bitcast.258, f32[8,256]{1,0:T(8,128)S(1)} %copy-done.44, ...), kind=kOutput, calls=%fused_computation.9 | convolution fusion | flops 146931712 | bytes 7103024 | tf_op jit(solution)/shard_map/rjhc,rjhv->rhcv/dot_general | solution.py:221
  110.3 2.8 %pad_maximum_fusion = f32[8,1,262,512]{3,2,0,1:T(8,128)} fusion(f32[8,1,6,512]{3,2,0,1:T(8,128)S(1)} %reshape.1337, f32[8,1,256,512]{3,2,0,1:T(8,128)S(1)} %select_bitcast_fusion), kind=kLoop, calls=%fused_computation.7 | loop fusion | flops 1073152 | bytes 8585216 | tf_op jit(solution)/shard_map/concatenate | solution.py:246
  113.1 1.2 copy-done.2
  114.3 2.5 %fusion.25 = bf16[256,512]{1,0:T(8,128)(2,1)S(1)} fusion(f32[4,64,1,512]{3,1,0,2:T(8,128)} %get-tuple-element.124, bf16[2048,512]{1,0:T(8,128)(2,1)} %param.21, f32[512]{0:T(512)S(1)} %copy-done.60, f32[256]{0:T(256)S(1)} %copy-done.52, f32[2048]{0:T(1024)S(1)} %copy-done.59, f32[256]{0:T(256)S(1)} %copy-done.54, bf16[256,2048]{1,0:T(8,128)(2,1)S(1)} %copy-done.2), kind=kOutput, calls=%fused_computation.59 | convolution fusion | flops 540278784 | bytes 3944448 | tf_op jit(solution)/shard_map/dot_general | solution.py:137
  116.9 1.7 convolution_convert_fusion
  118.5 1.8 reshape.1336
  120.4 3.0 %constant_dynamic-slice_fusion.3 = (bf16[256,1,512]{2,1,0:T(2,128)(2,1)}, bf16[256,1,512]{2,1,0:T(2,128)(2,1)S(1)}, bf16[256,1,512]{2,1,0:T(2,128)(2,1)S(1)}, bf16[256,1,512]{2,1,0:T(2,128)(2,1)S(1)}) fusion(bf16[256,4,512]{2,1,0:T(4,128)(2,1)S(1)} %reshape.1336, s32[]{:T(128)S(6)} %select_n.584, s32[]{:T(128)S(6)} %select_n.588, s32[]{:T(128)S(6)} %select_n.586, ...), kind=kLoop, calls=%fused_computation.171 | loop fusion | bytes 2097168 | tf_op jit(solution)/shard_map/jit(dynamic_index_in_dim)/dynamic_slice | solution.py:253
  124.1 1.6 collective-permute-start.6
  125.6 0.7 copy.83
  126.4 2.9 %collective-permute-start.7 = (bf16[256,512]{1,0:T(8,128)(2,1)}, bf16[256,512]{1,0:T(8,128)(2,1)}, u32[]{:S(2)}, u32[]{:S(2)}) collective-permute-start(bf16[256,512]{1,0:T(8,128)(2,1)} %bitcast.247), channel_id=1, source_target_pairs={{0,2},{1,3},{2,0},{3,1},{4,6},{5,7},{6,4},{7,5},{8,10},{9,11},{10,... | collective-permute-start | bytes 786440 | tf_op jit(solution)/shard_map/ppermute | solution.py:257
  129.3 0.7 copy.82
  130.0 1.3 collective-permute-start.8
  131.4 1.6 convert_element_type.282
  132.9 1.1 copy.85
  134.1 2.0 collective-permute-done.7
  136.7 1.4 pad_maximum_fusion.1
  138.1 1.2 fusion.22
  140.0 1.2 collective-permute-done.9
  141.9 3.6 %collective-permute-done.10 = bf16[8,2048]{1,0:T(8,128)(2,1)S(1)} collective-permute-done((bf16[8,2048]{1,0:T(8,128)(2,1)S(1)}, bf16[8,2048]{1,0:T(8,128)(2,1)S(1)}, u32[]{:S(2)}, u32[]{:S(2)}) %collective-permute-start.10) | collective-permute-done | bytes 32800 | tf_op jit(solution)/shard_map/ppermute | solution.py:27
  145.5 0.8 collective-permute-start.11
  146.3 4.7 %collective-permute-done.11 = bf16[8,2048]{1,0:T(8,128)(2,1)S(1)} collective-permute-done((bf16[8,2048]{1,0:T(8,128)(2,1)S(1)}, bf16[8,2048]{1,0:T(8,128)(2,1)S(1)}, u32[]{:S(2)}, u32[]{:S(2)}) %collective-permute-start.11) | collective-permute-done | bytes 32800 | tf_op jit(solution)/shard_map/ppermute | solution.py:27
  151.0 2.0 collective-permute-start.12
  153.0 2.0 collective-permute-done.12
  155.0 3.2 %collective-permute-start.13 = (bf16[8,2048]{1,0:T(8,128)(2,1)S(1)}, bf16[8,2048]{1,0:T(8,128)(2,1)S(1)}, u32[]{:S(2)}, u32[]{:S(2)}) collective-permute-start(bf16[8,2048]{1,0:T(8,128)(2,1)S(1)} %add.511), channel_id=1, source_target_pairs={{0,64},{4,68},{8,72},{12,76},{16,80},{20,84},{24,88},{28,92},{32,9... | collective-permute-start | bytes 98312 | tf_op jit(solution)/shard_map/ppermute | solution.py:27
  158.2 2.3 collective-permute-done.13
  160.6 2.3 collective-permute-start.14
  162.9 1.9 collective-permute-done.14
  164.8 2.7 %collective-permute-start.15 = (bf16[8,2048]{1,0:T(8,128)(2,1)S(1)}, bf16[8,2048]{1,0:T(8,128)(2,1)S(1)}, u32[]{:S(2)}, u32[]{:S(2)}) collective-permute-start(bf16[8,2048]{1,0:T(8,128)(2,1)S(1)} %add.513), channel_id=1, source_target_pairs={{0,2},{1,3},{2,0},{3,1},{4,6},{5,7},{6,4},{7,5},{8,10},{9,11},{10,... | collective-permute-start | bytes 98312 | tf_op jit(solution)/shard_map/ppermute | solution.py:27
  167.5 2.8 %collective-permute-done.15 = bf16[8,2048]{1,0:T(8,128)(2,1)S(1)} collective-permute-done((bf16[8,2048]{1,0:T(8,128)(2,1)S(1)}, bf16[8,2048]{1,0:T(8,128)(2,1)S(1)}, u32[]{:S(2)}, u32[]{:S(2)}) %collective-permute-start.15) | collective-permute-done | bytes 32800 | tf_op jit(solution)/shard_map/ppermute | solution.py:27
  171.0 1.0 convolution_reduce_fusion
  172.0 52.0 %all-reduce.2.cloned.1.call-done = f32[8,1,262,512]{3,2,0,1:T(8,128)} async-done(((f32[8,1,262,512]{3,2,0,1:T(8,128)}), f32[8,1,262,512]{3,2,0,1:T(8,128)}) %all-reduce.2.cloned.1.call-update) | async-done | bytes 4292624 | tf_op jit(solution)/shard_map/psum | solution.py:246
  224.0 0.9 slice.393
  225.7 4.6 %slice_bitcast_fusion = f32[8,1,256,512]{3,2,1,0:T(8,128)} fusion(f32[8,1,262,512]{3,2,0,1:T(8,128)} %all-reduce.2.cloned.1.call-done), kind=kLoop, calls=%fused_computation.8 | loop fusion | bytes 8388608
  (236 shorter events, 22.1 us)
Async XLA Ops:
  7.2 109.7 %copy-start = (bf16[512,2048]{1,0:T(8,128)(2,1)S(1)}, bf16[512,2048]{1,0:T(8,128)(2,1)}, u32[]{:S(2)}) copy-start(bf16[512,2048]{1,0:T(8,128)(2,1)} %param.23) | copy-start | bytes 6291460
  7.2 216.8 %all-reduce.2.cloned.1.call-start = ((), (), s32[]{:S(2)}) async-start(), calls=%async_computation | async-start | bytes 8650752 | tf_op jit(solution)/shard_map/psum | solution.py:246
  8.9 7.7 %copy-start.53 = (f32[256]{0:T(256)}, f32[256]{0:T(256)S(1)}, u32[]{:S(2)}) copy-start(f32[256]{0:T(256)S(1)} %add_rsqrt_fusion.1) | copy-start | bytes 3076
  8.9 6.1 %copy-start.55 = (s32[8]{0:T(128)S(1)}, s32[8]{0:T(128)}, u32[]{:S(2)}) copy-start(s32[8]{0:T(128)} %param.26) | copy-start | bytes 100
  8.9 6.1 %copy-start.62 = (s32[8]{0:T(128)S(1)}, s32[8]{0:T(128)}, u32[]{:S(2)}) copy-start(s32[8]{0:T(128)} %param.27) | copy-start | bytes 100
  8.9 7.7 %copy-start.1 = (bf16[256,2048]{1,0:T(8,128)(2,1)S(1)}, bf16[256,2048]{1,0:T(8,128)(2,1)}, u32[]{:S(2)}) copy-start(bf16[256,2048]{1,0:T(8,128)(2,1)} %param.14) | copy-start | bytes 3145732
  8.9 7.7 %copy-start.56 = (bf16[2048,16]{0,1:T(8,128)(2,1)S(1)}, bf16[2048,16]{0,1:T(8,128)(2,1)}, u32[]{:S(2)}) copy-start(bf16[2048,16]{0,1:T(8,128)(2,1)} %param.18) | copy-start | bytes 196612
  8.9 7.7 %copy-start.58 = (f32[2048]{0:T(1024)S(1)}, f32[2048]{0:T(1024)}, u32[]{:S(2)}) copy-start(f32[2048]{0:T(1024)} %param.15) | copy-start | bytes 24580
  9.0 8.2 %copy-start.57 = (bf16[16,256]{1,0:T(8,128)(2,1)S(1)}, bf16[16,256]{1,0:T(8,128)(2,1)}, u32[]{:S(2)}) copy-start(bf16[16,256]{1,0:T(8,128)(2,1)} %param.19) | copy-start | bytes 24580
  9.0 8.2 %copy-start.61 = (f32[256]{0:T(256)S(1)}, f32[256]{0:T(256)}, u32[]{:S(2)}) copy-start(f32[256]{0:T(256)} %param.20) | copy-start | bytes 3076
  13.7 19.9 %collective-permute-start = (bf16[3,1024]{1,0:T(4,128)(2,1)S(1)}, bf16[3,1024]{1,0:T(4,128)(2,1)S(1)}, u32[]{:S(2)}, u32[]{:S(2)}) collective-permute-start(bf16[3,1024]{1,0:T(4,128)(2,1)S(1)} %slice.346), channel_id=1, source_target_pairs={{0,4},{4,8},{8,12},{12,16},{16,20},{20,24},{24,28},{28,32},{32,36}... | collective-permute-start | bytes 18440 | tf_op jit(solution)/shard_map/ppermute | solution.py:19
  15.4 5.5 %copy-start.38 = (f32[4,1024]{1,0:T(4,128)S(1)}, f32[4,1024]{1,0:T(4,128)}, u32[]{:S(2)}) copy-start(f32[4,1024]{1,0:T(4,128)} %param.17) | copy-start | bytes 49156
  23.5 11.0 %copy-start.39 = (pred[8]{0:T(512)(128)(4,1)}, pred[8]{0:T(512)(128)(4,1)S(1)}, u32[]{:S(2)}) copy-start(pred[8]{0:T(512)(128)(4,1)S(1)} %get-tuple-element.29) | copy-start | bytes 28
  23.5 11.0 %copy-start.46 = (pred[8]{0:T(512)(128)(4,1)}, pred[8]{0:T(512)(128)(4,1)S(1)}, u32[]{:S(2)}) copy-start(pred[8]{0:T(512)(128)(4,1)S(1)} %get-tuple-element.106) | copy-start | bytes 28
  23.5 11.0 %copy-start.48 = (pred[8]{0:T(512)(128)(4,1)}, pred[8]{0:T(512)(128)(4,1)S(1)}, u32[]{:S(2)}) copy-start(pred[8]{0:T(512)(128)(4,1)S(1)} %get-tuple-element.107) | copy-start | bytes 28
  25.0 10.4 %copy-start.34 = (f32[8,256]{1,0:T(8,128)}, f32[8,256]{1,0:T(8,128)S(1)}, u32[]{:S(2)}) copy-start(f32[8,256]{1,0:T(8,128)S(1)} %gather_fusion.1) | copy-start | bytes 24580
  25.1 8.5 %copy-start.11 = (bf16[256,1024]{1,0:T(8,128)(2,1)S(1)}, bf16[256,1024]{1,0:T(8,128)(2,1)}, u32[]{:S(2)}) copy-start(bf16[256,1024]{1,0:T(8,128)(2,1)} %copy-done.10) | copy-start | bytes 1572868
  35.5 9.7 %copy-start.4 = (f32[256,1,256]{2,0,1:T(8,128)}, f32[256,1,256]{2,0,1:T(8,128)S(1)}, u32[]{:S(2)}) copy-start(f32[256,1,256]{2,0,1:T(8,128)S(1)} %get-tuple-element.58) | copy-start | bytes 786436
  35.5 9.7 %copy-start.16 = (f32[256,1,256]{2,0,1:T(8,128)}, f32[256,1,256]{2,0,1:T(8,128)S(1)}, u32[]{:S(2)}) copy-start(f32[256,1,256]{2,0,1:T(8,128)S(1)} %get-tuple-element.57) | copy-start | bytes 786436
  37.0 8.2 %copy-start.18 = (f32[4,64,1,256]{3,1,2,0:T(8,128)S(1)}, f32[4,64,1,256]{3,1,2,0:T(8,128)}, u32[]{:S(2)}) copy-start(f32[4,64,1,256]{3,1,2,0:T(8,128)} %copy.86) | copy-start | bytes 786436
  40.5 14.9 %collective-permute-start.1 = (bf16[1,257,512]{2,1,0:T(8,128)(2,1)S(1)}, bf16[1,257,512]{2,1,0:T(8,128)(2,1)S(1)}, u32[]{:S(2)}, u32[]{:S(2)}) collective-permute-start(bf16[1,257,512]{2,1,0:T(8,128)(2,1)S(1)} %pad_maximum_fusion.3), channel_id=1, source_target_pairs={{0,4},{4,8},{8,12},{12,16},{16,20},{20,24},{24,28},{28,32},{32,36}... | collective-permute-start | bytes 789512 | tf_op jit(solution)/shard_map/ppermute | solution.py:19
  55.4 29.8 %copy-start.30 = (f32[1,256]{1,0:T(1,128)}, f32[1,256]{1,0:T(1,128)S(1)}, u32[]{:S(2)}) copy-start(f32[1,256]{1,0:T(1,128)S(1)} %get-tuple-element.38) | copy-start | bytes 3076
  56.2 5.3 %collective-permute-start.2 = (bf16[1,257,512]{2,1,0:T(8,128)(2,1)}, bf16[1,257,512]{2,1,0:T(8,128)(2,1)S(1)}, u32[]{:S(2)}, u32[]{:S(2)}) collective-permute-start(bf16[1,257,512]{2,1,0:T(8,128)(2,1)} %pad_maximum_fusion.4), channel_id=1, source_target_pairs={{0,4},{4,8},{8,12},{12,16},{16,20},{20,24},{24,28},{28,32},{32,36}... | collective-permute-start | bytes 789512 | tf_op jit(solution)/shard_map/ppermute | solution.py:19
  61.6 23.7 %copy-start.32 = (f32[1,256]{1,0:T(1,128)}, f32[1,256]{1,0:T(1,128)S(1)}, u32[]{:S(2)}) copy-start(f32[1,256]{1,0:T(1,128)S(1)} %get-tuple-element.36) | copy-start | bytes 3076
  62.5 12.0 %collective-permute-start.3 = (bf16[1,257,512]{2,1,0:T(8,128)(2,1)}, bf16[1,257,512]{2,1,0:T(8,128)(2,1)}, u32[]{:S(2)}, u32[]{:S(2)}) collective-permute-start(bf16[1,257,512]{2,1,0:T(8,128)(2,1)} %pad_maximum_fusion.5), channel_id=1, source_target_pairs={{0,8},{4,12},{8,16},{12,20},{16,24},{20,28},{24,32},{28,36},{32,40... | collective-permute-start | bytes 789512 | tf_op jit(solution)/shard_map/ppermute | solution.py:19
  71.4 9.9 %copy-start.12 = (f32[1,256,512]{2,1,0:T(8,128)S(1)}, f32[1,256,512]{2,1,0:T(8,128)}, u32[]{:S(2)}) copy-start(f32[1,256,512]{2,1,0:T(8,128)} %get-tuple-element.40) | copy-start | bytes 1572868
  71.4 9.9 %copy-start.13 = (f32[1,256,512]{2,1,0:T(8,128)S(1)}, f32[1,256,512]{2,1,0:T(8,128)}, u32[]{:S(2)}) copy-start(f32[1,256,512]{2,1,0:T(8,128)} %get-tuple-element.41) | copy-start | bytes 1572868
  71.5 9.9 %copy-start.14 = (f32[1,1,256,512]{3,2,1,0:T(8,128)S(1)}, f32[1,1,256,512]{3,2,1,0:T(8,128)}, u32[]{:S(2)}) copy-start(f32[1,1,256,512]{3,2,1,0:T(8,128)} %get-tuple-element.46) | copy-start | bytes 1572868
  71.5 9.9 %copy-start.17 = (f32[256,1,256]{2,0,1:T(8,128)S(1)}, f32[256,1,256]{2,0,1:T(8,128)}, u32[]{:S(2)}) copy-start(f32[256,1,256]{2,0,1:T(8,128)} %copy-done.16) | copy-start | bytes 786436
  75.2 10.1 %copy-start.36 = (f32[1,256]{1,0:T(1,128)}, f32[1,256]{1,0:T(1,128)S(1)}, u32[]{:S(2)}) copy-start(f32[1,256]{1,0:T(1,128)S(1)} %get-tuple-element.34) | copy-start | bytes 3076
  76.5 8.7 %collective-permute-start.4 = (bf16[1,257,512]{2,1,0:T(8,128)(2,1)S(1)}, bf16[1,257,512]{2,1,0:T(8,128)(2,1)S(1)}, u32[]{:S(2)}, u32[]{:S(2)}) collective-permute-start(bf16[1,257,512]{2,1,0:T(8,128)(2,1)S(1)} %pad_maximum_fusion.6), channel_id=1, source_target_pairs={{0,16},{4,20},{8,24},{12,28},{16,32},{20,36},{24,40},{28,44},{32,4... | collective-permute-start | bytes 789512 | tf_op jit(solution)/shard_map/ppermute | solution.py:19
  83.6 16.0 %copy-start.6 = (bf16[256,1,512]{2,0,1:T(8,128)(2,1)S(1)}, bf16[256,1,512]{2,0,1:T(8,128)(2,1)}, u32[]{:S(2)}) copy-start(bf16[256,1,512]{2,0,1:T(8,128)(2,1)} %copy-done.5) | copy-start | bytes 786436
  85.2 11.7 %copy-start.41 = (f32[1,256]{1,0:T(1,128)}, f32[1,256]{1,0:T(1,128)S(1)}, u32[]{:S(2)}) copy-start(f32[1,256]{1,0:T(1,128)S(1)} %get-tuple-element.32) | copy-start | bytes 3076
  87.3 13.8 %collective-permute-start.5 = (bf16[1,257,512]{2,1,0:T(8,128)(2,1)}, bf16[1,257,512]{2,1,0:T(8,128)(2,1)}, u32[]{:S(2)}, u32[]{:S(2)}) collective-permute-start(bf16[1,257,512]{2,1,0:T(8,128)(2,1)} %pad_maximum_fusion.7), channel_id=1, source_target_pairs={{0,32},{4,36},{8,40},{12,44},{16,48},{20,52},{24,56},{28,60},{32,6... | collective-permute-start | bytes 789512 | tf_op jit(solution)/shard_map/ppermute | solution.py:19
  99.7 5.2 %copy-start.9 = (bf16[1,257,512]{2,1,0:T(8,128)(2,1)S(1)}, bf16[1,257,512]{2,1,0:T(8,128)(2,1)}, u32[]{:S(2)}) copy-start(bf16[1,257,512]{2,1,0:T(8,128)(2,1)} %copy-done.8) | copy-start | bytes 789508
  99.7 5.2 %copy-start.31 = (f32[1,256]{1,0:T(1,128)S(1)}, f32[1,256]{1,0:T(1,128)}, u32[]{:S(2)}) copy-start(f32[1,256]{1,0:T(1,128)} %copy-done.30) | copy-start | bytes 3076
  99.7 5.1 %copy-start.33 = (f32[1,256]{1,0:T(1,128)S(1)}, f32[1,256]{1,0:T(1,128)}, u32[]{:S(2)}) copy-start(f32[1,256]{1,0:T(1,128)} %copy-done.32) | copy-start | bytes 3076
  99.7 5.1 %copy-start.37 = (f32[1,256]{1,0:T(1,128)S(1)}, f32[1,256]{1,0:T(1,128)}, u32[]{:S(2)}) copy-start(f32[1,256]{1,0:T(1,128)} %copy-done.36) | copy-start | bytes 3076
  99.7 5.1 %copy-start.42 = (f32[1,256]{1,0:T(1,128)S(1)}, f32[1,256]{1,0:T(1,128)}, u32[]{:S(2)}) copy-start(f32[1,256]{1,0:T(1,128)} %copy-done.41) | copy-start | bytes 3076
  101.1 5.1 %copy-start.20 = (f32[64,256]{1,0:T(8,128)S(1)}, f32[64,256]{1,0:T(8,128)}, u32[]{:S(2)}) copy-start(f32[64,256]{1,0:T(8,128)} %copy-done.19) | copy-start | bytes 196612
  101.1 5.1 %copy-start.22 = (f32[64,256]{1,0:T(8,128)S(1)}, f32[64,256]{1,0:T(8,128)}, u32[]{:S(2)}) copy-start(f32[64,256]{1,0:T(8,128)} %copy-done.21) | copy-start | bytes 196612
  101.1 5.1 %copy-start.24 = (f32[64,256]{1,0:T(8,128)S(1)}, f32[64,256]{1,0:T(8,128)}, u32[]{:S(2)}) copy-start(f32[64,256]{1,0:T(8,128)} %copy-done.23) | copy-start | bytes 196612
  101.1 5.1 %copy-start.26 = (f32[64,256]{1,0:T(8,128)S(1)}, f32[64,256]{1,0:T(8,128)}, u32[]{:S(2)}) copy-start(f32[64,256]{1,0:T(8,128)} %copy-done.25) | copy-start | bytes 196612
  101.1 5.1 %copy-start.27 = (f32[64,256]{1,0:T(8,128)S(1)}, f32[64,256]{1,0:T(8,128)}, u32[]{:S(2)}) copy-start(f32[64,256]{1,0:T(8,128)} %get-tuple-element.59) | copy-start | bytes 196612
  101.1 5.1 %copy-start.28 = (f32[64,256]{1,0:T(8,128)S(1)}, f32[64,256]{1,0:T(8,128)}, u32[]{:S(2)}) copy-start(f32[64,256]{1,0:T(8,128)} %get-tuple-element.60) | copy-start | bytes 196612
  101.1 5.1 %copy-start.29 = (f32[64,256]{1,0:T(8,128)S(1)}, f32[64,256]{1,0:T(8,128)}, u32[]{:S(2)}) copy-start(f32[64,256]{1,0:T(8,128)} %get-tuple-element.61) | copy-start | bytes 196612
  101.1 5.1 %copy-start.35 = (f32[8,256]{1,0:T(8,128)S(1)}, f32[8,256]{1,0:T(8,128)}, u32[]{:S(2)}) copy-start(f32[8,256]{1,0:T(8,128)} %copy-done.34) | copy-start | bytes 24580
  101.1 5.1 %copy-start.40 = (pred[8]{0:T(512)(128)(4,1)S(1)}, pred[8]{0:T(512)(128)(4,1)}, u32[]{:S(2)}) copy-start(pred[8]{0:T(512)(128)(4,1)} %copy-done.39) | copy-start | bytes 28
  123.3 8.0 %copy-start.3 = (bf16[256,2048]{1,0:T(8,128)(2,1)S(1)}, bf16[256,2048]{1,0:T(8,128)(2,1)}, u32[]{:S(2)}) copy-start(bf16[256,2048]{1,0:T(8,128)(2,1)} %param.14) | copy-start | bytes 3145732
  124.1 10.0 %collective-permute-start.6 = (bf16[256,512]{1,0:T(8,128)(2,1)}, bf16[256,512]{1,0:T(8,128)(2,1)}, u32[]{:S(2)}, u32[]{:S(2)}) collective-permute-start(bf16[256,512]{1,0:T(8,128)(2,1)} %bitcast.248), channel_id=1, source_target_pairs={{0,1},{1,2},{2,3},{3,0},{4,5},{5,6},{6,7},{7,4},{8,9},{9,10},{10,1... | collective-permute-start | bytes 786440 | tf_op jit(solution)/shard_map/ppermute | solution.py:257
  126.4 6.6 %copy-start.51 = (s32[8]{0:T(128)S(1)}, s32[8]{0:T(128)}, u32[]{:S(2)}) copy-start(s32[8]{0:T(128)} %get-tuple-element.113) | copy-start | bytes 100
  126.4 9.6 %collective-permute-start.7 = (bf16[256,512]{1,0:T(8,128)(2,1)}, bf16[256,512]{1,0:T(8,128)(2,1)}, u32[]{:S(2)}, u32[]{:S(2)}) collective-permute-start(bf16[256,512]{1,0:T(8,128)(2,1)} %bitcast.247), channel_id=1, source_target_pairs={{0,2},{1,3},{2,0},{3,1},{4,6},{5,7},{6,4},{7,5},{8,10},{9,11},{10,... | collective-permute-start | bytes 786440 | tf_op jit(solution)/shard_map/ppermute | solution.py:257
  130.0 6.7 %collective-permute-start.8 = (bf16[256,512]{1,0:T(8,128)(2,1)}, bf16[256,512]{1,0:T(8,128)(2,1)}, u32[]{:S(2)}, u32[]{:S(2)}) collective-permute-start(bf16[256,512]{1,0:T(8,128)(2,1)} %bitcast.246), channel_id=1, source_target_pairs={{0,3},{1,0},{2,1},{3,2},{4,7},{5,4},{6,5},{7,6},{8,11},{9,8},{10,9... | collective-permute-start | bytes 786440 | tf_op jit(solution)/shard_map/ppermute | solution.py:257
  134.0 5.9 %copy-start.50 = (pred[8]{0:T(512)(128)(4,1)S(1)}, pred[8]{0:T(512)(128)(4,1)}, u32[]{:S(2)}) copy-start(pred[8]{0:T(512)(128)(4,1)} %get-tuple-element.97) | copy-start | bytes 28
  136.7 34.3 %copy-start.7 = (bf16[250,2048]{1,0:T(8,128)(2,1)S(1)}, bf16[250,2048]{1,0:T(8,128)(2,1)}, u32[]{:S(2)}) copy-start(bf16[250,2048]{1,0:T(8,128)(2,1)} %param.25) | copy-start | bytes 3072004
  136.7 34.3 %copy-start.43 = (f32[2048]{0:T(1024)S(1)}, f32[2048]{0:T(1024)}, u32[]{:S(2)}) copy-start(f32[2048]{0:T(1024)} %param.24) | copy-start | bytes 24580
  139.3 32.7 %copy-start.15 = (bf16[256,512]{1,0:T(8,128)(2,1)}, bf16[256,512]{1,0:T(8,128)(2,1)S(1)}, u32[]{:S(2)}) copy-start(bf16[256,512]{1,0:T(8,128)(2,1)S(1)} %fusion.22) | copy-start | bytes 786436
  140.0 1.2 collective-permute-start.9
  141.3 4.2 %collective-permute-start.10 = (bf16[8,2048]{1,0:T(8,128)(2,1)S(1)}, bf16[8,2048]{1,0:T(8,128)(2,1)S(1)}, u32[]{:S(2)}, u32[]{:S(2)}) collective-permute-start(bf16[8,2048]{1,0:T(8,128)(2,1)S(1)} %add_dynamic-update-slice_fusion), channel_id=1, source_target_pairs={{0,8},{4,12},{8,0},{12,4},{16,24},{20,28},{24,16},{28,20},{32,40},... | collective-permute-start | bytes 98312 | tf_op jit(solution)/shard_map/ppermute | solution.py:27
  145.5 5.5 %collective-permute-start.11 = (bf16[8,2048]{1,0:T(8,128)(2,1)S(1)}, bf16[8,2048]{1,0:T(8,128)(2,1)S(1)}, u32[]{:S(2)}, u32[]{:S(2)}) collective-permute-start(bf16[8,2048]{1,0:T(8,128)(2,1)S(1)} %add.509), channel_id=1, source_target_pairs={{0,16},{4,20},{8,24},{12,28},{16,0},{20,4},{24,8},{28,12},{32,48},... | collective-permute-start | bytes 98312 | tf_op jit(solution)/shard_map/ppermute | solution.py:27
  151.0 4.0 %collective-permute-start.12 = (bf16[8,2048]{1,0:T(8,128)(2,1)S(1)}, bf16[8,2048]{1,0:T(8,128)(2,1)S(1)}, u32[]{:S(2)}, u32[]{:S(2)}) collective-permute-start(bf16[8,2048]{1,0:T(8,128)(2,1)S(1)} %add.510), channel_id=1, source_target_pairs={{0,32},{4,36},{8,40},{12,44},{16,48},{20,52},{24,56},{28,60},{32,0... | collective-permute-start | bytes 98312 | tf_op jit(solution)/shard_map/ppermute | solution.py:27
  155.0 5.5 %collective-permute-start.13 = (bf16[8,2048]{1,0:T(8,128)(2,1)S(1)}, bf16[8,2048]{1,0:T(8,128)(2,1)S(1)}, u32[]{:S(2)}, u32[]{:S(2)}) collective-permute-start(bf16[8,2048]{1,0:T(8,128)(2,1)S(1)} %add.511), channel_id=1, source_target_pairs={{0,64},{4,68},{8,72},{12,76},{16,80},{20,84},{24,88},{28,92},{32,9... | collective-permute-start | bytes 98312 | tf_op jit(solution)/shard_map/ppermute | solution.py:27
  160.6 4.2 %collective-permute-start.14 = (bf16[8,2048]{1,0:T(8,128)(2,1)S(1)}, bf16[8,2048]{1,0:T(8,128)(2,1)S(1)}, u32[]{:S(2)}, u32[]{:S(2)}) collective-permute-start(bf16[8,2048]{1,0:T(8,128)(2,1)S(1)} %add.512), channel_id=1, source_target_pairs={{0,1},{1,0},{2,3},{3,2},{4,5},{5,4},{6,7},{7,6},{8,9},{9,8},{10,11... | collective-permute-start | bytes 98312 | tf_op jit(solution)/shard_map/ppermute | solution.py:27
  164.8 5.5 %collective-permute-start.15 = (bf16[8,2048]{1,0:T(8,128)(2,1)S(1)}, bf16[8,2048]{1,0:T(8,128)(2,1)S(1)}, u32[]{:S(2)}, u32[]{:S(2)}) collective-permute-start(bf16[8,2048]{1,0:T(8,128)(2,1)S(1)} %add.513), channel_id=1, source_target_pairs={{0,2},{1,3},{2,0},{3,1},{4,6},{5,7},{6,4},{7,5},{8,10},{9,11},{10,... | collective-permute-start | bytes 98312 | tf_op jit(solution)/shard_map/ppermute | solution.py:27
  (16 other events, 33.4 us)
Sparse Core Ops, SparseCore 0:
  113.2 110.6 all-reduce.1

commit v8 on v7

--- a/solution.py
+++ b/solution.py
@@ -40,14 +40,17 @@
 
 
 def state_prefix(decay_factor, local_state, axis, reach):
-    peers, place = lax.axis_size(axis), lax.axis_index(axis)
+    peers = lax.axis_size(axis)
+    limit = min(peers, reach)
     decay, state = send_pair(decay_factor, local_state, axis, 1)
     step = 1
-    while step < min(peers, reach):
-        earlier_decay, earlier_state = send_pair(decay, state, axis, step)
-        state = state + decay[..., None] * earlier_state
-        decay = jnp.where(place >= step, decay * earlier_decay, decay)
-        step *= 2
+    while step < limit:
+        radix = min(4, -(-limit // step))
+        earlier = [send_pair(decay, state, axis, k * step) for k in range(1, radix)]
+        for earlier_decay, earlier_state in earlier:
+            state = state + decay[..., None] * earlier_state
+            decay = decay * earlier_decay
+        step *= radix
     return state
 
 

time: 239 us -> 246 us (1.029)
  starting transfers between devices: 46.9 us -> 58.7 us
  waiting for transfers between devices: 77.1 us -> 72.7 us
  local copies, waits for them, and re-layouts: 33.7 us -> 31 us
    ppermute x7, starting transfers between devices: 11.6 us -> 19.7 us  [butterfly_sum(): array = array + lax.ppermute(array, axis, pairs)]
    ppermute x7, waiting for transfers between devices: 18.6 us -> 14.9 us  [butterfly_sum(): array = array + lax.ppermute(array, axis, pairs)]
    ppermute x6 -> x8, starting transfers between devices: 29.5 us -> 33.1 us  [passed_along(): return lax.ppermute(array, axis, pairs)]
    convert_element_type x4 -> x2, other arithmetic: 6.06 us -> 4.29 us  [send_pair(): packed = jnp.concatenate([state.astype(jnp.bfloat16), row], axis=1)]
    unnamed x137 -> x109, local copies, waits for them, and re-layouts: 13.7 us -> 12.9 us
  transfers between devices with their start and end apart: 17 -> 19, of which waited for: 12 -> 13; matrix products, arithmetic and copies ran while one was open for 24% -> 25% of each run, Pallas kernels for 0% -> 0%
where the time goes in v8:
time: 246 us; the launch traced here: 244 us
  waiting for transfers between devices  72.7 us (30%)
  starting transfers between devices  58.7 us (24%)
  other arithmetic  43.2 us (18%)
  local copies, waits for them, and re-layouts  31 us (13%)
  matrix products  22 us (9%)
  between operations  16.3 us (7%)
    psum x1, waiting for transfers between devices, shards(): payload = lax.psum(jnp.concatenate([end_states, edge_rows], axis=2), 'seq')  50.6 us
    ppermute x8, starting transfers between devices, passed_along(): return lax.ppermute(array, axis, pairs)  33.1 us
    ppermute x7, starting transfers between devices, butterfly_sum(): array = array + lax.ppermute(array, axis, pairs)  19.7 us
    ppermute x7, waiting for transfers between devices, butterfly_sum(): array = array + lax.ppermute(array, axis, pairs)  14.9 us
    unnamed x109, local copies, waits for them, and re-layouts  12.9 us
    reduce_sum x1, other arithmetic, shards(): jnp.sum(queries[:, :, None] * key_rows[:, None, :] * weights, axis=-1)  7.85 us
    ppermute x3, starting transfers between devices, shards(): lax.ppermute(outgoing, 'tp', [(i, (i + shift) % tp_size) for i in range(t...  5.85 us
    gather x3, local copies, waits for them, and re-layouts, shards(): padded[jnp.clip(located - start_row + KCONV - 1, 0, row_count + KCONV - 2)]  5.21 us
  transfers between devices with their start and end apart: 19, of which 13 were waited for; matrix products, arithmetic and copies ran while one was open for 25% of the time, Pallas kernels for 0%

profile of v8, /device:TPU:0, one launch (start us, length us, event | category | flops | bytes accessed | tf_op | source)
XLA Modules:
  0.0 243.8 jit_solution(3518963149102826179)
XLA Ops:
  7.2 1.6 multiply_reduce_fusion.1
  9.0 3.9 %convolution_convert_fusion.1 = bf16[256,1024]{1,0:T(8,128)(2,1)S(1)} fusion(bf16[2048,1024]{1,0:T(8,128)(2,1)} %param.16, f32[2048]{0:T(1024)} %param.15, f32[256]{0:T(256)S(1)} %add_rsqrt_fusion.1, bf16[256,2048]{1,0:T(8,128)(2,1)} %param.14), kind=kOutput, calls=%fused_computation.21 | convolution fusion | flops 1076101120 | bytes 5776384 | tf_op jit(solution)/shard_map/dot_general | solution.py:130
  12.9 0.8 copy-done.6
  13.7 1.3 collective-permute-start
  20.2 1.2 broadcast_compare_fusion.2
  29.0 3.8 %select_compare_fusion = (pred[8]{0:T(512)(128)(4,1)}, pred[8]{0:T(512)(128)(4,1)}) fusion(s32[8]{0:T(128)S(1)} %gather_fusion, s32[]{:T(128)} %bitcast.85, s32[]{:T(128)} %bitcast.84, s32[]{:T(128)} %bitcast.83, s32[]{:T(128)} %bitcast.82, s32[8]{0:T(128)S(1)} %get-tuple-element.30, s32[]{:T(128)} %bitcast.27), kind=kLoop, calls=%fused_computation.240 | loop fusion | flops 64 | bytes 100 | tf_op jit(solution)/shard_map/eq | solution.py:225
  34.8 1.0 pad_maximum_fusion.2
  35.8 0.9 fusion.33
  38.1 2.9 %fusion.21 = (bf16[1,256,512]{2,1,0:T(8,128)(2,1)S(1)}, f32[1,256,512]{2,1,0:T(8,128)S(1)}, f32[1,256,512]{2,1,0:T(8,128)S(1)}, f32[256,512]{1,0:T(8,128)}, f32[1,1,256,512]{3,2,1,0:T(8,128)S(1)}) fusion(f32[4,256,512]{2,1,0:T(8,128)S(1)} %fusion.62, f32[256]{0:T(256)S(1)} %bitcast.291, pred[]{:T(512)} %bitcast.24, f32[256]{0:T(256)S(1)} %bitcast.292, ...), kind=kLoop, calls=%fused_computation.50 | loop fusion | flops 1441792 | bytes 4460547 | tf_op jit(solution)/shard_map/convert_element_type | solution.py:36
  41.0 0.8 pad_maximum_fusion.3
  41.8 4.7 %collective-permute-start.1 = (bf16[1,257,512]{2,1,0:T(8,128)(2,1)}, bf16[1,257,512]{2,1,0:T(8,128)(2,1)S(1)}, u32[]{:S(2)}, u32[]{:S(2)}) collective-permute-start(bf16[1,257,512]{2,1,0:T(8,128)(2,1)} %pad_maximum_fusion.3), channel_id=1, source_target_pairs={{0,4},{4,8},{8,12},{12,16},{16,20},{20,24},{24,28},{28,32},{32,36}... | collective-permute-start | bytes 789512 | tf_op jit(solution)/shard_map/ppermute | solution.py:19
  46.5 7.9 %multiply_reduce_fusion = bf16[4,64,64]{2,1,0:T(8,128)(2,1)S(1)} fusion(f32[4,64,256]{2,1,0:T(8,128)S(1)} %bitcast.274, f32[4,64,256]{2,1,0:T(8,128)S(1)} %bitcast.261, f32[4,64,256]{2,1,0:T(8,128)S(1)} %bitcast.271, pred[4,64,64]{2,1,0:T(8,128)(4,1)S(1)} %compare_and_fusion), kind=kLoop, calls=%fused_computation.6 | loop fusion | flops 25149440 | bytes 835584 | tf_op jit(solution)/shard_map/reduce_sum | solution.py:172
  54.4 2.3 fusion.11
  57.4 1.8 gather_fusion.3
  59.2 2.1 fusion.9
  62.0 4.1 %collective-permute-start.4 = (bf16[1,257,512]{2,1,0:T(8,128)(2,1)}, bf16[1,257,512]{2,1,0:T(8,128)(2,1)}, u32[]{:S(2)}, u32[]{:S(2)}) collective-permute-start(bf16[1,257,512]{2,1,0:T(8,128)(2,1)} %pad_maximum_fusion.4), channel_id=1, source_target_pairs={{0,12},{4,16},{8,20},{12,24},{16,28},{20,32},{24,36},{28,40},{32,4... | collective-permute-start | bytes 789512 | tf_op jit(solution)/shard_map/ppermute | solution.py:19
  66.9 1.7 gather_fusion.2
  68.6 4.2 %collective-permute-start.3 = (bf16[1,257,512]{2,1,0:T(8,128)(2,1)}, bf16[1,257,512]{2,1,0:T(8,128)(2,1)}, u32[]{:S(2)}, u32[]{:S(2)}) collective-permute-start(bf16[1,257,512]{2,1,0:T(8,128)(2,1)} %pad_maximum_fusion.4), channel_id=1, source_target_pairs={{0,8},{4,12},{8,16},{12,20},{16,24},{20,28},{24,32},{28,36},{32,40... | collective-permute-start | bytes 789512 | tf_op jit(solution)/shard_map/ppermute | solution.py:19
  73.5 1.7 gather_fusion.4
  75.2 1.8 collective-permute-start.2
  77.8 1.4 collective-permute-done.3
  80.0 1.4 fusion.103
  82.1 8.5 %collective-permute-start.6 = (bf16[1,257,512]{2,1,0:T(8,128)(2,1)}, bf16[1,257,512]{2,1,0:T(8,128)(2,1)}, u32[]{:S(2)}, u32[]{:S(2)}) collective-permute-start(bf16[1,257,512]{2,1,0:T(8,128)(2,1)} %pad_maximum_fusion.5), channel_id=1, source_target_pairs={{0,32},{4,36},{8,40},{12,44},{16,48},{20,52},{24,56},{28,60},{32,6... | collective-permute-start | bytes 789512 | tf_op jit(solution)/shard_map/ppermute | solution.py:19
  90.6 3.6 %collective-permute-start.5 = (bf16[1,257,512]{2,1,0:T(8,128)(2,1)}, bf16[1,257,512]{2,1,0:T(8,128)(2,1)}, u32[]{:S(2)}, u32[]{:S(2)}) collective-permute-start(bf16[1,257,512]{2,1,0:T(8,128)(2,1)} %pad_maximum_fusion.5), channel_id=1, source_target_pairs={{0,16},{4,20},{8,24},{12,28},{16,32},{20,36},{24,40},{28,44},{32,4... | collective-permute-start | bytes 789512 | tf_op jit(solution)/shard_map/ppermute | solution.py:19
  94.4 1.1 fusion.39
  95.5 4.8 %collective-permute-start.7 = (bf16[1,257,512]{2,1,0:T(8,128)(2,1)}, bf16[1,257,512]{2,1,0:T(8,128)(2,1)S(1)}, u32[]{:S(2)}, u32[]{:S(2)}) collective-permute-start(bf16[1,257,512]{2,1,0:T(8,128)(2,1)} %pad_maximum_fusion.5), channel_id=1, source_target_pairs={{0,48},{4,52},{8,56},{12,60},{16,64},{20,68},{24,72},{28,76},{32,8... | collective-permute-start | bytes 789512 | tf_op jit(solution)/shard_map/ppermute | solution.py:19
  101.7 2.7 %collective-permute-done.7 = bf16[1,257,512]{2,1,0:T(8,128)(2,1)S(1)} collective-permute-done((bf16[1,257,512]{2,1,0:T(8,128)(2,1)}, bf16[1,257,512]{2,1,0:T(8,128)(2,1)S(1)}, u32[]{:S(2)}, u32[]{:S(2)}) %collective-permute-start.7) | collective-permute-done | bytes 263200 | tf_op jit(solution)/shard_map/ppermute | solution.py:19
  104.4 2.9 %multiply_reduce_fusion.2 = (f32[4,64]{1,0:T(4,128)S(1)}, f32[4,64,1,512]{3,1,0,2:T(8,128)}) fusion(f32[4,64,1,512]{3,1,0,2:T(8,128)} %fusion.9, f32[4,64,256]{2,1,0:T(8,128)S(1)} %bitcast.264, bf16[1,257,512]{2,1,0:T(8,128)(2,1)S(1)} %collective-permute-done.7, f32[256]{0:T(256)S(1)} %bitcast.284, bf16[1,257,512]{2,1,0:T(8,128)(2,1)} %collective-permute-done.6, ...), kind=kOutput, calls=%fused_computation.66 | convolution fusion | flops 404225792 | bytes 2625536 | tf_op jit(solution)/shard_map/bphc,hcv->bphv/dot_general | solution.py:235
  108.0 1.2 fusion.101
  109.4 4.0 %select_bitcast_fusion = f32[8,1,256,512]{3,2,0,1:T(8,128)S(1)} fusion(f32[256,512]{1,0:T(8,128)S(1)} %fusion.101, f32[8,256]{1,0:T(8,128)S(1)} %copy-done.24, f32[256,512]{1,0:T(8,128)} %get-tuple-element.47, f32[256,512]{1,0:T(8,128)} %bitcast.270, f32[256,512]{1,0:T(8,128)} %bitcast.268, f32[8,256]{1,0:T(8,128)S(1)} %copy-done.23, ...), kind=kOutput, calls=%fused_computation.9 | convolution fusion | flops 146931712 | bytes 7103024 | tf_op jit(solution)/shard_map/rjhc,rjhv->rhcv/dot_general | solution.py:224
  113.5 2.8 %pad_maximum_fusion = f32[8,1,262,512]{3,2,0,1:T(8,128)} fusion(f32[8,1,6,512]{3,2,0,1:T(8,128)S(1)} %reshape.1371, f32[8,1,256,512]{3,2,0,1:T(8,128)S(1)} %select_bitcast_fusion), kind=kLoop, calls=%fused_computation.7 | loop fusion | flops 1073152 | bytes 8585216 | tf_op jit(solution)/shard_map/concatenate | solution.py:249
  116.3 1.2 copy-done.2
  117.5 2.5 %fusion.25 = bf16[256,512]{1,0:T(8,128)(2,1)S(1)} fusion(f32[4,64,1,512]{3,1,0,2:T(8,128)} %get-tuple-element.126, bf16[2048,512]{1,0:T(8,128)(2,1)} %param.21, f32[512]{0:T(512)S(1)} %copy-done.45, f32[256]{0:T(256)S(1)} %copy-done.33, f32[2048]{0:T(1024)S(1)} %copy-done.44, f32[256]{0:T(256)S(1)} %copy-done.35, bf16[256,2048]{1,0:T(8,128)(2,1)S(1)} %copy-done.2), kind=kOutput, calls=%fused_computation.59 | convolution fusion | flops 540278784 | bytes 3944448 | tf_op jit(solution)/shard_map/dot_general | solution.py:140
  120.0 1.7 convolution_convert_fusion
  121.7 1.8 reshape.1370
  123.5 3.0 %constant_dynamic-slice_fusion.3 = (bf16[256,1,512]{2,1,0:T(2,128)(2,1)}, bf16[256,1,512]{2,1,0:T(2,128)(2,1)S(1)}, bf16[256,1,512]{2,1,0:T(2,128)(2,1)S(1)}, bf16[256,1,512]{2,1,0:T(2,128)(2,1)S(1)}) fusion(bf16[256,4,512]{2,1,0:T(4,128)(2,1)S(1)} %reshape.1370, s32[]{:T(128)S(6)} %select_n.558, s32[]{:T(128)S(6)} %select_n.562, s32[]{:T(128)S(6)} %select_n.560, ...), kind=kLoop, calls=%fused_computation.165 | loop fusion | bytes 2097168 | tf_op jit(solution)/shard_map/jit(dynamic_index_in_dim)/dynamic_slice | solution.py:256
  126.5 0.7 copy.84
  127.2 1.6 collective-permute-start.8
  128.9 0.7 copy.83
  129.6 2.9 %collective-permute-start.9 = (bf16[256,512]{1,0:T(8,128)(2,1)}, bf16[256,512]{1,0:T(8,128)(2,1)}, u32[]{:S(2)}, u32[]{:S(2)}) collective-permute-start(bf16[256,512]{1,0:T(8,128)(2,1)} %bitcast.255), channel_id=1, source_target_pairs={{0,2},{1,3},{2,0},{3,1},{4,6},{5,7},{6,4},{7,5},{8,10},{9,11},{10,... | collective-permute-start | bytes 786440 | tf_op jit(solution)/shard_map/ppermute | solution.py:260
  132.5 0.7 copy.82
  133.2 1.3 collective-permute-start.10
  134.6 1.6 convert_element_type.308
  136.2 1.1 copy.85
  137.4 2.8 %collective-permute-done.9 = bf16[256,512]{1,0:T(8,128)(2,1)} collective-permute-done((bf16[256,512]{1,0:T(8,128)(2,1)}, bf16[256,512]{1,0:T(8,128)(2,1)}, u32[]{:S(2)}, u32[]{:S(2)}) %collective-permute-start.9) | collective-permute-done | bytes 262176 | tf_op jit(solution)/shard_map/ppermute | solution.py:260
  140.3 1.3 pad_maximum_fusion.1
  141.7 1.2 fusion.22
  143.6 1.2 collective-permute-done.11
  144.9 1.7 collective-permute-start.12
  146.5 2.5 %collective-permute-done.12 = bf16[8,2048]{1,0:T(8,128)(2,1)S(1)} collective-permute-done((bf16[8,2048]{1,0:T(8,128)(2,1)S(1)}, bf16[8,2048]{1,0:T(8,128)(2,1)S(1)}, u32[]{:S(2)}, u32[]{:S(2)}) %collective-permute-start.12) | collective-permute-done | bytes 32800 | tf_op jit(solution)/shard_map/ppermute | solution.py:27
  149.0 5.1 %collective-permute-start.13 = (bf16[8,2048]{1,0:T(8,128)(2,1)S(1)}, bf16[8,2048]{1,0:T(8,128)(2,1)S(1)}, u32[]{:S(2)}, u32[]{:S(2)}) collective-permute-start(bf16[8,2048]{1,0:T(8,128)(2,1)S(1)} %add.525), channel_id=1, source_target_pairs={{0,16},{4,20},{8,24},{12,28},{16,0},{20,4},{24,8},{28,12},{32,48},... | collective-permute-start | bytes 98312 | tf_op jit(solution)/shard_map/ppermute | solution.py:27
  154.1 1.9 collective-permute-done.13
  156.0 0.8 collective-permute-start.14
  156.8 3.2 %collective-permute-done.14 = bf16[8,2048]{1,0:T(8,128)(2,1)S(1)} collective-permute-done((bf16[8,2048]{1,0:T(8,128)(2,1)S(1)}, bf16[8,2048]{1,0:T(8,128)(2,1)S(1)}, u32[]{:S(2)}, u32[]{:S(2)}) %collective-permute-start.14) | collective-permute-done | bytes 32800 | tf_op jit(solution)/shard_map/ppermute | solution.py:27
  160.0 6.8 %collective-permute-start.15 = (bf16[8,2048]{1,0:T(8,128)(2,1)S(1)}, bf16[8,2048]{1,0:T(8,128)(2,1)S(1)}, u32[]{:S(2)}, u32[]{:S(2)}) collective-permute-start(bf16[8,2048]{1,0:T(8,128)(2,1)S(1)} %add.527), channel_id=1, source_target_pairs={{0,64},{4,68},{8,72},{12,76},{16,80},{20,84},{24,88},{28,92},{32,9... | collective-permute-start | bytes 98312 | tf_op jit(solution)/shard_map/ppermute | solution.py:27
  166.9 2.0 collective-permute-done.15
  168.9 2.0 collective-permute-start.16
  170.9 2.0 collective-permute-done.16
  172.9 3.4 %collective-permute-start.17 = (bf16[8,2048]{1,0:T(8,128)(2,1)S(1)}, bf16[8,2048]{1,0:T(8,128)(2,1)S(1)}, u32[]{:S(2)}, u32[]{:S(2)}) collective-permute-start(bf16[8,2048]{1,0:T(8,128)(2,1)S(1)} %add.529), channel_id=1, source_target_pairs={{0,2},{1,3},{2,0},{3,1},{4,6},{5,7},{6,4},{7,5},{8,10},{9,11},{10,... | collective-permute-start | bytes 98312 | tf_op jit(solution)/shard_map/ppermute | solution.py:27
  176.2 2.1 collective-permute-done.17
  179.0 1.0 convolution_reduce_fusion
  180.1 50.6 %all-reduce.2.cloned.1.call-done = f32[8,1,262,512]{3,2,0,1:T(8,128)} async-done(((f32[8,1,262,512]{3,2,0,1:T(8,128)}), f32[8,1,262,512]{3,2,0,1:T(8,128)}) %all-reduce.2.cloned.1.call-update) | async-done | bytes 4292624 | tf_op jit(solution)/shard_map/psum | solution.py:249
  230.6 0.9 slice.433
  232.3 4.6 %slice_bitcast_fusion = f32[8,1,256,512]{3,2,1,0:T(8,128)} fusion(f32[8,1,262,512]{3,2,0,1:T(8,128)} %all-reduce.2.cloned.1.call-done), kind=kLoop, calls=%fused_computation.8 | loop fusion | bytes 8388608
  (205 shorter events, 24.6 us)
Async XLA Ops:
  7.2 112.8 %copy-start = (bf16[512,2048]{1,0:T(8,128)(2,1)S(1)}, bf16[512,2048]{1,0:T(8,128)(2,1)}, u32[]{:S(2)}) copy-start(bf16[512,2048]{1,0:T(8,128)(2,1)} %param.23) | copy-start | bytes 6291460
  7.2 223.4 %all-reduce.2.cloned.1.call-start = ((), (), s32[]{:S(2)}) async-start(), calls=%async_computation | async-start | bytes 8650752 | tf_op jit(solution)/shard_map/psum | solution.py:249
  8.9 8.3 %copy-start.34 = (f32[256]{0:T(256)}, f32[256]{0:T(256)S(1)}, u32[]{:S(2)}) copy-start(f32[256]{0:T(256)S(1)} %add_rsqrt_fusion.1) | copy-start | bytes 3076
  8.9 6.1 %copy-start.37 = (s32[8]{0:T(128)S(1)}, s32[8]{0:T(128)}, u32[]{:S(2)}) copy-start(s32[8]{0:T(128)} %param.26) | copy-start | bytes 100
  8.9 6.1 %copy-start.47 = (s32[8]{0:T(128)S(1)}, s32[8]{0:T(128)}, u32[]{:S(2)}) copy-start(s32[8]{0:T(128)} %param.27) | copy-start | bytes 100
  8.9 8.3 %copy-start.1 = (bf16[256,2048]{1,0:T(8,128)(2,1)S(1)}, bf16[256,2048]{1,0:T(8,128)(2,1)}, u32[]{:S(2)}) copy-start(bf16[256,2048]{1,0:T(8,128)(2,1)} %param.14) | copy-start | bytes 3145732
  8.9 8.3 %copy-start.41 = (bf16[2048,16]{0,1:T(8,128)(2,1)S(1)}, bf16[2048,16]{0,1:T(8,128)(2,1)}, u32[]{:S(2)}) copy-start(bf16[2048,16]{0,1:T(8,128)(2,1)} %param.18) | copy-start | bytes 196612
  8.9 8.3 %copy-start.43 = (f32[2048]{0:T(1024)S(1)}, f32[2048]{0:T(1024)}, u32[]{:S(2)}) copy-start(f32[2048]{0:T(1024)} %param.15) | copy-start | bytes 24580
  9.0 8.7 %copy-start.42 = (bf16[16,256]{1,0:T(8,128)(2,1)S(1)}, bf16[16,256]{1,0:T(8,128)(2,1)}, u32[]{:S(2)}) copy-start(bf16[16,256]{1,0:T(8,128)(2,1)} %param.19) | copy-start | bytes 24580
  9.0 8.7 %copy-start.46 = (f32[256]{0:T(256)S(1)}, f32[256]{0:T(256)}, u32[]{:S(2)}) copy-start(f32[256]{0:T(256)} %param.20) | copy-start | bytes 3076
  13.7 21.1 %collective-permute-start = (bf16[3,1024]{1,0:T(4,128)(2,1)S(1)}, bf16[3,1024]{1,0:T(4,128)(2,1)S(1)}, u32[]{:S(2)}, u32[]{:S(2)}) collective-permute-start(bf16[3,1024]{1,0:T(4,128)(2,1)S(1)} %slice.378), channel_id=1, source_target_pairs={{0,4},{4,8},{8,12},{12,16},{16,20},{20,24},{24,28},{28,32},{32,36}... | collective-permute-start | bytes 18440 | tf_op jit(solution)/shard_map/ppermute | solution.py:19
  15.4 6.0 %copy-start.19 = (f32[4,1024]{1,0:T(4,128)S(1)}, f32[4,1024]{1,0:T(4,128)}, u32[]{:S(2)}) copy-start(f32[4,1024]{1,0:T(4,128)} %param.17) | copy-start | bytes 49156
  24.2 9.4 %copy-start.20 = (pred[8]{0:T(512)(128)(4,1)}, pred[8]{0:T(512)(128)(4,1)S(1)}, u32[]{:S(2)}) copy-start(pred[8]{0:T(512)(128)(4,1)S(1)} %get-tuple-element.29) | copy-start | bytes 28
  24.2 11.6 %copy-start.25 = (pred[8]{0:T(512)(128)(4,1)}, pred[8]{0:T(512)(128)(4,1)S(1)}, u32[]{:S(2)}) copy-start(pred[8]{0:T(512)(128)(4,1)S(1)} %get-tuple-element.108) | copy-start | bytes 28
  24.2 11.6 %copy-start.27 = (pred[8]{0:T(512)(128)(4,1)}, pred[8]{0:T(512)(128)(4,1)S(1)}, u32[]{:S(2)}) copy-start(pred[8]{0:T(512)(128)(4,1)S(1)} %get-tuple-element.109) | copy-start | bytes 28
  24.2 0.8 copy-start.14
  25.7 9.1 %copy-start.7 = (bf16[256,1024]{1,0:T(8,128)(2,1)S(1)}, bf16[256,1024]{1,0:T(8,128)(2,1)}, u32[]{:S(2)}) copy-start(bf16[256,1024]{1,0:T(8,128)(2,1)} %copy-done.6) | copy-start | bytes 1572868
  35.8 1.7 copy-start.31
  38.0 8.4 %copy-start.11 = (f32[4,64,1,256]{3,1,2,0:T(8,128)S(1)}, f32[4,64,1,256]{3,1,2,0:T(8,128)}, u32[]{:S(2)}) copy-start(f32[4,64,1,256]{3,1,2,0:T(8,128)} %copy.86) | copy-start | bytes 786436
  41.0 13.4 %copy-start.8 = (f32[1,256,512]{2,1,0:T(8,128)}, f32[1,256,512]{2,1,0:T(8,128)S(1)}, u32[]{:S(2)}) copy-start(f32[1,256,512]{2,1,0:T(8,128)S(1)} %get-tuple-element.42) | copy-start | bytes 1572868
  41.0 13.4 %copy-start.9 = (f32[1,256,512]{2,1,0:T(8,128)}, f32[1,256,512]{2,1,0:T(8,128)S(1)}, u32[]{:S(2)}) copy-start(f32[1,256,512]{2,1,0:T(8,128)S(1)} %get-tuple-element.43) | copy-start | bytes 1572868
  41.8 19.5 %collective-permute-start.1 = (bf16[1,257,512]{2,1,0:T(8,128)(2,1)}, bf16[1,257,512]{2,1,0:T(8,128)(2,1)S(1)}, u32[]{:S(2)}, u32[]{:S(2)}) collective-permute-start(bf16[1,257,512]{2,1,0:T(8,128)(2,1)} %pad_maximum_fusion.3), channel_id=1, source_target_pairs={{0,4},{4,8},{8,12},{12,16},{16,20},{20,24},{24,28},{28,32},{32,36}... | collective-permute-start | bytes 789512 | tf_op jit(solution)/shard_map/ppermute | solution.py:19
  46.5 7.9 %copy-start.40 = (pred[4,64]{1,0:T(4,128)(4,1)S(1)}, pred[4,64]{1,0:T(4,128)(4,1)}, u32[]{:S(2)}) copy-start(pred[4,64]{1,0:T(4,128)(4,1)} %get-tuple-element.92) | copy-start | bytes 772
  46.5 7.9 %copy-start.48 = (f32[4]{0:T(128)S(1)}, f32[4]{0:T(128)}, u32[]{:S(2)}) copy-start(f32[4]{0:T(128)} %pad.25.clone) | copy-start | bytes 52
  61.2 29.3 %copy-start.30 = (pred[8]{0:T(512)(128)(4,1)S(1)}, pred[8]{0:T(512)(128)(4,1)}, u32[]{:S(2)}) copy-start(pred[8]{0:T(512)(128)(4,1)} %get-tuple-element.111) | copy-start | bytes 28
  61.3 18.7 %copy-start.5 = (bf16[1,257,512]{2,1,0:T(8,128)(2,1)}, bf16[1,257,512]{2,1,0:T(8,128)(2,1)S(1)}, u32[]{:S(2)}) copy-start(bf16[1,257,512]{2,1,0:T(8,128)(2,1)S(1)} %collective-permute-done.1) | copy-start | bytes 789508
  62.0 15.0 %collective-permute-start.4 = (bf16[1,257,512]{2,1,0:T(8,128)(2,1)}, bf16[1,257,512]{2,1,0:T(8,128)(2,1)}, u32[]{:S(2)}, u32[]{:S(2)}) collective-permute-start(bf16[1,257,512]{2,1,0:T(8,128)(2,1)} %pad_maximum_fusion.4), channel_id=1, source_target_pairs={{0,12},{4,16},{8,20},{12,24},{16,28},{20,32},{24,36},{28,40},{32,4... | collective-permute-start | bytes 789512 | tf_op jit(solution)/shard_map/ppermute | solution.py:19
  68.6 10.7 %collective-permute-start.3 = (bf16[1,257,512]{2,1,0:T(8,128)(2,1)}, bf16[1,257,512]{2,1,0:T(8,128)(2,1)}, u32[]{:S(2)}, u32[]{:S(2)}) collective-permute-start(bf16[1,257,512]{2,1,0:T(8,128)(2,1)} %pad_maximum_fusion.4), channel_id=1, source_target_pairs={{0,8},{4,12},{8,16},{12,20},{16,24},{20,28},{24,32},{28,36},{32,40... | collective-permute-start | bytes 789512 | tf_op jit(solution)/shard_map/ppermute | solution.py:19
  75.2 4.7 %collective-permute-start.2 = (bf16[1,257,512]{2,1,0:T(8,128)(2,1)}, bf16[1,257,512]{2,1,0:T(8,128)(2,1)S(1)}, u32[]{:S(2)}, u32[]{:S(2)}) collective-permute-start(bf16[1,257,512]{2,1,0:T(8,128)(2,1)} %pad_maximum_fusion.4), channel_id=1, source_target_pairs={{0,4},{4,8},{8,12},{12,16},{16,20},{20,24},{24,28},{28,32},{32,36}... | collective-permute-start | bytes 789512 | tf_op jit(solution)/shard_map/ppermute | solution.py:19
  82.1 18.2 %collective-permute-start.6 = (bf16[1,257,512]{2,1,0:T(8,128)(2,1)}, bf16[1,257,512]{2,1,0:T(8,128)(2,1)}, u32[]{:S(2)}, u32[]{:S(2)}) collective-permute-start(bf16[1,257,512]{2,1,0:T(8,128)(2,1)} %pad_maximum_fusion.5), channel_id=1, source_target_pairs={{0,32},{4,36},{8,40},{12,44},{16,48},{20,52},{24,56},{28,60},{32,6... | collective-permute-start | bytes 789512 | tf_op jit(solution)/shard_map/ppermute | solution.py:19
  90.6 10.3 %collective-permute-start.5 = (bf16[1,257,512]{2,1,0:T(8,128)(2,1)}, bf16[1,257,512]{2,1,0:T(8,128)(2,1)}, u32[]{:S(2)}, u32[]{:S(2)}) collective-permute-start(bf16[1,257,512]{2,1,0:T(8,128)(2,1)} %pad_maximum_fusion.5), channel_id=1, source_target_pairs={{0,16},{4,20},{8,24},{12,28},{16,32},{20,36},{24,40},{28,44},{32,4... | collective-permute-start | bytes 789512 | tf_op jit(solution)/shard_map/ppermute | solution.py:19
  95.5 8.9 %collective-permute-start.7 = (bf16[1,257,512]{2,1,0:T(8,128)(2,1)}, bf16[1,257,512]{2,1,0:T(8,128)(2,1)S(1)}, u32[]{:S(2)}, u32[]{:S(2)}) collective-permute-start(bf16[1,257,512]{2,1,0:T(8,128)(2,1)} %pad_maximum_fusion.5), channel_id=1, source_target_pairs={{0,48},{4,52},{8,56},{12,60},{16,64},{20,68},{24,72},{28,76},{32,8... | collective-permute-start | bytes 789512 | tf_op jit(solution)/shard_map/ppermute | solution.py:19
  104.4 4.9 %copy-start.13 = (f32[64,256]{1,0:T(8,128)S(1)}, f32[64,256]{1,0:T(8,128)}, u32[]{:S(2)}) copy-start(f32[64,256]{1,0:T(8,128)} %copy-done.12) | copy-start | bytes 196612
  104.4 5.0 %copy-start.15 = (f32[64,256]{1,0:T(8,128)S(1)}, f32[64,256]{1,0:T(8,128)}, u32[]{:S(2)}) copy-start(f32[64,256]{1,0:T(8,128)} %copy-done.14) | copy-start | bytes 196612
  104.4 5.0 %copy-start.17 = (f32[64,256]{1,0:T(8,128)S(1)}, f32[64,256]{1,0:T(8,128)}, u32[]{:S(2)}) copy-start(f32[64,256]{1,0:T(8,128)} %copy-done.16) | copy-start | bytes 196612
  104.4 5.0 %copy-start.21 = (pred[8]{0:T(512)(128)(4,1)S(1)}, pred[8]{0:T(512)(128)(4,1)}, u32[]{:S(2)}) copy-start(pred[8]{0:T(512)(128)(4,1)} %copy-done.20) | copy-start | bytes 28
  104.4 5.0 %copy-start.23 = (f32[8,256]{1,0:T(8,128)S(1)}, f32[8,256]{1,0:T(8,128)}, u32[]{:S(2)}) copy-start(f32[8,256]{1,0:T(8,128)} %get-tuple-element.75) | copy-start | bytes 24580
  104.4 5.0 %copy-start.24 = (f32[8,256]{1,0:T(8,128)S(1)}, f32[8,256]{1,0:T(8,128)}, u32[]{:S(2)}) copy-start(f32[8,256]{1,0:T(8,128)} %get-tuple-element.76) | copy-start | bytes 24580
  104.4 5.0 %copy-start.26 = (pred[8]{0:T(512)(128)(4,1)S(1)}, pred[8]{0:T(512)(128)(4,1)}, u32[]{:S(2)}) copy-start(pred[8]{0:T(512)(128)(4,1)} %copy-done.25) | copy-start | bytes 28
  104.4 5.0 %copy-start.28 = (pred[8]{0:T(512)(128)(4,1)S(1)}, pred[8]{0:T(512)(128)(4,1)}, u32[]{:S(2)}) copy-start(pred[8]{0:T(512)(128)(4,1)} %copy-done.27) | copy-start | bytes 28
  104.4 5.0 %copy-start.29 = (pred[8]{0:T(512)(128)(4,1)S(1)}, pred[8]{0:T(512)(128)(4,1)}, u32[]{:S(2)}) copy-start(pred[8]{0:T(512)(128)(4,1)} %get-tuple-element.99) | copy-start | bytes 28
  104.4 5.0 %copy-start.36 = (pred[8,64]{1,0:T(8,128)(4,1)S(1)}, pred[8,64]{1,0:T(8,128)(4,1)}, u32[]{:S(2)}) copy-start(pred[8,64]{1,0:T(8,128)(4,1)} %fusion.74) | copy-start | bytes 1540
  104.4 5.0 %copy-start.38 = (pred[8]{0:T(512)(128)(4,1)S(1)}, pred[8]{0:T(512)(128)(4,1)}, u32[]{:S(2)}) copy-start(pred[8]{0:T(512)(128)(4,1)} %get-tuple-element.100) | copy-start | bytes 28
  104.4 5.0 %copy-start.39 = (pred[8]{0:T(512)(128)(4,1)S(1)}, pred[8]{0:T(512)(128)(4,1)}, u32[]{:S(2)}) copy-start(pred[8]{0:T(512)(128)(4,1)} %get-tuple-element.101) | copy-start | bytes 28
  116.2 1.2 copy-start.2
  116.2 1.2 copy-start.33
  116.2 1.2 copy-start.35
  116.2 1.2 copy-start.44
  116.2 1.2 copy-start.45
  126.5 8.1 %copy-start.3 = (bf16[256,2048]{1,0:T(8,128)(2,1)S(1)}, bf16[256,2048]{1,0:T(8,128)(2,1)}, u32[]{:S(2)}) copy-start(bf16[256,2048]{1,0:T(8,128)(2,1)} %param.14) | copy-start | bytes 3145732
  127.2 10.1 %collective-permute-start.8 = (bf16[256,512]{1,0:T(8,128)(2,1)}, bf16[256,512]{1,0:T(8,128)(2,1)}, u32[]{:S(2)}, u32[]{:S(2)}) collective-permute-start(bf16[256,512]{1,0:T(8,128)(2,1)} %bitcast.256), channel_id=1, source_target_pairs={{0,1},{1,2},{2,3},{3,0},{4,5},{5,6},{6,7},{7,4},{8,9},{9,10},{10,1... | collective-permute-start | bytes 786440 | tf_op jit(solution)/shard_map/ppermute | solution.py:260
  129.6 6.6 %copy-start.32 = (s32[8]{0:T(128)S(1)}, s32[8]{0:T(128)}, u32[]{:S(2)}) copy-start(s32[8]{0:T(128)} %get-tuple-element.115) | copy-start | bytes 100
  129.6 10.6 %collective-permute-start.9 = (bf16[256,512]{1,0:T(8,128)(2,1)}, bf16[256,512]{1,0:T(8,128)(2,1)}, u32[]{:S(2)}, u32[]{:S(2)}) collective-permute-start(bf16[256,512]{1,0:T(8,128)(2,1)} %bitcast.255), channel_id=1, source_target_pairs={{0,2},{1,3},{2,0},{3,1},{4,6},{5,7},{6,4},{7,5},{8,10},{9,11},{10,... | collective-permute-start | bytes 786440 | tf_op jit(solution)/shard_map/ppermute | solution.py:260
  133.2 7.1 %collective-permute-start.10 = (bf16[256,512]{1,0:T(8,128)(2,1)}, bf16[256,512]{1,0:T(8,128)(2,1)}, u32[]{:S(2)}, u32[]{:S(2)}) collective-permute-start(bf16[256,512]{1,0:T(8,128)(2,1)} %bitcast.254), channel_id=1, source_target_pairs={{0,3},{1,0},{2,1},{3,2},{4,7},{5,4},{6,5},{7,6},{8,11},{9,8},{10,9... | collective-permute-start | bytes 786440 | tf_op jit(solution)/shard_map/ppermute | solution.py:260
  140.3 38.7 %copy-start.4 = (bf16[250,2048]{1,0:T(8,128)(2,1)S(1)}, bf16[250,2048]{1,0:T(8,128)(2,1)}, u32[]{:S(2)}) copy-start(bf16[250,2048]{1,0:T(8,128)(2,1)} %param.25) | copy-start | bytes 3072004
  140.3 38.7 %copy-start.22 = (f32[2048]{0:T(1024)S(1)}, f32[2048]{0:T(1024)}, u32[]{:S(2)}) copy-start(f32[2048]{0:T(1024)} %param.24) | copy-start | bytes 24580
  142.9 37.2 %copy-start.10 = (bf16[256,512]{1,0:T(8,128)(2,1)}, bf16[256,512]{1,0:T(8,128)(2,1)S(1)}, u32[]{:S(2)}) copy-start(bf16[256,512]{1,0:T(8,128)(2,1)S(1)} %fusion.22) | copy-start | bytes 786436
  143.6 1.2 collective-permute-start.11
  144.9 4.1 %collective-permute-start.12 = (bf16[8,2048]{1,0:T(8,128)(2,1)S(1)}, bf16[8,2048]{1,0:T(8,128)(2,1)S(1)}, u32[]{:S(2)}, u32[]{:S(2)}) collective-permute-start(bf16[8,2048]{1,0:T(8,128)(2,1)S(1)} %add_dynamic-update-slice_fusion), channel_id=1, source_target_pairs={{0,8},{4,12},{8,0},{12,4},{16,24},{20,28},{24,16},{28,20},{32,40},... | collective-permute-start | bytes 98312 | tf_op jit(solution)/shard_map/ppermute | solution.py:27
  149.0 7.0 %collective-permute-start.13 = (bf16[8,2048]{1,0:T(8,128)(2,1)S(1)}, bf16[8,2048]{1,0:T(8,128)(2,1)S(1)}, u32[]{:S(2)}, u32[]{:S(2)}) collective-permute-start(bf16[8,2048]{1,0:T(8,128)(2,1)S(1)} %add.525), channel_id=1, source_target_pairs={{0,16},{4,20},{8,24},{12,28},{16,0},{20,4},{24,8},{28,12},{32,48},... | collective-permute-start | bytes 98312 | tf_op jit(solution)/shard_map/ppermute | solution.py:27
  156.0 4.0 %collective-permute-start.14 = (bf16[8,2048]{1,0:T(8,128)(2,1)S(1)}, bf16[8,2048]{1,0:T(8,128)(2,1)S(1)}, u32[]{:S(2)}, u32[]{:S(2)}) collective-permute-start(bf16[8,2048]{1,0:T(8,128)(2,1)S(1)} %add.526), channel_id=1, source_target_pairs={{0,32},{4,36},{8,40},{12,44},{16,48},{20,52},{24,56},{28,60},{32,0... | collective-permute-start | bytes 98312 | tf_op jit(solution)/shard_map/ppermute | solution.py:27
  160.0 8.8 %collective-permute-start.15 = (bf16[8,2048]{1,0:T(8,128)(2,1)S(1)}, bf16[8,2048]{1,0:T(8,128)(2,1)S(1)}, u32[]{:S(2)}, u32[]{:S(2)}) collective-permute-start(bf16[8,2048]{1,0:T(8,128)(2,1)S(1)} %add.527), channel_id=1, source_target_pairs={{0,64},{4,68},{8,72},{12,76},{16,80},{20,84},{24,88},{28,92},{32,9... | collective-permute-start | bytes 98312 | tf_op jit(solution)/shard_map/ppermute | solution.py:27
  168.9 4.0 %collective-permute-start.16 = (bf16[8,2048]{1,0:T(8,128)(2,1)S(1)}, bf16[8,2048]{1,0:T(8,128)(2,1)S(1)}, u32[]{:S(2)}, u32[]{:S(2)}) collective-permute-start(bf16[8,2048]{1,0:T(8,128)(2,1)S(1)} %add.528), channel_id=1, source_target_pairs={{0,1},{1,0},{2,3},{3,2},{4,5},{5,4},{6,7},{7,6},{8,9},{9,8},{10,11... | collective-permute-start | bytes 98312 | tf_op jit(solution)/shard_map/ppermute | solution.py:27
  172.9 5.5 %collective-permute-start.17 = (bf16[8,2048]{1,0:T(8,128)(2,1)S(1)}, bf16[8,2048]{1,0:T(8,128)(2,1)S(1)}, u32[]{:S(2)}, u32[]{:S(2)}) collective-permute-start(bf16[8,2048]{1,0:T(8,128)(2,1)S(1)} %add.529), channel_id=1, source_target_pairs={{0,2},{1,3},{2,0},{3,1},{4,6},{5,7},{6,4},{7,5},{8,10},{9,11},{10,... | collective-permute-start | bytes 98312 | tf_op jit(solution)/shard_map/ppermute | solution.py:27
  (4 other events, 3.0 us)
Sparse Core Ops, SparseCore 0:
  116.4 114.1 all-reduce.1

commit v9 on v7

--- a/solution.py
+++ b/solution.py
@@ -140,15 +140,17 @@
 
     offset = last_index - start_row
     owned_here = (offset >= 0) & (offset < row_count)
-    edge_list = []
-    for tap in range(KCONV - 1):
-        located = last_index - (KCONV - 2) + tap
-        inside = owned_here & (located >= first_index)
-        picked = padded[jnp.clip(located - start_row + KCONV - 1, 0, row_count + KCONV - 2)].astype(
-            jnp.float32
-        )
-        edge_list.append(jnp.where(inside[:, None], picked, 0.0))
-    conv_edges = jnp.stack(edge_list, axis=1)
+    taps = jnp.arange(KCONV - 1)
+    located = last_index[:, None] - (KCONV - 2) + taps[None, :]
+    inside = owned_here[:, None] & (located >= first_index[:, None])
+    row_of = jnp.clip(located - start_row + KCONV - 1, 0, row_count + KCONV - 2)
+    one_hot = (
+        row_of.reshape(-1, 1) == jnp.arange(row_count + KCONV - 1)[None, :]
+    ).astype(jnp.bfloat16)
+    picked = jnp.dot(one_hot, padded, preferred_element_type=jnp.float32)
+    conv_edges = jnp.where(
+        inside[:, :, None], picked.reshape(request_count, KCONV - 1, -1), 0.0
+    )
 
     block_count = row_count // BLOCK
     queries = activated[:, :, :DK].astype(jnp.float32).reshape(block_count, BLOCK, head_count, DK)

time: 239 us -> 242 us (1.013)
  local copies, waits for them, and re-layouts: 33.7 us -> 26.8 us
  waiting for transfers between devices: 77.1 us -> 82.5 us
    ppermute x6, waiting for transfers between devices: 3.89 us -> 10.3 us  [passed_along(): return lax.ppermute(array, axis, pairs)]
    gather x3 -> x0, local copies, waits for them, and re-layouts: 5.09 us -> none  [shards(): padded[jnp.clip(located - start_row + KCONV - 1, 0, row_count + KCONV - 2)]]
    unnamed x137 -> x153, local copies, waits for them, and re-layouts: 13.7 us -> 13 us
  transfers between devices with their start and end apart: 17 -> 17, of which waited for: 12 -> 13; matrix products, arithmetic and copies ran while one was open for 24% -> 22% of each run, Pallas kernels for 0% -> 0%
where the time goes in v9:
time: 242 us; the launch traced here: 240 us
  waiting for transfers between devices  82.5 us (34%)
  starting transfers between devices  48.3 us (20%)
  other arithmetic  43.2 us (18%)
  local copies, waits for them, and re-layouts  26.8 us (11%)
  matrix products  22.3 us (9%)
  between operations  16.7 us (7%)
    psum x1, waiting for transfers between devices, shards(): payload = lax.psum(jnp.concatenate([end_states, edge_rows], axis=2), 'seq')  49.7 us
    ppermute x6, starting transfers between devices, passed_along(): return lax.ppermute(array, axis, pairs)  28.6 us
    ppermute x7, waiting for transfers between devices, butterfly_sum(): array = array + lax.ppermute(array, axis, pairs)  17.9 us
    ppermute x7, starting transfers between devices, butterfly_sum(): array = array + lax.ppermute(array, axis, pairs)  13.7 us
    unnamed x153, local copies, waits for them, and re-layouts  13 us
    ppermute x6, waiting for transfers between devices, passed_along(): return lax.ppermute(array, axis, pairs)  10.3 us
    reduce_sum x1, other arithmetic, shards(): jnp.sum(queries[:, :, None] * key_rows[:, None, :] * weights, axis=-1)  8.42 us
    ppermute x3, starting transfers between devices, shards(): lax.ppermute(outgoing, 'tp', [(i, (i + shift) % tp_size) for i in range(t...  5.91 us
  transfers between devices with their start and end apart: 17, of which 13 were waited for; matrix products, arithmetic and copies ran while one was open for 22% of the time, Pallas kernels for 0%

profile of v9, /device:TPU:0, one launch (start us, length us, event | category | flops | bytes accessed | tf_op | source)
XLA Modules:
  0.0 239.8 jit_solution(4970133040731604195)
XLA Ops:
  7.2 1.6 multiply_reduce_fusion.1
  9.0 3.9 %convolution_convert_fusion.1 = bf16[256,1024]{1,0:T(8,128)(2,1)S(1)} fusion(bf16[2048,1024]{1,0:T(8,128)(2,1)} %param.16, f32[2048]{0:T(1024)} %param.15, f32[256]{0:T(256)S(1)} %add_rsqrt_fusion.1, bf16[256,2048]{1,0:T(8,128)(2,1)} %param.14), kind=kOutput, calls=%fused_computation.18 | convolution fusion | flops 1076101120 | bytes 5776384 | tf_op jit(solution)/shard_map/dot_general | solution.py:127
  12.9 0.8 copy-done.12
  13.7 1.3 collective-permute-start
  21.3 1.3 broadcast_compare_fusion.2
  27.0 1.3 fusion.80
  30.2 4.2 %select_compare_fusion = (pred[8]{0:T(512)(128)(4,1)}, pred[8]{0:T(512)(128)(4,1)}) fusion(s32[8]{0:T(128)S(1)} %gather_fusion, s32[]{:T(128)} %bitcast.81, s32[]{:T(128)} %bitcast.80, s32[]{:T(128)} %bitcast.79, s32[]{:T(128)} %bitcast.78, s32[8]{0:T(128)} %copy-done.61, s32[]{:T(128)} %bitcast.27), kind=kLoop, calls=%fused_computation.232 | loop fusion | flops 64 | bytes 100 | tf_op jit(solution)/shard_map/eq | solution.py:224
  34.5 1.2 fusion.38
  35.7 1.6 fusion.33
  37.3 0.7 slice_convert_fusion.1
  38.1 0.7 copy-done.6
  39.4 3.4 %fusion.21 = (bf16[1,256,512]{2,1,0:T(8,128)(2,1)S(1)}, f32[1,256,512]{2,1,0:T(8,128)}, f32[1,256,512]{2,1,0:T(8,128)}, f32[256,512]{1,0:T(8,128)}, f32[1,1,256,512]{3,2,1,0:T(8,128)}) fusion(f32[4,256,512]{2,1,0:T(8,128)S(1)} %fusion.66, f32[256]{0:T(256)S(1)} %bitcast.272, pred[]{:T(512)} %bitcast.24, f32[256]{0:T(256)S(1)} %bitcast.273, pred[]{:T(512)} %bitcast.18, ...), kind=kLoop, calls=%fused_computation.47 | loop fusion | flops 1441792 | bytes 4460547 | tf_op jit(solution)/shard_map/convert_element_type | solution.py:36
  42.9 0.7 pad_maximum_fusion.4
  43.6 4.7 %collective-permute-start.1 = (bf16[1,257,512]{2,1,0:T(8,128)(2,1)}, bf16[1,257,512]{2,1,0:T(8,128)(2,1)S(1)}, u32[]{:S(2)}, u32[]{:S(2)}) collective-permute-start(bf16[1,257,512]{2,1,0:T(8,128)(2,1)} %pad_maximum_fusion.4), channel_id=1, source_target_pairs={{0,4},{4,8},{8,12},{12,16},{16,20},{20,24},{24,28},{28,32},{32,36}... | collective-permute-start | bytes 789512 | tf_op jit(solution)/shard_map/ppermute | solution.py:19
  48.3 0.7 copy.90
  49.0 0.7 copy.57
  50.8 3.2 %collective-permute-start.2 = (bf16[1,257,512]{2,1,0:T(8,128)(2,1)S(1)}, bf16[1,257,512]{2,1,0:T(8,128)(2,1)S(1)}, u32[]{:S(2)}, u32[]{:S(2)}) collective-permute-start(bf16[1,257,512]{2,1,0:T(8,128)(2,1)S(1)} %pad_maximum_fusion.5), channel_id=1, source_target_pairs={{0,4},{4,8},{8,12},{12,16},{16,20},{20,24},{24,28},{28,32},{32,36}... | collective-permute-start | bytes 789512 | tf_op jit(solution)/shard_map/ppermute | solution.py:19
  54.0 8.4 %multiply_reduce_fusion = bf16[4,64,64]{2,1,0:T(8,128)(2,1)} fusion(f32[4,64,256]{2,1,0:T(8,128)} %bitcast.247, f32[4,64,256]{2,1,0:T(8,128)} %bitcast.234, f32[4,64,256]{2,1,0:T(8,128)} %bitcast.243, pred[4,64,64]{2,1,0:T(8,128)(4,1)S(1)} %compare_and_fusion), kind=kLoop, calls=%fused_computation.3 | loop fusion | flops 25149440 | bytes 835584 | tf_op jit(solution)/shard_map/reduce_sum | solution.py:171
  62.6 4.2 %collective-permute-start.3 = (bf16[1,257,512]{2,1,0:T(8,128)(2,1)S(1)}, bf16[1,257,512]{2,1,0:T(8,128)(2,1)S(1)}, u32[]{:S(2)}, u32[]{:S(2)}) collective-permute-start(bf16[1,257,512]{2,1,0:T(8,128)(2,1)S(1)} %pad_maximum_fusion.6), channel_id=1, source_target_pairs={{0,8},{4,12},{8,16},{12,20},{16,24},{20,28},{24,32},{28,36},{32,40... | collective-permute-start | bytes 789512 | tf_op jit(solution)/shard_map/ppermute | solution.py:19
  66.8 0.7 slice_bitcast_fusion.8
  68.3 4.3 %collective-permute-done.3 = bf16[1,257,512]{2,1,0:T(8,128)(2,1)S(1)} collective-permute-done((bf16[1,257,512]{2,1,0:T(8,128)(2,1)S(1)}, bf16[1,257,512]{2,1,0:T(8,128)(2,1)S(1)}, u32[]{:S(2)}, u32[]{:S(2)}) %collective-permute-start.3) | collective-permute-done | bytes 263200 | tf_op jit(solution)/shard_map/ppermute | solution.py:19
  73.5 0.7 pad_maximum_fusion.7
  74.3 7.3 %collective-permute-start.4 = (bf16[1,257,512]{2,1,0:T(8,128)(2,1)}, bf16[1,257,512]{2,1,0:T(8,128)(2,1)}, u32[]{:S(2)}, u32[]{:S(2)}) collective-permute-start(bf16[1,257,512]{2,1,0:T(8,128)(2,1)} %pad_maximum_fusion.7), channel_id=1, source_target_pairs={{0,16},{4,20},{8,24},{12,28},{16,32},{20,36},{24,40},{28,44},{32,4... | collective-permute-start | bytes 789512 | tf_op jit(solution)/shard_map/ppermute | solution.py:19
  82.6 3.0 %fusion.11 = f32[4,1,512,64]{2,3,0,1:T(8,128)S(1)} fusion(f32[1,1,256,512]{3,2,1,0:T(8,128)} %bitcast.239, f32[1,1,256,512]{3,2,1,0:T(8,128)} %bitcast.241, f32[1,1,256,512]{3,2,1,0:T(8,128)} %get-tuple-element.44, f32[4]{0:T(128)S(1)} %pad.30.clone, f32[4,64,256]{2,1,0:T(8,128)} %bitcast.244, pred[4,64]{1,0:T(4,128)(4,1)S(1)} %copy-done.63, ...), kind=kOutput, calls=%fused_computation.27 | convolution fusion | flops 404422656 | bytes 2621712 | tf_op jit(solution)/shard_map/bphc,bhcv->bphv/dot_general | solution.py:195
  85.6 2.1 collective-permute-done.4
  88.5 1.2 fusion.39
  89.8 8.0 %collective-permute-start.5 = (bf16[1,257,512]{2,1,0:T(8,128)(2,1)S(1)}, bf16[1,257,512]{2,1,0:T(8,128)(2,1)S(1)}, u32[]{:S(2)}, u32[]{:S(2)}) collective-permute-start(bf16[1,257,512]{2,1,0:T(8,128)(2,1)S(1)} %pad_maximum_fusion.8), channel_id=1, source_target_pairs={{0,32},{4,36},{8,40},{12,44},{16,48},{20,52},{24,56},{28,60},{32,6... | collective-permute-start | bytes 789512 | tf_op jit(solution)/shard_map/ppermute | solution.py:19
  98.2 3.9 %collective-permute-done.5 = bf16[1,257,512]{2,1,0:T(8,128)(2,1)S(1)} collective-permute-done((bf16[1,257,512]{2,1,0:T(8,128)(2,1)S(1)}, bf16[1,257,512]{2,1,0:T(8,128)(2,1)S(1)}, u32[]{:S(2)}, u32[]{:S(2)}) %collective-permute-start.5) | collective-permute-done | bytes 263200 | tf_op jit(solution)/shard_map/ppermute | solution.py:19
  102.3 2.9 %multiply_reduce_fusion.2 = (f32[4,64]{1,0:T(4,128)S(1)}, f32[4,64,1,512]{3,1,0,2:T(8,128)}) fusion(f32[4,64,1,512]{3,1,0,2:T(8,128)S(1)} %fusion.9, f32[4,64,256]{2,1,0:T(8,128)S(1)} %bitcast.248, bf16[1,257,512]{2,1,0:T(8,128)(2,1)S(1)} %collective-permute-done.5, f32[256]{0:T(256)S(1)} %bitcast.267, bf16[1,257,512]{2,1,0:T(8,128)(2,1)} %collective-permute-done.4, ...), kind=kOutput, calls=%fused_computation.63 | convolution fusion | flops 404750080 | bytes 2626560 | tf_op jit(solution)/shard_map/bphc,hcv->bphv/dot_general | solution.py:234
  105.8 1.3 fusion.97
  107.3 4.0 %select_bitcast_fusion = f32[8,1,256,512]{3,2,0,1:T(8,128)S(1)} fusion(f32[256,512]{1,0:T(8,128)S(1)} %fusion.97, f32[8,256]{1,0:T(8,128)S(1)} %copy-done.45, f32[256,512]{1,0:T(8,128)} %get-tuple-element.43, f32[256,512]{1,0:T(8,128)} %bitcast.242, f32[256,512]{1,0:T(8,128)} %bitcast.240, f32[8,256]{1,0:T(8,128)S(1)} %copy-done.44, ...), kind=kOutput, calls=%fused_computation.6 | convolution fusion | flops 146931712 | bytes 7103024 | tf_op jit(solution)/shard_map/rjhc,rjhv->rhcv/dot_general | solution.py:223
  111.4 2.8 %pad_maximum_fusion = f32[8,1,262,512]{3,2,0,1:T(8,128)} fusion(f32[8,1,6,512]{3,2,0,1:T(8,128)S(1)} %broadcast_select_fusion, f32[8,1,256,512]{3,2,0,1:T(8,128)S(1)} %select_bitcast_fusion), kind=kLoop, calls=%fused_computation.4 | loop fusion | flops 1073152 | bytes 8585216 | tf_op jit(solution)/shard_map/concatenate | solution.py:248
  114.2 1.2 copy-done.2
  115.4 2.5 %fusion.25 = bf16[256,512]{1,0:T(8,128)(2,1)S(1)} fusion(f32[4,64,1,512]{3,1,0,2:T(8,128)} %get-tuple-element.109, bf16[2048,512]{1,0:T(8,128)(2,1)} %param.21, f32[512]{0:T(512)S(1)} %copy-done.68, f32[256]{0:T(256)S(1)} %copy-done.58, f32[2048]{0:T(1024)S(1)} %copy-done.67, f32[256]{0:T(256)S(1)} %copy-done.60, bf16[256,2048]{1,0:T(8,128)(2,1)S(1)} %copy-done.2), kind=kOutput, calls=%fused_computation.56 | convolution fusion | flops 540278784 | bytes 3944448 | tf_op jit(solution)/shard_map/dot_general | solution.py:137
  117.9 1.7 convolution_convert_fusion
  119.6 1.8 reshape.1243
  121.5 3.0 %constant_dynamic-slice_fusion.3 = (bf16[256,1,512]{2,1,0:T(2,128)(2,1)}, bf16[256,1,512]{2,1,0:T(2,128)(2,1)S(1)}, bf16[256,1,512]{2,1,0:T(2,128)(2,1)S(1)}, bf16[256,1,512]{2,1,0:T(2,128)(2,1)S(1)}) fusion(bf16[256,4,512]{2,1,0:T(4,128)(2,1)S(1)} %reshape.1243, s32[]{:T(128)S(6)} %select_n.534, s32[]{:T(128)S(6)} %select_n.538, s32[]{:T(128)S(6)} %select_n.536, ...), kind=kLoop, calls=%fused_computation.170 | loop fusion | bytes 2097168 | tf_op jit(solution)/shard_map/jit(dynamic_index_in_dim)/dynamic_slice | solution.py:255
  124.5 1.7 collective-permute-start.6
  126.1 0.7 copy.87
  126.9 2.9 %collective-permute-start.7 = (bf16[256,512]{1,0:T(8,128)(2,1)}, bf16[256,512]{1,0:T(8,128)(2,1)}, u32[]{:S(2)}, u32[]{:S(2)}) collective-permute-start(bf16[256,512]{1,0:T(8,128)(2,1)} %bitcast.228), channel_id=1, source_target_pairs={{0,2},{1,3},{2,0},{3,1},{4,6},{5,7},{6,4},{7,5},{8,10},{9,11},{10,... | collective-permute-start | bytes 786440 | tf_op jit(solution)/shard_map/ppermute | solution.py:259
  129.8 0.7 copy.86
  130.5 1.3 collective-permute-start.8
  131.9 1.5 convert_element_type.244
  133.4 1.1 copy.89
  134.5 4.2 %collective-permute-done.7 = bf16[256,512]{1,0:T(8,128)(2,1)} collective-permute-done((bf16[256,512]{1,0:T(8,128)(2,1)}, bf16[256,512]{1,0:T(8,128)(2,1)}, u32[]{:S(2)}, u32[]{:S(2)}) %collective-permute-start.7) | collective-permute-done | bytes 262176 | tf_op jit(solution)/shard_map/ppermute | solution.py:259
  139.1 1.3 pad_maximum_fusion.1
  140.4 1.2 fusion.22
  142.4 1.2 collective-permute-done.9
  143.6 1.0 collective-permute-start.10
  144.6 3.2 %collective-permute-done.10 = bf16[8,2048]{1,0:T(8,128)(2,1)S(1)} collective-permute-done((bf16[8,2048]{1,0:T(8,128)(2,1)S(1)}, bf16[8,2048]{1,0:T(8,128)(2,1)S(1)}, u32[]{:S(2)}, u32[]{:S(2)}) %collective-permute-start.10) | collective-permute-done | bytes 32800 | tf_op jit(solution)/shard_map/ppermute | solution.py:27
  147.8 1.4 collective-permute-start.11
  149.2 4.1 %collective-permute-done.11 = bf16[8,2048]{1,0:T(8,128)(2,1)S(1)} collective-permute-done((bf16[8,2048]{1,0:T(8,128)(2,1)S(1)}, bf16[8,2048]{1,0:T(8,128)(2,1)S(1)}, u32[]{:S(2)}, u32[]{:S(2)}) %collective-permute-start.11) | collective-permute-done | bytes 32800 | tf_op jit(solution)/shard_map/ppermute | solution.py:27
  153.4 2.3 collective-permute-start.12
  155.6 1.9 collective-permute-done.12
  157.5 3.6 %collective-permute-start.13 = (bf16[8,2048]{1,0:T(8,128)(2,1)S(1)}, bf16[8,2048]{1,0:T(8,128)(2,1)S(1)}, u32[]{:S(2)}, u32[]{:S(2)}) collective-permute-start(bf16[8,2048]{1,0:T(8,128)(2,1)S(1)} %add.445), channel_id=1, source_target_pairs={{0,64},{4,68},{8,72},{12,76},{16,80},{20,84},{24,88},{28,92},{32,9... | collective-permute-start | bytes 98312 | tf_op jit(solution)/shard_map/ppermute | solution.py:27
  161.2 1.9 collective-permute-done.13
  163.1 3.6 %collective-permute-start.14 = (bf16[8,2048]{1,0:T(8,128)(2,1)S(1)}, bf16[8,2048]{1,0:T(8,128)(2,1)S(1)}, u32[]{:S(2)}, u32[]{:S(2)}) collective-permute-start(bf16[8,2048]{1,0:T(8,128)(2,1)S(1)} %add.446), channel_id=1, source_target_pairs={{0,1},{1,0},{2,3},{3,2},{4,5},{5,4},{6,7},{7,6},{8,9},{9,8},{10,11... | collective-permute-start | bytes 98312 | tf_op jit(solution)/shard_map/ppermute | solution.py:27
  166.6 1.9 collective-permute-done.14
  168.5 1.8 collective-permute-start.15
  170.3 3.7 %collective-permute-done.15 = bf16[8,2048]{1,0:T(8,128)(2,1)S(1)} collective-permute-done((bf16[8,2048]{1,0:T(8,128)(2,1)S(1)}, bf16[8,2048]{1,0:T(8,128)(2,1)S(1)}, u32[]{:S(2)}, u32[]{:S(2)}) %collective-permute-start.15) | collective-permute-done | bytes 32800 | tf_op jit(solution)/shard_map/ppermute | solution.py:27
  174.7 2.2 convolution_reduce_fusion
  176.9 49.7 %all-reduce.2.cloned.1.call-done = f32[8,1,262,512]{3,2,0,1:T(8,128)} async-done(((f32[8,1,262,512]{3,2,0,1:T(8,128)}), f32[8,1,262,512]{3,2,0,1:T(8,128)}) %all-reduce.2.cloned.1.call-update) | async-done | bytes 4292624 | tf_op jit(solution)/shard_map/psum | solution.py:248
  226.6 0.9 slice.387
  228.3 4.6 %slice_bitcast_fusion = f32[8,1,256,512]{3,2,1,0:T(8,128)} fusion(f32[8,1,262,512]{3,2,0,1:T(8,128)} %all-reduce.2.cloned.1.call-done), kind=kLoop, calls=%fused_computation.5 | loop fusion | bytes 8388608
  (253 shorter events, 20.2 us)
Async XLA Ops:
  7.2 110.7 %copy-start = (bf16[512,2048]{1,0:T(8,128)(2,1)S(1)}, bf16[512,2048]{1,0:T(8,128)(2,1)}, u32[]{:S(2)}) copy-start(bf16[512,2048]{1,0:T(8,128)(2,1)} %param.23) | copy-start | bytes 6291460
  7.2 219.4 %all-reduce.2.cloned.1.call-start = ((), (), s32[]{:S(2)}) async-start(), calls=%async_computation | async-start | bytes 8650752 | tf_op jit(solution)/shard_map/psum | solution.py:248
  8.9 8.9 %copy-start.59 = (f32[256]{0:T(256)}, f32[256]{0:T(256)S(1)}, u32[]{:S(2)}) copy-start(f32[256]{0:T(256)S(1)} %add_rsqrt_fusion.1) | copy-start | bytes 3076
  8.9 6.1 %copy-start.62 = (s32[8]{0:T(128)S(1)}, s32[8]{0:T(128)}, u32[]{:S(2)}) copy-start(s32[8]{0:T(128)} %param.26) | copy-start | bytes 100
  8.9 6.1 %copy-start.70 = (s32[8]{0:T(128)S(1)}, s32[8]{0:T(128)}, u32[]{:S(2)}) copy-start(s32[8]{0:T(128)} %param.27) | copy-start | bytes 100
  8.9 8.9 %copy-start.1 = (bf16[256,2048]{1,0:T(8,128)(2,1)S(1)}, bf16[256,2048]{1,0:T(8,128)(2,1)}, u32[]{:S(2)}) copy-start(bf16[256,2048]{1,0:T(8,128)(2,1)} %param.14) | copy-start | bytes 3145732
  8.9 8.9 %copy-start.64 = (bf16[2048,16]{0,1:T(8,128)(2,1)S(1)}, bf16[2048,16]{0,1:T(8,128)(2,1)}, u32[]{:S(2)}) copy-start(bf16[2048,16]{0,1:T(8,128)(2,1)} %param.18) | copy-start | bytes 196612
  8.9 8.9 %copy-start.66 = (f32[2048]{0:T(1024)S(1)}, f32[2048]{0:T(1024)}, u32[]{:S(2)}) copy-start(f32[2048]{0:T(1024)} %param.15) | copy-start | bytes 24580
  9.0 9.4 %copy-start.65 = (bf16[16,256]{1,0:T(8,128)(2,1)S(1)}, bf16[16,256]{1,0:T(8,128)(2,1)}, u32[]{:S(2)}) copy-start(bf16[16,256]{1,0:T(8,128)(2,1)} %param.19) | copy-start | bytes 24580
  9.0 9.3 %copy-start.69 = (f32[256]{0:T(256)S(1)}, f32[256]{0:T(256)}, u32[]{:S(2)}) copy-start(f32[256]{0:T(256)} %param.20) | copy-start | bytes 3076
  13.7 20.8 %collective-permute-start = (bf16[3,1024]{1,0:T(4,128)(2,1)S(1)}, bf16[3,1024]{1,0:T(4,128)(2,1)S(1)}, u32[]{:S(2)}, u32[]{:S(2)}) collective-permute-start(bf16[3,1024]{1,0:T(4,128)(2,1)S(1)} %slice.340), channel_id=1, source_target_pairs={{0,4},{4,8},{8,12},{12,16},{16,20},{20,24},{24,28},{28,32},{32,36}... | collective-permute-start | bytes 18440 | tf_op jit(solution)/shard_map/ppermute | solution.py:19
  15.2 7.4 %copy-start.41 = (f32[4,1024]{1,0:T(4,128)S(1)}, f32[4,1024]{1,0:T(4,128)}, u32[]{:S(2)}) copy-start(f32[4,1024]{1,0:T(4,128)} %param.17) | copy-start | bytes 49156
  17.8 10.4 %copy-start.52 = (pred[8]{0:T(512)(128)(4,1)}, pred[8]{0:T(512)(128)(4,1)S(1)}, u32[]{:S(2)}) copy-start(pred[8]{0:T(512)(128)(4,1)S(1)} %compare_and_fusion.1) | copy-start | bytes 28
  19.5 6.1 %copy-start.61 = (s32[8]{0:T(128)}, s32[8]{0:T(128)S(1)}, u32[]{:S(2)}) copy-start(s32[8]{0:T(128)S(1)} %get-tuple-element.28) | copy-start | bytes 100
  19.5 17.8 %copy-start.46 = (pred[8]{0:T(512)(128)(4,1)}, pred[8]{0:T(512)(128)(4,1)S(1)}, u32[]{:S(2)}) copy-start(pred[8]{0:T(512)(128)(4,1)S(1)} %get-tuple-element.27) | copy-start | bytes 28
  24.7 12.6 %copy-start.48 = (pred[8]{0:T(512)(128)(4,1)}, pred[8]{0:T(512)(128)(4,1)S(1)}, u32[]{:S(2)}) copy-start(pred[8]{0:T(512)(128)(4,1)S(1)} %get-tuple-element.96) | copy-start | bytes 28
  24.7 12.6 %copy-start.50 = (pred[8]{0:T(512)(128)(4,1)}, pred[8]{0:T(512)(128)(4,1)S(1)}, u32[]{:S(2)}) copy-start(pred[8]{0:T(512)(128)(4,1)S(1)} %get-tuple-element.97) | copy-start | bytes 28
  24.7 11.0 %copy-start.16 = (f32[64,256]{1,0:T(8,128)}, f32[64,256]{1,0:T(8,128)S(1)}, u32[]{:S(2)}) copy-start(f32[64,256]{1,0:T(8,128)S(1)} %get-tuple-element.110) | copy-start | bytes 196612
  24.7 11.0 %copy-start.18 = (f32[64,256]{1,0:T(8,128)}, f32[64,256]{1,0:T(8,128)S(1)}, u32[]{:S(2)}) copy-start(f32[64,256]{1,0:T(8,128)S(1)} %get-tuple-element.111) | copy-start | bytes 196612
  24.7 11.0 %copy-start.20 = (f32[64,256]{1,0:T(8,128)}, f32[64,256]{1,0:T(8,128)S(1)}, u32[]{:S(2)}) copy-start(f32[64,256]{1,0:T(8,128)S(1)} %get-tuple-element.112) | copy-start | bytes 196612
  24.7 11.0 %copy-start.22 = (f32[64,256]{1,0:T(8,128)}, f32[64,256]{1,0:T(8,128)S(1)}, u32[]{:S(2)}) copy-start(f32[64,256]{1,0:T(8,128)S(1)} %get-tuple-element.113) | copy-start | bytes 196612
  25.6 11.7 %copy-start.35 = (f32[8,256]{1,0:T(8,128)}, f32[8,256]{1,0:T(8,128)S(1)}, u32[]{:S(2)}) copy-start(f32[8,256]{1,0:T(8,128)S(1)} %gather_fusion.1) | copy-start | bytes 24580
  43.6 7.1 %collective-permute-start.1 = (bf16[1,257,512]{2,1,0:T(8,128)(2,1)}, bf16[1,257,512]{2,1,0:T(8,128)(2,1)S(1)}, u32[]{:S(2)}, u32[]{:S(2)}) collective-permute-start(bf16[1,257,512]{2,1,0:T(8,128)(2,1)} %pad_maximum_fusion.4), channel_id=1, source_target_pairs={{0,4},{4,8},{8,12},{12,16},{16,20},{20,24},{24,28},{28,32},{32,36}... | collective-permute-start | bytes 789512 | tf_op jit(solution)/shard_map/ppermute | solution.py:19
  50.7 37.8 %copy-start.29 = (f32[1,256]{1,0:T(1,128)}, f32[1,256]{1,0:T(1,128)S(1)}, u32[]{:S(2)}) copy-start(f32[1,256]{1,0:T(1,128)S(1)} %get-tuple-element.36) | copy-start | bytes 3076
  50.8 11.6 %collective-permute-start.2 = (bf16[1,257,512]{2,1,0:T(8,128)(2,1)S(1)}, bf16[1,257,512]{2,1,0:T(8,128)(2,1)S(1)}, u32[]{:S(2)}, u32[]{:S(2)}) collective-permute-start(bf16[1,257,512]{2,1,0:T(8,128)(2,1)S(1)} %pad_maximum_fusion.5), channel_id=1, source_target_pairs={{0,4},{4,8},{8,12},{12,16},{16,20},{20,24},{24,28},{28,32},{32,36}... | collective-permute-start | bytes 789512 | tf_op jit(solution)/shard_map/ppermute | solution.py:19
  54.0 12.9 %copy-start.5 = (f32[256,1,256]{2,0,1:T(8,128)S(1)}, f32[256,1,256]{2,0,1:T(8,128)}, u32[]{:S(2)}) copy-start(f32[256,1,256]{2,0,1:T(8,128)} %copy-done.4) | copy-start | bytes 786436
  62.4 19.2 %copy-start.13 = (bf16[256,1024]{1,0:T(8,128)(2,1)S(1)}, bf16[256,1024]{1,0:T(8,128)(2,1)}, u32[]{:S(2)}) copy-start(bf16[256,1024]{1,0:T(8,128)(2,1)} %copy-done.12) | copy-start | bytes 1572868
  62.4 26.0 %copy-start.32 = (f32[1,256]{1,0:T(1,128)}, f32[1,256]{1,0:T(1,128)S(1)}, u32[]{:S(2)}) copy-start(f32[1,256]{1,0:T(1,128)S(1)} %get-tuple-element.34) | copy-start | bytes 3076
  62.6 20.0 %copy-start.63 = (pred[4,64]{1,0:T(4,128)(4,1)S(1)}, pred[4,64]{1,0:T(4,128)(4,1)}, u32[]{:S(2)}) copy-start(pred[4,64]{1,0:T(4,128)(4,1)} %get-tuple-element.86) | copy-start | bytes 772
  62.6 10.0 %collective-permute-start.3 = (bf16[1,257,512]{2,1,0:T(8,128)(2,1)S(1)}, bf16[1,257,512]{2,1,0:T(8,128)(2,1)S(1)}, u32[]{:S(2)}, u32[]{:S(2)}) collective-permute-start(bf16[1,257,512]{2,1,0:T(8,128)(2,1)S(1)} %pad_maximum_fusion.6), channel_id=1, source_target_pairs={{0,8},{4,12},{8,16},{12,20},{16,24},{20,28},{24,32},{28,36},{32,40... | collective-permute-start | bytes 789512 | tf_op jit(solution)/shard_map/ppermute | solution.py:19
  72.6 15.8 %copy-start.37 = (f32[1,256]{1,0:T(1,128)}, f32[1,256]{1,0:T(1,128)S(1)}, u32[]{:S(2)}) copy-start(f32[1,256]{1,0:T(1,128)S(1)} %get-tuple-element.32) | copy-start | bytes 3076
  74.3 13.4 %collective-permute-start.4 = (bf16[1,257,512]{2,1,0:T(8,128)(2,1)}, bf16[1,257,512]{2,1,0:T(8,128)(2,1)}, u32[]{:S(2)}, u32[]{:S(2)}) collective-permute-start(bf16[1,257,512]{2,1,0:T(8,128)(2,1)} %pad_maximum_fusion.7), channel_id=1, source_target_pairs={{0,16},{4,20},{8,24},{12,28},{16,32},{20,36},{24,40},{28,44},{32,4... | collective-permute-start | bytes 789512 | tf_op jit(solution)/shard_map/ppermute | solution.py:19
  82.6 5.9 %copy-start.9 = (bf16[1,257,512]{2,1,0:T(8,128)(2,1)S(1)}, bf16[1,257,512]{2,1,0:T(8,128)(2,1)}, u32[]{:S(2)}) copy-start(bf16[1,257,512]{2,1,0:T(8,128)(2,1)} %copy-done.8) | copy-start | bytes 789508
  82.6 15.2 %copy-start.14 = (f32[8,1,6,512]{3,2,0,1:T(8,128)S(1)}, f32[8,1,6,512]{3,2,0,1:T(8,128)}, u32[]{:S(2)}) copy-start(f32[8,1,6,512]{3,2,0,1:T(8,128)} %reshape.1244) | copy-start | bytes 294916
  82.6 15.2 %copy-start.55 = (pred[8,6]{1,0:T(8,128)(4,1)S(1)}, pred[8,6]{1,0:T(8,128)(4,1)}, u32[]{:S(2)}) copy-start(pred[8,6]{1,0:T(8,128)(4,1)} %copy.52) | copy-start | bytes 148
  82.6 15.3 %copy-start.11 = (f32[4,64,1,256]{3,1,2,0:T(8,128)S(1)}, f32[4,64,1,256]{3,1,2,0:T(8,128)}, u32[]{:S(2)}) copy-start(f32[4,64,1,256]{3,1,2,0:T(8,128)} %copy.57) | copy-start | bytes 786436
  82.6 15.3 %copy-start.40 = (f32[4,256]{1,0:T(4,128)S(1)}, f32[4,256]{1,0:T(4,128)}, u32[]{:S(2)}) copy-start(f32[4,256]{1,0:T(4,128)} %maximum_bitcast_fusion.6) | copy-start | bytes 12292
  82.6 15.3 %copy-start.57 = (pred[256]{0:T(512)(128)(4,1)S(1)}, pred[256]{0:T(512)(128)(4,1)}, u32[]{:S(2)}) copy-start(pred[256]{0:T(512)(128)(4,1)} %get-tuple-element.80) | copy-start | bytes 772
  85.6 12.4 %copy-start.7 = (bf16[256,1,512]{2,0,1:T(8,128)(2,1)S(1)}, bf16[256,1,512]{2,0,1:T(8,128)(2,1)}, u32[]{:S(2)}) copy-start(bf16[256,1,512]{2,0,1:T(8,128)(2,1)} %copy-done.6) | copy-start | bytes 786436
  85.6 12.4 %copy-start.28 = (bf16[4,64,64]{2,1,0:T(8,128)(2,1)S(1)}, bf16[4,64,64]{2,1,0:T(8,128)(2,1)}, u32[]{:S(2)}) copy-start(bf16[4,64,64]{2,1,0:T(8,128)(2,1)} %multiply_reduce_fusion) | copy-start | bytes 98308
  88.4 16.8 %copy-start.42 = (f32[1,256]{1,0:T(1,128)}, f32[1,256]{1,0:T(1,128)S(1)}, u32[]{:S(2)}) copy-start(f32[1,256]{1,0:T(1,128)S(1)} %get-tuple-element.30) | copy-start | bytes 3076
  89.7 12.4 %copy-start.30 = (f32[1,256]{1,0:T(1,128)S(1)}, f32[1,256]{1,0:T(1,128)}, u32[]{:S(2)}) copy-start(f32[1,256]{1,0:T(1,128)} %copy-done.29) | copy-start | bytes 3076
  89.7 12.4 %copy-start.33 = (f32[1,256]{1,0:T(1,128)S(1)}, f32[1,256]{1,0:T(1,128)}, u32[]{:S(2)}) copy-start(f32[1,256]{1,0:T(1,128)} %copy-done.32) | copy-start | bytes 3076
  89.7 12.4 %copy-start.38 = (f32[1,256]{1,0:T(1,128)S(1)}, f32[1,256]{1,0:T(1,128)}, u32[]{:S(2)}) copy-start(f32[1,256]{1,0:T(1,128)} %copy-done.37) | copy-start | bytes 3076
  89.8 12.3 %collective-permute-start.5 = (bf16[1,257,512]{2,1,0:T(8,128)(2,1)S(1)}, bf16[1,257,512]{2,1,0:T(8,128)(2,1)S(1)}, u32[]{:S(2)}, u32[]{:S(2)}) collective-permute-start(bf16[1,257,512]{2,1,0:T(8,128)(2,1)S(1)} %pad_maximum_fusion.8), channel_id=1, source_target_pairs={{0,32},{4,36},{8,40},{12,44},{16,48},{20,52},{24,56},{28,60},{32,6... | collective-permute-start | bytes 789512 | tf_op jit(solution)/shard_map/ppermute | solution.py:19
  98.0 7.8 %copy-start.10 = (bf16[1,257,512]{2,1,0:T(8,128)(2,1)S(1)}, bf16[1,257,512]{2,1,0:T(8,128)(2,1)}, u32[]{:S(2)}) copy-start(bf16[1,257,512]{2,1,0:T(8,128)(2,1)} %copy-done.8) | copy-start | bytes 789508
  98.0 7.8 %copy-start.31 = (f32[1,256]{1,0:T(1,128)S(1)}, f32[1,256]{1,0:T(1,128)}, u32[]{:S(2)}) copy-start(f32[1,256]{1,0:T(1,128)} %copy-done.29) | copy-start | bytes 3076
  98.0 7.8 %copy-start.34 = (f32[1,256]{1,0:T(1,128)S(1)}, f32[1,256]{1,0:T(1,128)}, u32[]{:S(2)}) copy-start(f32[1,256]{1,0:T(1,128)} %copy-done.32) | copy-start | bytes 3076
  98.0 7.8 %copy-start.39 = (f32[1,256]{1,0:T(1,128)S(1)}, f32[1,256]{1,0:T(1,128)}, u32[]{:S(2)}) copy-start(f32[1,256]{1,0:T(1,128)} %copy-done.37) | copy-start | bytes 3076
  124.4 7.4 %copy-start.3 = (bf16[256,2048]{1,0:T(8,128)(2,1)S(1)}, bf16[256,2048]{1,0:T(8,128)(2,1)}, u32[]{:S(2)}) copy-start(bf16[256,2048]{1,0:T(8,128)(2,1)} %param.14) | copy-start | bytes 3145732
  124.5 10.1 %collective-permute-start.6 = (bf16[256,512]{1,0:T(8,128)(2,1)S(1)}, bf16[256,512]{1,0:T(8,128)(2,1)}, u32[]{:S(2)}, u32[]{:S(2)}) collective-permute-start(bf16[256,512]{1,0:T(8,128)(2,1)S(1)} %bitcast.245), channel_id=1, source_target_pairs={{0,1},{1,2},{2,3},{3,0},{4,5},{5,6},{6,7},{7,4},{8,9},{9,10},{10,1... | collective-permute-start | bytes 786440 | tf_op jit(solution)/shard_map/ppermute | solution.py:259
  126.9 6.6 %copy-start.56 = (s32[8]{0:T(128)S(1)}, s32[8]{0:T(128)}, u32[]{:S(2)}) copy-start(s32[8]{0:T(128)} %get-tuple-element.25) | copy-start | bytes 100
  126.9 11.9 %collective-permute-start.7 = (bf16[256,512]{1,0:T(8,128)(2,1)}, bf16[256,512]{1,0:T(8,128)(2,1)}, u32[]{:S(2)}, u32[]{:S(2)}) collective-permute-start(bf16[256,512]{1,0:T(8,128)(2,1)} %bitcast.228), channel_id=1, source_target_pairs={{0,2},{1,3},{2,0},{3,1},{4,6},{5,7},{6,4},{7,5},{8,10},{9,11},{10,... | collective-permute-start | bytes 786440 | tf_op jit(solution)/shard_map/ppermute | solution.py:259
  130.5 8.6 %collective-permute-start.8 = (bf16[256,512]{1,0:T(8,128)(2,1)}, bf16[256,512]{1,0:T(8,128)(2,1)}, u32[]{:S(2)}, u32[]{:S(2)}) collective-permute-start(bf16[256,512]{1,0:T(8,128)(2,1)} %bitcast.227), channel_id=1, source_target_pairs={{0,3},{1,0},{2,1},{3,2},{4,7},{5,4},{6,5},{7,6},{8,11},{9,8},{10,9... | collective-permute-start | bytes 786440 | tf_op jit(solution)/shard_map/ppermute | solution.py:259
  134.5 7.7 %copy-start.54 = (pred[8]{0:T(512)(128)(4,1)S(1)}, pred[8]{0:T(512)(128)(4,1)}, u32[]{:S(2)}) copy-start(pred[8]{0:T(512)(128)(4,1)} %copy-done.52) | copy-start | bytes 28
  139.1 35.6 %copy-start.43 = (f32[2048]{0:T(1024)S(1)}, f32[2048]{0:T(1024)}, u32[]{:S(2)}) copy-start(f32[2048]{0:T(1024)} %param.24) | copy-start | bytes 24580
  141.6 91.3 %copy-start.15 = (bf16[256,512]{1,0:T(8,128)(2,1)}, bf16[256,512]{1,0:T(8,128)(2,1)S(1)}, u32[]{:S(2)}) copy-start(bf16[256,512]{1,0:T(8,128)(2,1)S(1)} %fusion.22) | copy-start | bytes 786436
  142.3 1.2 collective-permute-start.9
  143.6 4.2 %collective-permute-start.10 = (bf16[8,2048]{1,0:T(8,128)(2,1)S(1)}, bf16[8,2048]{1,0:T(8,128)(2,1)S(1)}, u32[]{:S(2)}, u32[]{:S(2)}) collective-permute-start(bf16[8,2048]{1,0:T(8,128)(2,1)S(1)} %add_dynamic-update-slice_fusion), channel_id=1, source_target_pairs={{0,8},{4,12},{8,0},{12,4},{16,24},{20,28},{24,16},{28,20},{32,40},... | collective-permute-start | bytes 98312 | tf_op jit(solution)/shard_map/ppermute | solution.py:27
  147.8 5.5 %collective-permute-start.11 = (bf16[8,2048]{1,0:T(8,128)(2,1)S(1)}, bf16[8,2048]{1,0:T(8,128)(2,1)S(1)}, u32[]{:S(2)}, u32[]{:S(2)}) collective-permute-start(bf16[8,2048]{1,0:T(8,128)(2,1)S(1)} %add.443), channel_id=1, source_target_pairs={{0,16},{4,20},{8,24},{12,28},{16,0},{20,4},{24,8},{28,12},{32,48},... | collective-permute-start | bytes 98312 | tf_op jit(solution)/shard_map/ppermute | solution.py:27
  153.4 4.2 %collective-permute-start.12 = (bf16[8,2048]{1,0:T(8,128)(2,1)S(1)}, bf16[8,2048]{1,0:T(8,128)(2,1)S(1)}, u32[]{:S(2)}, u32[]{:S(2)}) collective-permute-start(bf16[8,2048]{1,0:T(8,128)(2,1)S(1)} %add.444), channel_id=1, source_target_pairs={{0,32},{4,36},{8,40},{12,44},{16,48},{20,52},{24,56},{28,60},{32,0... | collective-permute-start | bytes 98312 | tf_op jit(solution)/shard_map/ppermute | solution.py:27
  157.5 5.5 %collective-permute-start.13 = (bf16[8,2048]{1,0:T(8,128)(2,1)S(1)}, bf16[8,2048]{1,0:T(8,128)(2,1)S(1)}, u32[]{:S(2)}, u32[]{:S(2)}) collective-permute-start(bf16[8,2048]{1,0:T(8,128)(2,1)S(1)} %add.445), channel_id=1, source_target_pairs={{0,64},{4,68},{8,72},{12,76},{16,80},{20,84},{24,88},{28,92},{32,9... | collective-permute-start | bytes 98312 | tf_op jit(solution)/shard_map/ppermute | solution.py:27
  163.1 5.5 %collective-permute-start.14 = (bf16[8,2048]{1,0:T(8,128)(2,1)S(1)}, bf16[8,2048]{1,0:T(8,128)(2,1)S(1)}, u32[]{:S(2)}, u32[]{:S(2)}) collective-permute-start(bf16[8,2048]{1,0:T(8,128)(2,1)S(1)} %add.446), channel_id=1, source_target_pairs={{0,1},{1,0},{2,3},{3,2},{4,5},{5,4},{6,7},{7,6},{8,9},{9,8},{10,11... | collective-permute-start | bytes 98312 | tf_op jit(solution)/shard_map/ppermute | solution.py:27
  168.5 5.5 %collective-permute-start.15 = (bf16[8,2048]{1,0:T(8,128)(2,1)S(1)}, bf16[8,2048]{1,0:T(8,128)(2,1)S(1)}, u32[]{:S(2)}, u32[]{:S(2)}) collective-permute-start(bf16[8,2048]{1,0:T(8,128)(2,1)S(1)} %add.447), channel_id=1, source_target_pairs={{0,2},{1,3},{2,0},{3,1},{4,6},{5,7},{6,4},{7,5},{8,10},{9,11},{10,... | collective-permute-start | bytes 98312 | tf_op jit(solution)/shard_map/ppermute | solution.py:27
  (24 other events, 87.3 us)
Sparse Core Ops, SparseCore 0:
  114.3 112.2 all-reduce.1

commit v10 on v7

--- a/solution.py
+++ b/solution.py
@@ -39,16 +39,17 @@
     return tail[:, :DK] + tail[:, DK:], got[:, :DK].astype(jnp.float32)
 
 
-def state_prefix(decay_factor, local_state, axis, reach):
+def state_prefix(decay_factor, local_state, axis, reach, companion):
     peers, place = lax.axis_size(axis), lax.axis_index(axis)
     decay, state = send_pair(decay_factor, local_state, axis, 1)
+    companion, decay, state = lax.optimization_barrier((companion, decay, state))
     step = 1
     while step < min(peers, reach):
         earlier_decay, earlier_state = send_pair(decay, state, axis, step)
         state = state + decay[..., None] * earlier_state
         decay = jnp.where(place >= step, decay * earlier_decay, decay)
         step *= 2
-    return state
+    return state, companion
 
 
 def segments(lengths, packed_order, positions):
@@ -225,7 +226,9 @@
 
     through_shard = segment[-1] == segment_prior
     decay_factor = jnp.where(through_shard, priors[-1] * block_decay[-1], 0.0)
-    incoming = state_prefix(decay_factor, local_state, "seq", -(-MAXLEN // row_count))
+    incoming, local_ends = state_prefix(
+        decay_factor, local_state, "seq", -(-MAXLEN // row_count), local_ends
+    )
 
     reach = jnp.exp(cumulative) * priors[:, None]
     from_before = (block_segment == segment_prior)[:, :, None, None]

time: 239 us -> 257 us (1.075)
  other arithmetic: 41.6 us -> 59.8 us
  local copies, waits for them, and re-layouts: 33.7 us -> 28.7 us
  waiting for transfers between devices: 77.1 us -> 80.6 us
    ppermute x6, waiting for transfers between devices: 3.89 us -> 8.2 us  [passed_along(): return lax.ppermute(array, axis, pairs)]
    gather x3, local copies, waits for them, and re-layouts: 5.09 us -> 2.21 us  [shards(): padded[jnp.clip(located - start_row + KCONV - 1, 0, row_count + KCONV - 2)]]
    select_n x0 -> x1, other arithmetic: none -> 2.86 us  [shards(): end_states = jnp.where(owned_here[:, None, None, None], end_states, 0.0)]
    unnamed x137 -> x117, local copies, waits for them, and re-layouts: 13.7 us -> 12.6 us
    convert_element_type x4 -> x5, other arithmetic: 6.06 us -> 5.34 us  [send_pair(): packed = jnp.concatenate([state.astype(jnp.bfloat16), row], axis=1)]
  transfers between devices with their start and end apart: 17 -> 17, of which waited for: 12 -> 13; matrix products, arithmetic and copies ran while one was open for 24% -> 29% of each run, Pallas kernels for 0% -> 0%
where the time goes in v10:
time: 257 us; the launch traced here: 255 us
  waiting for transfers between devices  80.6 us (31%)
  other arithmetic  59.8 us (23%)
  starting transfers between devices  47.5 us (18%)
  local copies, waits for them, and re-layouts  28.7 us (11%)
  matrix products  21.8 us (8%)
  between operations  16.3 us (6%)
    psum x1, waiting for transfers between devices, shards(): payload = lax.psum(jnp.concatenate([end_states, edge_rows], axis=2), 'seq')  50.6 us
    ppermute x6, starting transfers between devices, passed_along(): return lax.ppermute(array, axis, pairs)  27.9 us
    ppermute x7, waiting for transfers between devices, butterfly_sum(): array = array + lax.ppermute(array, axis, pairs)  17.5 us
    ppermute x7, starting transfers between devices, butterfly_sum(): array = array + lax.ppermute(array, axis, pairs)  13.7 us
    unnamed x117, local copies, waits for them, and re-layouts  12.6 us
    reduce_sum x1, other arithmetic, shards(): jnp.sum(queries[:, :, None] * key_rows[:, None, :] * weights, axis=-1)  8.4 us
    ppermute x6, waiting for transfers between devices, passed_along(): return lax.ppermute(array, axis, pairs)  8.2 us
    ppermute x3, starting transfers between devices, shards(): lax.ppermute(outgoing, 'tp', [(i, (i + shift) % tp_size) for i in range(t...  5.83 us
  transfers between devices with their start and end apart: 17, of which 13 were waited for; matrix products, arithmetic and copies ran while one was open for 29% of the time, Pallas kernels for 0%

profile of v10, /device:TPU:0, one launch (start us, length us, event | category | flops | bytes accessed | tf_op | source)
XLA Modules:
  0.0 254.7 jit_solution(17508589413289671056)
XLA Ops:
  7.3 1.7 multiply_reduce_fusion.1
  9.0 3.8 %convolution_convert_fusion.1 = bf16[256,1024]{1,0:T(8,128)(2,1)S(1)} fusion(bf16[2048,1024]{1,0:T(8,128)(2,1)} %param.16, f32[2048]{0:T(1024)} %param.15, f32[256]{0:T(256)S(1)} %add_rsqrt_fusion.1, bf16[256,2048]{1,0:T(8,128)(2,1)} %param.14), kind=kOutput, calls=%fused_computation.22 | convolution fusion | flops 1076101120 | bytes 5776384 | tf_op jit(solution)/shard_map/dot_general | solution.py:128
  14.2 1.9 collective-permute-start
  24.3 1.3 broadcast_compare_fusion.2
  31.1 0.9 select_bitcast_fusion
  34.8 1.4 compare_and_fusion
  36.2 1.3 pad_clamp_fusion.1
  37.5 1.2 multiply_select_fusion.1
  40.2 1.3 pad_clamp_fusion.2
  41.5 1.3 maximum_bitcast_fusion.6
  42.8 1.4 select_multiply_fusion
  44.2 4.2 %broadcast_compare_fusion.3 = (pred[8]{0:T(512)(128)(4,1)}, pred[8]{0:T(512)(128)(4,1)S(1)}) fusion(s32[8]{0:T(128)S(1)} %gather_fusion, s32[]{:T(128)} %bitcast.46, s32[]{:T(128)} %bitcast.38, s32[]{:T(128)} %bitcast.37, s32[8]{0:T(128)} %copy-done.39, s32[]{:T(128)} %bitcast.36, s32[]{:T(128)} %bitcast.35), kind=kLoop, calls=%fused_computation.248 | loop fusion | flops 64 | bytes 100 | tf_op jit(solution)/shard_map/eq | solution.py:243
  51.1 1.2 pad_maximum_fusion.2
  52.3 1.6 fusion.33
  54.8 2.9 %fusion.21 = (bf16[1,256,512]{2,1,0:T(8,128)(2,1)S(1)}, f32[1,256,512]{2,1,0:T(8,128)S(1)}, f32[1,256,512]{2,1,0:T(8,128)S(1)}, f32[256,512]{1,0:T(8,128)S(1)}, f32[1,1,256,512]{3,2,1,0:T(8,128)}) fusion(f32[4,256,512]{2,1,0:T(8,128)S(1)} %fusion.64, f32[256]{0:T(256)S(1)} %bitcast.284, pred[]{:T(512)} %bitcast.43, f32[256]{0:T(256)S(1)} %bitcast.285, ...), kind=kLoop, calls=%fused_computation.51 | loop fusion | flops 1441792 | bytes 4460547 | tf_op jit(solution)/shard_map/convert_element_type | solution.py:36
  57.7 4.1 %collective-permute-start.1 = (bf16[1,257,512]{2,1,0:T(8,128)(2,1)S(1)}, bf16[1,257,512]{2,1,0:T(8,128)(2,1)S(1)}, u32[]{:S(2)}, u32[]{:S(2)}) collective-permute-start(bf16[1,257,512]{2,1,0:T(8,128)(2,1)S(1)} %pad_maximum_fusion.3), channel_id=1, source_target_pairs={{0,4},{4,8},{8,12},{12,16},{16,20},{20,24},{24,28},{28,32},{32,36}... | collective-permute-start | bytes 789512 | tf_op jit(solution)/shard_map/ppermute | solution.py:19
  61.9 3.6 %add_bitcast_fusion = f32[8,1,256,512]{3,2,0,1:T(8,128)} fusion(f32[256,512]{1,0:T(8,128)S(1)} %get-tuple-element.51, f32[256,512]{1,0:T(8,128)S(1)} %bitcast.261, f32[256,512]{1,0:T(8,128)S(1)} %bitcast.259, f32[8,256]{1,0:T(8,128)S(1)} %get-tuple-element.80, pred[8]{0:T(512)(128)(4,1)S(1)} %copy-done.31, pred[8]{0:T(512)(128)(4,1)S(1)} %copy-done.30, ...), kind=kOutput, calls=%fused_computation.10 | convolution fusion | flops 142737408 | bytes 6570528 | tf_op jit(solution)/shard_map/rjhc,rjhv->rhcv/dot_general | solution.py:222
  66.4 2.6 %collective-permute-start.2 = (bf16[1,257,512]{2,1,0:T(8,128)(2,1)}, bf16[1,257,512]{2,1,0:T(8,128)(2,1)}, u32[]{:S(2)}, u32[]{:S(2)}) collective-permute-start(bf16[1,257,512]{2,1,0:T(8,128)(2,1)} %pad_maximum_fusion.4), channel_id=1, source_target_pairs={{0,4},{4,8},{8,12},{12,16},{16,20},{20,24},{24,28},{28,32},{32,36}... | collective-permute-start | bytes 789512 | tf_op jit(solution)/shard_map/ppermute | solution.py:19
  69.0 8.4 %multiply_reduce_fusion = bf16[4,64,64]{2,1,0:T(8,128)(2,1)} fusion(f32[4,64,256]{2,1,0:T(8,128)S(1)} %bitcast.266, f32[4,64,256]{2,1,0:T(8,128)S(1)} %bitcast.253, f32[4,64,256]{2,1,0:T(8,128)S(1)} %bitcast.263, pred[4,64,64]{2,1,0:T(8,128)(4,1)S(1)} %copy-done.22), kind=kLoop, calls=%fused_computation.6 | loop fusion | flops 25149440 | bytes 835584 | tf_op jit(solution)/shard_map/reduce_sum | solution.py:170
  77.4 0.8 gather_fusion.3
  79.0 1.1 fusion.36
  80.8 4.0 %collective-permute-start.3 = (bf16[1,257,512]{2,1,0:T(8,128)(2,1)}, bf16[1,257,512]{2,1,0:T(8,128)(2,1)}, u32[]{:S(2)}, u32[]{:S(2)}) collective-permute-start(bf16[1,257,512]{2,1,0:T(8,128)(2,1)} %pad_maximum_fusion.5), channel_id=1, source_target_pairs={{0,8},{4,12},{8,16},{12,20},{16,24},{20,28},{24,32},{28,36},{32,40... | collective-permute-start | bytes 789512 | tf_op jit(solution)/shard_map/ppermute | solution.py:19
  86.4 3.9 %collective-permute-done.3 = bf16[1,257,512]{2,1,0:T(8,128)(2,1)} collective-permute-done((bf16[1,257,512]{2,1,0:T(8,128)(2,1)}, bf16[1,257,512]{2,1,0:T(8,128)(2,1)}, u32[]{:S(2)}, u32[]{:S(2)}) %collective-permute-start.3) | collective-permute-done | bytes 263200 | tf_op jit(solution)/shard_map/ppermute | solution.py:19
  91.0 1.2 fusion.98
  92.3 6.8 %collective-permute-start.4 = (bf16[1,257,512]{2,1,0:T(8,128)(2,1)S(1)}, bf16[1,257,512]{2,1,0:T(8,128)(2,1)S(1)}, u32[]{:S(2)}, u32[]{:S(2)}) collective-permute-start(bf16[1,257,512]{2,1,0:T(8,128)(2,1)S(1)} %pad_maximum_fusion.6), channel_id=1, source_target_pairs={{0,16},{4,20},{8,24},{12,28},{16,32},{20,36},{24,40},{28,44},{32,4... | collective-permute-start | bytes 789512 | tf_op jit(solution)/shard_map/ppermute | solution.py:19
  99.2 3.7 %fusion.11 = f32[4,1,512,64]{2,3,0,1:T(8,128)} fusion(f32[1,1,256,512]{3,2,1,0:T(8,128)} %bitcast.260, f32[1,1,256,512]{3,2,1,0:T(8,128)} %bitcast.262, f32[1,1,256,512]{3,2,1,0:T(8,128)} %get-tuple-element.52, f32[4]{0:T(128)S(1)} %copy-done.52, f32[4,64,256]{2,1,0:T(8,128)} %bitcast.264, pred[4,64]{1,0:T(4,128)(4,1)S(1)} %copy-done.44, ...), kind=kOutput, calls=%fused_computation.31 | convolution fusion | flops 404422656 | bytes 2621712 | tf_op jit(solution)/shard_map/bphc,bhcv->bphv/dot_general | solution.py:194
  102.9 2.6 %collective-permute-done.4 = bf16[1,257,512]{2,1,0:T(8,128)(2,1)S(1)} collective-permute-done((bf16[1,257,512]{2,1,0:T(8,128)(2,1)S(1)}, bf16[1,257,512]{2,1,0:T(8,128)(2,1)S(1)}, u32[]{:S(2)}, u32[]{:S(2)}) %collective-permute-start.4) | collective-permute-done | bytes 263200 | tf_op jit(solution)/shard_map/ppermute | solution.py:19
  107.1 8.5 %collective-permute-start.5 = (bf16[1,257,512]{2,1,0:T(8,128)(2,1)}, bf16[1,257,512]{2,1,0:T(8,128)(2,1)}, u32[]{:S(2)}, u32[]{:S(2)}) collective-permute-start(bf16[1,257,512]{2,1,0:T(8,128)(2,1)} %pad_maximum_fusion.7), channel_id=1, source_target_pairs={{0,32},{4,36},{8,40},{12,44},{16,48},{20,52},{24,56},{28,60},{32,6... | collective-permute-start | bytes 789512 | tf_op jit(solution)/shard_map/ppermute | solution.py:19
  115.7 1.0 fusion.41
  116.7 1.3 fusion.9
  118.0 1.7 collective-permute-done.5
  119.7 2.7 %multiply_reduce_fusion.2 = (f32[4,64]{1,0:T(4,128)S(1)}, f32[4,64,1,512]{3,1,0,2:T(8,128)}) fusion(f32[4,64,1,512]{3,1,0,2:T(8,128)S(1)} %fusion.9, f32[4,64,256]{2,1,0:T(8,128)S(1)} %bitcast.256, bf16[1,257,512]{2,1,0:T(8,128)(2,1)} %collective-permute-done.5, f32[256]{0:T(256)} %bitcast.273, f32[1,256,512]{2,1,0:T(8,128)S(1)} %get-tuple-element.36, ...), kind=kOutput, calls=%fused_computation.62 | convolution fusion | flops 403832576 | bytes 2362368 | tf_op jit(solution)/shard_map/bphc,hcv->bphv/dot_general | solution.py:235
  122.5 1.2 fusion.94
  123.7 2.9 %add_select_fusion = f32[8,1,256,512]{3,2,0,1:T(8,128)S(1)} fusion(f32[8,1,256,512]{3,2,0,1:T(8,128)} %add_bitcast_fusion, f32[256,512]{1,0:T(8,128)S(1)} %fusion.94, f32[8,256]{1,0:T(8,128)S(1)} %copy-done.23, pred[8]{0:T(512)(128)(4,1)} %get-tuple-element.106, pred[8]{0:T(512)(128)(4,1)} %get-tuple-element.108), kind=kLoop, calls=%fused_computation.9 | loop fusion | flops 4194304 | bytes 8921104 | tf_op jit(solution)/shard_map/jit(_where)/select_n | solution.py:247
  126.6 2.6 %pad_maximum_fusion = f32[8,1,262,512]{3,2,0,1:T(8,128)} fusion(f32[8,1,6,512]{3,2,0,1:T(8,128)S(1)} %reshape.1341, f32[8,1,256,512]{3,2,0,1:T(8,128)S(1)} %add_select_fusion), kind=kLoop, calls=%fused_computation.7 | loop fusion | flops 1073152 | bytes 8585216 | tf_op jit(solution)/shard_map/concatenate | solution.py:249
  129.2 1.2 copy-done.2
  130.4 2.5 fusion.25
  132.9 1.7 convolution_convert_fusion
  134.6 1.8 reshape.1340
  136.4 3.0 %constant_dynamic-slice_fusion.3 = (bf16[256,1,512]{2,1,0:T(2,128)(2,1)}, bf16[256,1,512]{2,1,0:T(2,128)(2,1)S(1)}, bf16[256,1,512]{2,1,0:T(2,128)(2,1)S(1)}, bf16[256,1,512]{2,1,0:T(2,128)(2,1)S(1)}) fusion(bf16[256,4,512]{2,1,0:T(4,128)(2,1)S(1)} %reshape.1340, s32[]{:T(128)S(6)} %select_n.616, s32[]{:T(128)S(6)} %select_n.620, s32[]{:T(128)S(6)} %select_n.618, ...), kind=kLoop, calls=%fused_computation.173 | loop fusion | bytes 2097168 | tf_op jit(solution)/shard_map/jit(dynamic_index_in_dim)/dynamic_slice | solution.py:256
  140.2 1.6 collective-permute-start.6
  142.5 2.9 %collective-permute-start.7 = (bf16[256,512]{1,0:T(8,128)(2,1)}, bf16[256,512]{1,0:T(8,128)(2,1)}, u32[]{:S(2)}, u32[]{:S(2)}) collective-permute-start(bf16[256,512]{1,0:T(8,128)(2,1)} %bitcast.247), channel_id=1, source_target_pairs={{0,2},{1,3},{2,0},{3,1},{4,6},{5,7},{6,4},{7,5},{8,10},{9,11},{10,... | collective-permute-start | bytes 786440 | tf_op jit(solution)/shard_map/ppermute | solution.py:260
  146.1 1.3 collective-permute-start.8
  147.5 2.8 %convert_element_type.284 = f32[256,2048]{1,0:T(8,128)} convert(bf16[256,2048]{1,0:T(8,128)(2,1)} %param.14) | non-fusion elementwise | flops 524288 | bytes 3145728 | tf_op jit(solution)/shard_map/convert_element_type | solution.py:122
  150.4 4.2 %collective-permute-done.7 = bf16[256,512]{1,0:T(8,128)(2,1)} collective-permute-done((bf16[256,512]{1,0:T(8,128)(2,1)}, bf16[256,512]{1,0:T(8,128)(2,1)}, u32[]{:S(2)}, u32[]{:S(2)}) %collective-permute-start.7) | collective-permute-done | bytes 262176 | tf_op jit(solution)/shard_map/ppermute | solution.py:260
  154.7 1.3 pad_maximum_fusion.1
  156.0 1.2 fusion.22
  157.9 1.2 collective-permute-done.9
  159.2 1.0 collective-permute-start.10
  160.2 3.2 %collective-permute-done.10 = bf16[8,2048]{1,0:T(8,128)(2,1)S(1)} collective-permute-done((bf16[8,2048]{1,0:T(8,128)(2,1)S(1)}, bf16[8,2048]{1,0:T(8,128)(2,1)S(1)}, u32[]{:S(2)}, u32[]{:S(2)}) %collective-permute-start.10) | collective-permute-done | bytes 32800 | tf_op jit(solution)/shard_map/ppermute | solution.py:27
  163.4 1.2 collective-permute-start.11
  164.6 4.3 %collective-permute-done.11 = bf16[8,2048]{1,0:T(8,128)(2,1)S(1)} collective-permute-done((bf16[8,2048]{1,0:T(8,128)(2,1)S(1)}, bf16[8,2048]{1,0:T(8,128)(2,1)S(1)}, u32[]{:S(2)}, u32[]{:S(2)}) %collective-permute-start.11) | collective-permute-done | bytes 32800 | tf_op jit(solution)/shard_map/ppermute | solution.py:27
  168.9 2.3 collective-permute-start.12
  171.2 1.9 collective-permute-done.12
  173.2 3.6 %collective-permute-start.13 = (bf16[8,2048]{1,0:T(8,128)(2,1)S(1)}, bf16[8,2048]{1,0:T(8,128)(2,1)S(1)}, u32[]{:S(2)}, u32[]{:S(2)}) collective-permute-start(bf16[8,2048]{1,0:T(8,128)(2,1)S(1)} %add.513), channel_id=1, source_target_pairs={{0,64},{4,68},{8,72},{12,76},{16,80},{20,84},{24,88},{28,92},{32,9... | collective-permute-start | bytes 98312 | tf_op jit(solution)/shard_map/ppermute | solution.py:27
  176.8 1.9 collective-permute-done.13
  178.7 3.2 %collective-permute-start.14 = (bf16[8,2048]{1,0:T(8,128)(2,1)S(1)}, bf16[8,2048]{1,0:T(8,128)(2,1)S(1)}, u32[]{:S(2)}, u32[]{:S(2)}) collective-permute-start(bf16[8,2048]{1,0:T(8,128)(2,1)S(1)} %add.514), channel_id=1, source_target_pairs={{0,1},{1,0},{2,3},{3,2},{4,5},{5,4},{6,7},{7,6},{8,9},{9,8},{10,11... | collective-permute-start | bytes 98312 | tf_op jit(solution)/shard_map/ppermute | solution.py:27
  181.8 1.9 collective-permute-done.14
  183.8 2.3 collective-permute-start.15
  186.1 3.2 %collective-permute-done.15 = bf16[8,2048]{1,0:T(8,128)(2,1)S(1)} collective-permute-done((bf16[8,2048]{1,0:T(8,128)(2,1)S(1)}, bf16[8,2048]{1,0:T(8,128)(2,1)S(1)}, u32[]{:S(2)}, u32[]{:S(2)}) %collective-permute-start.15) | collective-permute-done | bytes 32800 | tf_op jit(solution)/shard_map/ppermute | solution.py:27
  189.9 1.0 convolution_reduce_fusion
  190.9 50.6 %all-reduce.2.cloned.1.call-done = f32[8,1,262,512]{3,2,0,1:T(8,128)} async-done(((f32[8,1,262,512]{3,2,0,1:T(8,128)}), f32[8,1,262,512]{3,2,0,1:T(8,128)}) %all-reduce.2.cloned.1.call-update) | async-done | bytes 4292624 | tf_op jit(solution)/shard_map/psum | solution.py:249
  241.5 0.9 slice.393
  243.2 4.6 %slice_bitcast_fusion = f32[8,1,256,512]{3,2,1,0:T(8,128)} fusion(f32[8,1,262,512]{3,2,0,1:T(8,128)} %all-reduce.2.cloned.1.call-done), kind=kLoop, calls=%fused_computation.8 | loop fusion | bytes 8388608
  (218 shorter events, 32.5 us)
Async XLA Ops:
  7.2 125.7 %copy-start = (bf16[512,2048]{1,0:T(8,128)(2,1)S(1)}, bf16[512,2048]{1,0:T(8,128)(2,1)}, u32[]{:S(2)}) copy-start(bf16[512,2048]{1,0:T(8,128)(2,1)} %param.23) | copy-start | bytes 6291460
  7.2 11.1 %copy-start.1 = (bf16[256,2048]{1,0:T(8,128)(2,1)S(1)}, bf16[256,2048]{1,0:T(8,128)(2,1)}, u32[]{:S(2)}) copy-start(bf16[256,2048]{1,0:T(8,128)(2,1)} %param.14) | copy-start | bytes 3145732
  7.2 11.1 %copy-start.47 = (f32[2048]{0:T(1024)S(1)}, f32[2048]{0:T(1024)}, u32[]{:S(2)}) copy-start(f32[2048]{0:T(1024)} %param.15) | copy-start | bytes 24580
  7.2 8.9 %copy-start.43 = (s32[8]{0:T(128)S(1)}, s32[8]{0:T(128)}, u32[]{:S(2)}) copy-start(s32[8]{0:T(128)} %param.26) | copy-start | bytes 100
  7.2 8.9 %copy-start.51 = (s32[8]{0:T(128)S(1)}, s32[8]{0:T(128)}, u32[]{:S(2)}) copy-start(s32[8]{0:T(128)} %param.27) | copy-start | bytes 100
  7.2 11.1 %copy-start.45 = (bf16[2048,16]{0,1:T(8,128)(2,1)S(1)}, bf16[2048,16]{0,1:T(8,128)(2,1)}, u32[]{:S(2)}) copy-start(bf16[2048,16]{0,1:T(8,128)(2,1)} %param.18) | copy-start | bytes 196612
  7.2 234.3 %all-reduce.2.cloned.1.call-start = ((), (), s32[]{:S(2)}) async-start(), calls=%async_computation | async-start | bytes 8650752 | tf_op jit(solution)/shard_map/psum | solution.py:249
  9.0 9.8 %copy-start.41 = (f32[256]{0:T(256)}, f32[256]{0:T(256)S(1)}, u32[]{:S(2)}) copy-start(f32[256]{0:T(256)S(1)} %add_rsqrt_fusion.1) | copy-start | bytes 3076
  9.0 9.8 %copy-start.46 = (bf16[16,256]{1,0:T(8,128)(2,1)S(1)}, bf16[16,256]{1,0:T(8,128)(2,1)}, u32[]{:S(2)}) copy-start(bf16[16,256]{1,0:T(8,128)(2,1)} %param.19) | copy-start | bytes 24580
  9.0 9.8 %copy-start.50 = (f32[256]{0:T(256)S(1)}, f32[256]{0:T(256)}, u32[]{:S(2)}) copy-start(f32[256]{0:T(256)} %param.20) | copy-start | bytes 3076
  9.0 16.6 %copy-start.26 = (f32[4,1024]{1,0:T(4,128)S(1)}, f32[4,1024]{1,0:T(4,128)}, u32[]{:S(2)}) copy-start(f32[4,1024]{1,0:T(4,128)} %param.17) | copy-start | bytes 49156
  14.2 36.8 %collective-permute-start = (bf16[3,1024]{1,0:T(4,128)(2,1)}, bf16[3,1024]{1,0:T(4,128)(2,1)}, u32[]{:S(2)}, u32[]{:S(2)}) collective-permute-start(bf16[3,1024]{1,0:T(4,128)(2,1)} %slice.346), channel_id=1, source_target_pairs={{0,4},{4,8},{8,12},{12,16},{16,20},{20,24},{24,28},{28,32},{32,36}... | collective-permute-start | bytes 18440 | tf_op jit(solution)/shard_map/ppermute | solution.py:19
  31.1 19.9 %copy-start.16 = (f32[64,256]{1,0:T(8,128)}, f32[64,256]{1,0:T(8,128)S(1)}, u32[]{:S(2)}) copy-start(f32[64,256]{1,0:T(8,128)S(1)} %get-tuple-element.135) | copy-start | bytes 196612
  31.1 19.9 %copy-start.18 = (f32[64,256]{1,0:T(8,128)}, f32[64,256]{1,0:T(8,128)S(1)}, u32[]{:S(2)}) copy-start(f32[64,256]{1,0:T(8,128)S(1)} %get-tuple-element.136) | copy-start | bytes 196612
  32.7 18.4 %copy-start.20 = (f32[8,256]{1,0:T(8,128)}, f32[8,256]{1,0:T(8,128)S(1)}, u32[]{:S(2)}) copy-start(f32[8,256]{1,0:T(8,128)S(1)} %gather_fusion.1) | copy-start | bytes 24580
  51.0 3.1 %copy-start.38 = (pred[4,64]{1,0:T(4,128)(4,1)S(1)}, pred[4,64]{1,0:T(4,128)(4,1)}, u32[]{:S(2)}) copy-start(pred[4,64]{1,0:T(4,128)(4,1)} %get-tuple-element.97) | copy-start | bytes 772
  52.3 2.5 copy-start.32
  52.3 2.5 copy-start.33
  52.3 2.5 copy-start.34
  53.9 3.8 %copy-start.3 = (bf16[256,1,1024]{2,0,1:T(8,128)(2,1)}, bf16[256,1,1024]{2,0,1:T(8,128)(2,1)S(1)}, u32[]{:S(2)}) copy-start(bf16[256,1,1024]{2,0,1:T(8,128)(2,1)S(1)} %fusion.33) | copy-start | bytes 1572868
  54.0 15.0 %copy-start.14 = (f32[256,1,256]{2,0,1:T(8,128)}, f32[256,1,256]{2,0,1:T(8,128)S(1)}, u32[]{:S(2)}) copy-start(f32[256,1,256]{2,0,1:T(8,128)S(1)} %get-tuple-element.63) | copy-start | bytes 786436
  54.0 3.7 %copy-start.4 = (bf16[256,1,512]{2,0,1:T(8,128)(2,1)}, bf16[256,1,512]{2,0,1:T(8,128)(2,1)S(1)}, u32[]{:S(2)}) copy-start(bf16[256,1,512]{2,0,1:T(8,128)(2,1)S(1)} %slice.353) | copy-start | bytes 786436
  54.1 7.8 %copy-start.17 = (f32[64,256]{1,0:T(8,128)S(1)}, f32[64,256]{1,0:T(8,128)}, u32[]{:S(2)}) copy-start(f32[64,256]{1,0:T(8,128)} %copy-done.16) | copy-start | bytes 196612
  54.1 7.8 %copy-start.19 = (f32[64,256]{1,0:T(8,128)S(1)}, f32[64,256]{1,0:T(8,128)}, u32[]{:S(2)}) copy-start(f32[64,256]{1,0:T(8,128)} %copy-done.18) | copy-start | bytes 196612
  54.1 7.8 %copy-start.21 = (f32[8,256]{1,0:T(8,128)S(1)}, f32[8,256]{1,0:T(8,128)}, u32[]{:S(2)}) copy-start(f32[8,256]{1,0:T(8,128)} %copy-done.20) | copy-start | bytes 24580
  54.1 7.8 %copy-start.27 = (pred[8]{0:T(512)(128)(4,1)S(1)}, pred[8]{0:T(512)(128)(4,1)}, u32[]{:S(2)}) copy-start(pred[8]{0:T(512)(128)(4,1)} %get-tuple-element.109) | copy-start | bytes 28
  54.1 7.8 %copy-start.30 = (pred[8]{0:T(512)(128)(4,1)S(1)}, pred[8]{0:T(512)(128)(4,1)}, u32[]{:S(2)}) copy-start(pred[8]{0:T(512)(128)(4,1)} %get-tuple-element.121) | copy-start | bytes 28
  54.1 7.8 %copy-start.31 = (pred[8]{0:T(512)(128)(4,1)S(1)}, pred[8]{0:T(512)(128)(4,1)}, u32[]{:S(2)}) copy-start(pred[8]{0:T(512)(128)(4,1)} %get-tuple-element.122) | copy-start | bytes 28
  57.7 7.8 %copy-start.11 = (f32[1,256,512]{2,1,0:T(8,128)}, f32[1,256,512]{2,1,0:T(8,128)S(1)}, u32[]{:S(2)}) copy-start(f32[1,256,512]{2,1,0:T(8,128)S(1)} %get-tuple-element.42) | copy-start | bytes 1572868
  57.7 7.8 %copy-start.12 = (f32[1,256,512]{2,1,0:T(8,128)}, f32[1,256,512]{2,1,0:T(8,128)S(1)}, u32[]{:S(2)}) copy-start(f32[1,256,512]{2,1,0:T(8,128)S(1)} %get-tuple-element.43) | copy-start | bytes 1572868
  57.7 7.8 %collective-permute-start.1 = (bf16[1,257,512]{2,1,0:T(8,128)(2,1)S(1)}, bf16[1,257,512]{2,1,0:T(8,128)(2,1)S(1)}, u32[]{:S(2)}, u32[]{:S(2)}) collective-permute-start(bf16[1,257,512]{2,1,0:T(8,128)(2,1)S(1)} %pad_maximum_fusion.3), channel_id=1, source_target_pairs={{0,4},{4,8},{8,12},{12,16},{16,20},{20,24},{24,28},{28,32},{32,36}... | collective-permute-start | bytes 789512 | tf_op jit(solution)/shard_map/ppermute | solution.py:19
  61.9 7.1 %copy-start.15 = (f32[4,64,1,256]{3,1,2,0:T(8,128)S(1)}, f32[4,64,1,256]{3,1,2,0:T(8,128)}, u32[]{:S(2)}) copy-start(f32[4,64,1,256]{3,1,2,0:T(8,128)} %copy.86) | copy-start | bytes 786436
  61.9 7.1 %copy-start.22 = (pred[4,64,64]{2,1,0:T(8,128)(4,1)S(1)}, pred[4,64,64]{2,1,0:T(8,128)(4,1)}, u32[]{:S(2)}) copy-start(pred[4,64,64]{2,1,0:T(8,128)(4,1)} %compare_and_fusion) | copy-start | bytes 49156
  66.4 11.9 %collective-permute-start.2 = (bf16[1,257,512]{2,1,0:T(8,128)(2,1)}, bf16[1,257,512]{2,1,0:T(8,128)(2,1)}, u32[]{:S(2)}, u32[]{:S(2)}) collective-permute-start(bf16[1,257,512]{2,1,0:T(8,128)(2,1)} %pad_maximum_fusion.4), channel_id=1, source_target_pairs={{0,4},{4,8},{8,12},{12,16},{16,20},{20,24},{24,28},{28,32},{32,36}... | collective-permute-start | bytes 789512 | tf_op jit(solution)/shard_map/ppermute | solution.py:19
  69.0 15.8 %copy-start.37 = (pred[8]{0:T(512)(128)(4,1)S(1)}, pred[8]{0:T(512)(128)(4,1)}, u32[]{:S(2)}) copy-start(pred[8]{0:T(512)(128)(4,1)} %get-tuple-element.100) | copy-start | bytes 28
  69.0 17.3 %copy-start.36 = (pred[8]{0:T(512)(128)(4,1)S(1)}, pred[8]{0:T(512)(128)(4,1)}, u32[]{:S(2)}) copy-start(pred[8]{0:T(512)(128)(4,1)} %get-tuple-element.98) | copy-start | bytes 28
  77.4 21.7 %copy-start.35 = (pred[8]{0:T(512)(128)(4,1)S(1)}, pred[8]{0:T(512)(128)(4,1)}, u32[]{:S(2)}) copy-start(pred[8]{0:T(512)(128)(4,1)} %get-tuple-element.99) | copy-start | bytes 28
  77.4 21.7 %copy-start.44 = (pred[4,64]{1,0:T(4,128)(4,1)S(1)}, pred[4,64]{1,0:T(4,128)(4,1)}, u32[]{:S(2)}) copy-start(pred[4,64]{1,0:T(4,128)(4,1)} %get-tuple-element.96) | copy-start | bytes 772
  77.4 21.7 %copy-start.52 = (f32[4]{0:T(128)S(1)}, f32[4]{0:T(128)}, u32[]{:S(2)}) copy-start(f32[4]{0:T(128)} %pad.33.clone) | copy-start | bytes 52
  80.8 9.4 %collective-permute-start.3 = (bf16[1,257,512]{2,1,0:T(8,128)(2,1)}, bf16[1,257,512]{2,1,0:T(8,128)(2,1)}, u32[]{:S(2)}, u32[]{:S(2)}) collective-permute-start(bf16[1,257,512]{2,1,0:T(8,128)(2,1)} %pad_maximum_fusion.5), channel_id=1, source_target_pairs={{0,8},{4,12},{8,16},{12,20},{16,24},{20,28},{24,32},{28,36},{32,40... | collective-permute-start | bytes 789512 | tf_op jit(solution)/shard_map/ppermute | solution.py:19
  91.0 24.7 %copy-start.24 = (f32[4,256]{1,0:T(4,128)S(1)}, f32[4,256]{1,0:T(4,128)}, u32[]{:S(2)}) copy-start(f32[4,256]{1,0:T(4,128)} %maximum_bitcast_fusion.6) | copy-start | bytes 12292
  92.2 23.5 %copy-start.9 = (f32[4,64,1,256]{3,1,2,0:T(8,128)S(1)}, f32[4,64,1,256]{3,1,2,0:T(8,128)}, u32[]{:S(2)}) copy-start(f32[4,64,1,256]{3,1,2,0:T(8,128)} %copy.57) | copy-start | bytes 786436
  92.2 24.5 %copy-start.5 = (bf16[256,1,512]{2,0,1:T(8,128)(2,1)S(1)}, bf16[256,1,512]{2,0,1:T(8,128)(2,1)}, u32[]{:S(2)}) copy-start(bf16[256,1,512]{2,0,1:T(8,128)(2,1)} %copy-done.4) | copy-start | bytes 786436
  92.3 13.3 %collective-permute-start.4 = (bf16[1,257,512]{2,1,0:T(8,128)(2,1)S(1)}, bf16[1,257,512]{2,1,0:T(8,128)(2,1)S(1)}, u32[]{:S(2)}, u32[]{:S(2)}) collective-permute-start(bf16[1,257,512]{2,1,0:T(8,128)(2,1)S(1)} %pad_maximum_fusion.6), channel_id=1, source_target_pairs={{0,16},{4,20},{8,24},{12,28},{16,32},{20,36},{24,40},{28,44},{32,4... | collective-permute-start | bytes 789512 | tf_op jit(solution)/shard_map/ppermute | solution.py:19
  102.9 20.8 %copy-start.23 = (f32[8,256]{1,0:T(8,128)S(1)}, f32[8,256]{1,0:T(8,128)}, u32[]{:S(2)}) copy-start(f32[8,256]{1,0:T(8,128)} %get-tuple-element.79) | copy-start | bytes 24580
  105.5 10.0 %copy-start.25 = (f32[1,256]{1,0:T(1,128)}, f32[1,256]{1,0:T(1,128)S(1)}, u32[]{:S(2)}) copy-start(f32[1,256]{1,0:T(1,128)S(1)} %get-tuple-element.34) | copy-start | bytes 3076
  107.1 12.6 %collective-permute-start.5 = (bf16[1,257,512]{2,1,0:T(8,128)(2,1)}, bf16[1,257,512]{2,1,0:T(8,128)(2,1)}, u32[]{:S(2)}, u32[]{:S(2)}) collective-permute-start(bf16[1,257,512]{2,1,0:T(8,128)(2,1)} %pad_maximum_fusion.7), channel_id=1, source_target_pairs={{0,32},{4,36},{8,40},{12,44},{16,48},{20,52},{24,56},{28,60},{32,6... | collective-permute-start | bytes 789512 | tf_op jit(solution)/shard_map/ppermute | solution.py:19
  129.1 1.2 copy-start.49
  136.4 13.9 %copy-start.40 = (s32[8]{0:T(128)S(1)}, s32[8]{0:T(128)}, u32[]{:S(2)}) copy-start(s32[8]{0:T(128)} %get-tuple-element.113) | copy-start | bytes 100
  139.4 10.9 %copy-start.7 = (bf16[256,1,512]{2,1,0:T(2,128)(2,1)S(1)}, bf16[256,1,512]{2,1,0:T(2,128)(2,1)}, u32[]{:S(2)}) copy-start(bf16[256,1,512]{2,1,0:T(2,128)(2,1)} %get-tuple-element.53) | copy-start | bytes 786436
  140.2 10.2 %collective-permute-start.6 = (bf16[256,512]{1,0:T(8,128)(2,1)}, bf16[256,512]{1,0:T(8,128)(2,1)}, u32[]{:S(2)}, u32[]{:S(2)}) collective-permute-start(bf16[256,512]{1,0:T(8,128)(2,1)} %bitcast.248), channel_id=1, source_target_pairs={{0,1},{1,2},{2,3},{3,0},{4,5},{5,6},{6,7},{7,4},{8,9},{9,10},{10,1... | collective-permute-start | bytes 786440 | tf_op jit(solution)/shard_map/ppermute | solution.py:260
  142.5 12.1 %collective-permute-start.7 = (bf16[256,512]{1,0:T(8,128)(2,1)}, bf16[256,512]{1,0:T(8,128)(2,1)}, u32[]{:S(2)}, u32[]{:S(2)}) collective-permute-start(bf16[256,512]{1,0:T(8,128)(2,1)} %bitcast.247), channel_id=1, source_target_pairs={{0,2},{1,3},{2,0},{3,1},{4,6},{5,7},{6,4},{7,5},{8,10},{9,11},{10,... | collective-permute-start | bytes 786440 | tf_op jit(solution)/shard_map/ppermute | solution.py:260
  146.1 11.7 %copy-start.29 = (pred[8]{0:T(512)(128)(4,1)S(1)}, pred[8]{0:T(512)(128)(4,1)}, u32[]{:S(2)}) copy-start(pred[8]{0:T(512)(128)(4,1)} %get-tuple-element.108) | copy-start | bytes 28
  146.1 8.6 %collective-permute-start.8 = (bf16[256,512]{1,0:T(8,128)(2,1)}, bf16[256,512]{1,0:T(8,128)(2,1)}, u32[]{:S(2)}, u32[]{:S(2)}) collective-permute-start(bf16[256,512]{1,0:T(8,128)(2,1)} %bitcast.246), channel_id=1, source_target_pairs={{0,3},{1,0},{2,1},{3,2},{4,7},{5,4},{6,5},{7,6},{8,11},{9,8},{10,9... | collective-permute-start | bytes 786440 | tf_op jit(solution)/shard_map/ppermute | solution.py:260
  147.5 42.4 %copy-start.28 = (f32[2048]{0:T(1024)S(1)}, f32[2048]{0:T(1024)}, u32[]{:S(2)}) copy-start(f32[2048]{0:T(1024)} %param.24) | copy-start | bytes 24580
  150.4 39.5 %copy-start.8 = (bf16[250,2048]{1,0:T(8,128)(2,1)S(1)}, bf16[250,2048]{1,0:T(8,128)(2,1)}, u32[]{:S(2)}) copy-start(bf16[250,2048]{1,0:T(8,128)(2,1)} %param.25) | copy-start | bytes 3072004
  157.2 33.7 %copy-start.13 = (bf16[256,512]{1,0:T(8,128)(2,1)}, bf16[256,512]{1,0:T(8,128)(2,1)S(1)}, u32[]{:S(2)}) copy-start(bf16[256,512]{1,0:T(8,128)(2,1)S(1)} %fusion.22) | copy-start | bytes 786436
  157.9 1.2 collective-permute-start.9
  159.2 4.2 %collective-permute-start.10 = (bf16[8,2048]{1,0:T(8,128)(2,1)S(1)}, bf16[8,2048]{1,0:T(8,128)(2,1)S(1)}, u32[]{:S(2)}, u32[]{:S(2)}) collective-permute-start(bf16[8,2048]{1,0:T(8,128)(2,1)S(1)} %add_dynamic-update-slice_fusion), channel_id=1, source_target_pairs={{0,8},{4,12},{8,0},{12,4},{16,24},{20,28},{24,16},{28,20},{32,40},... | collective-permute-start | bytes 98312 | tf_op jit(solution)/shard_map/ppermute | solution.py:27
  163.4 5.5 %collective-permute-start.11 = (bf16[8,2048]{1,0:T(8,128)(2,1)S(1)}, bf16[8,2048]{1,0:T(8,128)(2,1)S(1)}, u32[]{:S(2)}, u32[]{:S(2)}) collective-permute-start(bf16[8,2048]{1,0:T(8,128)(2,1)S(1)} %add.511), channel_id=1, source_target_pairs={{0,16},{4,20},{8,24},{12,28},{16,0},{20,4},{24,8},{28,12},{32,48},... | collective-permute-start | bytes 98312 | tf_op jit(solution)/shard_map/ppermute | solution.py:27
  168.9 4.2 %collective-permute-start.12 = (bf16[8,2048]{1,0:T(8,128)(2,1)S(1)}, bf16[8,2048]{1,0:T(8,128)(2,1)S(1)}, u32[]{:S(2)}, u32[]{:S(2)}) collective-permute-start(bf16[8,2048]{1,0:T(8,128)(2,1)S(1)} %add.512), channel_id=1, source_target_pairs={{0,32},{4,36},{8,40},{12,44},{16,48},{20,52},{24,56},{28,60},{32,0... | collective-permute-start | bytes 98312 | tf_op jit(solution)/shard_map/ppermute | solution.py:27
  173.2 5.5 %collective-permute-start.13 = (bf16[8,2048]{1,0:T(8,128)(2,1)S(1)}, bf16[8,2048]{1,0:T(8,128)(2,1)S(1)}, u32[]{:S(2)}, u32[]{:S(2)}) collective-permute-start(bf16[8,2048]{1,0:T(8,128)(2,1)S(1)} %add.513), channel_id=1, source_target_pairs={{0,64},{4,68},{8,72},{12,76},{16,80},{20,84},{24,88},{28,92},{32,9... | collective-permute-start | bytes 98312 | tf_op jit(solution)/shard_map/ppermute | solution.py:27
  178.7 5.1 %collective-permute-start.14 = (bf16[8,2048]{1,0:T(8,128)(2,1)S(1)}, bf16[8,2048]{1,0:T(8,128)(2,1)S(1)}, u32[]{:S(2)}, u32[]{:S(2)}) collective-permute-start(bf16[8,2048]{1,0:T(8,128)(2,1)S(1)} %add.514), channel_id=1, source_target_pairs={{0,1},{1,0},{2,3},{3,2},{4,5},{5,4},{6,7},{7,6},{8,9},{9,8},{10,11... | collective-permute-start | bytes 98312 | tf_op jit(solution)/shard_map/ppermute | solution.py:27
  183.8 5.5 %collective-permute-start.15 = (bf16[8,2048]{1,0:T(8,128)(2,1)S(1)}, bf16[8,2048]{1,0:T(8,128)(2,1)S(1)}, u32[]{:S(2)}, u32[]{:S(2)}) collective-permute-start(bf16[8,2048]{1,0:T(8,128)(2,1)S(1)} %add.515), channel_id=1, source_target_pairs={{0,2},{1,3},{2,0},{3,1},{4,6},{5,7},{6,4},{7,5},{8,10},{9,11},{10,... | collective-permute-start | bytes 98312 | tf_op jit(solution)/shard_map/ppermute | solution.py:27
  (6 other events, 5.7 us)
Sparse Core Ops, SparseCore 0:
  129.3 112.1 all-reduce.1

commit v11 on v7

--- a/solution.py
+++ b/solution.py
@@ -160,15 +160,30 @@
     segment_before = segment_all[KCONV - 2 : KCONV - 2 + row_count : BLOCK]
     cumulative = jnp.cumsum(decays.reshape(block_count, BLOCK, head_count, DK), axis=1)
     indices = jnp.arange(BLOCK)
-    causal = (indices[None, :] <= indices[:, None])[None] & (
-        block_segment[:, None, :] == block_segment[:, :, None]
-    )
-    allowed = causal[:, :, :, None, None]
-    spread = jnp.where(allowed, cumulative[:, :, None] - cumulative[:, None, :], 0.0)
-    weights = jnp.where(allowed, jnp.exp(spread), 0.0)
-    scores = jnp.sum(queries[:, :, None] * key_rows[:, None, :] * weights, axis=-1).astype(
-        jnp.bfloat16
-    )
+    half = BLOCK // 2
+
+    def score_part(rows, cols, diagonal):
+        allowed = block_segment[:, rows, None] == block_segment[:, None, cols]
+        if diagonal:
+            allowed = allowed & (indices[None, :half] <= indices[:half, None])[None]
+        allowed = allowed[:, :, :, None, None]
+        spread = jnp.where(
+            allowed, cumulative[:, rows][:, :, None] - cumulative[:, cols][:, None, :], 0.0
+        )
+        weights = jnp.where(allowed, jnp.exp(spread), 0.0)
+        return jnp.sum(
+            queries[:, rows][:, :, None] * key_rows[:, cols][:, None, :] * weights, axis=-1
+        )
+
+    first, second = slice(0, half), slice(half, BLOCK)
+    upper = score_part(first, first, True)
+    scores = jnp.concatenate(
+        [
+            jnp.concatenate([upper, jnp.zeros_like(upper)], axis=2),
+            jnp.concatenate([score_part(second, first, False), score_part(second, second, True)], axis=2),
+        ],
+        axis=1,
+    ).astype(jnp.bfloat16)
     inside = jnp.einsum("bpqh,bqhv->bphv", scores, values, preferred_element_type=jnp.float32)
 
     same_tail = (block_segment == block_segment[:, -1:])[:, :, None, None]

time: 239 us -> 264 us (1.10)
  other arithmetic: 41.6 us -> 57.7 us
  local copies, waits for them, and re-layouts: 33.7 us -> 39 us
    unnamed x137 -> x125, local copies, waits for them, and re-layouts: 13.7 us -> 11.9 us
  transfers between devices with their start and end apart: 17 -> 17, of which waited for: 12 -> 12; matrix products, arithmetic and copies ran while one was open for 24% -> 31% of each run, Pallas kernels for 0% -> 0%
where the time goes in v11:
time: 264 us; the launch traced here: 261 us
  waiting for transfers between devices  77.2 us (29%)
  other arithmetic  57.7 us (22%)
  starting transfers between devices  48.5 us (18%)
  local copies, waits for them, and re-layouts  39 us (15%)
  matrix products  22.6 us (9%)
  between operations  16.3 us (6%)
    psum x1, waiting for transfers between devices, shards(): payload = lax.psum(jnp.concatenate([end_states, edge_rows], axis=2), 'seq')  52.9 us
    ppermute x6, starting transfers between devices, passed_along(): return lax.ppermute(array, axis, pairs)  30.7 us
    ppermute x7, waiting for transfers between devices, butterfly_sum(): array = array + lax.ppermute(array, axis, pairs)  18.8 us
    unnamed x125, local copies, waits for them, and re-layouts  11.9 us
    ppermute x7, starting transfers between devices, butterfly_sum(): array = array + lax.ppermute(array, axis, pairs)  11.9 us
    reduce_sum x1, other arithmetic, score_part(): jnp.sum(queries[:, rows][:, :, None] * key_rows[:, cols][:, None, :] * we...  7.5 us
    gather x3, local copies, waits for them, and re-layouts, shards(): padded[jnp.clip(located - start_row + KCONV - 1, 0, row_count + KCONV - 2)]  7.25 us
    ppermute x3, starting transfers between devices, shards(): lax.ppermute(outgoing, 'tp', [(i, (i + shift) % tp_size) for i in range(t...  5.9 us
  transfers between devices with their start and end apart: 17, of which 12 were waited for; matrix products, arithmetic and copies ran while one was open for 31% of the time, Pallas kernels for 0%

profile of v11, /device:TPU:0, one launch (start us, length us, event | category | flops | bytes accessed | tf_op | source)
XLA Modules:
  0.0 261.2 jit_solution(18155113645150690747)
XLA Ops:
  7.3 1.7 multiply_reduce_fusion.3
  9.0 3.8 %convolution_convert_fusion.1 = bf16[256,1024]{1,0:T(8,128)(2,1)S(1)} fusion(bf16[2048,1024]{1,0:T(8,128)(2,1)} %param.16, f32[2048]{0:T(1024)} %param.15, f32[256]{0:T(256)S(1)} %add_rsqrt_fusion.1, bf16[256,2048]{1,0:T(8,128)(2,1)} %param.14), kind=kOutput, calls=%fused_computation.23 | convolution fusion | flops 1076101120 | bytes 5776384 | tf_op jit(solution)/shard_map/dot_general | solution.py:127
  14.3 1.9 collective-permute-start
  24.5 1.3 broadcast_compare_fusion.4
  34.8 1.3 pad_clamp_fusion.1
  36.1 1.8 multiply_select_fusion.1
  37.9 1.3 maximum_bitcast_fusion.8
  39.9 1.4 fusion.84
  41.2 1.2 pad_clamp_fusion.2
  42.5 1.5 compare_and_fusion
  43.9 1.3 maximum_bitcast_fusion.7
  45.3 1.3 fusion.115
  46.6 4.4 %select_compare_fusion = (pred[8]{0:T(512)(128)(4,1)}, pred[8]{0:T(512)(128)(4,1)}) fusion(s32[8]{0:T(128)S(1)} %gather_fusion, s32[]{:T(128)} %bitcast.92, s32[]{:T(128)} %bitcast.91, s32[]{:T(128)} %bitcast.90, s32[]{:T(128)} %bitcast.89, s32[8]{0:T(128)} %copy-done.42, s32[]{:T(128)} %bitcast.38), kind=kLoop, calls=%fused_computation.263 | loop fusion | flops 64 | bytes 100 | tf_op jit(solution)/shard_map/eq | solution.py:237
  53.0 2.0 pad_maximum_fusion.2
  55.0 1.6 fusion.33
  56.7 1.3 fusion.69
  58.1 3.4 %fusion.21 = (bf16[1,256,512]{2,1,0:T(8,128)(2,1)S(1)}, f32[1,256,512]{2,1,0:T(8,128)}, f32[1,256,512]{2,1,0:T(8,128)}, f32[256,512]{1,0:T(8,128)}, f32[1,1,256,512]{3,2,1,0:T(8,128)}) fusion(f32[4,256,512]{2,1,0:T(8,128)S(1)} %fusion.69, f32[256]{0:T(256)S(1)} %bitcast.326, pred[]{:T(512)} %bitcast.35, f32[256]{0:T(256)S(1)} %bitcast.327, pred[]{:T(512)} %bitcast.28, ...), kind=kLoop, calls=%fused_computation.52 | loop fusion | flops 1441792 | bytes 4460547 | tf_op jit(solution)/shard_map/convert_element_type | solution.py:36
  61.5 4.1 %collective-permute-start.1 = (bf16[1,257,512]{2,1,0:T(8,128)(2,1)S(1)}, bf16[1,257,512]{2,1,0:T(8,128)(2,1)S(1)}, u32[]{:S(2)}, u32[]{:S(2)}) collective-permute-start(bf16[1,257,512]{2,1,0:T(8,128)(2,1)S(1)} %pad_maximum_fusion.3), channel_id=1, source_target_pairs={{0,4},{4,8},{8,12},{12,16},{16,20},{20,24},{24,28},{28,32},{32,36}... | collective-permute-start | bytes 789512 | tf_op jit(solution)/shard_map/ppermute | solution.py:19
  66.4 2.4 gather_fusion.3
  68.9 7.5 %multiply_reduce_fusion.2 = (bf16[4,32,32]{2,1,0:T(8,128)(2,1)}, bf16[4,32,32]{2,1,0:T(8,128)(2,1)}, bf16[4,32,32]{2,1,0:T(8,128)(2,1)}) fusion(f32[4,32,256]{2,1,0:T(8,128)} %get-tuple-element.140, f32[4,32,256]{2,1,0:T(8,128)} %get-tuple-element.71, f32[4,32,256]{2,1,0:T(8,128)} %get-tuple-element.141, pred[4,32,32]{2,1,0:T(8,128)(4,1)} %get-tuple-element.90, ...), kind=kLoop, calls=%fused_computation.11 | loop fusion | flops 18862080 | bytes 823296 | tf_op jit(solution)/shard_map/reduce_sum | solution.py:174
  77.1 2.4 gather_fusion.2
  79.5 2.4 gather_fusion.4
  83.0 1.9 collective-permute-start.2
  86.7 8.3 %collective-permute-start.3 = (bf16[1,257,512]{2,1,0:T(8,128)(2,1)S(1)}, bf16[1,257,512]{2,1,0:T(8,128)(2,1)S(1)}, u32[]{:S(2)}, u32[]{:S(2)}) collective-permute-start(bf16[1,257,512]{2,1,0:T(8,128)(2,1)S(1)} %pad_maximum_fusion.5), channel_id=1, source_target_pairs={{0,8},{4,12},{8,16},{12,20},{16,24},{20,28},{24,32},{28,36},{32,40... | collective-permute-start | bytes 789512 | tf_op jit(solution)/shard_map/ppermute | solution.py:19
  95.7 1.7 slice_bitcast_fusion.8
  97.4 2.7 %collective-permute-done.3 = bf16[1,257,512]{2,1,0:T(8,128)(2,1)S(1)} collective-permute-done((bf16[1,257,512]{2,1,0:T(8,128)(2,1)S(1)}, bf16[1,257,512]{2,1,0:T(8,128)(2,1)S(1)}, u32[]{:S(2)}, u32[]{:S(2)}) %collective-permute-start.3) | collective-permute-done | bytes 263200 | tf_op jit(solution)/shard_map/ppermute | solution.py:19
  100.4 4.9 %collective-permute-start.4 = (bf16[1,257,512]{2,1,0:T(8,128)(2,1)S(1)}, bf16[1,257,512]{2,1,0:T(8,128)(2,1)S(1)}, u32[]{:S(2)}, u32[]{:S(2)}) collective-permute-start(bf16[1,257,512]{2,1,0:T(8,128)(2,1)S(1)} %pad_maximum_fusion.6), channel_id=1, source_target_pairs={{0,16},{4,20},{8,24},{12,28},{16,32},{20,36},{24,40},{28,44},{32,4... | collective-permute-start | bytes 789512 | tf_op jit(solution)/shard_map/ppermute | solution.py:19
  106.0 3.2 %fusion.11 = f32[4,1,512,64]{2,3,0,1:T(8,128)} fusion(f32[1,1,256,512]{3,2,1,0:T(8,128)S(1)} %bitcast.293, f32[1,1,256,512]{3,2,1,0:T(8,128)S(1)} %bitcast.296, f32[1,1,256,512]{3,2,1,0:T(8,128)S(1)} %copy-done.14, f32[4]{0:T(128)S(1)} %copy-done.56, f32[4,64,256]{2,1,0:T(8,128)} %bitcast.291, pred[4,64]{1,0:T(4,128)(4,1)S(1)} %copy-done.48, ...), kind=kOutput, calls=%fused_computation.32 | convolution fusion | flops 404422656 | bytes 2621712 | tf_op jit(solution)/shard_map/bphc,bhcv->bphv/dot_general | solution.py:208
  110.3 9.6 %collective-permute-start.5 = (bf16[1,257,512]{2,1,0:T(8,128)(2,1)}, bf16[1,257,512]{2,1,0:T(8,128)(2,1)}, u32[]{:S(2)}, u32[]{:S(2)}) collective-permute-start(bf16[1,257,512]{2,1,0:T(8,128)(2,1)} %pad_maximum_fusion.7), channel_id=1, source_target_pairs={{0,32},{4,36},{8,40},{12,44},{16,48},{20,52},{24,56},{28,60},{32,6... | collective-permute-start | bytes 789512 | tf_op jit(solution)/shard_map/ppermute | solution.py:19
  120.8 1.0 fusion.47
  121.8 1.3 fusion.9
  123.5 2.9 %multiply_reduce_fusion.4 = (f32[4,64]{1,0:T(4,128)S(1)}, f32[4,64,1,512]{3,1,0,2:T(8,128)}) fusion(f32[4,64,1,512]{3,1,0,2:T(8,128)S(1)} %fusion.9, f32[4,64,256]{2,1,0:T(8,128)S(1)} %bitcast.299, bf16[1,257,512]{2,1,0:T(8,128)(2,1)} %collective-permute-done.5, f32[256]{0:T(256)} %bitcast.321, bf16[1,257,512]{2,1,0:T(8,128)(2,1)} %copy-done.9, ...), kind=kOutput, calls=%fused_computation.68 | convolution fusion | flops 404750080 | bytes 2626560 | tf_op jit(solution)/shard_map/bphc,hcv->bphv/dot_general | solution.py:247
  127.0 1.4 rsqrt.29
  128.3 1.4 fusion.103
  129.8 3.9 %select_bitcast_fusion = f32[8,1,256,512]{3,2,0,1:T(8,128)S(1)} fusion(f32[256,512]{1,0:T(8,128)S(1)} %fusion.103, f32[8,256]{1,0:T(8,128)} %get-tuple-element.83, f32[256,512]{1,0:T(8,128)} %get-tuple-element.48, f32[256,512]{1,0:T(8,128)} %bitcast.295, f32[256,512]{1,0:T(8,128)S(1)} %bitcast.294, f32[8,256]{1,0:T(8,128)} %get-tuple-element.82, ...), kind=kOutput, calls=%fused_computation.8 | convolution fusion | flops 146931712 | bytes 7103024 | tf_op jit(solution)/shard_map/rjhc,rjhv->rhcv/dot_general | solution.py:236
  133.7 2.8 %pad_maximum_fusion = f32[8,1,262,512]{3,2,0,1:T(8,128)} fusion(f32[8,1,6,512]{3,2,0,1:T(8,128)S(1)} %reshape.1450, f32[8,1,256,512]{3,2,0,1:T(8,128)S(1)} %select_bitcast_fusion), kind=kLoop, calls=%fused_computation.6 | loop fusion | flops 1073152 | bytes 8585216 | tf_op jit(solution)/shard_map/concatenate | solution.py:261
  136.5 1.2 copy-done.2
  137.7 2.5 fusion.25
  140.2 1.7 convolution_convert_fusion
  142.0 1.8 reshape.1449
  143.8 3.0 %constant_dynamic-slice_fusion.3 = (bf16[256,1,512]{2,1,0:T(2,128)(2,1)}, bf16[256,1,512]{2,1,0:T(2,128)(2,1)S(1)}, bf16[256,1,512]{2,1,0:T(2,128)(2,1)S(1)}, bf16[256,1,512]{2,1,0:T(2,128)(2,1)S(1)}) fusion(bf16[256,4,512]{2,1,0:T(4,128)(2,1)S(1)} %reshape.1449, s32[]{:T(128)S(6)} %select_n.632, s32[]{:T(128)S(6)} %select_n.636, s32[]{:T(128)S(6)} %select_n.634, ...), kind=kLoop, calls=%fused_computation.192 | loop fusion | bytes 2097168 | tf_op jit(solution)/shard_map/jit(dynamic_index_in_dim)/dynamic_slice | solution.py:268
  146.8 1.6 collective-permute-start.6
  149.2 2.9 %collective-permute-start.7 = (bf16[256,512]{1,0:T(8,128)(2,1)}, bf16[256,512]{1,0:T(8,128)(2,1)}, u32[]{:S(2)}, u32[]{:S(2)}) collective-permute-start(bf16[256,512]{1,0:T(8,128)(2,1)} %bitcast.280), channel_id=1, source_target_pairs={{0,2},{1,3},{2,0},{3,1},{4,6},{5,7},{6,4},{7,5},{8,10},{9,11},{10,... | collective-permute-start | bytes 786440 | tf_op jit(solution)/shard_map/ppermute | solution.py:272
  152.9 1.3 collective-permute-start.8
  154.2 2.8 %convert_element_type.280 = f32[256,2048]{1,0:T(8,128)} convert(bf16[256,2048]{1,0:T(8,128)(2,1)} %param.14) | non-fusion elementwise | flops 524288 | bytes 3145728 | tf_op jit(solution)/shard_map/convert_element_type | solution.py:121
  157.1 1.5 collective-permute-done.7
  158.6 0.9 collective-permute-done.8
  159.5 1.3 pad_maximum_fusion.1
  160.8 1.2 fusion.22
  162.8 1.2 collective-permute-done.9
  164.1 3.9 %collective-permute-done.10 = bf16[8,2048]{1,0:T(8,128)(2,1)S(1)} collective-permute-done((bf16[8,2048]{1,0:T(8,128)(2,1)S(1)}, bf16[8,2048]{1,0:T(8,128)(2,1)S(1)}, u32[]{:S(2)}, u32[]{:S(2)}) %collective-permute-start.10) | collective-permute-done | bytes 32800 | tf_op jit(solution)/shard_map/ppermute | solution.py:27
  168.1 5.4 %collective-permute-done.11 = bf16[8,2048]{1,0:T(8,128)(2,1)S(1)} collective-permute-done((bf16[8,2048]{1,0:T(8,128)(2,1)S(1)}, bf16[8,2048]{1,0:T(8,128)(2,1)S(1)}, u32[]{:S(2)}, u32[]{:S(2)}) %collective-permute-start.11) | collective-permute-done | bytes 32800 | tf_op jit(solution)/shard_map/ppermute | solution.py:27
  173.5 2.9 %collective-permute-start.12 = (bf16[8,2048]{1,0:T(8,128)(2,1)S(1)}, bf16[8,2048]{1,0:T(8,128)(2,1)S(1)}, u32[]{:S(2)}, u32[]{:S(2)}) collective-permute-start(bf16[8,2048]{1,0:T(8,128)(2,1)S(1)} %add.512), channel_id=1, source_target_pairs={{0,32},{4,36},{8,40},{12,44},{16,48},{20,52},{24,56},{28,60},{32,0... | collective-permute-start | bytes 98312 | tf_op jit(solution)/shard_map/ppermute | solution.py:27
  176.3 1.9 collective-permute-done.12
  178.3 3.7 %collective-permute-start.13 = (bf16[8,2048]{1,0:T(8,128)(2,1)S(1)}, bf16[8,2048]{1,0:T(8,128)(2,1)S(1)}, u32[]{:S(2)}, u32[]{:S(2)}) collective-permute-start(bf16[8,2048]{1,0:T(8,128)(2,1)S(1)} %add.513), channel_id=1, source_target_pairs={{0,64},{4,68},{8,72},{12,76},{16,80},{20,84},{24,88},{28,92},{32,9... | collective-permute-start | bytes 98312 | tf_op jit(solution)/shard_map/ppermute | solution.py:27
  181.9 1.9 collective-permute-done.13
  183.9 2.2 collective-permute-start.14
  186.1 2.0 collective-permute-done.14
  188.0 3.0 %collective-permute-start.15 = (bf16[8,2048]{1,0:T(8,128)(2,1)S(1)}, bf16[8,2048]{1,0:T(8,128)(2,1)S(1)}, u32[]{:S(2)}, u32[]{:S(2)}) collective-permute-start(bf16[8,2048]{1,0:T(8,128)(2,1)S(1)} %add.515), channel_id=1, source_target_pairs={{0,2},{1,3},{2,0},{3,1},{4,6},{5,7},{6,4},{7,5},{8,10},{9,11},{10,... | collective-permute-start | bytes 98312 | tf_op jit(solution)/shard_map/ppermute | solution.py:27
  191.0 2.5 collective-permute-done.15
  194.2 1.0 convolution_reduce_fusion
  195.2 52.9 %all-reduce.3.cloned.1.call-done = f32[8,1,262,512]{3,2,0,1:T(8,128)} async-done(((f32[8,1,262,512]{3,2,0,1:T(8,128)}), f32[8,1,262,512]{3,2,0,1:T(8,128)}) %all-reduce.3.cloned.1.call-update) | async-done | bytes 4292624 | tf_op jit(solution)/shard_map/psum | solution.py:261
  248.1 0.9 slice.450
  249.8 4.6 %slice_bitcast_fusion = f32[8,1,256,512]{3,2,1,0:T(8,128)} fusion(f32[8,1,262,512]{3,2,0,1:T(8,128)} %all-reduce.3.cloned.1.call-done), kind=kLoop, calls=%fused_computation.7 | loop fusion | bytes 8388608
  (230 shorter events, 32.9 us)
Async XLA Ops:
  7.2 133.1 %copy-start = (bf16[512,2048]{1,0:T(8,128)(2,1)S(1)}, bf16[512,2048]{1,0:T(8,128)(2,1)}, u32[]{:S(2)}) copy-start(bf16[512,2048]{1,0:T(8,128)(2,1)} %param.23) | copy-start | bytes 6291460
  7.2 11.8 %copy-start.1 = (bf16[256,2048]{1,0:T(8,128)(2,1)S(1)}, bf16[256,2048]{1,0:T(8,128)(2,1)}, u32[]{:S(2)}) copy-start(bf16[256,2048]{1,0:T(8,128)(2,1)} %param.14) | copy-start | bytes 3145732
  7.2 11.8 %copy-start.51 = (f32[2048]{0:T(1024)S(1)}, f32[2048]{0:T(1024)}, u32[]{:S(2)}) copy-start(f32[2048]{0:T(1024)} %param.15) | copy-start | bytes 24580
  7.2 8.9 %copy-start.47 = (s32[8]{0:T(128)S(1)}, s32[8]{0:T(128)}, u32[]{:S(2)}) copy-start(s32[8]{0:T(128)} %param.26) | copy-start | bytes 100
  7.2 8.9 %copy-start.55 = (s32[8]{0:T(128)S(1)}, s32[8]{0:T(128)}, u32[]{:S(2)}) copy-start(s32[8]{0:T(128)} %param.27) | copy-start | bytes 100
  7.2 11.8 %copy-start.49 = (bf16[2048,16]{0,1:T(8,128)(2,1)S(1)}, bf16[2048,16]{0,1:T(8,128)(2,1)}, u32[]{:S(2)}) copy-start(bf16[2048,16]{0,1:T(8,128)(2,1)} %param.18) | copy-start | bytes 196612
  7.2 240.8 %all-reduce.3.cloned.1.call-start = ((), (), s32[]{:S(2)}) async-start(), calls=%async_computation | async-start | bytes 8650752 | tf_op jit(solution)/shard_map/psum | solution.py:261
  9.0 10.5 %copy-start.45 = (f32[256]{0:T(256)}, f32[256]{0:T(256)S(1)}, u32[]{:S(2)}) copy-start(f32[256]{0:T(256)S(1)} %add_rsqrt_fusion.1) | copy-start | bytes 3076
  9.0 10.5 %copy-start.50 = (bf16[16,256]{1,0:T(8,128)(2,1)S(1)}, bf16[16,256]{1,0:T(8,128)(2,1)}, u32[]{:S(2)}) copy-start(bf16[16,256]{1,0:T(8,128)(2,1)} %param.19) | copy-start | bytes 24580
  9.0 10.5 %copy-start.54 = (f32[256]{0:T(256)S(1)}, f32[256]{0:T(256)}, u32[]{:S(2)}) copy-start(f32[256]{0:T(256)} %param.20) | copy-start | bytes 3076
  13.6 12.2 %copy-start.29 = (f32[4,1024]{1,0:T(4,128)S(1)}, f32[4,1024]{1,0:T(4,128)}, u32[]{:S(2)}) copy-start(f32[4,1024]{1,0:T(4,128)} %param.17) | copy-start | bytes 49156
  14.3 38.8 %collective-permute-start = (bf16[3,1024]{1,0:T(4,128)(2,1)}, bf16[3,1024]{1,0:T(4,128)(2,1)}, u32[]{:S(2)}, u32[]{:S(2)}) collective-permute-start(bf16[3,1024]{1,0:T(4,128)(2,1)} %slice.397), channel_id=1, source_target_pairs={{0,4},{4,8},{8,12},{12,16},{16,20},{20,24},{24,28},{28,32},{32,36}... | collective-permute-start | bytes 18440 | tf_op jit(solution)/shard_map/ppermute | solution.py:19
  29.6 2.4 copy-start.28
  31.9 1.5 copy-start.30
  33.4 23.2 %copy-start.25 = (f32[8,256]{1,0:T(8,128)}, f32[8,256]{1,0:T(8,128)S(1)}, u32[]{:S(2)}) copy-start(f32[8,256]{1,0:T(8,128)S(1)} %gather_fusion.1) | copy-start | bytes 24580
  55.0 3.0 %copy-start.37 = (f32[1,1,1,256]{3,2,1,0:T(1,128)S(1)}, f32[1,1,1,256]{3,2,1,0:T(1,128)}, u32[]{:S(2)}) copy-start(f32[1,1,1,256]{3,2,1,0:T(1,128)} %get-tuple-element.85) | copy-start | bytes 3076
  55.0 3.0 %copy-start.38 = (f32[1,1,1,256]{3,2,1,0:T(1,128)S(1)}, f32[1,1,1,256]{3,2,1,0:T(1,128)}, u32[]{:S(2)}) copy-start(f32[1,1,1,256]{3,2,1,0:T(1,128)} %get-tuple-element.86) | copy-start | bytes 3076
  55.0 3.0 %copy-start.39 = (f32[1,1,1,256]{3,2,1,0:T(1,128)S(1)}, f32[1,1,1,256]{3,2,1,0:T(1,128)}, u32[]{:S(2)}) copy-start(f32[1,1,1,256]{3,2,1,0:T(1,128)} %get-tuple-element.87) | copy-start | bytes 3076
  55.0 3.1 %copy-start.40 = (f32[256]{0:T(256)S(1)}, f32[256]{0:T(256)}, u32[]{:S(2)}) copy-start(f32[256]{0:T(256)} %multiply_select_fusion.1) | copy-start | bytes 3076
  56.6 4.8 %copy-start.3 = (bf16[256,1,1024]{2,0,1:T(8,128)(2,1)}, bf16[256,1,1024]{2,0,1:T(8,128)(2,1)S(1)}, u32[]{:S(2)}) copy-start(bf16[256,1,1024]{2,0,1:T(8,128)(2,1)S(1)} %fusion.33) | copy-start | bytes 1572868
  56.7 4.8 %copy-start.33 = (bf16[1,1,512]{2,1,0:T(2,128)(2,1)S(1)}, bf16[1,1,512]{2,1,0:T(2,128)(2,1)}, u32[]{:S(2)}) copy-start(bf16[1,1,512]{2,1,0:T(2,128)(2,1)} %maximum_bitcast_fusion.8) | copy-start | bytes 3076
  56.7 8.9 %copy-start.8 = (f32[256,1,256]{2,0,1:T(8,128)}, f32[256,1,256]{2,0,1:T(8,128)S(1)}, u32[]{:S(2)}) copy-start(f32[256,1,256]{2,0,1:T(8,128)S(1)} %get-tuple-element.60) | copy-start | bytes 786436
  61.5 21.3 %collective-permute-start.1 = (bf16[1,257,512]{2,1,0:T(8,128)(2,1)S(1)}, bf16[1,257,512]{2,1,0:T(8,128)(2,1)S(1)}, u32[]{:S(2)}, u32[]{:S(2)}) collective-permute-start(bf16[1,257,512]{2,1,0:T(8,128)(2,1)S(1)} %pad_maximum_fusion.3), channel_id=1, source_target_pairs={{0,4},{4,8},{8,12},{12,16},{16,20},{20,24},{24,28},{28,32},{32,36}... | collective-permute-start | bytes 789512 | tf_op jit(solution)/shard_map/ppermute | solution.py:19
  68.9 7.5 %copy-start.20 = (bf16[8,1024]{1,0:T(8,128)(2,1)S(1)}, bf16[8,1024]{1,0:T(8,128)(2,1)}, u32[]{:S(2)}) copy-start(bf16[8,1024]{1,0:T(8,128)(2,1)} %gather_fusion.3) | copy-start | bytes 49156
  68.9 7.5 %copy-start.41 = (pred[8]{0:T(512)(128)(4,1)S(1)}, pred[8]{0:T(512)(128)(4,1)}, u32[]{:S(2)}) copy-start(pred[8]{0:T(512)(128)(4,1)} %get-tuple-element.122) | copy-start | bytes 28
  81.9 23.4 %copy-start.26 = (bf16[4,32,32]{2,1,0:T(8,128)(2,1)S(1)}, bf16[4,32,32]{2,1,0:T(8,128)(2,1)}, u32[]{:S(2)}) copy-start(bf16[4,32,32]{2,1,0:T(8,128)(2,1)} %get-tuple-element.25) | copy-start | bytes 24580
  81.9 24.0 %copy-start.11 = (f32[1,256,512]{2,1,0:T(8,128)S(1)}, f32[1,256,512]{2,1,0:T(8,128)}, u32[]{:S(2)}) copy-start(f32[1,256,512]{2,1,0:T(8,128)} %get-tuple-element.43) | copy-start | bytes 1572868
  81.9 24.0 %copy-start.13 = (f32[1,256,512]{2,1,0:T(8,128)S(1)}, f32[1,256,512]{2,1,0:T(8,128)}, u32[]{:S(2)}) copy-start(f32[1,256,512]{2,1,0:T(8,128)} %get-tuple-element.44) | copy-start | bytes 1572868
  81.9 24.0 %copy-start.14 = (f32[1,1,256,512]{3,2,1,0:T(8,128)S(1)}, f32[1,1,256,512]{3,2,1,0:T(8,128)}, u32[]{:S(2)}) copy-start(f32[1,1,256,512]{3,2,1,0:T(8,128)} %get-tuple-element.49) | copy-start | bytes 1572868
  81.9 24.0 %copy-start.48 = (pred[4,64]{1,0:T(4,128)(4,1)S(1)}, pred[4,64]{1,0:T(4,128)(4,1)}, u32[]{:S(2)}) copy-start(pred[4,64]{1,0:T(4,128)(4,1)} %get-tuple-element.104) | copy-start | bytes 772
  81.9 24.0 %copy-start.56 = (f32[4]{0:T(128)S(1)}, f32[4]{0:T(128)}, u32[]{:S(2)}) copy-start(f32[4]{0:T(128)} %pad.35.clone) | copy-start | bytes 52
  82.9 26.4 %copy-start.21 = (f32[1,256]{1,0:T(1,128)}, f32[1,256]{1,0:T(1,128)S(1)}, u32[]{:S(2)}) copy-start(f32[1,256]{1,0:T(1,128)S(1)} %get-tuple-element.41) | copy-start | bytes 3076
  83.0 3.4 %collective-permute-start.2 = (bf16[1,257,512]{2,1,0:T(8,128)(2,1)S(1)}, bf16[1,257,512]{2,1,0:T(8,128)(2,1)S(1)}, u32[]{:S(2)}, u32[]{:S(2)}) collective-permute-start(bf16[1,257,512]{2,1,0:T(8,128)(2,1)S(1)} %pad_maximum_fusion.4), channel_id=1, source_target_pairs={{0,4},{4,8},{8,12},{12,16},{16,20},{20,24},{24,28},{28,32},{32,36}... | collective-permute-start | bytes 789512 | tf_op jit(solution)/shard_map/ppermute | solution.py:19
  86.4 23.2 %copy-start.22 = (f32[1,256]{1,0:T(1,128)}, f32[1,256]{1,0:T(1,128)S(1)}, u32[]{:S(2)}) copy-start(f32[1,256]{1,0:T(1,128)S(1)} %get-tuple-element.39) | copy-start | bytes 3076
  86.6 33.3 %copy-start.23 = (bf16[4,32,32]{2,1,0:T(8,128)(2,1)S(1)}, bf16[4,32,32]{2,1,0:T(8,128)(2,1)}, u32[]{:S(2)}) copy-start(bf16[4,32,32]{2,1,0:T(8,128)(2,1)} %get-tuple-element.26) | copy-start | bytes 24580
  86.6 33.3 %copy-start.24 = (bf16[4,32,32]{2,1,0:T(8,128)(2,1)S(1)}, bf16[4,32,32]{2,1,0:T(8,128)(2,1)}, u32[]{:S(2)}) copy-start(bf16[4,32,32]{2,1,0:T(8,128)(2,1)} %get-tuple-element.27) | copy-start | bytes 24580
  86.7 13.4 %collective-permute-start.3 = (bf16[1,257,512]{2,1,0:T(8,128)(2,1)S(1)}, bf16[1,257,512]{2,1,0:T(8,128)(2,1)S(1)}, u32[]{:S(2)}, u32[]{:S(2)}) collective-permute-start(bf16[1,257,512]{2,1,0:T(8,128)(2,1)S(1)} %pad_maximum_fusion.5), channel_id=1, source_target_pairs={{0,8},{4,12},{8,16},{12,20},{16,24},{20,28},{24,32},{28,36},{32,40... | collective-permute-start | bytes 789512 | tf_op jit(solution)/shard_map/ppermute | solution.py:19
  95.7 25.1 %copy-start.7 = (f32[4,64,1,256]{3,1,2,0:T(8,128)S(1)}, f32[4,64,1,256]{3,1,2,0:T(8,128)}, u32[]{:S(2)}) copy-start(f32[4,64,1,256]{3,1,2,0:T(8,128)} %copy.57) | copy-start | bytes 786436
  100.1 9.2 %copy-start.4 = (bf16[1,257,512]{2,1,0:T(8,128)(2,1)}, bf16[1,257,512]{2,1,0:T(8,128)(2,1)S(1)}, u32[]{:S(2)}) copy-start(bf16[1,257,512]{2,1,0:T(8,128)(2,1)S(1)} %collective-permute-done.3) | copy-start | bytes 789508
  100.1 20.5 %copy-start.27 = (f32[1,256]{1,0:T(1,128)}, f32[1,256]{1,0:T(1,128)S(1)}, u32[]{:S(2)}) copy-start(f32[1,256]{1,0:T(1,128)S(1)} %get-tuple-element.37) | copy-start | bytes 3076
  100.4 8.8 %collective-permute-start.4 = (bf16[1,257,512]{2,1,0:T(8,128)(2,1)S(1)}, bf16[1,257,512]{2,1,0:T(8,128)(2,1)S(1)}, u32[]{:S(2)}, u32[]{:S(2)}) collective-permute-start(bf16[1,257,512]{2,1,0:T(8,128)(2,1)S(1)} %pad_maximum_fusion.6), channel_id=1, source_target_pairs={{0,16},{4,20},{8,24},{12,28},{16,32},{20,36},{24,40},{28,44},{32,4... | collective-permute-start | bytes 789512 | tf_op jit(solution)/shard_map/ppermute | solution.py:19
  109.3 11.4 %copy-start.31 = (f32[1,256]{1,0:T(1,128)}, f32[1,256]{1,0:T(1,128)S(1)}, u32[]{:S(2)}) copy-start(f32[1,256]{1,0:T(1,128)S(1)} %get-tuple-element.35) | copy-start | bytes 3076
  110.3 13.2 %collective-permute-start.5 = (bf16[1,257,512]{2,1,0:T(8,128)(2,1)}, bf16[1,257,512]{2,1,0:T(8,128)(2,1)}, u32[]{:S(2)}, u32[]{:S(2)}) collective-permute-start(bf16[1,257,512]{2,1,0:T(8,128)(2,1)} %pad_maximum_fusion.7), channel_id=1, source_target_pairs={{0,32},{4,36},{8,40},{12,44},{16,48},{20,52},{24,56},{28,60},{32,6... | collective-permute-start | bytes 789512 | tf_op jit(solution)/shard_map/ppermute | solution.py:19
  120.8 9.0 %copy-start.17 = (f32[64,256]{1,0:T(8,128)S(1)}, f32[64,256]{1,0:T(8,128)}, u32[]{:S(2)}) copy-start(f32[64,256]{1,0:T(8,128)} %copy-done.16) | copy-start | bytes 196612
  120.8 9.0 %copy-start.19 = (f32[64,256]{1,0:T(8,128)S(1)}, f32[64,256]{1,0:T(8,128)}, u32[]{:S(2)}) copy-start(f32[64,256]{1,0:T(8,128)} %copy-done.18) | copy-start | bytes 196612
  123.1 6.6 %copy-start.12 = (f32[1,256,512]{2,1,0:T(8,128)S(1)}, f32[1,256,512]{2,1,0:T(8,128)}, u32[]{:S(2)}) copy-start(f32[1,256,512]{2,1,0:T(8,128)} %get-tuple-element.43) | copy-start | bytes 1572868
  136.5 1.2 copy-start.46
  136.5 1.2 copy-start.52
  143.8 13.2 %copy-start.43 = (s32[8]{0:T(128)S(1)}, s32[8]{0:T(128)}, u32[]{:S(2)}) copy-start(s32[8]{0:T(128)} %get-tuple-element.127) | copy-start | bytes 100
  146.8 10.3 %copy-start.5 = (bf16[256,1,512]{2,1,0:T(2,128)(2,1)S(1)}, bf16[256,1,512]{2,1,0:T(2,128)(2,1)}, u32[]{:S(2)}) copy-start(bf16[256,1,512]{2,1,0:T(2,128)(2,1)} %get-tuple-element.50) | copy-start | bytes 786436
  146.8 10.3 %collective-permute-start.6 = (bf16[256,512]{1,0:T(8,128)(2,1)S(1)}, bf16[256,512]{1,0:T(8,128)(2,1)}, u32[]{:S(2)}, u32[]{:S(2)}) collective-permute-start(bf16[256,512]{1,0:T(8,128)(2,1)S(1)} %bitcast.297), channel_id=1, source_target_pairs={{0,1},{1,2},{2,3},{3,0},{4,5},{5,6},{6,7},{7,4},{8,9},{9,10},{10,1... | collective-permute-start | bytes 786440 | tf_op jit(solution)/shard_map/ppermute | solution.py:272
  149.2 9.4 %collective-permute-start.7 = (bf16[256,512]{1,0:T(8,128)(2,1)}, bf16[256,512]{1,0:T(8,128)(2,1)}, u32[]{:S(2)}, u32[]{:S(2)}) collective-permute-start(bf16[256,512]{1,0:T(8,128)(2,1)} %bitcast.280), channel_id=1, source_target_pairs={{0,2},{1,3},{2,0},{3,1},{4,6},{5,7},{6,4},{7,5},{8,10},{9,11},{10,... | collective-permute-start | bytes 786440 | tf_op jit(solution)/shard_map/ppermute | solution.py:272
  152.9 9.8 %copy-start.36 = (pred[8]{0:T(512)(128)(4,1)S(1)}, pred[8]{0:T(512)(128)(4,1)}, u32[]{:S(2)}) copy-start(pred[8]{0:T(512)(128)(4,1)} %get-tuple-element.111) | copy-start | bytes 28
  152.9 6.7 %collective-permute-start.8 = (bf16[256,512]{1,0:T(8,128)(2,1)}, bf16[256,512]{1,0:T(8,128)(2,1)}, u32[]{:S(2)}, u32[]{:S(2)}) collective-permute-start(bf16[256,512]{1,0:T(8,128)(2,1)} %bitcast.279), channel_id=1, source_target_pairs={{0,3},{1,0},{2,1},{3,2},{4,7},{5,4},{6,5},{7,6},{8,11},{9,8},{10,9... | collective-permute-start | bytes 786440 | tf_op jit(solution)/shard_map/ppermute | solution.py:272
  154.2 40.0 %copy-start.32 = (f32[2048]{0:T(1024)S(1)}, f32[2048]{0:T(1024)}, u32[]{:S(2)}) copy-start(f32[2048]{0:T(1024)} %param.24) | copy-start | bytes 24580
  157.1 37.1 %copy-start.6 = (bf16[250,2048]{1,0:T(8,128)(2,1)S(1)}, bf16[250,2048]{1,0:T(8,128)(2,1)}, u32[]{:S(2)}) copy-start(bf16[250,2048]{1,0:T(8,128)(2,1)} %param.25) | copy-start | bytes 3072004
  162.0 92.3 %copy-start.15 = (bf16[256,512]{1,0:T(8,128)(2,1)}, bf16[256,512]{1,0:T(8,128)(2,1)S(1)}, u32[]{:S(2)}) copy-start(bf16[256,512]{1,0:T(8,128)(2,1)S(1)} %fusion.22) | copy-start | bytes 786436
  162.7 1.2 collective-permute-start.9
  164.0 3.9 %collective-permute-start.10 = (bf16[8,2048]{1,0:T(8,128)(2,1)S(1)}, bf16[8,2048]{1,0:T(8,128)(2,1)S(1)}, u32[]{:S(2)}, u32[]{:S(2)}) collective-permute-start(bf16[8,2048]{1,0:T(8,128)(2,1)S(1)} %add_dynamic-update-slice_fusion), channel_id=1, source_target_pairs={{0,8},{4,12},{8,0},{12,4},{16,24},{20,28},{24,16},{28,20},{32,40},... | collective-permute-start | bytes 98312 | tf_op jit(solution)/shard_map/ppermute | solution.py:27
  168.0 5.5 %collective-permute-start.11 = (bf16[8,2048]{1,0:T(8,128)(2,1)S(1)}, bf16[8,2048]{1,0:T(8,128)(2,1)S(1)}, u32[]{:S(2)}, u32[]{:S(2)}) collective-permute-start(bf16[8,2048]{1,0:T(8,128)(2,1)S(1)} %add.511), channel_id=1, source_target_pairs={{0,16},{4,20},{8,24},{12,28},{16,0},{20,4},{24,8},{28,12},{32,48},... | collective-permute-start | bytes 98312 | tf_op jit(solution)/shard_map/ppermute | solution.py:27
  173.5 4.7 %collective-permute-start.12 = (bf16[8,2048]{1,0:T(8,128)(2,1)S(1)}, bf16[8,2048]{1,0:T(8,128)(2,1)S(1)}, u32[]{:S(2)}, u32[]{:S(2)}) collective-permute-start(bf16[8,2048]{1,0:T(8,128)(2,1)S(1)} %add.512), channel_id=1, source_target_pairs={{0,32},{4,36},{8,40},{12,44},{16,48},{20,52},{24,56},{28,60},{32,0... | collective-permute-start | bytes 98312 | tf_op jit(solution)/shard_map/ppermute | solution.py:27
  178.3 5.6 %collective-permute-start.13 = (bf16[8,2048]{1,0:T(8,128)(2,1)S(1)}, bf16[8,2048]{1,0:T(8,128)(2,1)S(1)}, u32[]{:S(2)}, u32[]{:S(2)}) collective-permute-start(bf16[8,2048]{1,0:T(8,128)(2,1)S(1)} %add.513), channel_id=1, source_target_pairs={{0,64},{4,68},{8,72},{12,76},{16,80},{20,84},{24,88},{28,92},{32,9... | collective-permute-start | bytes 98312 | tf_op jit(solution)/shard_map/ppermute | solution.py:27
  183.9 4.2 %collective-permute-start.14 = (bf16[8,2048]{1,0:T(8,128)(2,1)S(1)}, bf16[8,2048]{1,0:T(8,128)(2,1)S(1)}, u32[]{:S(2)}, u32[]{:S(2)}) collective-permute-start(bf16[8,2048]{1,0:T(8,128)(2,1)S(1)} %add.514), channel_id=1, source_target_pairs={{0,1},{1,0},{2,3},{3,2},{4,5},{5,4},{6,7},{7,6},{8,9},{9,8},{10,11... | collective-permute-start | bytes 98312 | tf_op jit(solution)/shard_map/ppermute | solution.py:27
  188.0 5.5 %collective-permute-start.15 = (bf16[8,2048]{1,0:T(8,128)(2,1)S(1)}, bf16[8,2048]{1,0:T(8,128)(2,1)S(1)}, u32[]{:S(2)}, u32[]{:S(2)}) collective-permute-start(bf16[8,2048]{1,0:T(8,128)(2,1)S(1)} %add.515), channel_id=1, source_target_pairs={{0,2},{1,3},{2,0},{3,1},{4,6},{5,7},{6,4},{7,5},{8,10},{9,11},{10,... | collective-permute-start | bytes 98312 | tf_op jit(solution)/shard_map/ppermute | solution.py:27
  (10 other events, 9.4 us)
Sparse Core Ops, SparseCore 0:
  136.6 111.3 all-reduce.2
